TPU v7x, 32 devices: a whole 2x2x4 slice. The times are simulated.
32 devices in a mesh: grp: 8 (over z, x), split: 4 (over y, core).
Axes of the slice: x: 2, y: 2, z: 4, core: 2. Of those that a mesh axis runs over, the one named last changes fastest.
Arguments:
- states: bfloat16 [12288, 4096], P(('grp', 'split'))
- weight: bfloat16 [4096, 1024], replicated, may hold values from -0.09375 to 0.09375
- cluster_id: int32 [12288], P(('grp', 'split')), may hold values from 0 to 31, as said below
- block: int32 [12288], P(('grp', 'split')), may hold values from 0 to 3
- order: int32 [12288], P(('grp', 'split')), may hold values from 0 to 12287, each once
Outputs:
- maxcos: float32 [12288], P(('grp', 'split'))
Inputs may be any that keep to these rules, and one draw needn't show every extreme that they name: Cluster c is owned by group c // 4; the pair (cluster_id // 4, block) names a device of the mesh; at most 24 documents of one device go to one such device, and in every draw some devices take exactly 24 documents from every device. `order`: distinct over all documents.
All inputs are finite; a program needn't handle non-finite values.
Results may differ from a plain program's by a relative error of at most 0.0003.
Values may be sent and summed in bfloat16 or wider, within the bound.
No kernel may reach another device: no remote copies, remote signals or barrier semaphores. Data moves between devices by JAX's collectives and lax.ppermute only.
A program may use at most 64 MiB of HBM per device.

v0:
```python
import jax
import jax.numpy as jnp
from jax import lax
from jax.sharding import PartitionSpec as P

CL_GRP = 4


EPS = 1e-06


def from_behind(block, axis, distance):
    devices = range(lax.axis_size(axis))
    route = [(i - distance, i) for i in devices if i - distance in devices]
    return lax.ppermute(block, axis, route)


def embed_rows(rows, weight):
    proj = jnp.einsum("...h,he->...e", rows, weight, preferred_element_type=jnp.float32)
    scale = lax.rsqrt(jnp.sum(proj * proj, axis=-1, keepdims=True) + EPS)
    return (proj * scale).astype(jnp.bfloat16)


def block_best(query_emb, query_lab, query_rank, keys):
    key_emb, key_lab, key_rank = keys
    scores = jnp.einsum("qe,ke->qk", query_emb, key_emb, preferred_element_type=jnp.float32)
    hits = (
        (query_lab[:, None] == key_lab[None, :])
        & (query_lab[:, None] > 0)
        & (key_rank[None, :] < query_rank[:, None])
    )
    return jnp.max(jnp.where(hits, scores, jnp.float32(-1.0)), axis=1)


def local(states, weight, cluster_id, block, order):
    n_doc = states.shape[0]
    n_grp = lax.axis_size("grp")
    n_split = lax.axis_size("split")
    n_dev = n_grp * n_split
    n_all = n_doc * n_dev
    cap = max(2, 2 * n_doc // n_dev)
    owner_of = cluster_id // CL_GRP
    target = owner_of * n_split + block
    onehot = (target[:, None] == jnp.arange(n_dev, dtype=jnp.int32)[None, :]).astype(jnp.float32)
    lower = (jnp.arange(n_doc)[:, None] > jnp.arange(n_doc)[None, :]).astype(jnp.float32)
    before = jnp.dot(lower, onehot, precision=lax.Precision.HIGHEST)
    slot = jnp.sum(before * onehot, axis=1).astype(jnp.int32)
    place = target * cap + slot
    rank = block * n_all + order
    label_buf = jnp.zeros((n_dev * cap,), jnp.int32).at[place].set(cluster_id + 1)
    rank_buf = jnp.zeros((n_dev * cap,), jnp.int32).at[place].set(rank)
    embeds = embed_rows(states, weight)
    row_buf = jnp.zeros((n_dev * cap, embeds.shape[1]), jnp.bfloat16).at[place].set(embeds)
    got, labels, ranks = (
        lax.all_to_all(
            row_buf.reshape(n_dev, cap, -1),
            ("grp", "split"),
            split_axis=0,
            concat_axis=0,
            tiled=True,
        ),
        lax.all_to_all(
            label_buf.reshape(n_dev, cap), ("grp", "split"), split_axis=0, concat_axis=0, tiled=True
        ),
        lax.all_to_all(
            rank_buf.reshape(n_dev, cap), ("grp", "split"), split_axis=0, concat_axis=0, tiled=True
        ),
    )
    query_emb = got.reshape(n_dev * cap, -1)
    query_lab = labels.reshape(-1)
    query_rank = ranks.reshape(-1)
    best = jnp.full((n_dev * cap,), -1.0, jnp.float32)
    keys = (query_emb, query_lab, query_rank)
    for step in range(n_split):
        if step > 0:
            keys = from_behind((keys[0], keys[1], keys[2]), "split", 1)
        best = jnp.maximum(best, block_best(query_emb, query_lab, query_rank, keys))
    returned = lax.all_to_all(
        best.reshape(n_dev, cap), ("grp", "split"), split_axis=0, concat_axis=0, tiled=True
    )
    return returned.reshape(-1)[place]


def solution(mesh):
    in_specs = (
        P(("grp", "split"), None),
        P(),
        P(("grp", "split")),
        P(("grp", "split")),
        P(("grp", "split")),
    )
    out_specs = P(("grp", "split"))
    return jax.shard_map(local, mesh=mesh, in_specs=in_specs, out_specs=out_specs, check_vma=False)
```

profile of v0, /device:TPU:0, one launch (start us, length us, event | category | flops | bytes accessed | tf_op | source)
XLA Modules:
  0.0 175.2 jit_solution(16048926873169510573)
XLA Ops:
  0.0 0.9 broadcast_add_fusion
  1.1 0.8 copy-done
  1.9 7.1 %multiply_reduce_fusion = (f32[384]{0:T(512)S(1)}, f32[384,1024]{1,0:T(8,128)}) fusion(bf16[384,4096]{1,0:T(8,128)(2,1)S(1)} %copy-done, bf16[4096,1024]{1,0:T(8,128)(2,1)} %param.6), kind=kOutput, calls=%fused_computation.9 | convolution fusion | flops 3222011392 | bytes 13108736 | tf_op jit(solution)/shard_map/...h,he->...e/dot_general | solution.py:19
  9.1 4.3 %scatter_custom_fusion.2 = bf16[768,1024]{1,0:T(8,128)(2,1)} fusion(s32[384]{0:T(512)S(1)} %compare_select_fusion, f32[384,1024]{1,0:T(8,128)} %get-tuple-element.12, f32[384]{0:T(512)S(1)} %add_rsqrt_fusion, bf16[]{:T(256)} %constant.36.clone.1), kind=kCustom, calls=%fused_computation.12 | custom fusion | flops 786432 | bytes 3147778 | tf_op jit(solution)/shard_map/scatter | solution.py:53
  13.4 45.3 %all_to_all.29 = bf16[32,24,1024]{2,1,0:T(8,128)(2,1)S(1)} all-to-all(bf16[32,24,1024]{2,1,0:T(8,128)(2,1)} %bitcast.15), channel_id=1, replica_groups=mesh['grp'=8,'split'=4] {'grp','split'}, dimensions={0} | all-to-all | bytes 3145728 | tf_op jit(solution)/shard_map/all_to_all | solution.py:55
  58.7 1.2 copy-done.1
  59.8 1.9 %collective-permute-start.2 = (bf16[768,1024]{1,0:T(8,128)(2,1)S(1)}, bf16[768,1024]{1,0:T(8,128)(2,1)S(1)}, u32[]{:S(2)}, u32[]{:S(2)}) collective-permute-start(bf16[768,1024]{1,0:T(8,128)(2,1)S(1)} %bitcast.16), channel_id=1, source_target_pairs={{0,1},{1,2},{2,3},{4,5},{5,6},{6,7},{8,9},{9,10},{10,11},{12,13},{... | collective-permute-start | bytes 4718600 | tf_op jit(solution)/shard_map/ppermute | solution.py:15
  61.7 2.9 %collective-permute-done.2 = bf16[768,1024]{1,0:T(8,128)(2,1)S(1)} collective-permute-done((bf16[768,1024]{1,0:T(8,128)(2,1)S(1)}, bf16[768,1024]{1,0:T(8,128)(2,1)S(1)}, u32[]{:S(2)}, u32[]{:S(2)}) %collective-permute-start.2) | collective-permute-done | bytes 1572896 | tf_op jit(solution)/shard_map/ppermute | solution.py:15
  64.7 18.6 %collective-permute-start.5 = (bf16[768,1024]{1,0:T(8,128)(2,1)S(1)}, bf16[768,1024]{1,0:T(8,128)(2,1)}, u32[]{:S(2)}, u32[]{:S(2)}) collective-permute-start(bf16[768,1024]{1,0:T(8,128)(2,1)S(1)} %collective-permute-done.2), channel_id=1, source_target_pairs={{0,1},{1,2},{2,3},{4,5},{5,6},{6,7},{8,9},{9,10},{10,11},{12,13},{... | collective-permute-start | bytes 4718600 | tf_op jit(solution)/shard_map/ppermute | solution.py:15
  83.2 2.0 %collective-permute-done.5 = bf16[768,1024]{1,0:T(8,128)(2,1)} collective-permute-done((bf16[768,1024]{1,0:T(8,128)(2,1)S(1)}, bf16[768,1024]{1,0:T(8,128)(2,1)}, u32[]{:S(2)}, u32[]{:S(2)}) %collective-permute-start.5) | collective-permute-done | bytes 1572896 | tf_op jit(solution)/shard_map/ppermute | solution.py:15
  85.2 19.7 %collective-permute-start.8 = (bf16[768,1024]{1,0:T(8,128)(2,1)}, bf16[768,1024]{1,0:T(8,128)(2,1)}, u32[]{:S(2)}, u32[]{:S(2)}) collective-permute-start(bf16[768,1024]{1,0:T(8,128)(2,1)} %collective-permute-done.5), channel_id=1, source_target_pairs={{0,1},{1,2},{2,3},{4,5},{5,6},{6,7},{8,9},{9,10},{10,11},{12,13},{... | collective-permute-start | bytes 4718600 | tf_op jit(solution)/shard_map/ppermute | solution.py:15
  105.0 2.9 %scatter_custom_fusion = s32[768]{0:T(1024)S(1)} fusion(s32[384]{0:T(512)S(1)} %compare_select_fusion, s32[384]{0:T(512)S(1)} %get-tuple-element.8, s32[]{:T(128)} %constant.14.clone.1), kind=kCustom, calls=%fused_computation.34 | custom fusion | bytes 3076 | tf_op jit(solution)/shard_map/scatter | solution.py:50
  108.6 3.7 %all-to-all-start = ((s32[32,1,24]{2,1,0:T(1,128)}), s32[32,1,24]{2,1,0:T(1,128)S(1)}, u32[]{:S(2)}, u32[]{:S(2)}) async-start(s32[32,1,24]{2,1,0:T(1,128)} %bitcast), calls=%async_computation | async-start | bytes 32768 | tf_op jit(solution)/shard_map/all_to_all | solution.py:62
  112.3 2.9 %scatter_custom_fusion.1 = s32[768]{0:T(1024)S(1)} fusion(s32[384]{0:T(512)S(1)} %compare_select_fusion, s32[384]{0:T(512)S(1)} %get-tuple-element.10, s32[]{:T(128)} %constant.14.clone.1), kind=kCustom, calls=%fused_computation.31 | custom fusion | bytes 3076 | tf_op jit(solution)/shard_map/scatter | solution.py:51
  115.9 3.5 %all-to-all-done = s32[32,1,24]{2,1,0:T(1,128)S(1)} async-done(((s32[32,1,24]{2,1,0:T(1,128)}), s32[32,1,24]{2,1,0:T(1,128)S(1)}, u32[]{:S(2)}, u32[]{:S(2)}) %all-to-all-start) | async-done | bytes 3104 | tf_op jit(solution)/shard_map/all_to_all | solution.py:62
  119.4 9.2 %all-to-all-start.1 = ((s32[32,1,24]{2,1,0:T(1,128)}), s32[32,1,24]{2,1,0:T(1,128)S(1)}, u32[]{:S(2)}, u32[]{:S(2)}) async-start(s32[32,1,24]{2,1,0:T(1,128)} %bitcast.1), calls=%async_computation.1 | async-start | bytes 32768 | tf_op jit(solution)/shard_map/all_to_all | solution.py:65
  130.0 2.2 %collective-permute-start = (s32[768]{0:T(1024)S(1)}, s32[768]{0:T(1024)S(1)}, u32[]{:S(2)}, u32[]{:S(2)}) collective-permute-start(s32[768]{0:T(1024)S(1)} %eq.29), channel_id=1, source_target_pairs={{0,1},{1,2},{2,3},{4,5},{5,6},{6,7},{8,9},{9,10},{10,11},{12,13},{... | collective-permute-start | bytes 9224 | tf_op jit(solution)/shard_map/ppermute | solution.py:15
  132.1 3.7 %all-to-all-done.1 = s32[32,1,24]{2,1,0:T(1,128)S(1)} async-done(((s32[32,1,24]{2,1,0:T(1,128)}), s32[32,1,24]{2,1,0:T(1,128)S(1)}, u32[]{:S(2)}, u32[]{:S(2)}) %all-to-all-start.1) | async-done | bytes 3104 | tf_op jit(solution)/shard_map/all_to_all | solution.py:65
  135.8 0.7 reduce.9
  136.6 1.8 %collective-permute-start.1 = (s32[768]{0:T(1024)S(1)}, s32[768]{0:T(1024)S(1)}, u32[]{:S(2)}, u32[]{:S(2)}) collective-permute-start(s32[768]{0:T(1024)S(1)} %lt.23), channel_id=1, source_target_pairs={{0,1},{1,2},{2,3},{4,5},{5,6},{6,7},{8,9},{9,10},{10,11},{12,13},{... | collective-permute-start | bytes 9224 | tf_op jit(solution)/shard_map/ppermute | solution.py:15
  138.4 2.7 %collective-permute-start.3 = (s32[768]{0:T(1024)S(1)}, s32[768]{0:T(1024)S(1)}, u32[]{:S(2)}, u32[]{:S(2)}) collective-permute-start(s32[768]{0:T(1024)S(1)} %collective-permute-done), channel_id=1, source_target_pairs={{0,1},{1,2},{2,3},{4,5},{5,6},{6,7},{8,9},{9,10},{10,11},{12,13},{... | collective-permute-start | bytes 9224 | tf_op jit(solution)/shard_map/ppermute | solution.py:15
  141.1 1.9 %collective-permute-start.4 = (s32[768]{0:T(1024)S(1)}, s32[768]{0:T(1024)S(1)}, u32[]{:S(2)}, u32[]{:S(2)}) collective-permute-start(s32[768]{0:T(1024)S(1)} %collective-permute-done.1), channel_id=1, source_target_pairs={{0,1},{1,2},{2,3},{4,5},{5,6},{6,7},{8,9},{9,10},{10,11},{12,13},{... | collective-permute-start | bytes 9224 | tf_op jit(solution)/shard_map/ppermute | solution.py:15
  143.1 3.2 %collective-permute-start.6 = (s32[768]{0:T(1024)S(1)}, s32[768]{0:T(1024)S(1)}, u32[]{:S(2)}, u32[]{:S(2)}) collective-permute-start(s32[768]{0:T(1024)S(1)} %collective-permute-done.3), channel_id=1, source_target_pairs={{0,1},{1,2},{2,3},{4,5},{5,6},{6,7},{8,9},{9,10},{10,11},{12,13},{... | collective-permute-start | bytes 9224 | tf_op jit(solution)/shard_map/ppermute | solution.py:15
  146.3 2.1 %collective-permute-start.7 = (s32[768]{0:T(1024)S(1)}, s32[768]{0:T(1024)S(1)}, u32[]{:S(2)}, u32[]{:S(2)}) collective-permute-start(s32[768]{0:T(1024)S(1)} %collective-permute-done.4), channel_id=1, source_target_pairs={{0,1},{1,2},{2,3},{4,5},{5,6},{6,7},{8,9},{9,10},{10,11},{12,13},{... | collective-permute-start | bytes 9224 | tf_op jit(solution)/shard_map/ppermute | solution.py:15
  148.4 3.6 %select_reduce_fusion.3 = f32[768]{0:T(1024)S(1)} fusion(bf16[768,1024]{1,0:T(8,128)(2,1)} %bitcast.17, s32[768]{0:T(1024)S(1)} %lt.23, s32[768]{0:T(1024)S(1)} %eq.29, pred[768]{0:T(1024)(128)(4,1)S(1)} %broadcast_compare_fusion), kind=kOutput, calls=%fused_computation.7 | convolution fusion | flops 1211497728 | bytes 1582848 | tf_op jit(solution)/shard_map/qe,ke->qk/dot_general | solution.py:26
  152.0 1.4 fusion.13
  153.5 2.8 %fusion.14 = f32[768,768]{0,1:T(8,128)S(1)} fusion(bf16[768,1024]{1,0:T(8,128)(2,1)S(1)} %bitcast.19, bf16[768,1024]{1,0:T(8,128)(2,1)} %collective-permute-done.5), kind=kOutput, calls=%fused_computation.39 | convolution fusion | flops 1207959552 | bytes 5505024 | tf_op jit(solution)/shard_map/qe,ke->qk/dot_general | solution.py:26
  156.3 4.1 %select_reduce_fusion.2 = (f32[768]{0:T(1024)S(1)}, f32[768]{0:T(1024)S(1)}, f32[768]{0:T(1024)S(1)}) fusion(f32[768,768]{0,1:T(8,128)S(1)} %fusion.13, s32[768]{0:T(1024)S(1)} %lt.23, s32[768]{0:T(1024)S(1)} %eq.29, s32[768]{0:T(1024)S(1)} %collective-permute-done.1, s32[768]{0:T(1024)S(1)} %collective-permute-done, ...), kind=kOutput, calls=%fused_computation.6 | convolution fusion | flops 1218574080 | bytes 7898880 | tf_op jit(solution)/shard_map/qe,ke->qk/dot_general | solution.py:26
  161.2 2.6 %all-to-all-start.3 = ((f32[32,1,24]{2,1,0:T(1,128)}), f32[32,1,24]{2,1,0:T(1,128)S(1)}, u32[]{:S(2)}, u32[]{:S(2)}) async-start(f32[32,1,24]{2,1,0:T(1,128)} %bitcast.4), calls=%async_computation.3 | async-start | bytes 32768 | tf_op jit(solution)/shard_map/all_to_all | solution.py:78
  163.8 7.1 %all-to-all-done.3 = f32[32,1,24]{2,1,0:T(1,128)S(1)} async-done(((f32[32,1,24]{2,1,0:T(1,128)}), f32[32,1,24]{2,1,0:T(1,128)S(1)}, u32[]{:S(2)}, u32[]{:S(2)}) %all-to-all-start.3) | async-done | bytes 3104 | tf_op jit(solution)/shard_map/all_to_all | solution.py:78
  171.4 0.7 reduce.11
  172.2 3.0 %gather_fusion = f32[384]{0:T(512)} fusion(f32[768]{0:T(1024)S(1)} %reshape.105, s32[1024]{0:T(1024)S(1)} %pad_clamp_fusion), kind=kCustom, calls=%fused_computation | custom fusion | bytes 4608 | tf_op jit(solution)/shard_map/gather | solution.py:81
  (30 shorter events, 4.3 us)
Async XLA Ops:
  0.0 1.9 %copy-start = (bf16[384,4096]{1,0:T(8,128)(2,1)S(1)}, bf16[384,4096]{1,0:T(8,128)(2,1)}, u32[]{:S(2)}) copy-start(bf16[384,4096]{1,0:T(8,128)(2,1)} %param.5) | copy-start | bytes 9437188
  58.7 1.2 copy-start.1
  59.8 4.8 %collective-permute-start.2 = (bf16[768,1024]{1,0:T(8,128)(2,1)S(1)}, bf16[768,1024]{1,0:T(8,128)(2,1)S(1)}, u32[]{:S(2)}, u32[]{:S(2)}) collective-permute-start(bf16[768,1024]{1,0:T(8,128)(2,1)S(1)} %bitcast.16), channel_id=1, source_target_pairs={{0,1},{1,2},{2,3},{4,5},{5,6},{6,7},{8,9},{9,10},{10,11},{12,13},{... | collective-permute-start | bytes 4718600 | tf_op jit(solution)/shard_map/ppermute | solution.py:15
  64.7 40.3 %copy-start.3 = (bf16[768,1024]{1,0:T(8,128)(2,1)}, bf16[768,1024]{1,0:T(8,128)(2,1)S(1)}, u32[]{:S(2)}) copy-start(bf16[768,1024]{1,0:T(8,128)(2,1)S(1)} %collective-permute-done.2) | copy-start | bytes 4718596
  64.7 20.6 %collective-permute-start.5 = (bf16[768,1024]{1,0:T(8,128)(2,1)S(1)}, bf16[768,1024]{1,0:T(8,128)(2,1)}, u32[]{:S(2)}, u32[]{:S(2)}) collective-permute-start(bf16[768,1024]{1,0:T(8,128)(2,1)S(1)} %collective-permute-done.2), channel_id=1, source_target_pairs={{0,1},{1,2},{2,3},{4,5},{5,6},{6,7},{8,9},{9,10},{10,11},{12,13},{... | collective-permute-start | bytes 4718600 | tf_op jit(solution)/shard_map/ppermute | solution.py:15
  85.2 71.1 %collective-permute-start.8 = (bf16[768,1024]{1,0:T(8,128)(2,1)}, bf16[768,1024]{1,0:T(8,128)(2,1)}, u32[]{:S(2)}, u32[]{:S(2)}) collective-permute-start(bf16[768,1024]{1,0:T(8,128)(2,1)} %collective-permute-done.5), channel_id=1, source_target_pairs={{0,1},{1,2},{2,3},{4,5},{5,6},{6,7},{8,9},{9,10},{10,11},{12,13},{... | collective-permute-start | bytes 4718600 | tf_op jit(solution)/shard_map/ppermute | solution.py:15
  108.6 10.9 %all-to-all-start = ((s32[32,1,24]{2,1,0:T(1,128)}), s32[32,1,24]{2,1,0:T(1,128)S(1)}, u32[]{:S(2)}, u32[]{:S(2)}) async-start(s32[32,1,24]{2,1,0:T(1,128)} %bitcast), calls=%async_computation | async-start | bytes 32768 | tf_op jit(solution)/shard_map/all_to_all | solution.py:62
  119.4 16.4 %all-to-all-start.1 = ((s32[32,1,24]{2,1,0:T(1,128)}), s32[32,1,24]{2,1,0:T(1,128)S(1)}, u32[]{:S(2)}, u32[]{:S(2)}) async-start(s32[32,1,24]{2,1,0:T(1,128)} %bitcast.1), calls=%async_computation.1 | async-start | bytes 32768 | tf_op jit(solution)/shard_map/all_to_all | solution.py:65
  130.0 8.4 %collective-permute-start = (s32[768]{0:T(1024)S(1)}, s32[768]{0:T(1024)S(1)}, u32[]{:S(2)}, u32[]{:S(2)}) collective-permute-start(s32[768]{0:T(1024)S(1)} %eq.29), channel_id=1, source_target_pairs={{0,1},{1,2},{2,3},{4,5},{5,6},{6,7},{8,9},{9,10},{10,11},{12,13},{... | collective-permute-start | bytes 9224 | tf_op jit(solution)/shard_map/ppermute | solution.py:15
  136.6 4.5 %collective-permute-start.1 = (s32[768]{0:T(1024)S(1)}, s32[768]{0:T(1024)S(1)}, u32[]{:S(2)}, u32[]{:S(2)}) collective-permute-start(s32[768]{0:T(1024)S(1)} %lt.23), channel_id=1, source_target_pairs={{0,1},{1,2},{2,3},{4,5},{5,6},{6,7},{8,9},{9,10},{10,11},{12,13},{... | collective-permute-start | bytes 9224 | tf_op jit(solution)/shard_map/ppermute | solution.py:15
  138.4 4.7 %collective-permute-start.3 = (s32[768]{0:T(1024)S(1)}, s32[768]{0:T(1024)S(1)}, u32[]{:S(2)}, u32[]{:S(2)}) collective-permute-start(s32[768]{0:T(1024)S(1)} %collective-permute-done), channel_id=1, source_target_pairs={{0,1},{1,2},{2,3},{4,5},{5,6},{6,7},{8,9},{9,10},{10,11},{12,13},{... | collective-permute-start | bytes 9224 | tf_op jit(solution)/shard_map/ppermute | solution.py:15
  141.1 5.2 %collective-permute-start.4 = (s32[768]{0:T(1024)S(1)}, s32[768]{0:T(1024)S(1)}, u32[]{:S(2)}, u32[]{:S(2)}) collective-permute-start(s32[768]{0:T(1024)S(1)} %collective-permute-done.1), channel_id=1, source_target_pairs={{0,1},{1,2},{2,3},{4,5},{5,6},{6,7},{8,9},{9,10},{10,11},{12,13},{... | collective-permute-start | bytes 9224 | tf_op jit(solution)/shard_map/ppermute | solution.py:15
  143.1 9.0 %copy-start.2 = (bf16[32,24,1024]{2,1,0:T(8,128)(2,1)S(1)}, bf16[32,24,1024]{2,1,0:T(8,128)(2,1)}, u32[]{:S(2)}) copy-start(bf16[32,24,1024]{2,1,0:T(8,128)(2,1)} %copy-done.1) | copy-start | bytes 4718596
  143.1 9.0 %copy-start.4 = (bf16[768,1024]{1,0:T(8,128)(2,1)S(1)}, bf16[768,1024]{1,0:T(8,128)(2,1)}, u32[]{:S(2)}) copy-start(bf16[768,1024]{1,0:T(8,128)(2,1)} %copy-done.3) | copy-start | bytes 4718596
  143.1 13.2 %collective-permute-start.6 = (s32[768]{0:T(1024)S(1)}, s32[768]{0:T(1024)S(1)}, u32[]{:S(2)}, u32[]{:S(2)}) collective-permute-start(s32[768]{0:T(1024)S(1)} %collective-permute-done.3), channel_id=1, source_target_pairs={{0,1},{1,2},{2,3},{4,5},{5,6},{6,7},{8,9},{9,10},{10,11},{12,13},{... | collective-permute-start | bytes 9224 | tf_op jit(solution)/shard_map/ppermute | solution.py:15
  146.3 10.0 %collective-permute-start.7 = (s32[768]{0:T(1024)S(1)}, s32[768]{0:T(1024)S(1)}, u32[]{:S(2)}, u32[]{:S(2)}) collective-permute-start(s32[768]{0:T(1024)S(1)} %collective-permute-done.4), channel_id=1, source_target_pairs={{0,1},{1,2},{2,3},{4,5},{5,6},{6,7},{8,9},{9,10},{10,11},{12,13},{... | collective-permute-start | bytes 9224 | tf_op jit(solution)/shard_map/ppermute | solution.py:15
  161.2 9.7 %all-to-all-start.3 = ((f32[32,1,24]{2,1,0:T(1,128)}), f32[32,1,24]{2,1,0:T(1,128)S(1)}, u32[]{:S(2)}, u32[]{:S(2)}) async-start(f32[32,1,24]{2,1,0:T(1,128)} %bitcast.4), calls=%async_computation.3 | async-start | bytes 32768 | tf_op jit(solution)/shard_map/all_to_all | solution.py:78
where the time goes:
time: 176 us; the launch traced here: 175 us
  starting transfers between devices  69.5 us (39%)
  blocking collectives  45.3 us (26%)
  matrix products  19.3 us (11%)
  waiting for transfers between devices  19.3 us (11%)
  local copies, waits for them, and re-layouts  14.2 us (8%)
  other arithmetic  7.28 us (4%)
    ppermute x9, starting transfers between devices, from_behind(): return lax.ppermute(block, axis, route)  54.1 us
    all_to_all x1, blocking collectives, local(): lax.all_to_all(row_buf.reshape(n_dev, cap, -1), ('grp', 'split'), split_a...  45.3 us
    dot_general x4, matrix products, block_best(): jnp.einsum('qe,ke->qk', query_emb, key_emb, preferred_element_type=jnp.fl...  12 us
    all_to_all x1, starting transfers between devices, local(): lax.all_to_all(rank_buf.reshape(n_dev, cap), ('grp', 'split'), split_axis...  9.23 us
    all_to_all x1, waiting for transfers between devices, local(): lax.all_to_all(best.reshape(n_dev, cap), ('grp', 'split'), split_axis=0,...  7.13 us
    dot_general x1, matrix products, embed_rows(): jnp.einsum('...h,he->...e', rows, weight, preferred_element_type=jnp.floa...  7.11 us
    ppermute x9, waiting for transfers between devices, from_behind(): return lax.ppermute(block, axis, route)  4.95 us
    scatter x1, other arithmetic, local(): jnp.zeros((n_dev * cap, embeds.shape[1]), jnp.bfloat16).at[place]  4.31 us
  transfers between devices with their start and end apart: 12, of which 5 were waited for; matrix products, arithmetic and copies ran while one was open for 9% of the time, Pallas kernels for 0%

commit v1 on v0

v1 whole, which is shorter than its diff:
```python
import jax
import jax.numpy as jnp
from jax import lax
from jax.sharding import PartitionSpec as P

CL_GRP = 4


EPS = 1e-06
META = 128


def embed_rows(rows, weight):
    proj = jnp.einsum("...h,he->...e", rows, weight, preferred_element_type=jnp.float32)
    scale = lax.rsqrt(jnp.sum(proj * proj, axis=-1, keepdims=True) + EPS)
    return (proj * scale).astype(jnp.bfloat16)


def shift_keys(keys, n_split):
    if n_split == 4:
        up = lax.ppermute(keys, "split", [(0, 2), (1, 3)])
        near = lax.ppermute(keys, "split", [(0, 1), (2, 3)])
        swap = lax.ppermute(up, "split", [(2, 3), (3, 2)])
        return [up, near, swap]
    out = []
    for d in range(1, n_split):
        route = [(i - d, i) for i in range(d, n_split)]
        out.append(lax.ppermute(keys, "split", route))
    return out


def unpack(buf, emb_w):
    emb = buf[:, :emb_w]
    lab = buf[:, emb_w].astype(jnp.float32)
    order = buf[:, emb_w + 1].astype(jnp.float32) * 256.0 + buf[:, emb_w + 2].astype(jnp.float32)
    return emb, lab, order


def local(states, weight, cluster_id, block, order):
    n_doc = states.shape[0]
    n_grp = lax.axis_size("grp")
    n_split = lax.axis_size("split")
    n_dev = n_grp * n_split
    cap = max(2, 2 * n_doc // n_dev)
    n_slot = n_dev * cap
    owner_of = cluster_id // CL_GRP
    target = owner_of * n_split + block
    onehot = (target[:, None] == jnp.arange(n_dev, dtype=jnp.int32)[None, :]).astype(jnp.bfloat16)
    lower = (jnp.arange(n_doc)[:, None] > jnp.arange(n_doc)[None, :]).astype(jnp.bfloat16)
    before = jnp.dot(lower, onehot, preferred_element_type=jnp.float32)
    slot = jnp.sum(before * onehot.astype(jnp.float32), axis=1).astype(jnp.int32)
    place = target * cap + slot

    embeds = embed_rows(states, weight)
    emb_w = embeds.shape[1]
    label = (cluster_id - owner_of * CL_GRP + 1).astype(jnp.float32)
    meta_cols = jnp.stack(
        [label, (order // 256).astype(jnp.float32), (order % 256).astype(jnp.float32)], axis=1
    )
    meta = jnp.concatenate(
        [meta_cols, jnp.zeros((n_doc, META - meta_cols.shape[1]), jnp.float32)], axis=1
    ).astype(jnp.bfloat16)
    rows = jnp.concatenate([embeds, meta], axis=1)
    pick = place[None, :] == jnp.arange(n_slot, dtype=jnp.int32)[:, None]
    send = jnp.dot(pick.astype(jnp.bfloat16), rows, preferred_element_type=jnp.float32).astype(
        jnp.bfloat16
    )
    got = lax.all_to_all(
        send.reshape(n_dev, cap, -1), ("grp", "split"), split_axis=0, concat_axis=0, tiled=True
    ).reshape(n_slot, -1)

    q_emb, q_lab, q_ord = unpack(got, emb_w)
    scores = jnp.einsum("qe,ke->qk", q_emb, q_emb, preferred_element_type=jnp.float32)
    hits = (q_lab[:, None] == q_lab[None, :]) & (q_lab[None, :] > 0) & (q_ord[None, :] < q_ord[:, None])
    best = jnp.max(jnp.where(hits, scores, jnp.float32(-1.0)), axis=1)
    for keys in shift_keys(got, n_split):
        k_emb, k_lab, _ = unpack(keys, emb_w)
        scores = jnp.einsum("qe,ke->qk", q_emb, k_emb, preferred_element_type=jnp.float32)
        hits = (q_lab[:, None] == k_lab[None, :]) & (k_lab[None, :] > 0)
        best = jnp.maximum(best, jnp.max(jnp.where(hits, scores, jnp.float32(-1.0)), axis=1))

    returned = lax.all_to_all(
        best.reshape(n_dev, cap), ("grp", "split"), split_axis=0, concat_axis=0, tiled=True
    ).reshape(n_slot)
    return jnp.max(jnp.where(pick, returned[:, None], -jnp.inf), axis=0)


def solution(mesh):
    in_specs = (
        P(("grp", "split"), None),
        P(),
        P(("grp", "split")),
        P(("grp", "split")),
        P(("grp", "split")),
    )
    out_specs = P(("grp", "split"))
    return jax.shard_map(local, mesh=mesh, in_specs=in_specs, out_specs=out_specs, check_vma=False)
```

time: 176 us -> 127 us (0.72)
  starting transfers between devices: 69.5 us -> 6.22 us
  waiting for transfers between devices: 19.3 us -> 35.8 us
  blocking collectives: 45.3 us -> 61.5 us
  local copies, waits for them, and re-layouts: 14.2 us -> 4.97 us
  matrix products: 19.3 us -> 14.6 us
  other arithmetic: 7.28 us -> 3.39 us
    ppermute x9 -> x3, starting transfers between devices: 54.1 us -> 6.22 us  [the longest x1 3.53 us: shift_keys(): up = lax.ppermute(keys, 'split', [(0, 2), (1, 3)])]
    ppermute x9 -> x3, waiting for transfers between devices: 4.95 us -> 35.8 us  [the longest x1 35.8 us: shift_keys(): up = lax.ppermute(keys, 'split', [(0, 2), (1, 3)])]
    all_to_all x1 -> x2, blocking collectives: 45.3 us -> 61.5 us  [the longest x1 48.8 us: local(): lax.all_to_all(send.reshape(n_dev, cap, -1), ('grp', 'split'), split_axis...]
    all_to_all x3 -> x0, starting transfers between devices: 15.5 us -> none  [the longest x1 9.23 us: local(): lax.all_to_all(rank_buf.reshape(n_dev, cap), ('grp', 'split'), split_axis...]
    all_to_all x3 -> x0, waiting for transfers between devices: 14.4 us -> none  [the longest x1 7.13 us: local(): lax.all_to_all(best.reshape(n_dev, cap), ('grp', 'split'), split_axis=0,...]
    scatter x2 -> x0, local copies, waits for them, and re-layouts: 5.84 us -> none  [the longest x1 2.92 us: local(): rank_buf = jnp.zeros((n_dev * cap,), jnp.int32).at[place].set(rank)]
    scatter x1 -> x0, other arithmetic: 4.31 us -> none  [local(): jnp.zeros((n_dev * cap, embeds.shape[1]), jnp.bfloat16).at[place]]
    dot_general x5 -> x6, matrix products: 12.2 us -> 8.64 us  [the longest x3 4.57 us: local(): jnp.einsum('qe,ke->qk', q_emb, k_emb, preferred_element_type=jnp.float32)]
  transfers between devices with their start and end apart: 12 -> 3, of which waited for: 5 -> 1; matrix products, arithmetic and copies ran while one was open for 9% -> 4% of each run, Pallas kernels for 0% -> 0%
where the time goes in v1:
time: 127 us
  blocking collectives  61.5 us (48%)
  waiting for transfers between devices  35.8 us (28%)
  matrix products  14.6 us (11%)
  starting transfers between devices  6.22 us (5%)
  local copies, waits for them, and re-layouts  4.97 us (4%)
  other arithmetic  3.39 us (3%)
    all_to_all x1, blocking collectives, local(): lax.all_to_all(send.reshape(n_dev, cap, -1), ('grp', 'split'), split_axis...  48.8 us
    ppermute x1, waiting for transfers between devices, shift_keys(): up = lax.ppermute(keys, 'split', [(0, 2), (1, 3)])  35.8 us
    all_to_all x1, blocking collectives, local(): lax.all_to_all(best.reshape(n_dev, cap), ('grp', 'split'), split_axis=0,...  12.7 us
    dot_general x1, matrix products, embed_rows(): jnp.einsum('...h,he->...e', rows, weight, preferred_element_type=jnp.floa...  5.95 us
    dot_general x3, matrix products, local(): jnp.einsum('qe,ke->qk', q_emb, k_emb, preferred_element_type=jnp.float32)  4.57 us
    ppermute x1, starting transfers between devices, shift_keys(): up = lax.ppermute(keys, 'split', [(0, 2), (1, 3)])  3.53 us
  transfers between devices with their start and end apart: 3, of which 1 were waited for; matrix products, arithmetic and copies ran while one was open for 4% of the time, Pallas kernels for 0%

profile of v1, /device:TPU:0, one launch (start us, length us, event | category | flops | bytes accessed | tf_op | source)
XLA Modules:
  0.0 126.6 jit_solution(1824492863414018531)
XLA Ops:
  0.0 0.0 copy-start
  0.0 1.9 %copy-done = bf16[384,4096]{1,0:T(8,128)(2,1)S(1)} copy-done((bf16[384,4096]{1,0:T(8,128)(2,1)S(1)}, bf16[384,4096]{1,0:T(8,128)(2,1)}, u32[]{:S(2)}) %copy-start) | copy-done | bytes 3145752
  1.9 5.9 %multiply_reduce_fusion = (f32[384]{0:T(512)S(1)}, f32[384,1024]{1,0:T(8,128)S(1)}) fusion(bf16[384,4096]{1,0:T(8,128)(2,1)S(1)} %copy-done, bf16[4096,1024]{1,0:T(8,128)(2,1)} %param.6), kind=kOutput, calls=%fused_computation.12 | convolution fusion | flops 3222011392 | bytes 13108736 | tf_op jit(solution)/shard_map/...h,he->...e/dot_general | solution.py:14
  7.9 0.0 copy-done.1
  7.9 0.1 stack.15
  8.1 0.1 stack.16
  8.2 0.1 stack.17
  8.3 0.2 fusion.12
  8.5 1.0 multiply_convert_fusion
  9.6 2.1 %concatenate.6 = bf16[384,1152]{1,0:T(8,128)(2,1)} concatenate(bf16[384,1024]{1,0:T(8,128)(2,1)} %multiply_convert_fusion, bf16[384,1]{1,0:T(8,128)(2,1)S(1)} %stack.15, bf16[384,1]{1,0:T(8,128)(2,1)S(1)} %stack.16, bf16[384,1]{1,0:T(8,128)(2,1)S(1)} %stack.17, bf16[384,125]{1,0:T(8,128)(2,1)S(1)} %broadcast_in_dim.19), dimensions={1} | concatenate | bytes 1769472 | tf_op jit(solution)/shard_map/concatenate | solution.py:63
  11.6 2.3 %convolution_convert_fusion = bf16[768,1152]{1,0:T(8,128)(2,1)S(1)} fusion(bf16[384,1152]{1,0:T(8,128)(2,1)} %concatenate.6, s32[384]{0:T(512)S(1)} %convert_add_fusion), kind=kOutput, calls=%fused_computation | convolution fusion | flops 680656896 | bytes 2655744 | tf_op jit(solution)/shard_map/dot_general | solution.py:65
  13.9 48.8 %all_to_all.11 = bf16[32,24,1152]{2,1,0:T(8,128)(2,1)S(1)} all-to-all(bf16[32,24,1152]{2,1,0:T(8,128)(2,1)S(1)} %bitcast.13), channel_id=1, replica_groups=mesh['grp'=8,'split'=4] {'grp','split'}, dimensions={0} | all-to-all | bytes 3538944 | tf_op jit(solution)/shard_map/all_to_all | solution.py:68
  62.7 3.5 %collective-permute-start = (bf16[768,1152]{1,0:T(8,128)(2,1)S(1)}, bf16[768,1152]{1,0:T(8,128)(2,1)S(1)}, u32[]{:S(2)}, u32[]{:S(2)}) collective-permute-start(bf16[768,1152]{1,0:T(8,128)(2,1)S(1)} %bitcast.6), channel_id=1, source_target_pairs={{0,2},{1,3},{4,6},{5,7},{8,10},{9,11},{12,14},{13,15},{16,18},{17,... | collective-permute-start | bytes 5308424 | tf_op jit(solution)/shard_map/ppermute | solution.py:21
  66.2 1.9 %collective-permute-start.1 = (bf16[768,1152]{1,0:T(8,128)(2,1)S(1)}, bf16[768,1152]{1,0:T(8,128)(2,1)S(1)}, u32[]{:S(2)}, u32[]{:S(2)}) collective-permute-start(bf16[768,1152]{1,0:T(8,128)(2,1)S(1)} %bitcast.7), channel_id=1, source_target_pairs={{0,1},{2,3},{4,5},{6,7},{8,9},{10,11},{12,13},{14,15},{16,17},{18,... | collective-permute-start | bytes 5308424 | tf_op jit(solution)/shard_map/ppermute | solution.py:22
  68.2 0.4 add_reduce_fusion
  68.6 35.8 %collective-permute-done = bf16[768,1152]{1,0:T(8,128)(2,1)S(1)} collective-permute-done((bf16[768,1152]{1,0:T(8,128)(2,1)S(1)}, bf16[768,1152]{1,0:T(8,128)(2,1)S(1)}, u32[]{:S(2)}, u32[]{:S(2)}) %collective-permute-start) | collective-permute-done | bytes 1769504 | tf_op jit(solution)/shard_map/ppermute | solution.py:21
  104.3 0.8 collective-permute-start.2
  105.1 1.6 %select_reduce_fusion.3 = f32[768]{0:T(1024)S(1)} fusion(f32[768]{0:T(1024)S(1)} %get-tuple-element.5, f32[768]{0:T(1024)S(1)} %get-tuple-element.6, pred[768]{0:T(1024)(128)(4,1)S(1)} %broadcast_compare_fusion.3, bf16[768,1152]{1,0:T(8,128)(2,1)S(1)} %bitcast.9), kind=kOutput, calls=%fused_computation.4 | convolution fusion | flops 1211497728 | bytes 1593344 | tf_op jit(solution)/shard_map/qe,ke->qk/dot_general | solution.py:73
  106.7 0.1 convert_reduce_fusion.2
  106.8 0.0 collective-permute-done.1
  106.9 0.1 convert_reduce_fusion.1
  107.0 1.5 %select_reduce_fusion.1 = f32[768]{0:T(1024)S(1)} fusion(bf16[768,1152]{1,0:T(8,128)(2,1)S(1)} %collective-permute-done.1, f32[768]{0:T(1024)S(1)} %get-tuple-element.6, f32[768]{0:T(1024)S(1)} %convert_reduce_fusion.1, pred[768]{0:T(1024)(128)(4,1)S(1)} %broadcast_compare_fusion.1, bf16[768,1152]{1,0:T(8,128)(2,1)S(1)} %bitcast.10), kind=kOutput, calls=%fused_computation.2 | convolution fusion | flops 1210318080 | bytes 3158016 | tf_op jit(solution)/shard_map/qe,ke->qk/dot_general | solution.py:78
  108.6 1.5 %select_reduce_fusion.2 = f32[768]{0:T(1024)S(1)} fusion(bf16[768,1152]{1,0:T(8,128)(2,1)S(1)} %collective-permute-done, f32[768]{0:T(1024)S(1)} %get-tuple-element.6, f32[768]{0:T(1024)S(1)} %convert_reduce_fusion.2, pred[768]{0:T(1024)(128)(4,1)S(1)} %broadcast_compare_fusion.2, bf16[768,1152]{1,0:T(8,128)(2,1)S(1)} %bitcast.11), kind=kOutput, calls=%fused_computation.3 | convolution fusion | flops 1210318080 | bytes 3158016 | tf_op jit(solution)/shard_map/qe,ke->qk/dot_general | solution.py:78
  110.1 0.0 collective-permute-done.2
  110.1 0.1 convert_reduce_fusion
  110.3 1.5 %select_reduce_fusion = f32[768]{0:T(1024)S(1)} fusion(bf16[768,1152]{1,0:T(8,128)(2,1)S(1)} %collective-permute-done.2, f32[768]{0:T(1024)S(1)} %get-tuple-element.6, f32[768]{0:T(1024)S(1)} %convert_reduce_fusion, pred[768]{0:T(1024)(128)(4,1)S(1)} %broadcast_compare_fusion, bf16[768,1152]{1,0:T(8,128)(2,1)S(1)} %bitcast.12), kind=kOutput, calls=%fused_computation.1 | convolution fusion | flops 1210318080 | bytes 3158016 | tf_op jit(solution)/shard_map/qe,ke->qk/dot_general | solution.py:78
  111.8 0.1 max.41
  111.9 12.7 %all_to_all.12 = f32[32,1,24]{2,1,0:T(1,128)S(1)} all-to-all(f32[32,1,24]{2,1,0:T(1,128)S(1)} %bitcast.14), channel_id=1, replica_groups=mesh['grp'=8,'split'=4] {'grp','split'}, dimensions={0} | all-to-all | bytes 6144 | tf_op jit(solution)/shard_map/all_to_all | solution.py:82
  124.5 0.5 broadcast.96
  125.1 0.7 reduce.13
  125.8 0.1 broadcast_in_dim.21
  125.8 0.8 select_reduce_fusion.4
  (15 shorter events, 0.1 us)
Async XLA Ops:
  0.0 1.9 %copy-start = (bf16[384,4096]{1,0:T(8,128)(2,1)S(1)}, bf16[384,4096]{1,0:T(8,128)(2,1)}, u32[]{:S(2)}) copy-start(bf16[384,4096]{1,0:T(8,128)(2,1)} %param.5) | copy-start | bytes 9437188
  0.0 7.9 %copy-start.1 = (s32[384]{0:T(512)S(1)}, s32[384]{0:T(512)}, u32[]{:S(2)}) copy-start(s32[384]{0:T(512)} %param.8) | copy-start | bytes 4612
  0.0 7.9 %copy-start.2 = (s32[384]{0:T(512)S(1)}, s32[384]{0:T(512)}, u32[]{:S(2)}) copy-start(s32[384]{0:T(512)} %param.7) | copy-start | bytes 4612
  1.9 6.1 %copy-start.3 = (s32[384]{0:T(512)S(1)}, s32[384]{0:T(512)}, u32[]{:S(2)}) copy-start(s32[384]{0:T(512)} %param.9) | copy-start | bytes 4612
  62.7 41.6 %collective-permute-start = (bf16[768,1152]{1,0:T(8,128)(2,1)S(1)}, bf16[768,1152]{1,0:T(8,128)(2,1)S(1)}, u32[]{:S(2)}, u32[]{:S(2)}) collective-permute-start(bf16[768,1152]{1,0:T(8,128)(2,1)S(1)} %bitcast.6), channel_id=1, source_target_pairs={{0,2},{1,3},{4,6},{5,7},{8,10},{9,11},{12,14},{13,15},{16,18},{17,... | collective-permute-start | bytes 5308424 | tf_op jit(solution)/shard_map/ppermute | solution.py:21
  66.2 40.6 %collective-permute-start.1 = (bf16[768,1152]{1,0:T(8,128)(2,1)S(1)}, bf16[768,1152]{1,0:T(8,128)(2,1)S(1)}, u32[]{:S(2)}, u32[]{:S(2)}) collective-permute-start(bf16[768,1152]{1,0:T(8,128)(2,1)S(1)} %bitcast.7), channel_id=1, source_target_pairs={{0,1},{2,3},{4,5},{6,7},{8,9},{10,11},{12,13},{14,15},{16,17},{18,... | collective-permute-start | bytes 5308424 | tf_op jit(solution)/shard_map/ppermute | solution.py:22
  104.3 5.8 %collective-permute-start.2 = (bf16[768,1152]{1,0:T(8,128)(2,1)S(1)}, bf16[768,1152]{1,0:T(8,128)(2,1)S(1)}, u32[]{:S(2)}, u32[]{:S(2)}) collective-permute-start(bf16[768,1152]{1,0:T(8,128)(2,1)S(1)} %collective-permute-done), channel_id=1, source_target_pairs={{2,3},{3,2},{6,7},{7,6},{10,11},{11,10},{14,15},{15,14},{18,19},{1... | collective-permute-start | bytes 5308424 | tf_op jit(solution)/shard_map/ppermute | solution.py:23

commit v2 on v1

--- a/solution.py
+++ b/solution.py
@@ -53,6 +53,7 @@
 
     embeds = embed_rows(states, weight)
     emb_w = embeds.shape[1]
+    half = emb_w // 2
     label = (cluster_id - owner_of * CL_GRP + 1).astype(jnp.float32)
     meta_cols = jnp.stack(
         [label, (order // 256).astype(jnp.float32), (order % 256).astype(jnp.float32)], axis=1
@@ -60,22 +61,31 @@
     meta = jnp.concatenate(
         [meta_cols, jnp.zeros((n_doc, META - meta_cols.shape[1]), jnp.float32)], axis=1
     ).astype(jnp.bfloat16)
-    rows = jnp.concatenate([embeds, meta], axis=1)
     pick = place[None, :] == jnp.arange(n_slot, dtype=jnp.int32)[:, None]
-    send = jnp.dot(pick.astype(jnp.bfloat16), rows, preferred_element_type=jnp.float32).astype(
-        jnp.bfloat16
-    )
-    got = lax.all_to_all(
-        send.reshape(n_dev, cap, -1), ("grp", "split"), split_axis=0, concat_axis=0, tiled=True
-    ).reshape(n_slot, -1)
 
-    q_emb, q_lab, q_ord = unpack(got, emb_w)
-    scores = jnp.einsum("qe,ke->qk", q_emb, q_emb, preferred_element_type=jnp.float32)
+    def route(rows):
+        send = jnp.dot(pick.astype(jnp.bfloat16), rows, preferred_element_type=jnp.float32)
+        send = send.astype(jnp.bfloat16).reshape(n_dev, cap, -1)
+        got = lax.all_to_all(send, ("grp", "split"), split_axis=0, concat_axis=0, tiled=True)
+        return got.reshape(n_slot, -1)
+
+    got_a = route(jnp.concatenate([embeds[:, :half], meta], axis=1))
+    keys_a = shift_keys(got_a, n_split)
+    got_b = route(embeds[:, half:])
+    keys_b = shift_keys(got_b, n_split)
+
+    q_emb, q_lab, q_ord = unpack(got_a, half)
+
+    def dots(k_a, k_b):
+        s = jnp.einsum("qe,ke->qk", q_emb, k_a[:, :half], preferred_element_type=jnp.float32)
+        return s + jnp.einsum("qe,ke->qk", got_b, k_b, preferred_element_type=jnp.float32)
+
+    scores = dots(got_a, got_b)
     hits = (q_lab[:, None] == q_lab[None, :]) & (q_lab[None, :] > 0) & (q_ord[None, :] < q_ord[:, None])
     best = jnp.max(jnp.where(hits, scores, jnp.float32(-1.0)), axis=1)
-    for keys in shift_keys(got, n_split):
-        k_emb, k_lab, _ = unpack(keys, emb_w)
-        scores = jnp.einsum("qe,ke->qk", q_emb, k_emb, preferred_element_type=jnp.float32)
+    for k_a, k_b in zip(keys_a, keys_b):
+        _, k_lab, _ = unpack(k_a, half)
+        scores = dots(k_a, k_b)
         hits = (q_lab[:, None] == k_lab[None, :]) & (k_lab[None, :] > 0)
         best = jnp.maximum(best, jnp.max(jnp.where(hits, scores, jnp.float32(-1.0)), axis=1))
 

time: 127 us -> 119 us (0.937)
  blocking collectives: 61.5 us -> 13.6 us
  starting transfers between devices: 6.22 us -> 24.7 us
  matrix products: 14.6 us -> 27.7 us
  waiting for transfers between devices: 35.8 us -> 39.8 us
  local copies, waits for them, and re-layouts: 4.97 us -> 7.15 us
    all_to_all x1 -> x0, blocking collectives: 48.8 us -> none  [local(): lax.all_to_all(send.reshape(n_dev, cap, -1), ('grp', 'split'), split_axis...]
    all_to_all x0 -> x2, waiting for transfers between devices: none -> 30.8 us  [route(): lax.all_to_all(send, ('grp', 'split'), split_axis=0, concat_axis=0, tiled...]
    ppermute x1 -> x2, waiting for transfers between devices: 35.8 us -> 8.95 us  [shift_keys(): up = lax.ppermute(keys, 'split', [(0, 2), (1, 3)])]
    dot_general x5 -> x10, matrix products: 8.43 us -> 21.6 us  [the longest x4 8.76 us: dots(): jnp.einsum('qe,ke->qk', got_b, k_b, preferred_element_type=jnp.float32)]
    all_to_all x0 -> x2, starting transfers between devices: none -> 11.1 us  [route(): lax.all_to_all(send, ('grp', 'split'), split_axis=0, concat_axis=0, tiled...]
    ppermute x1 -> x2, starting transfers between devices: 3.53 us -> 7.94 us  [shift_keys(): up = lax.ppermute(keys, 'split', [(0, 2), (1, 3)])]
    ppermute x1 -> x2, starting transfers between devices: 1.93 us -> 4.23 us  [shift_keys(): near = lax.ppermute(keys, 'split', [(0, 1), (2, 3)])]
    another operation x3, local copies, waits for them, and re-layouts: 0.34 us -> 2.25 us  [local(): jnp.stack([label, (order // 256).astype(jnp.float32), (order % 256).astyp...]
  transfers between devices with their start and end apart: 3 -> 8, of which waited for: 1 -> 3; matrix products, arithmetic and copies ran while one was open for 4% -> 21% of each run, Pallas kernels for 0% -> 0%
where the time goes in v2:
time: 119 us; the launch traced here: 118 us
  waiting for transfers between devices  39.8 us (33%)
  matrix products  27.7 us (23%)
  starting transfers between devices  24.7 us (21%)
  blocking collectives  13.6 us (11%)
  local copies, waits for them, and re-layouts  7.15 us (6%)
  other arithmetic  4.47 us (4%)
    all_to_all x2, waiting for transfers between devices, route(): lax.all_to_all(send, ('grp', 'split'), split_axis=0, concat_axis=0, tiled...  30.8 us
    all_to_all x1, blocking collectives, local(): lax.all_to_all(best.reshape(n_dev, cap), ('grp', 'split'), split_axis=0,...  13.6 us
    all_to_all x2, starting transfers between devices, route(): lax.all_to_all(send, ('grp', 'split'), split_axis=0, concat_axis=0, tiled...  11.1 us
    ppermute x2, waiting for transfers between devices, shift_keys(): up = lax.ppermute(keys, 'split', [(0, 2), (1, 3)])  8.95 us
    dot_general x4, matrix products, dots(): jnp.einsum('qe,ke->qk', got_b, k_b, preferred_element_type=jnp.float32)  8.76 us
    dot_general x4, matrix products, dots(): jnp.einsum('qe,ke->qk', q_emb, k_a[:, :half], preferred_element_type=jnp....  8.66 us
    ppermute x2, starting transfers between devices, shift_keys(): up = lax.ppermute(keys, 'split', [(0, 2), (1, 3)])  7.94 us
    dot_general x1, matrix products, embed_rows(): jnp.einsum('...h,he->...e', rows, weight, preferred_element_type=jnp.floa...  5.94 us
  transfers between devices with their start and end apart: 8, of which 3 were waited for; matrix products, arithmetic and copies ran while one was open for 21% of the time, Pallas kernels for 0%

profile of v2, /device:TPU:0, one launch (start us, length us, event | category | flops | bytes accessed | tf_op | source)
XLA Modules:
  0.0 117.7 jit_solution(2610457205512233127)
XLA Ops:
  0.0 0.9 convert_convert_fusion
  1.1 0.8 copy-done
  1.9 5.9 %multiply_reduce_fusion = (f32[384]{0:T(512)S(1)}, f32[384,1024]{1,0:T(8,128)S(1)}) fusion(bf16[384,4096]{1,0:T(8,128)(2,1)S(1)} %copy-done, bf16[4096,1024]{1,0:T(8,128)(2,1)} %param.6), kind=kOutput, calls=%fused_computation.5 | convolution fusion | flops 3222011392 | bytes 13108736 | tf_op jit(solution)/shard_map/...h,he->...e/dot_general | solution.py:14
  8.0 0.9 copy-done.1
  8.9 1.5 %convolution_convert_fusion.1 = bf16[768,512]{1,0:T(8,128)(2,1)} fusion(s32[384]{0:T(512)S(1)} %convert_add_fusion, bf16[384,1024]{1,0:T(8,128)(2,1)S(1)} %multiply_convert_fusion), kind=kOutput, calls=%fused_computation.7 | convolution fusion | flops 302678016 | bytes 1181696 | tf_op jit(solution)/shard_map/dot_general | solution.py:67
  10.4 7.4 %all-to-all-start.1 = ((bf16[32,24,512]{2,1,0:T(8,128)(2,1)}), bf16[32,24,512]{2,1,0:T(8,128)(2,1)}, u32[]{:S(2)}, u32[]{:S(2)}) async-start(bf16[32,24,512]{2,1,0:T(8,128)(2,1)} %bitcast.17), calls=%async_computation.1 | async-start | bytes 1572864 | tf_op jit(solution)/shard_map/all_to_all | solution.py:69
  17.8 0.7 stack.15
  18.6 0.8 stack.16
  19.3 0.8 stack.17
  20.7 1.8 %concatenate.6 = bf16[384,640]{1,0:T(8,128)(2,1)} concatenate(bf16[384,512]{1,0:T(8,128)(2,1)S(1)} %slice-done, bf16[384,1]{1,0:T(8,128)(2,1)} %stack.15, bf16[384,1]{1,0:T(8,128)(2,1)} %stack.16, bf16[384,1]{1,0:T(8,128)(2,1)} %stack.17, bf16[384,125]{1,0:T(8,128)(2,1)} %broadcast_in_dim.19), dimensions={1} | concatenate | bytes 983040 | tf_op jit(solution)/shard_map/concatenate | solution.py:72
  22.6 2.7 %convolution_convert_fusion = bf16[768,640]{1,0:T(8,128)(2,1)} fusion(bf16[384,640]{1,0:T(8,128)(2,1)} %concatenate.6, s32[384]{0:T(512)S(1)} %convert_add_fusion), kind=kOutput, calls=%fused_computation.6 | convolution fusion | flops 378273792 | bytes 1476096 | tf_op jit(solution)/shard_map/dot_general | solution.py:67
  25.3 13.1 %all-to-all-done.1 = bf16[32,24,512]{2,1,0:T(8,128)(2,1)} async-done(((bf16[32,24,512]{2,1,0:T(8,128)(2,1)}), bf16[32,24,512]{2,1,0:T(8,128)(2,1)}, u32[]{:S(2)}, u32[]{:S(2)}) %all-to-all-start.1) | async-done | bytes 786464 | tf_op jit(solution)/shard_map/all_to_all | solution.py:69
  38.4 3.7 %all-to-all-start = ((bf16[32,24,640]{2,1,0:T(8,128)(2,1)}), bf16[32,24,640]{2,1,0:T(8,128)(2,1)}, u32[]{:S(2)}, u32[]{:S(2)}) async-start(bf16[32,24,640]{2,1,0:T(8,128)(2,1)} %bitcast.16), calls=%async_computation | async-start | bytes 1966080 | tf_op jit(solution)/shard_map/all_to_all | solution.py:69
  42.2 4.5 %collective-permute-start.1 = (bf16[768,512]{1,0:T(8,128)(2,1)}, bf16[768,512]{1,0:T(8,128)(2,1)}, u32[]{:S(2)}, u32[]{:S(2)}) collective-permute-start(bf16[768,512]{1,0:T(8,128)(2,1)} %bitcast.3), channel_id=1, source_target_pairs={{0,2},{1,3},{4,6},{5,7},{8,10},{9,11},{12,14},{13,15},{16,18},{17,... | collective-permute-start | bytes 2359304 | tf_op jit(solution)/shard_map/ppermute | solution.py:21
  46.7 2.7 %collective-permute-start.3 = (bf16[768,512]{1,0:T(8,128)(2,1)}, bf16[768,512]{1,0:T(8,128)(2,1)}, u32[]{:S(2)}, u32[]{:S(2)}) collective-permute-start(bf16[768,512]{1,0:T(8,128)(2,1)} %bitcast.3), channel_id=1, source_target_pairs={{0,1},{2,3},{4,5},{6,7},{8,9},{10,11},{12,13},{14,15},{16,17},{18,... | collective-permute-start | bytes 2359304 | tf_op jit(solution)/shard_map/ppermute | solution.py:22
  49.3 17.7 %all-to-all-done = bf16[32,24,640]{2,1,0:T(8,128)(2,1)} async-done(((bf16[32,24,640]{2,1,0:T(8,128)(2,1)}), bf16[32,24,640]{2,1,0:T(8,128)(2,1)}, u32[]{:S(2)}, u32[]{:S(2)}) %all-to-all-start) | async-done | bytes 983072 | tf_op jit(solution)/shard_map/all_to_all | solution.py:69
  67.0 3.4 %collective-permute-start = (bf16[768,640]{1,0:T(8,128)(2,1)}, bf16[768,640]{1,0:T(8,128)(2,1)S(1)}, u32[]{:S(2)}, u32[]{:S(2)}) collective-permute-start(bf16[768,640]{1,0:T(8,128)(2,1)} %bitcast.1), channel_id=1, source_target_pairs={{0,2},{1,3},{4,6},{5,7},{8,10},{9,11},{12,14},{13,15},{16,18},{17,... | collective-permute-start | bytes 2949128 | tf_op jit(solution)/shard_map/ppermute | solution.py:21
  70.4 2.3 %fusion.9 = f32[768,768]{0,1:T(8,128)S(1)} fusion(bf16[768,640]{1,0:T(8,128)(2,1)} %bitcast.1), kind=kOutput, calls=%fused_computation.21 | convolution fusion | flops 603979776 | bytes 3145728 | tf_op jit(solution)/shard_map/qe,ke->qk/dot_general | solution.py:80
  72.7 1.6 %collective-permute-start.2 = (bf16[768,640]{1,0:T(8,128)(2,1)}, bf16[768,640]{1,0:T(8,128)(2,1)S(1)}, u32[]{:S(2)}, u32[]{:S(2)}) collective-permute-start(bf16[768,640]{1,0:T(8,128)(2,1)} %bitcast.1), channel_id=1, source_target_pairs={{0,1},{2,3},{4,5},{6,7},{8,9},{10,11},{12,13},{14,15},{16,17},{18,... | collective-permute-start | bytes 2949128 | tf_op jit(solution)/shard_map/ppermute | solution.py:22
  74.3 1.5 %add_reduce_fusion = (f32[768]{0:T(1024)S(1)}, f32[768]{0:T(1024)S(1)}) fusion(bf16[768,640]{1,0:T(8,128)(2,1)} %bitcast.1), kind=kLoop, calls=%fused_computation.28 | loop fusion | flops 3840 | bytes 10752 | tf_op jit(solution)/shard_map/add | solution.py:35
  75.8 2.5 %select_reduce_fusion.3 = f32[768]{0:T(1024)S(1)} fusion(f32[768,768]{0,1:T(8,128)S(1)} %fusion.9, bf16[768,512]{1,0:T(8,128)(2,1)} %bitcast.3, f32[768]{0:T(1024)S(1)} %get-tuple-element.5, f32[768]{0:T(1024)S(1)} %get-tuple-element.6, pred[768]{0:T(1024)(128)(4,1)S(1)} %broadcast_compare_fusion.3), kind=kOutput, calls=%fused_computation.3 | convolution fusion | flops 608107776 | bytes 3155712 | tf_op jit(solution)/shard_map/qe,ke->qk/dot_general | solution.py:81
  78.3 0.7 collective-permute-start.5
  79.0 2.2 %fusion.23 = f32[768,768]{0,1:T(8,128)S(1)} fusion(bf16[768,512]{1,0:T(8,128)(2,1)} %bitcast.3, bf16[768,512]{1,0:T(8,128)(2,1)} %collective-permute-done.1), kind=kOutput, calls=%fused_computation.61 | convolution fusion | flops 603979776 | bytes 3932160 | tf_op jit(solution)/shard_map/qe,ke->qk/dot_general | solution.py:81
  81.2 2.2 %fusion.24 = f32[768,768]{0,1:T(8,128)S(1)} fusion(bf16[768,512]{1,0:T(8,128)(2,1)} %bitcast.3, bf16[768,512]{1,0:T(8,128)(2,1)} %collective-permute-done.3), kind=kOutput, calls=%fused_computation.62 | convolution fusion | flops 603979776 | bytes 3932160 | tf_op jit(solution)/shard_map/qe,ke->qk/dot_general | solution.py:81
  83.4 9.0 %collective-permute-done = bf16[768,640]{1,0:T(8,128)(2,1)S(1)} collective-permute-done((bf16[768,640]{1,0:T(8,128)(2,1)}, bf16[768,640]{1,0:T(8,128)(2,1)S(1)}, u32[]{:S(2)}, u32[]{:S(2)}) %collective-permute-start) | collective-permute-done | bytes 983072 | tf_op jit(solution)/shard_map/ppermute | solution.py:21
  92.3 0.7 collective-permute-start.4
  93.2 2.1 %select_reduce_fusion.2 = f32[768]{0:T(1024)S(1)} fusion(f32[768,768]{0,1:T(8,128)S(1)} %fusion.23, f32[768]{0:T(1024)S(1)} %get-tuple-element.6, f32[768]{0:T(1024)S(1)} %convert_reduce_fusion.2, pred[768]{0:T(1024)(128)(4,1)S(1)} %broadcast_compare_fusion.2, bf16[768,640]{1,0:T(8,128)(2,1)S(1)} %collective-permute-done, bf16[768,640]{1,0:T(8,128)(2,1)} %bitcast.1), kind=kOutput, calls=%fused_computation.2 | convolution fusion | flops 606928128 | bytes 3944448 | tf_op jit(solution)/shard_map/qe,ke->qk/dot_general | solution.py:80
  95.5 2.1 %select_reduce_fusion.1 = f32[768]{0:T(1024)S(1)} fusion(f32[768,768]{0,1:T(8,128)S(1)} %fusion.24, f32[768]{0:T(1024)S(1)} %get-tuple-element.6, f32[768]{0:T(1024)S(1)} %convert_reduce_fusion.1, pred[768]{0:T(1024)(128)(4,1)S(1)} %broadcast_compare_fusion.1, bf16[768,640]{1,0:T(8,128)(2,1)S(1)} %collective-permute-done.2, bf16[768,640]{1,0:T(8,128)(2,1)} %bitcast.1), kind=kOutput, calls=%fused_computation.1 | convolution fusion | flops 606928128 | bytes 3944448 | tf_op jit(solution)/shard_map/qe,ke->qk/dot_general | solution.py:80
  97.7 1.9 %fusion.25 = f32[768,768]{0,1:T(8,128)S(1)} fusion(bf16[768,512]{1,0:T(8,128)(2,1)} %bitcast.3, bf16[768,512]{1,0:T(8,128)(2,1)S(1)} %collective-permute-done.5), kind=kOutput, calls=%fused_computation.63 | convolution fusion | flops 603979776 | bytes 3932160 | tf_op jit(solution)/shard_map/qe,ke->qk/dot_general | solution.py:81
  99.8 2.1 %select_reduce_fusion = f32[768]{0:T(1024)S(1)} fusion(f32[768,768]{0,1:T(8,128)S(1)} %fusion.25, f32[768]{0:T(1024)S(1)} %get-tuple-element.6, f32[768]{0:T(1024)S(1)} %convert_reduce_fusion, pred[768]{0:T(1024)(128)(4,1)S(1)} %broadcast_compare_fusion, bf16[768,640]{1,0:T(8,128)(2,1)S(1)} %collective-permute-done.4, bf16[768,640]{1,0:T(8,128)(2,1)} %bitcast.1), kind=kOutput, calls=%fused_computation | convolution fusion | flops 606928128 | bytes 3944448 | tf_op jit(solution)/shard_map/qe,ke->qk/dot_general | solution.py:80
  102.0 13.6 %all_to_all.16 = f32[32,1,24]{2,1,0:T(1,128)S(1)} all-to-all(f32[32,1,24]{2,1,0:T(1,128)S(1)} %bitcast.18), channel_id=1, replica_groups=mesh['grp'=8,'split'=4] {'grp','split'}, dimensions={0} | all-to-all | bytes 6144 | tf_op jit(solution)/shard_map/all_to_all | solution.py:92
  116.9 0.8 select_reduce_fusion.4
  (29 shorter events, 2.9 us)
Async XLA Ops:
  0.0 1.9 %copy-start = (bf16[384,4096]{1,0:T(8,128)(2,1)S(1)}, bf16[384,4096]{1,0:T(8,128)(2,1)}, u32[]{:S(2)}) copy-start(bf16[384,4096]{1,0:T(8,128)(2,1)} %param.5) | copy-start | bytes 9437188
  8.0 0.9 copy-start.1
  8.9 9.6 %copy-start.2 = (s32[384]{0:T(512)S(1)}, s32[384]{0:T(512)}, u32[]{:S(2)}) copy-start(s32[384]{0:T(512)} %param.9) | copy-start | bytes 4612
  10.4 10.3 %slice-start = ((bf16[384,1024]{1,0:T(8,128)(2,1)}), bf16[384,512]{1,0:T(8,128)(2,1)S(1)}, s32[]{:S(2)}) async-start(bf16[384,1024]{1,0:T(8,128)(2,1)} %copy-done.1), calls=%async_computation.3 | async-start | bytes 786432 | tf_op jit(solution)/shard_map/slice | solution.py:72
  10.4 28.0 %all-to-all-start.1 = ((bf16[32,24,512]{2,1,0:T(8,128)(2,1)}), bf16[32,24,512]{2,1,0:T(8,128)(2,1)}, u32[]{:S(2)}, u32[]{:S(2)}) async-start(bf16[32,24,512]{2,1,0:T(8,128)(2,1)} %bitcast.17), calls=%async_computation.1 | async-start | bytes 1572864 | tf_op jit(solution)/shard_map/all_to_all | solution.py:69
  38.4 28.6 %all-to-all-start = ((bf16[32,24,640]{2,1,0:T(8,128)(2,1)}), bf16[32,24,640]{2,1,0:T(8,128)(2,1)}, u32[]{:S(2)}, u32[]{:S(2)}) async-start(bf16[32,24,640]{2,1,0:T(8,128)(2,1)} %bitcast.16), calls=%async_computation | async-start | bytes 1966080 | tf_op jit(solution)/shard_map/all_to_all | solution.py:69
  42.2 36.1 %collective-permute-start.1 = (bf16[768,512]{1,0:T(8,128)(2,1)}, bf16[768,512]{1,0:T(8,128)(2,1)}, u32[]{:S(2)}, u32[]{:S(2)}) collective-permute-start(bf16[768,512]{1,0:T(8,128)(2,1)} %bitcast.3), channel_id=1, source_target_pairs={{0,2},{1,3},{4,6},{5,7},{8,10},{9,11},{12,14},{13,15},{16,18},{17,... | collective-permute-start | bytes 2359304 | tf_op jit(solution)/shard_map/ppermute | solution.py:21
  46.7 34.5 %collective-permute-start.3 = (bf16[768,512]{1,0:T(8,128)(2,1)}, bf16[768,512]{1,0:T(8,128)(2,1)}, u32[]{:S(2)}, u32[]{:S(2)}) collective-permute-start(bf16[768,512]{1,0:T(8,128)(2,1)} %bitcast.3), channel_id=1, source_target_pairs={{0,1},{2,3},{4,5},{6,7},{8,9},{10,11},{12,13},{14,15},{16,17},{18,... | collective-permute-start | bytes 2359304 | tf_op jit(solution)/shard_map/ppermute | solution.py:22
  67.0 25.4 %collective-permute-start = (bf16[768,640]{1,0:T(8,128)(2,1)}, bf16[768,640]{1,0:T(8,128)(2,1)S(1)}, u32[]{:S(2)}, u32[]{:S(2)}) collective-permute-start(bf16[768,640]{1,0:T(8,128)(2,1)} %bitcast.1), channel_id=1, source_target_pairs={{0,2},{1,3},{4,6},{5,7},{8,10},{9,11},{12,14},{13,15},{16,18},{17,... | collective-permute-start | bytes 2949128 | tf_op jit(solution)/shard_map/ppermute | solution.py:21
  72.7 22.6 %collective-permute-start.2 = (bf16[768,640]{1,0:T(8,128)(2,1)}, bf16[768,640]{1,0:T(8,128)(2,1)S(1)}, u32[]{:S(2)}, u32[]{:S(2)}) collective-permute-start(bf16[768,640]{1,0:T(8,128)(2,1)} %bitcast.1), channel_id=1, source_target_pairs={{0,1},{2,3},{4,5},{6,7},{8,9},{10,11},{12,13},{14,15},{16,17},{18,... | collective-permute-start | bytes 2949128 | tf_op jit(solution)/shard_map/ppermute | solution.py:22
  78.3 19.3 %collective-permute-start.5 = (bf16[768,512]{1,0:T(8,128)(2,1)}, bf16[768,512]{1,0:T(8,128)(2,1)S(1)}, u32[]{:S(2)}, u32[]{:S(2)}) collective-permute-start(bf16[768,512]{1,0:T(8,128)(2,1)} %collective-permute-done.1), channel_id=1, source_target_pairs={{2,3},{3,2},{6,7},{7,6},{10,11},{11,10},{14,15},{15,14},{18,19},{1... | collective-permute-start | bytes 2359304 | tf_op jit(solution)/shard_map/ppermute | solution.py:23
  92.3 7.2 %collective-permute-start.4 = (bf16[768,640]{1,0:T(8,128)(2,1)S(1)}, bf16[768,640]{1,0:T(8,128)(2,1)S(1)}, u32[]{:S(2)}, u32[]{:S(2)}) collective-permute-start(bf16[768,640]{1,0:T(8,128)(2,1)S(1)} %collective-permute-done), channel_id=1, source_target_pairs={{2,3},{3,2},{6,7},{7,6},{10,11},{11,10},{14,15},{15,14},{18,19},{1... | collective-permute-start | bytes 2949128 | tf_op jit(solution)/shard_map/ppermute | solution.py:23

commit v3 on v2

v3 whole, which is shorter than its diff:
```python
import jax
import jax.numpy as jnp
from jax import lax
from jax.sharding import PartitionSpec as P

CL_GRP = 4


EPS = 1e-06
META = 128


def embed_rows(rows, weight):
    proj = jnp.einsum("...h,he->...e", rows, weight, preferred_element_type=jnp.float32)
    scale = lax.rsqrt(jnp.sum(proj * proj, axis=-1, keepdims=True) + EPS)
    return (proj * scale).astype(jnp.bfloat16)


def gather_split(rows, n_split):
    if n_split == 4:
        cross = lax.ppermute(rows, "split", [(0, 2), (1, 3), (2, 0), (3, 1)])
        pair = [(0, 1), (1, 0), (2, 3), (3, 2)]
        return [cross, lax.ppermute(rows, "split", pair), lax.ppermute(cross, "split", pair)]
    return [
        lax.ppermute(rows, "split", [(i, (i + d) % n_split) for i in range(n_split)])
        for d in range(1, n_split)
    ]


def unpack(buf, emb_w, n_all):
    emb = buf[:, :emb_w]
    lab = buf[:, emb_w].astype(jnp.float32)
    digits = [buf[:, emb_w + i].astype(jnp.float32) for i in (1, 2, 3)]
    return emb, lab, (digits[0] * n_all + digits[1] * 256.0) + digits[2]


def local(states, weight, cluster_id, block, order):
    n_doc = states.shape[0]
    n_grp = lax.axis_size("grp")
    n_split = lax.axis_size("split")
    n_dev = n_grp * n_split
    n_all = n_doc * n_dev
    cap = n_split * max(2, 2 * n_doc // n_dev)
    n_slot = n_grp * cap
    owner_of = cluster_id // CL_GRP
    onehot = (owner_of[:, None] == jnp.arange(n_grp, dtype=jnp.int32)[None, :]).astype(jnp.bfloat16)
    lower = (jnp.arange(n_doc)[:, None] > jnp.arange(n_doc)[None, :]).astype(jnp.bfloat16)
    before = jnp.dot(lower, onehot, preferred_element_type=jnp.float32)
    slot = jnp.sum(before * onehot.astype(jnp.float32), axis=1).astype(jnp.int32)
    place = owner_of * cap + slot

    embeds = embed_rows(states, weight)
    emb_w = embeds.shape[1]
    half = emb_w // 2
    label = (cluster_id - owner_of * CL_GRP + 1).astype(jnp.float32)
    meta_cols = jnp.stack(
        [label, block.astype(jnp.float32), (order // 256).astype(jnp.float32),
         (order % 256).astype(jnp.float32)],
        axis=1,
    )
    meta = jnp.concatenate(
        [meta_cols, jnp.zeros((n_doc, META - meta_cols.shape[1]), jnp.float32)], axis=1
    ).astype(jnp.bfloat16)
    pick = place[None, :] == jnp.arange(n_slot, dtype=jnp.int32)[:, None]

    def route(rows):
        send = jnp.dot(pick.astype(jnp.bfloat16), rows, preferred_element_type=jnp.float32)
        send = send.astype(jnp.bfloat16).reshape(n_grp, cap, -1)
        got = lax.all_to_all(send, "grp", split_axis=0, concat_axis=0, tiled=True)
        return got.reshape(n_slot, -1)

    got_a = route(jnp.concatenate([embeds[:, :half], meta], axis=1))
    keys_a = gather_split(got_a, n_split)
    got_b = route(embeds[:, half:])
    keys_b = gather_split(got_b, n_split)

    q_emb, q_lab, q_ord = unpack(got_a, half, n_all)

    def dots(k_a, k_b):
        s = jnp.einsum("qe,ke->qk", q_emb, k_a[:, :half], preferred_element_type=jnp.float32)
        return s + jnp.einsum("qe,ke->qk", got_b, k_b, preferred_element_type=jnp.float32)

    scores = dots(got_a, got_b)
    hits = (q_lab[:, None] == q_lab[None, :]) & (q_lab[None, :] > 0) & (q_ord[None, :] < q_ord[:, None])
    best = jnp.max(jnp.where(hits, scores, jnp.float32(-1.0)), axis=1)
    for k_a, k_b in zip(keys_a, keys_b):
        _, k_lab, k_ord = unpack(k_a, half, n_all)
        scores = dots(k_a, k_b)
        hits = (q_lab[:, None] == k_lab[None, :]) & (k_lab[None, :] > 0) & (k_ord[None, :] < q_ord[:, None])
        best = jnp.maximum(best, jnp.max(jnp.where(hits, scores, jnp.float32(-1.0)), axis=1))

    returned = lax.all_to_all(
        best.reshape(n_grp, cap), "grp", split_axis=0, concat_axis=0, tiled=True
    ).reshape(n_slot)
    return jnp.max(jnp.where(pick, returned[:, None], -jnp.inf), axis=0)


def solution(mesh):
    in_specs = (
        P(("grp", "split"), None),
        P(),
        P(("grp", "split")),
        P(("grp", "split")),
        P(("grp", "split")),
    )
    out_specs = P(("grp", "split"))
    return jax.shard_map(local, mesh=mesh, in_specs=in_specs, out_specs=out_specs, check_vma=False)
```

time: 119 us -> 117 us (0.983)
  starting transfers between devices: 24.7 us -> 15.4 us
  waiting for transfers between devices: 39.8 us -> 44.6 us
  local copies, waits for them, and re-layouts: 7.15 us -> 10.3 us
  blocking collectives: 13.6 us -> 11.4 us
  matrix products: 27.7 us -> 29.5 us
    ppermute x6, starting transfers between devices: 13.6 us -> 3.75 us  [the longest x2 3.17 us: gather_split(): cross = lax.ppermute(rows, 'split', [(0, 2), (1, 3), (2, 0), (3, 1)])]
    all_to_all x2, waiting for transfers between devices: 30.8 us -> 34.6 us  [route(): got = lax.all_to_all(send, 'grp', split_axis=0, concat_axis=0, tiled=True)]
    reshape x0 -> x1, local copies, waits for them, and re-layouts: none -> 2.29 us  [route(): return got.reshape(n_slot, -1)]
    all_to_all x1, blocking collectives: 13.6 us -> 11.4 us  [local(): lax.all_to_all(best.reshape(n_grp, cap), 'grp', split_axis=0, concat_axis...]
    dot_general x4, matrix products: 8.66 us -> 10.4 us  [dots(): jnp.einsum('qe,ke->qk', q_emb, k_a[:, :half], preferred_element_type=jnp....]
    another operation x3 -> x4, local copies, waits for them, and re-layouts: 2.25 us -> 3 us  [local(): jnp.stack([label, block.astype(jnp.float32), (order // 256).astype(jnp.fl...]
  transfers between devices with their start and end apart: 8 -> 8, of which waited for: 3 -> 3; matrix products, arithmetic and copies ran while one was open for 21% -> 25% of each run, Pallas kernels for 0% -> 0%
where the time goes in v3:
time: 117 us; the launch traced here: 116 us
  waiting for transfers between devices  44.6 us (38%)
  matrix products  29.5 us (25%)
  starting transfers between devices  15.4 us (13%)
  blocking collectives  11.4 us (10%)
  local copies, waits for them, and re-layouts  10.3 us (9%)
  other arithmetic  4.5 us (4%)
    all_to_all x2, waiting for transfers between devices, route(): got = lax.all_to_all(send, 'grp', split_axis=0, concat_axis=0, tiled=True)  34.6 us
    all_to_all x2, starting transfers between devices, route(): got = lax.all_to_all(send, 'grp', split_axis=0, concat_axis=0, tiled=True)  11.6 us
    all_to_all x1, blocking collectives, local(): lax.all_to_all(best.reshape(n_grp, cap), 'grp', split_axis=0, concat_axis...  11.4 us
    dot_general x4, matrix products, dots(): jnp.einsum('qe,ke->qk', q_emb, k_a[:, :half], preferred_element_type=jnp....  10.4 us
    ppermute x2, waiting for transfers between devices, gather_split(): cross = lax.ppermute(rows, 'split', [(0, 2), (1, 3), (2, 0), (3, 1)])  9.94 us
    dot_general x4, matrix products, dots(): jnp.einsum('qe,ke->qk', got_b, k_b, preferred_element_type=jnp.float32)  8.74 us
    dot_general x1, matrix products, embed_rows(): jnp.einsum('...h,he->...e', rows, weight, preferred_element_type=jnp.floa...  5.94 us
    dot_general x2, matrix products, route(): jnp.dot(pick.astype(jnp.bfloat16), rows, preferred_element_type=jnp.float32)  4.18 us
  transfers between devices with their start and end apart: 8, of which 3 were waited for; matrix products, arithmetic and copies ran while one was open for 25% of the time, Pallas kernels for 0%

profile of v3, /device:TPU:0, one launch (start us, length us, event | category | flops | bytes accessed | tf_op | source)
XLA Modules:
  0.0 115.8 jit_solution(10329228395812095064)
XLA Ops:
  0.0 0.8 convert_convert_fusion.1
  1.1 0.8 copy-done
  1.9 5.9 %multiply_reduce_fusion = (f32[384]{0:T(512)S(1)}, f32[384,1024]{1,0:T(8,128)S(1)}) fusion(bf16[384,4096]{1,0:T(8,128)(2,1)S(1)} %copy-done, bf16[4096,1024]{1,0:T(8,128)(2,1)} %param.6), kind=kOutput, calls=%fused_computation.5 | convolution fusion | flops 3222011392 | bytes 13108736 | tf_op jit(solution)/shard_map/...h,he->...e/dot_general | solution.py:14
  8.0 0.9 copy-done.1
  8.9 1.5 %convolution_convert_fusion.1 = bf16[768,512]{1,0:T(8,128)(2,1)} fusion(s32[384]{0:T(512)S(1)} %convert_add_fusion, bf16[384,1024]{1,0:T(8,128)(2,1)S(1)} %multiply_convert_fusion), kind=kOutput, calls=%fused_computation.7 | convolution fusion | flops 302678016 | bytes 1181696 | tf_op jit(solution)/shard_map/dot_general | solution.py:67
  10.4 7.4 %all-to-all-start.1 = ((bf16[8,96,512]{2,1,0:T(8,128)(2,1)}), bf16[8,96,512]{2,1,0:T(8,128)(2,1)}, u32[]{:S(2)}, u32[]{:S(2)}) async-start(bf16[8,96,512]{2,1,0:T(8,128)(2,1)} %bitcast.16), calls=%async_computation.1 | async-start | bytes 1572864 | tf_op jit(solution)/shard_map/all_to_all | solution.py:69
  17.8 0.7 stack.20
  18.5 0.8 stack.21
  19.3 0.8 stack.22
  20.1 0.7 stack.23
  21.4 1.9 %concatenate.6 = bf16[384,640]{1,0:T(8,128)(2,1)} concatenate(bf16[384,512]{1,0:T(8,128)(2,1)S(1)} %slice-done, bf16[384,1]{1,0:T(8,128)(2,1)} %stack.20, bf16[384,1]{1,0:T(8,128)(2,1)} %stack.21, bf16[384,1]{1,0:T(8,128)(2,1)} %stack.22, bf16[384,1]{1,0:T(8,128)(2,1)} %stack.23, bf16[384,124]{1,0:T(8,128)(2,1)} %broadcast_in_dim.19), dimensions={1} | concatenate | bytes 983040 | tf_op jit(solution)/shard_map/concatenate | solution.py:72
  23.3 2.7 %convolution_convert_fusion = bf16[768,640]{1,0:T(8,128)(2,1)} fusion(bf16[384,640]{1,0:T(8,128)(2,1)} %concatenate.6, s32[384]{0:T(512)S(1)} %convert_add_fusion), kind=kOutput, calls=%fused_computation.6 | convolution fusion | flops 378273792 | bytes 1476096 | tf_op jit(solution)/shard_map/dot_general | solution.py:67
  26.1 12.0 %all-to-all-done.1 = bf16[8,96,512]{2,1,0:T(8,128)(2,1)} async-done(((bf16[8,96,512]{2,1,0:T(8,128)(2,1)}), bf16[8,96,512]{2,1,0:T(8,128)(2,1)}, u32[]{:S(2)}, u32[]{:S(2)}) %all-to-all-start.1) | async-done | bytes 786464 | tf_op jit(solution)/shard_map/all_to_all | solution.py:69
  38.1 4.2 %all-to-all-start = ((bf16[8,96,640]{2,1,0:T(8,128)(2,1)}), bf16[8,96,640]{2,1,0:T(8,128)(2,1)}, u32[]{:S(2)}, u32[]{:S(2)}) async-start(bf16[8,96,640]{2,1,0:T(8,128)(2,1)} %bitcast.15), calls=%async_computation | async-start | bytes 1966080 | tf_op jit(solution)/shard_map/all_to_all | solution.py:69
  42.3 1.6 %collective-permute-start.1 = (bf16[768,512]{1,0:T(8,128)(2,1)}, bf16[768,512]{1,0:T(8,128)(2,1)}, u32[]{:S(2)}, u32[]{:S(2)}) collective-permute-start(bf16[768,512]{1,0:T(8,128)(2,1)} %bitcast.3), channel_id=1, source_target_pairs={{0,2},{1,3},{2,0},{3,1},{4,6},{5,7},{6,4},{7,5},{8,10},{9,11},{10,... | collective-permute-start | bytes 2359304 | tf_op jit(solution)/shard_map/ppermute | solution.py:21
  43.9 22.6 %all-to-all-done = bf16[8,96,640]{2,1,0:T(8,128)(2,1)} async-done(((bf16[8,96,640]{2,1,0:T(8,128)(2,1)}), bf16[8,96,640]{2,1,0:T(8,128)(2,1)}, u32[]{:S(2)}, u32[]{:S(2)}) %all-to-all-start) | async-done | bytes 983072 | tf_op jit(solution)/shard_map/all_to_all | solution.py:69
  66.5 2.3 %copy.23 = bf16[768,640]{0,1:T(8,128)(2,1)} copy(bf16[768,640]{1,0:T(8,128)(2,1)} %bitcast.1) | data formatting | bytes 1966080 | tf_op jit(solution)/shard_map/reshape | solution.py:70
  68.8 1.1 convert_reduce_fusion
  69.9 1.6 %collective-permute-start = (bf16[768,640]{0,1:T(8,128)(2,1)}, bf16[768,640]{0,1:T(8,128)(2,1)S(1)}, u32[]{:S(2)}, u32[]{:S(2)}) collective-permute-start(bf16[768,640]{0,1:T(8,128)(2,1)} %copy.23), channel_id=1, source_target_pairs={{0,2},{1,3},{2,0},{3,1},{4,6},{5,7},{6,4},{7,5},{8,10},{9,11},{10,... | collective-permute-start | bytes 2949128 | tf_op jit(solution)/shard_map/ppermute | solution.py:21
  71.4 2.3 %fusion.9 = f32[768,768]{0,1:T(8,128)S(1)} fusion(bf16[768,640]{1,0:T(8,128)(2,1)} %bitcast.1), kind=kOutput, calls=%fused_computation.21 | convolution fusion | flops 603979776 | bytes 3145728 | tf_op jit(solution)/shard_map/qe,ke->qk/dot_general | solution.py:80
  73.7 0.8 fusion.33
  74.6 2.5 %select_reduce_fusion.3 = f32[768]{0:T(1024)S(1)} fusion(f32[768,768]{0,1:T(8,128)S(1)} %fusion.9, bf16[768,512]{1,0:T(8,128)(2,1)} %bitcast.3, f32[768]{0:T(1024)S(1)} %fusion.33, f32[768]{0:T(1024)S(1)} %convert_reduce_fusion, pred[768]{0:T(1024)(128)(4,1)S(1)} %broadcast_compare_fusion.3), kind=kOutput, calls=%fused_computation.3 | convolution fusion | flops 608107776 | bytes 3155712 | tf_op jit(solution)/shard_map/qe,ke->qk/dot_general | solution.py:81
  77.6 2.2 %fusion.44 = f32[768,768]{0,1:T(8,128)S(1)} fusion(bf16[768,512]{1,0:T(8,128)(2,1)} %bitcast.3, bf16[768,512]{1,0:T(8,128)(2,1)} %collective-permute-done.1), kind=kOutput, calls=%fused_computation.94 | convolution fusion | flops 603979776 | bytes 3932160 | tf_op jit(solution)/shard_map/qe,ke->qk/dot_general | solution.py:81
  79.8 2.2 %fusion.45 = f32[768,768]{0,1:T(8,128)S(1)} fusion(bf16[768,512]{1,0:T(8,128)(2,1)} %bitcast.3, bf16[768,512]{1,0:T(8,128)(2,1)} %collective-permute-done.3), kind=kOutput, calls=%fused_computation.95 | convolution fusion | flops 603979776 | bytes 3932160 | tf_op jit(solution)/shard_map/qe,ke->qk/dot_general | solution.py:81
  82.1 9.9 %collective-permute-done = bf16[768,640]{0,1:T(8,128)(2,1)S(1)} collective-permute-done((bf16[768,640]{0,1:T(8,128)(2,1)}, bf16[768,640]{0,1:T(8,128)(2,1)S(1)}, u32[]{:S(2)}, u32[]{:S(2)}) %collective-permute-start) | collective-permute-done | bytes 983072 | tf_op jit(solution)/shard_map/ppermute | solution.py:21
  92.0 2.7 %select_reduce_fusion.1 = f32[768]{0:T(1024)S(1)} fusion(f32[768,768]{0,1:T(8,128)S(1)} %fusion.45, f32[768]{0:T(1024)S(1)} %fusion.33, f32[768]{0:T(1024)S(1)} %convert_reduce_fusion, f32[768]{0:T(1024)S(1)} %get-tuple-element.8, f32[768]{0:T(1024)S(1)} %get-tuple-element.7, pred[768]{0:T(1024)(128)(4,1)S(1)} %broadcast_compare_fusion.1, ...), kind=kOutput, calls=%fused_computation.1 | convolution fusion | flops 608107776 | bytes 3952640 | tf_op jit(solution)/shard_map/qe,ke->qk/dot_general | solution.py:80
  94.8 2.7 %select_reduce_fusion.2 = f32[768]{0:T(1024)S(1)} fusion(f32[768,768]{0,1:T(8,128)S(1)} %fusion.44, f32[768]{0:T(1024)S(1)} %fusion.33, f32[768]{0:T(1024)S(1)} %convert_reduce_fusion, f32[768]{0:T(1024)S(1)} %get-tuple-element.6, f32[768]{0:T(1024)S(1)} %get-tuple-element.5, pred[768]{0:T(1024)(128)(4,1)S(1)} %broadcast_compare_fusion.2, ...), kind=kOutput, calls=%fused_computation.2 | convolution fusion | flops 608107776 | bytes 3952640 | tf_op jit(solution)/shard_map/qe,ke->qk/dot_general | solution.py:80
  97.5 1.9 %fusion.46 = f32[768,768]{0,1:T(8,128)S(1)} fusion(bf16[768,512]{1,0:T(8,128)(2,1)} %bitcast.3, bf16[768,512]{1,0:T(8,128)(2,1)S(1)} %collective-permute-done.5), kind=kOutput, calls=%fused_computation.96 | convolution fusion | flops 603979776 | bytes 3932160 | tf_op jit(solution)/shard_map/qe,ke->qk/dot_general | solution.py:81
  99.5 2.7 %select_reduce_fusion = f32[768]{0:T(1024)S(1)} fusion(f32[768,768]{0,1:T(8,128)S(1)} %fusion.46, f32[768]{0:T(1024)S(1)} %fusion.33, f32[768]{0:T(1024)S(1)} %convert_reduce_fusion, f32[768]{0:T(1024)S(1)} %get-tuple-element.10, f32[768]{0:T(1024)S(1)} %get-tuple-element.9, pred[768]{0:T(1024)(128)(4,1)S(1)} %broadcast_compare_fusion, ...), kind=kOutput, calls=%fused_computation | convolution fusion | flops 608107776 | bytes 3952640 | tf_op jit(solution)/shard_map/qe,ke->qk/dot_general | solution.py:80
  102.3 11.4 %all_to_all.16 = f32[8,1,96]{2,1,0:T(1,128)S(1)} all-to-all(f32[8,1,96]{2,1,0:T(1,128)S(1)} %max.41), channel_id=1, replica_groups=mesh['grp'=8,'split'=4] {'grp'}, dimensions={0} | all-to-all | bytes 6144 | tf_op jit(solution)/shard_map/all_to_all | solution.py:92
  114.2 0.7 reduce.19
  115.0 0.8 select_reduce_fusion.4
  (35 shorter events, 2.4 us)
Async XLA Ops:
  0.0 1.9 %copy-start = (bf16[384,4096]{1,0:T(8,128)(2,1)S(1)}, bf16[384,4096]{1,0:T(8,128)(2,1)}, u32[]{:S(2)}) copy-start(bf16[384,4096]{1,0:T(8,128)(2,1)} %param.5) | copy-start | bytes 9437188
  8.0 0.9 copy-start.1
  8.9 9.6 %copy-start.2 = (s32[384]{0:T(512)S(1)}, s32[384]{0:T(512)}, u32[]{:S(2)}) copy-start(s32[384]{0:T(512)} %param.8) | copy-start | bytes 4612
  8.9 10.3 %copy-start.3 = (s32[384]{0:T(512)S(1)}, s32[384]{0:T(512)}, u32[]{:S(2)}) copy-start(s32[384]{0:T(512)} %param.9) | copy-start | bytes 4612
  10.4 11.1 %slice-start = ((bf16[384,1024]{1,0:T(8,128)(2,1)}), bf16[384,512]{1,0:T(8,128)(2,1)S(1)}, s32[]{:S(2)}) async-start(bf16[384,1024]{1,0:T(8,128)(2,1)} %copy-done.1), calls=%async_computation.3 | async-start | bytes 786432 | tf_op jit(solution)/shard_map/slice | solution.py:72
  10.4 27.7 %all-to-all-start.1 = ((bf16[8,96,512]{2,1,0:T(8,128)(2,1)}), bf16[8,96,512]{2,1,0:T(8,128)(2,1)}, u32[]{:S(2)}, u32[]{:S(2)}) async-start(bf16[8,96,512]{2,1,0:T(8,128)(2,1)} %bitcast.16), calls=%async_computation.1 | async-start | bytes 1572864 | tf_op jit(solution)/shard_map/all_to_all | solution.py:69
  38.1 28.4 %all-to-all-start = ((bf16[8,96,640]{2,1,0:T(8,128)(2,1)}), bf16[8,96,640]{2,1,0:T(8,128)(2,1)}, u32[]{:S(2)}, u32[]{:S(2)}) async-start(bf16[8,96,640]{2,1,0:T(8,128)(2,1)} %bitcast.15), calls=%async_computation | async-start | bytes 1966080 | tf_op jit(solution)/shard_map/all_to_all | solution.py:69
  42.3 34.8 %collective-permute-start.1 = (bf16[768,512]{1,0:T(8,128)(2,1)}, bf16[768,512]{1,0:T(8,128)(2,1)}, u32[]{:S(2)}, u32[]{:S(2)}) collective-permute-start(bf16[768,512]{1,0:T(8,128)(2,1)} %bitcast.3), channel_id=1, source_target_pairs={{0,2},{1,3},{2,0},{3,1},{4,6},{5,7},{6,4},{7,5},{8,10},{9,11},{10,... | collective-permute-start | bytes 2359304 | tf_op jit(solution)/shard_map/ppermute | solution.py:21
  43.9 35.9 %collective-permute-start.3 = (bf16[768,512]{1,0:T(8,128)(2,1)}, bf16[768,512]{1,0:T(8,128)(2,1)}, u32[]{:S(2)}, u32[]{:S(2)}) collective-permute-start(bf16[768,512]{1,0:T(8,128)(2,1)} %bitcast.3), channel_id=1, source_target_pairs={{0,1},{1,0},{2,3},{3,2},{4,5},{5,4},{6,7},{7,6},{8,9},{9,8},{10,11... | collective-permute-start | bytes 2359304 | tf_op jit(solution)/shard_map/ppermute | solution.py:23
  69.9 22.2 %collective-permute-start = (bf16[768,640]{0,1:T(8,128)(2,1)}, bf16[768,640]{0,1:T(8,128)(2,1)S(1)}, u32[]{:S(2)}, u32[]{:S(2)}) collective-permute-start(bf16[768,640]{0,1:T(8,128)(2,1)} %copy.23), channel_id=1, source_target_pairs={{0,2},{1,3},{2,0},{3,1},{4,6},{5,7},{6,4},{7,5},{8,10},{9,11},{10,... | collective-permute-start | bytes 2949128 | tf_op jit(solution)/shard_map/ppermute | solution.py:21
  71.4 10.6 %collective-permute-start.2 = (bf16[768,640]{0,1:T(8,128)(2,1)}, bf16[768,640]{0,1:T(8,128)(2,1)S(1)}, u32[]{:S(2)}, u32[]{:S(2)}) collective-permute-start(bf16[768,640]{0,1:T(8,128)(2,1)} %copy.23), channel_id=1, source_target_pairs={{0,1},{1,0},{2,3},{3,2},{4,5},{5,4},{6,7},{7,6},{8,9},{9,8},{10,11... | collective-permute-start | bytes 2949128 | tf_op jit(solution)/shard_map/ppermute | solution.py:23
  77.1 20.4 %collective-permute-start.5 = (bf16[768,512]{1,0:T(8,128)(2,1)}, bf16[768,512]{1,0:T(8,128)(2,1)S(1)}, u32[]{:S(2)}, u32[]{:S(2)}) collective-permute-start(bf16[768,512]{1,0:T(8,128)(2,1)} %collective-permute-done.1), channel_id=1, source_target_pairs={{0,1},{1,0},{2,3},{3,2},{4,5},{5,4},{6,7},{7,6},{8,9},{9,8},{10,11... | collective-permute-start | bytes 2359304 | tf_op jit(solution)/shard_map/ppermute | solution.py:23
  92.0 7.4 %collective-permute-start.4 = (bf16[768,640]{0,1:T(8,128)(2,1)S(1)}, bf16[768,640]{0,1:T(8,128)(2,1)S(1)}, u32[]{:S(2)}, u32[]{:S(2)}) collective-permute-start(bf16[768,640]{0,1:T(8,128)(2,1)S(1)} %collective-permute-done), channel_id=1, source_target_pairs={{0,1},{1,0},{2,3},{3,2},{4,5},{5,4},{6,7},{7,6},{8,9},{9,8},{10,11... | collective-permute-start | bytes 2949128 | tf_op jit(solution)/shard_map/ppermute | solution.py:23

commit v4 on v3

--- a/solution.py
+++ b/solution.py
@@ -70,21 +70,21 @@
         return got.reshape(n_slot, -1)
 
     got_a = route(jnp.concatenate([embeds[:, :half], meta], axis=1))
-    keys_a = gather_split(got_a, n_split)
+    q_emb, q_lab, q_ord = unpack(got_a, half, n_all)
+    keys_a = gather_split(q_emb, n_split)
+    keys_m = gather_split(jnp.stack([q_lab, q_ord]), n_split)
     got_b = route(embeds[:, half:])
     keys_b = gather_split(got_b, n_split)
 
-    q_emb, q_lab, q_ord = unpack(got_a, half, n_all)
-
     def dots(k_a, k_b):
-        s = jnp.einsum("qe,ke->qk", q_emb, k_a[:, :half], preferred_element_type=jnp.float32)
+        s = jnp.einsum("qe,ke->qk", q_emb, k_a, preferred_element_type=jnp.float32)
         return s + jnp.einsum("qe,ke->qk", got_b, k_b, preferred_element_type=jnp.float32)
 
-    scores = dots(got_a, got_b)
+    scores = dots(q_emb, got_b)
     hits = (q_lab[:, None] == q_lab[None, :]) & (q_lab[None, :] > 0) & (q_ord[None, :] < q_ord[:, None])
     best = jnp.max(jnp.where(hits, scores, jnp.float32(-1.0)), axis=1)
-    for k_a, k_b in zip(keys_a, keys_b):
-        _, k_lab, k_ord = unpack(k_a, half, n_all)
+    for k_a, k_b, k_m in zip(keys_a, keys_b, keys_m):
+        k_lab, k_ord = k_m[0], k_m[1]
         scores = dots(k_a, k_b)
         hits = (q_lab[:, None] == k_lab[None, :]) & (k_lab[None, :] > 0) & (k_ord[None, :] < q_ord[:, None])
         best = jnp.maximum(best, jnp.max(jnp.where(hits, scores, jnp.float32(-1.0)), axis=1))

time: 117 us -> 115 us (0.983)
  blocking collectives: 11.4 us -> 9.62 us
  waiting for transfers between devices: 44.6 us -> 46.1 us
  matrix products: 29.5 us -> 28.1 us
    reshape x1 -> x0, local copies, waits for them, and re-layouts: 2.29 us -> none  [route(): return got.reshape(n_slot, -1)]
    all_to_all x1, blocking collectives: 11.4 us -> 9.62 us  [local(): lax.all_to_all(best.reshape(n_grp, cap), 'grp', split_axis=0, concat_axis...]
    ppermute x2 -> x3, waiting for transfers between devices: 0.01 us -> 1.61 us  [gather_split(): lax.ppermute(cross, 'split', pair)]
    dot_general x4, matrix products: 10.4 us -> 9.04 us  [dots(): s = jnp.einsum('qe,ke->qk', q_emb, k_a, preferred_element_type=jnp.float32)]
    slice x0 -> x4, local copies, waits for them, and re-layouts: none -> 1.25 us  [the longest x1 1.18 us: unpack(): emb = buf[:, :emb_w]]
    ppermute x2 -> x3, starting transfers between devices: 3.17 us -> 3.75 us  [gather_split(): cross = lax.ppermute(rows, 'split', [(0, 2), (1, 3), (2, 0), (3, 1)])]
    ppermute x2 -> x3, waiting for transfers between devices: 9.94 us -> 9.91 us  [gather_split(): cross = lax.ppermute(rows, 'split', [(0, 2), (1, 3), (2, 0), (3, 1)])]
  transfers between devices with their start and end apart: 8 -> 11, of which waited for: 3 -> 4; matrix products, arithmetic and copies ran while one was open for 25% -> 24% of each run, Pallas kernels for 0% -> 0%
where the time goes in v4:
time: 115 us; the launch traced here: 114 us
  waiting for transfers between devices  46.1 us (40%)
  matrix products  28.1 us (24%)
  starting transfers between devices  16.3 us (14%)
  blocking collectives  9.62 us (8%)
  local copies, waits for them, and re-layouts  9.22 us (8%)
  other arithmetic  4.27 us (4%)
    all_to_all x2, waiting for transfers between devices, route(): got = lax.all_to_all(send, 'grp', split_axis=0, concat_axis=0, tiled=True)  34.6 us
    all_to_all x2, starting transfers between devices, route(): got = lax.all_to_all(send, 'grp', split_axis=0, concat_axis=0, tiled=True)  11.6 us
    ppermute x3, waiting for transfers between devices, gather_split(): cross = lax.ppermute(rows, 'split', [(0, 2), (1, 3), (2, 0), (3, 1)])  9.91 us
    all_to_all x1, blocking collectives, local(): lax.all_to_all(best.reshape(n_grp, cap), 'grp', split_axis=0, concat_axis...  9.62 us
    dot_general x4, matrix products, dots(): s = jnp.einsum('qe,ke->qk', q_emb, k_a, preferred_element_type=jnp.float32)  9.04 us
    dot_general x4, matrix products, dots(): jnp.einsum('qe,ke->qk', got_b, k_b, preferred_element_type=jnp.float32)  8.74 us
    dot_general x1, matrix products, embed_rows(): jnp.einsum('...h,he->...e', rows, weight, preferred_element_type=jnp.floa...  5.94 us
    dot_general x2, matrix products, route(): jnp.dot(pick.astype(jnp.bfloat16), rows, preferred_element_type=jnp.float32)  4.18 us
  transfers between devices with their start and end apart: 11, of which 4 were waited for; matrix products, arithmetic and copies ran while one was open for 24% of the time, Pallas kernels for 0%

profile of v4, /device:TPU:0, one launch (start us, length us, event | category | flops | bytes accessed | tf_op | source)
XLA Modules:
  0.0 113.9 jit_solution(10144226282593655526)
XLA Ops:
  0.0 0.8 convert_convert_fusion.1
  1.1 0.8 copy-done
  1.9 5.9 %multiply_reduce_fusion = (f32[384]{0:T(512)S(1)}, f32[384,1024]{1,0:T(8,128)S(1)}) fusion(bf16[384,4096]{1,0:T(8,128)(2,1)S(1)} %copy-done, bf16[4096,1024]{1,0:T(8,128)(2,1)} %param.6), kind=kOutput, calls=%fused_computation.5 | convolution fusion | flops 3222011392 | bytes 13108736 | tf_op jit(solution)/shard_map/...h,he->...e/dot_general | solution.py:14
  8.0 0.9 copy-done.1
  8.9 1.5 %convolution_convert_fusion.1 = bf16[768,512]{1,0:T(8,128)(2,1)} fusion(s32[384]{0:T(512)S(1)} %convert_add_fusion, bf16[384,1024]{1,0:T(8,128)(2,1)S(1)} %multiply_convert_fusion), kind=kOutput, calls=%fused_computation.7 | convolution fusion | flops 302678016 | bytes 1181696 | tf_op jit(solution)/shard_map/dot_general | solution.py:67
  10.4 7.4 %all-to-all-start.1 = ((bf16[8,96,512]{2,1,0:T(8,128)(2,1)}), bf16[8,96,512]{2,1,0:T(8,128)(2,1)}, u32[]{:S(2)}, u32[]{:S(2)}) async-start(bf16[8,96,512]{2,1,0:T(8,128)(2,1)} %bitcast.19), calls=%async_computation.1 | async-start | bytes 1572864 | tf_op jit(solution)/shard_map/all_to_all | solution.py:69
  17.8 0.7 stack.26
  18.5 0.8 stack.27
  19.3 0.8 stack.28
  20.1 0.7 stack.29
  21.4 1.9 %concatenate.6 = bf16[384,640]{1,0:T(8,128)(2,1)} concatenate(bf16[384,512]{1,0:T(8,128)(2,1)S(1)} %slice-done, bf16[384,1]{1,0:T(8,128)(2,1)} %stack.26, bf16[384,1]{1,0:T(8,128)(2,1)} %stack.27, bf16[384,1]{1,0:T(8,128)(2,1)} %stack.28, bf16[384,1]{1,0:T(8,128)(2,1)} %stack.29, bf16[384,124]{1,0:T(8,128)(2,1)} %broadcast_in_dim.19), dimensions={1} | concatenate | bytes 983040 | tf_op jit(solution)/shard_map/concatenate | solution.py:72
  23.3 2.7 %convolution_convert_fusion = bf16[768,640]{1,0:T(8,128)(2,1)} fusion(bf16[384,640]{1,0:T(8,128)(2,1)} %concatenate.6, s32[384]{0:T(512)S(1)} %convert_add_fusion), kind=kOutput, calls=%fused_computation.6 | convolution fusion | flops 378273792 | bytes 1476096 | tf_op jit(solution)/shard_map/dot_general | solution.py:67
  26.1 12.0 %all-to-all-done.1 = bf16[8,96,512]{2,1,0:T(8,128)(2,1)} async-done(((bf16[8,96,512]{2,1,0:T(8,128)(2,1)}), bf16[8,96,512]{2,1,0:T(8,128)(2,1)}, u32[]{:S(2)}, u32[]{:S(2)}) %all-to-all-start.1) | async-done | bytes 786464 | tf_op jit(solution)/shard_map/all_to_all | solution.py:69
  38.1 4.2 %all-to-all-start = ((bf16[8,96,640]{2,1,0:T(8,128)(2,1)}), bf16[8,96,640]{2,1,0:T(8,128)(2,1)}, u32[]{:S(2)}, u32[]{:S(2)}) async-start(bf16[8,96,640]{2,1,0:T(8,128)(2,1)} %bitcast.18), calls=%async_computation | async-start | bytes 1966080 | tf_op jit(solution)/shard_map/all_to_all | solution.py:69
  42.3 1.6 %collective-permute-start.2 = (bf16[768,512]{1,0:T(8,128)(2,1)}, bf16[768,512]{1,0:T(8,128)(2,1)}, u32[]{:S(2)}, u32[]{:S(2)}) collective-permute-start(bf16[768,512]{1,0:T(8,128)(2,1)} %bitcast.3), channel_id=1, source_target_pairs={{0,2},{1,3},{2,0},{3,1},{4,6},{5,7},{6,4},{7,5},{8,10},{9,11},{10,... | collective-permute-start | bytes 2359304 | tf_op jit(solution)/shard_map/ppermute | solution.py:21
  43.9 22.6 %all-to-all-done = bf16[8,96,640]{2,1,0:T(8,128)(2,1)} async-done(((bf16[8,96,640]{2,1,0:T(8,128)(2,1)}), bf16[8,96,640]{2,1,0:T(8,128)(2,1)}, u32[]{:S(2)}, u32[]{:S(2)}) %all-to-all-start) | async-done | bytes 983072 | tf_op jit(solution)/shard_map/all_to_all | solution.py:69
  66.5 1.2 %slice.57 = bf16[768,512]{1,0:T(8,128)(2,1)S(1)} slice(bf16[768,640]{1,0:T(8,128)(2,1)} %bitcast.1), slice={[0:768], [0:512]} | slice | bytes 1572864 | tf_op jit(solution)/shard_map/slice | solution.py:31
  67.7 1.7 %convert_reduce_fusion = (f32[768]{0:T(1024)S(1)}, f32[768]{0:T(1024)S(1)}) fusion(bf16[768,640]{1,0:T(8,128)(2,1)} %bitcast.1), kind=kLoop, calls=%fused_computation.16 | loop fusion | flops 6144 | bytes 12288 | tf_op jit(solution)/shard_map/eq | solution.py:84
  69.4 1.6 %collective-permute-start = (f32[2,768]{1,0:T(2,128)S(1)}, f32[2,768]{1,0:T(2,128)S(1)}, u32[]{:S(2)}, u32[]{:S(2)}) collective-permute-start(f32[2,768]{1,0:T(2,128)S(1)} %pad_maximum_fusion), channel_id=1, source_target_pairs={{0,2},{1,3},{2,0},{3,1},{4,6},{5,7},{6,4},{7,5},{8,10},{9,11},{10,... | collective-permute-start | bytes 18440 | tf_op jit(solution)/shard_map/ppermute | solution.py:21
  71.0 2.3 %fusion.16 = f32[768,768]{0,1:T(8,128)S(1)} fusion(bf16[768,640]{1,0:T(8,128)(2,1)} %bitcast.1), kind=kOutput, calls=%fused_computation.59 | convolution fusion | flops 603979776 | bytes 3145728 | tf_op jit(solution)/shard_map/qe,ke->qk/dot_general | solution.py:80
  73.9 2.5 %select_reduce_fusion.3 = f32[768]{0:T(1024)S(1)} fusion(f32[768,768]{0,1:T(8,128)S(1)} %fusion.16, bf16[768,512]{1,0:T(8,128)(2,1)} %bitcast.3, f32[768]{0:T(1024)S(1)} %get-tuple-element.6, f32[768]{0:T(1024)S(1)} %get-tuple-element.5, pred[768]{0:T(1024)(128)(4,1)S(1)} %broadcast_compare_fusion), kind=kOutput, calls=%fused_computation.3 | convolution fusion | flops 608107776 | bytes 3155712 | tf_op jit(solution)/shard_map/qe,ke->qk/dot_general | solution.py:81
  77.1 1.6 %collective-permute-done.6 = f32[2,768]{1,0:T(2,128)S(1)} collective-permute-done((f32[2,768]{1,0:T(2,128)S(1)}, f32[2,768]{1,0:T(2,128)S(1)}, u32[]{:S(2)}, u32[]{:S(2)}) %collective-permute-start.6) | collective-permute-done | bytes 6176 | tf_op jit(solution)/shard_map/ppermute | solution.py:23
  79.1 2.2 %fusion.18 = f32[768,768]{0,1:T(8,128)S(1)} fusion(bf16[768,512]{1,0:T(8,128)(2,1)} %bitcast.3, bf16[768,512]{1,0:T(8,128)(2,1)} %collective-permute-done.2), kind=kOutput, calls=%fused_computation.61 | convolution fusion | flops 603979776 | bytes 3932160 | tf_op jit(solution)/shard_map/qe,ke->qk/dot_general | solution.py:81
  81.3 2.2 %fusion.19 = f32[768,768]{0,1:T(8,128)S(1)} fusion(bf16[768,512]{1,0:T(8,128)(2,1)} %bitcast.3, bf16[768,512]{1,0:T(8,128)(2,1)} %collective-permute-done.5), kind=kOutput, calls=%fused_computation.62 | convolution fusion | flops 603979776 | bytes 3932160 | tf_op jit(solution)/shard_map/qe,ke->qk/dot_general | solution.py:81
  83.4 9.9 %collective-permute-done.1 = bf16[768,512]{1,0:T(8,128)(2,1)S(1)} collective-permute-done((bf16[768,512]{1,0:T(8,128)(2,1)S(1)}, bf16[768,512]{1,0:T(8,128)(2,1)S(1)}, u32[]{:S(2)}, u32[]{:S(2)}) %collective-permute-start.1) | collective-permute-done | bytes 786464 | tf_op jit(solution)/shard_map/ppermute | solution.py:21
  93.3 2.3 %select_reduce_fusion.2 = f32[768]{0:T(1024)S(1)} fusion(f32[768,768]{0,1:T(8,128)S(1)} %fusion.18, bf16[768,512]{1,0:T(8,128)(2,1)S(1)} %collective-permute-done.1, f32[768]{0:T(1024)S(1)} %get-tuple-element.6, f32[768]{0:T(1024)S(1)} %get-tuple-element.5, f32[768]{0:T(1024)S(1)} %get-tuple-element.8, f32[768]{0:T(1024)S(1)} %get-tuple-element.7, ...), kind=kOutput, calls=%fused_computation.2 | convolution fusion | flops 608107776 | bytes 3948288 | tf_op jit(solution)/shard_map/qe,ke->qk/dot_general | solution.py:80
  95.6 2.3 %select_reduce_fusion.1 = f32[768]{0:T(1024)S(1)} fusion(f32[768,768]{0,1:T(8,128)S(1)} %fusion.19, bf16[768,512]{1,0:T(8,128)(2,1)S(1)} %collective-permute-done.4, f32[768]{0:T(1024)S(1)} %get-tuple-element.6, f32[768]{0:T(1024)S(1)} %get-tuple-element.5, f32[768]{0:T(1024)S(1)} %get-tuple-element.10, f32[768]{0:T(1024)S(1)} %get-tuple-element.9, ...), kind=kOutput, calls=%fused_computation.1 | convolution fusion | flops 608107776 | bytes 3948288 | tf_op jit(solution)/shard_map/qe,ke->qk/dot_general | solution.py:80
  97.9 1.9 %fusion.20 = f32[768,768]{0,1:T(8,128)S(1)} fusion(bf16[768,512]{1,0:T(8,128)(2,1)} %bitcast.3, bf16[768,512]{1,0:T(8,128)(2,1)S(1)} %collective-permute-done.8), kind=kOutput, calls=%fused_computation.63 | convolution fusion | flops 603979776 | bytes 3932160 | tf_op jit(solution)/shard_map/qe,ke->qk/dot_general | solution.py:81
  99.8 2.2 %select_reduce_fusion = f32[768]{0:T(1024)S(1)} fusion(f32[768,768]{0,1:T(8,128)S(1)} %fusion.20, bf16[768,512]{1,0:T(8,128)(2,1)S(1)} %collective-permute-done.7, f32[768]{0:T(1024)S(1)} %get-tuple-element.6, f32[768]{0:T(1024)S(1)} %get-tuple-element.5, f32[768]{0:T(1024)S(1)} %get-tuple-element.12, f32[768]{0:T(1024)S(1)} %get-tuple-element.11, ...), kind=kOutput, calls=%fused_computation | convolution fusion | flops 608107776 | bytes 3948288 | tf_op jit(solution)/shard_map/qe,ke->qk/dot_general | solution.py:80
  102.2 9.6 %all_to_all.16 = f32[8,1,96]{2,1,0:T(1,128)S(1)} all-to-all(f32[8,1,96]{2,1,0:T(1,128)S(1)} %max.41), channel_id=1, replica_groups=mesh['grp'=8,'split'=4] {'grp'}, dimensions={0} | all-to-all | bytes 6144 | tf_op jit(solution)/shard_map/all_to_all | solution.py:92
  112.3 0.7 reduce.27
  113.1 0.8 select_reduce_fusion.4
  (43 shorter events, 3.4 us)
Async XLA Ops:
  0.0 1.9 %copy-start = (bf16[384,4096]{1,0:T(8,128)(2,1)S(1)}, bf16[384,4096]{1,0:T(8,128)(2,1)}, u32[]{:S(2)}) copy-start(bf16[384,4096]{1,0:T(8,128)(2,1)} %param.5) | copy-start | bytes 9437188
  8.0 0.9 copy-start.1
  8.9 9.6 %copy-start.2 = (s32[384]{0:T(512)S(1)}, s32[384]{0:T(512)}, u32[]{:S(2)}) copy-start(s32[384]{0:T(512)} %param.8) | copy-start | bytes 4612
  8.9 10.3 %copy-start.3 = (s32[384]{0:T(512)S(1)}, s32[384]{0:T(512)}, u32[]{:S(2)}) copy-start(s32[384]{0:T(512)} %param.9) | copy-start | bytes 4612
  10.4 11.1 %slice-start = ((bf16[384,1024]{1,0:T(8,128)(2,1)}), bf16[384,512]{1,0:T(8,128)(2,1)S(1)}, s32[]{:S(2)}) async-start(bf16[384,1024]{1,0:T(8,128)(2,1)} %copy-done.1), calls=%async_computation.3 | async-start | bytes 786432 | tf_op jit(solution)/shard_map/slice | solution.py:72
  10.4 27.7 %all-to-all-start.1 = ((bf16[8,96,512]{2,1,0:T(8,128)(2,1)}), bf16[8,96,512]{2,1,0:T(8,128)(2,1)}, u32[]{:S(2)}, u32[]{:S(2)}) async-start(bf16[8,96,512]{2,1,0:T(8,128)(2,1)} %bitcast.19), calls=%async_computation.1 | async-start | bytes 1572864 | tf_op jit(solution)/shard_map/all_to_all | solution.py:69
  38.1 28.4 %all-to-all-start = ((bf16[8,96,640]{2,1,0:T(8,128)(2,1)}), bf16[8,96,640]{2,1,0:T(8,128)(2,1)}, u32[]{:S(2)}, u32[]{:S(2)}) async-start(bf16[8,96,640]{2,1,0:T(8,128)(2,1)} %bitcast.18), calls=%async_computation | async-start | bytes 1966080 | tf_op jit(solution)/shard_map/all_to_all | solution.py:69
  42.3 36.5 %collective-permute-start.2 = (bf16[768,512]{1,0:T(8,128)(2,1)}, bf16[768,512]{1,0:T(8,128)(2,1)}, u32[]{:S(2)}, u32[]{:S(2)}) collective-permute-start(bf16[768,512]{1,0:T(8,128)(2,1)} %bitcast.3), channel_id=1, source_target_pairs={{0,2},{1,3},{2,0},{3,1},{4,6},{5,7},{6,4},{7,5},{8,10},{9,11},{10,... | collective-permute-start | bytes 2359304 | tf_op jit(solution)/shard_map/ppermute | solution.py:21
  43.9 37.4 %collective-permute-start.5 = (bf16[768,512]{1,0:T(8,128)(2,1)}, bf16[768,512]{1,0:T(8,128)(2,1)}, u32[]{:S(2)}, u32[]{:S(2)}) collective-permute-start(bf16[768,512]{1,0:T(8,128)(2,1)} %bitcast.3), channel_id=1, source_target_pairs={{0,1},{1,0},{2,3},{3,2},{4,5},{5,4},{6,7},{7,6},{8,9},{9,8},{10,11... | collective-permute-start | bytes 2359304 | tf_op jit(solution)/shard_map/ppermute | solution.py:23
  69.4 7.3 %collective-permute-start = (f32[2,768]{1,0:T(2,128)S(1)}, f32[2,768]{1,0:T(2,128)S(1)}, u32[]{:S(2)}, u32[]{:S(2)}) collective-permute-start(f32[2,768]{1,0:T(2,128)S(1)} %pad_maximum_fusion), channel_id=1, source_target_pairs={{0,2},{1,3},{2,0},{3,1},{4,6},{5,7},{6,4},{7,5},{8,10},{9,11},{10,... | collective-permute-start | bytes 18440 | tf_op jit(solution)/shard_map/ppermute | solution.py:21
  71.0 5.4 %collective-permute-start.3 = (f32[2,768]{1,0:T(2,128)S(1)}, f32[2,768]{1,0:T(2,128)S(1)}, u32[]{:S(2)}, u32[]{:S(2)}) collective-permute-start(f32[2,768]{1,0:T(2,128)S(1)} %pad_maximum_fusion), channel_id=1, source_target_pairs={{0,1},{1,0},{2,3},{3,2},{4,5},{5,4},{6,7},{7,6},{8,9},{9,8},{10,11... | collective-permute-start | bytes 18440 | tf_op jit(solution)/shard_map/ppermute | solution.py:23
  73.3 20.0 %collective-permute-start.1 = (bf16[768,512]{1,0:T(8,128)(2,1)S(1)}, bf16[768,512]{1,0:T(8,128)(2,1)S(1)}, u32[]{:S(2)}, u32[]{:S(2)}) collective-permute-start(bf16[768,512]{1,0:T(8,128)(2,1)S(1)} %slice.57), channel_id=1, source_target_pairs={{0,2},{1,3},{2,0},{3,1},{4,6},{5,7},{6,4},{7,5},{8,10},{9,11},{10,... | collective-permute-start | bytes 2359304 | tf_op jit(solution)/shard_map/ppermute | solution.py:21
  76.4 19.2 %collective-permute-start.4 = (bf16[768,512]{1,0:T(8,128)(2,1)S(1)}, bf16[768,512]{1,0:T(8,128)(2,1)S(1)}, u32[]{:S(2)}, u32[]{:S(2)}) collective-permute-start(bf16[768,512]{1,0:T(8,128)(2,1)S(1)} %slice.57), channel_id=1, source_target_pairs={{0,1},{1,0},{2,3},{3,2},{4,5},{5,4},{6,7},{7,6},{8,9},{9,8},{10,11... | collective-permute-start | bytes 2359304 | tf_op jit(solution)/shard_map/ppermute | solution.py:23
  76.7 2.0 %collective-permute-start.6 = (f32[2,768]{1,0:T(2,128)S(1)}, f32[2,768]{1,0:T(2,128)S(1)}, u32[]{:S(2)}, u32[]{:S(2)}) collective-permute-start(f32[2,768]{1,0:T(2,128)S(1)} %collective-permute-done), channel_id=1, source_target_pairs={{0,1},{1,0},{2,3},{3,2},{4,5},{5,4},{6,7},{7,6},{8,9},{9,8},{10,11... | collective-permute-start | bytes 18440 | tf_op jit(solution)/shard_map/ppermute | solution.py:23
  78.8 19.1 %collective-permute-start.8 = (bf16[768,512]{1,0:T(8,128)(2,1)}, bf16[768,512]{1,0:T(8,128)(2,1)S(1)}, u32[]{:S(2)}, u32[]{:S(2)}) collective-permute-start(bf16[768,512]{1,0:T(8,128)(2,1)} %collective-permute-done.2), channel_id=1, source_target_pairs={{0,1},{1,0},{2,3},{3,2},{4,5},{5,4},{6,7},{7,6},{8,9},{9,8},{10,11... | collective-permute-start | bytes 2359304 | tf_op jit(solution)/shard_map/ppermute | solution.py:23
  93.3 6.5 %collective-permute-start.7 = (bf16[768,512]{1,0:T(8,128)(2,1)S(1)}, bf16[768,512]{1,0:T(8,128)(2,1)S(1)}, u32[]{:S(2)}, u32[]{:S(2)}) collective-permute-start(bf16[768,512]{1,0:T(8,128)(2,1)S(1)} %collective-permute-done.1), channel_id=1, source_target_pairs={{0,1},{1,0},{2,3},{3,2},{4,5},{5,4},{6,7},{7,6},{8,9},{9,8},{10,11... | collective-permute-start | bytes 2359304 | tf_op jit(solution)/shard_map/ppermute | solution.py:23

commit v5 on v4

--- a/solution.py
+++ b/solution.py
@@ -51,7 +51,7 @@
 
     embeds = embed_rows(states, weight)
     emb_w = embeds.shape[1]
-    half = emb_w // 2
+    half = emb_w - 3 * emb_w // 8
     label = (cluster_id - owner_of * CL_GRP + 1).astype(jnp.float32)
     meta_cols = jnp.stack(
         [label, block.astype(jnp.float32), (order // 256).astype(jnp.float32),

time: 115 us -> 118 us (1.026)
  matrix products: 28.1 us -> 32.2 us
  waiting for transfers between devices: 46.1 us -> 43.7 us
  blocking collectives: 9.62 us -> 11.6 us
    all_to_all x2, waiting for transfers between devices: 34.6 us -> 15.1 us  [route(): got = lax.all_to_all(send, 'grp', split_axis=0, concat_axis=0, tiled=True)]
    ppermute x3, waiting for transfers between devices: 9.91 us -> 27.6 us  [gather_split(): cross = lax.ppermute(rows, 'split', [(0, 2), (1, 3), (2, 0), (3, 1)])]
    another operation x4, local copies, waits for them, and re-layouts: 3 us -> 0.45 us  [local(): jnp.stack([label, block.astype(jnp.float32), (order // 256).astype(jnp.fl...]
    dot_general x4, matrix products: 8.74 us -> 11.1 us  [dots(): jnp.einsum('qe,ke->qk', got_b, k_b, preferred_element_type=jnp.float32)]
    all_to_all x1, blocking collectives: 9.62 us -> 11.6 us  [local(): lax.all_to_all(best.reshape(n_grp, cap), 'grp', split_axis=0, concat_axis...]
    slice x2 -> x1, local copies, waits for them, and re-layouts: 0.01 us -> 1.87 us  [local(): got_a = route(jnp.concatenate([embeds[:, :half], meta], axis=1))]
    dot_general x4, matrix products: 9.04 us -> 10.8 us  [dots(): s = jnp.einsum('qe,ke->qk', q_emb, k_a, preferred_element_type=jnp.float32)]
  transfers between devices with their start and end apart: 11 -> 11, of which waited for: 4 -> 5; matrix products, arithmetic and copies ran while one was open for 24% -> 26% of each run, Pallas kernels for 0% -> 0%
where the time goes in v5:
time: 118 us; the launch traced here: 117 us
  waiting for transfers between devices  43.7 us (37%)
  matrix products  32.2 us (27%)
  starting transfers between devices  15.7 us (13%)
  blocking collectives  11.6 us (10%)
  local copies, waits for them, and re-layouts  8.68 us (7%)
  other arithmetic  4.6 us (4%)
    ppermute x3, waiting for transfers between devices, gather_split(): cross = lax.ppermute(rows, 'split', [(0, 2), (1, 3), (2, 0), (3, 1)])  27.6 us
    all_to_all x2, waiting for transfers between devices, route(): got = lax.all_to_all(send, 'grp', split_axis=0, concat_axis=0, tiled=True)  15.1 us
    all_to_all x1, blocking collectives, local(): lax.all_to_all(best.reshape(n_grp, cap), 'grp', split_axis=0, concat_axis...  11.6 us
    all_to_all x2, starting transfers between devices, route(): got = lax.all_to_all(send, 'grp', split_axis=0, concat_axis=0, tiled=True)  11.5 us
    dot_general x4, matrix products, dots(): jnp.einsum('qe,ke->qk', got_b, k_b, preferred_element_type=jnp.float32)  11.1 us
    dot_general x4, matrix products, dots(): s = jnp.einsum('qe,ke->qk', q_emb, k_a, preferred_element_type=jnp.float32)  10.8 us
    dot_general x1, matrix products, embed_rows(): jnp.einsum('...h,he->...e', rows, weight, preferred_element_type=jnp.floa...  5.94 us
    dot_general x2, matrix products, route(): jnp.dot(pick.astype(jnp.bfloat16), rows, preferred_element_type=jnp.float32)  4.18 us
  transfers between devices with their start and end apart: 11, of which 5 were waited for; matrix products, arithmetic and copies ran while one was open for 26% of the time, Pallas kernels for 0%

profile of v5, /device:TPU:0, one launch (start us, length us, event | category | flops | bytes accessed | tf_op | source)
XLA Modules:
  0.0 116.8 jit_solution(600303140979087403)
XLA Ops:
  0.0 0.8 convert_convert_fusion.1
  1.1 0.8 copy-done
  1.9 5.9 %multiply_reduce_fusion = (f32[384]{0:T(512)S(1)}, f32[384,1024]{1,0:T(8,128)S(1)}) fusion(bf16[384,4096]{1,0:T(8,128)(2,1)S(1)} %copy-done, bf16[4096,1024]{1,0:T(8,128)(2,1)} %param.6), kind=kOutput, calls=%fused_computation.5 | convolution fusion | flops 3222011392 | bytes 13108736 | tf_op jit(solution)/shard_map/...h,he->...e/dot_general | solution.py:14
  8.0 0.9 copy-done.3
  8.9 1.3 %convolution_convert_fusion.1 = bf16[768,384]{1,0:T(8,128)(2,1)} fusion(s32[384]{0:T(512)S(1)} %convert_add_fusion, bf16[384,1024]{1,0:T(8,128)(2,1)S(1)} %multiply_convert_fusion), kind=kOutput, calls=%fused_computation.7 | convolution fusion | flops 227082240 | bytes 886784 | tf_op jit(solution)/shard_map/dot_general | solution.py:67
  10.2 7.3 %all-to-all-start.1 = ((bf16[8,96,384]{2,1,0:T(8,128)(2,1)}), bf16[8,96,384]{2,1,0:T(8,128)(2,1)}, u32[]{:S(2)}, u32[]{:S(2)}) async-start(bf16[8,96,384]{2,1,0:T(8,128)(2,1)} %bitcast.19), calls=%async_computation.1 | async-start | bytes 1179648 | tf_op jit(solution)/shard_map/all_to_all | solution.py:69
  17.5 1.9 %slice.52 = bf16[384,640]{1,0:T(8,128)(2,1)} slice(bf16[384,1024]{1,0:T(8,128)(2,1)} %copy-done.3), slice={[0:384], [0:640]} | slice | bytes 983040 | tf_op jit(solution)/shard_map/slice | solution.py:72
  19.9 0.7 broadcast_in_dim.19
  20.6 1.9 %concatenate.6 = bf16[384,768]{1,0:T(8,128)(2,1)} concatenate(bf16[384,640]{1,0:T(8,128)(2,1)} %slice.52, bf16[384,1]{1,0:T(8,128)(2,1)S(1)} %stack.26, bf16[384,1]{1,0:T(8,128)(2,1)S(1)} %stack.27, bf16[384,1]{1,0:T(8,128)(2,1)S(1)} %stack.28, bf16[384,1]{1,0:T(8,128)(2,1)S(1)} %stack.29, bf16[384,124]{1,0:T(8,128)(2,1)} %broadcast_in_dim.19), dimensions={1} | concatenate | bytes 1179648 | tf_op jit(solution)/shard_map/concatenate | solution.py:72
  22.5 2.9 %convolution_convert_fusion = bf16[768,768]{1,0:T(8,128)(2,1)} fusion(bf16[384,768]{1,0:T(8,128)(2,1)} %concatenate.6, s32[384]{0:T(512)S(1)} %convert_add_fusion), kind=kOutput, calls=%fused_computation.6 | convolution fusion | flops 453869568 | bytes 1771008 | tf_op jit(solution)/shard_map/dot_general | solution.py:67
  25.3 8.1 %all-to-all-done.1 = bf16[8,96,384]{2,1,0:T(8,128)(2,1)} async-done(((bf16[8,96,384]{2,1,0:T(8,128)(2,1)}), bf16[8,96,384]{2,1,0:T(8,128)(2,1)}, u32[]{:S(2)}, u32[]{:S(2)}) %all-to-all-start.1) | async-done | bytes 589856 | tf_op jit(solution)/shard_map/all_to_all | solution.py:69
  33.5 4.3 %all-to-all-start = ((bf16[8,96,768]{2,1,0:T(8,128)(2,1)}), bf16[8,96,768]{2,1,0:T(8,128)(2,1)}, u32[]{:S(2)}, u32[]{:S(2)}) async-start(bf16[8,96,768]{2,1,0:T(8,128)(2,1)} %bitcast.18), calls=%async_computation | async-start | bytes 2359296 | tf_op jit(solution)/shard_map/all_to_all | solution.py:69
  37.8 1.6 %collective-permute-start.2 = (bf16[768,384]{1,0:T(8,128)(2,1)}, bf16[768,384]{1,0:T(8,128)(2,1)}, u32[]{:S(2)}, u32[]{:S(2)}) collective-permute-start(bf16[768,384]{1,0:T(8,128)(2,1)} %bitcast.3), channel_id=1, source_target_pairs={{0,2},{1,3},{2,0},{3,1},{4,6},{5,7},{6,4},{7,5},{8,10},{9,11},{10,... | collective-permute-start | bytes 1769480 | tf_op jit(solution)/shard_map/ppermute | solution.py:21
  39.4 13.1 %collective-permute-done.2 = bf16[768,384]{1,0:T(8,128)(2,1)} collective-permute-done((bf16[768,384]{1,0:T(8,128)(2,1)}, bf16[768,384]{1,0:T(8,128)(2,1)}, u32[]{:S(2)}, u32[]{:S(2)}) %collective-permute-start.2) | collective-permute-done | bytes 589856 | tf_op jit(solution)/shard_map/ppermute | solution.py:21
  52.4 3.4 %fusion.18 = f32[768,768]{0,1:T(8,128)} fusion(bf16[768,384]{1,0:T(8,128)(2,1)} %bitcast.3, bf16[768,384]{1,0:T(8,128)(2,1)} %collective-permute-done.2), kind=kOutput, calls=%fused_computation.61 | convolution fusion | flops 452984832 | bytes 3538944 | tf_op jit(solution)/shard_map/qe,ke->qk/dot_general | solution.py:81
  55.8 3.3 %fusion.19 = f32[768,768]{0,1:T(8,128)} fusion(bf16[768,384]{1,0:T(8,128)(2,1)} %bitcast.3, bf16[768,384]{1,0:T(8,128)(2,1)S(1)} %collective-permute-done.5), kind=kOutput, calls=%fused_computation.62 | convolution fusion | flops 452984832 | bytes 3538944 | tf_op jit(solution)/shard_map/qe,ke->qk/dot_general | solution.py:81
  59.1 7.0 %all-to-all-done = bf16[8,96,768]{2,1,0:T(8,128)(2,1)} async-done(((bf16[8,96,768]{2,1,0:T(8,128)(2,1)}), bf16[8,96,768]{2,1,0:T(8,128)(2,1)}, u32[]{:S(2)}, u32[]{:S(2)}) %all-to-all-start) | async-done | bytes 1179680 | tf_op jit(solution)/shard_map/all_to_all | solution.py:69
  66.1 1.3 %slice.57 = bf16[768,640]{1,0:T(8,128)(2,1)S(1)} slice(bf16[768,768]{1,0:T(8,128)(2,1)} %bitcast.1), slice={[0:768], [0:640]} | slice | bytes 1966080 | tf_op jit(solution)/shard_map/slice | solution.py:31
  67.4 2.0 %convert_reduce_fusion = (f32[768]{0:T(1024)S(1)}, f32[768]{0:T(1024)S(1)}) fusion(bf16[768,768]{1,0:T(8,128)(2,1)} %bitcast.1), kind=kLoop, calls=%fused_computation.15 | loop fusion | flops 6144 | bytes 12288 | tf_op jit(solution)/shard_map/eq | solution.py:84
  69.4 1.6 %collective-permute-start.1 = (bf16[768,640]{1,0:T(8,128)(2,1)S(1)}, bf16[768,640]{1,0:T(8,128)(2,1)S(1)}, u32[]{:S(2)}, u32[]{:S(2)}) collective-permute-start(bf16[768,640]{1,0:T(8,128)(2,1)S(1)} %slice.57), channel_id=1, source_target_pairs={{0,2},{1,3},{2,0},{3,1},{4,6},{5,7},{6,4},{7,5},{8,10},{9,11},{10,... | collective-permute-start | bytes 2949128 | tf_op jit(solution)/shard_map/ppermute | solution.py:21
  71.0 0.6 collective-permute-start
  71.8 2.7 %fusion.16 = f32[768,768]{0,1:T(8,128)S(1)} fusion(bf16[768,768]{1,0:T(8,128)(2,1)} %bitcast.1), kind=kOutput, calls=%fused_computation.59 | convolution fusion | flops 754974720 | bytes 3342336 | tf_op jit(solution)/shard_map/qe,ke->qk/dot_general | solution.py:80
  74.6 2.3 %select_reduce_fusion.3 = f32[768]{0:T(1024)S(1)} fusion(f32[768,768]{0,1:T(8,128)S(1)} %fusion.16, bf16[768,384]{1,0:T(8,128)(2,1)} %bitcast.3, f32[768]{0:T(1024)S(1)} %get-tuple-element.6, f32[768]{0:T(1024)S(1)} %get-tuple-element.5, pred[768]{0:T(1024)(128)(4,1)S(1)} %broadcast_compare_fusion), kind=kOutput, calls=%fused_computation.3 | convolution fusion | flops 457112832 | bytes 2959104 | tf_op jit(solution)/shard_map/qe,ke->qk/dot_general | solution.py:81
  76.9 14.5 %collective-permute-done = f32[2,768]{1,0:T(2,128)S(1)} collective-permute-done((f32[2,768]{1,0:T(2,128)S(1)}, f32[2,768]{1,0:T(2,128)S(1)}, u32[]{:S(2)}, u32[]{:S(2)}) %collective-permute-start) | collective-permute-done | bytes 6176 | tf_op jit(solution)/shard_map/ppermute | solution.py:21
  91.5 1.1 collective-permute-done.6
  92.9 2.0 %fusion.20 = f32[768,768]{0,1:T(8,128)S(1)} fusion(bf16[768,384]{1,0:T(8,128)(2,1)} %bitcast.3, bf16[768,384]{1,0:T(8,128)(2,1)} %collective-permute-done.8), kind=kOutput, calls=%fused_computation.63 | convolution fusion | flops 452984832 | bytes 3538944 | tf_op jit(solution)/shard_map/qe,ke->qk/dot_general | solution.py:81
  95.0 2.8 %select_reduce_fusion.2 = f32[768]{0:T(1024)S(1)} fusion(f32[768,768]{0,1:T(8,128)S(1)} %copy-done.2, bf16[768,640]{1,0:T(8,128)(2,1)S(1)} %collective-permute-done.1, f32[768]{0:T(1024)S(1)} %get-tuple-element.6, f32[768]{0:T(1024)S(1)} %get-tuple-element.5, f32[768]{0:T(1024)S(1)} %get-tuple-element.8, f32[768]{0:T(1024)S(1)} %get-tuple-element.7, ...), kind=kOutput, calls=%fused_computation.2 | convolution fusion | flops 759102720 | bytes 4341504 | tf_op jit(solution)/shard_map/qe,ke->qk/dot_general | solution.py:80
  97.8 2.6 %select_reduce_fusion.1 = f32[768]{0:T(1024)S(1)} fusion(f32[768,768]{0,1:T(8,128)S(1)} %copy-done.1, bf16[768,640]{1,0:T(8,128)(2,1)S(1)} %collective-permute-done.4, f32[768]{0:T(1024)S(1)} %get-tuple-element.6, f32[768]{0:T(1024)S(1)} %get-tuple-element.5, f32[768]{0:T(1024)S(1)} %get-tuple-element.10, f32[768]{0:T(1024)S(1)} %get-tuple-element.9, ...), kind=kOutput, calls=%fused_computation.1 | convolution fusion | flops 759102720 | bytes 4341504 | tf_op jit(solution)/shard_map/qe,ke->qk/dot_general | solution.py:80
  100.4 2.6 %select_reduce_fusion = f32[768]{0:T(1024)S(1)} fusion(f32[768,768]{0,1:T(8,128)S(1)} %fusion.20, bf16[768,640]{1,0:T(8,128)(2,1)S(1)} %collective-permute-done.7, f32[768]{0:T(1024)S(1)} %get-tuple-element.6, f32[768]{0:T(1024)S(1)} %get-tuple-element.5, f32[768]{0:T(1024)S(1)} %get-tuple-element.12, f32[768]{0:T(1024)S(1)} %get-tuple-element.11, ...), kind=kOutput, calls=%fused_computation | convolution fusion | flops 759102720 | bytes 4341504 | tf_op jit(solution)/shard_map/qe,ke->qk/dot_general | solution.py:80
  103.1 11.6 %all_to_all.16 = f32[8,1,96]{2,1,0:T(1,128)S(1)} all-to-all(f32[8,1,96]{2,1,0:T(1,128)S(1)} %max.41), channel_id=1, replica_groups=mesh['grp'=8,'split'=4] {'grp'}, dimensions={0} | all-to-all | bytes 6144 | tf_op jit(solution)/shard_map/all_to_all | solution.py:92
  115.3 0.7 reduce.27
  116.0 0.8 select_reduce_fusion.4
  (46 shorter events, 2.2 us)
Async XLA Ops:
  0.0 1.9 %copy-start = (bf16[384,4096]{1,0:T(8,128)(2,1)S(1)}, bf16[384,4096]{1,0:T(8,128)(2,1)}, u32[]{:S(2)}) copy-start(bf16[384,4096]{1,0:T(8,128)(2,1)} %param.5) | copy-start | bytes 9437188
  7.9 11.6 %copy-start.4 = (s32[384]{0:T(512)S(1)}, s32[384]{0:T(512)}, u32[]{:S(2)}) copy-start(s32[384]{0:T(512)} %param.8) | copy-start | bytes 4612
  8.0 0.9 copy-start.3
  8.9 10.7 %copy-start.5 = (s32[384]{0:T(512)S(1)}, s32[384]{0:T(512)}, u32[]{:S(2)}) copy-start(s32[384]{0:T(512)} %param.9) | copy-start | bytes 4612
  10.2 23.2 %all-to-all-start.1 = ((bf16[8,96,384]{2,1,0:T(8,128)(2,1)}), bf16[8,96,384]{2,1,0:T(8,128)(2,1)}, u32[]{:S(2)}, u32[]{:S(2)}) async-start(bf16[8,96,384]{2,1,0:T(8,128)(2,1)} %bitcast.19), calls=%async_computation.1 | async-start | bytes 1179648 | tf_op jit(solution)/shard_map/all_to_all | solution.py:69
  33.5 32.6 %all-to-all-start = ((bf16[8,96,768]{2,1,0:T(8,128)(2,1)}), bf16[8,96,768]{2,1,0:T(8,128)(2,1)}, u32[]{:S(2)}, u32[]{:S(2)}) async-start(bf16[8,96,768]{2,1,0:T(8,128)(2,1)} %bitcast.18), calls=%async_computation | async-start | bytes 2359296 | tf_op jit(solution)/shard_map/all_to_all | solution.py:69
  37.8 14.6 %collective-permute-start.2 = (bf16[768,384]{1,0:T(8,128)(2,1)}, bf16[768,384]{1,0:T(8,128)(2,1)}, u32[]{:S(2)}, u32[]{:S(2)}) collective-permute-start(bf16[768,384]{1,0:T(8,128)(2,1)} %bitcast.3), channel_id=1, source_target_pairs={{0,2},{1,3},{2,0},{3,1},{4,6},{5,7},{6,4},{7,5},{8,10},{9,11},{10,... | collective-permute-start | bytes 1769480 | tf_op jit(solution)/shard_map/ppermute | solution.py:21
  39.3 16.5 %collective-permute-start.5 = (bf16[768,384]{1,0:T(8,128)(2,1)}, bf16[768,384]{1,0:T(8,128)(2,1)S(1)}, u32[]{:S(2)}, u32[]{:S(2)}) collective-permute-start(bf16[768,384]{1,0:T(8,128)(2,1)} %bitcast.3), channel_id=1, source_target_pairs={{0,1},{1,0},{2,3},{3,2},{4,5},{5,4},{6,7},{7,6},{8,9},{9,8},{10,11... | collective-permute-start | bytes 1769480 | tf_op jit(solution)/shard_map/ppermute | solution.py:23
  52.4 40.5 %collective-permute-start.8 = (bf16[768,384]{1,0:T(8,128)(2,1)}, bf16[768,384]{1,0:T(8,128)(2,1)}, u32[]{:S(2)}, u32[]{:S(2)}) collective-permute-start(bf16[768,384]{1,0:T(8,128)(2,1)} %collective-permute-done.2), channel_id=1, source_target_pairs={{0,1},{1,0},{2,3},{3,2},{4,5},{5,4},{6,7},{7,6},{8,9},{9,8},{10,11... | collective-permute-start | bytes 1769480 | tf_op jit(solution)/shard_map/ppermute | solution.py:23
  69.4 23.2 %collective-permute-start.1 = (bf16[768,640]{1,0:T(8,128)(2,1)S(1)}, bf16[768,640]{1,0:T(8,128)(2,1)S(1)}, u32[]{:S(2)}, u32[]{:S(2)}) collective-permute-start(bf16[768,640]{1,0:T(8,128)(2,1)S(1)} %slice.57), channel_id=1, source_target_pairs={{0,2},{1,3},{2,0},{3,1},{4,6},{5,7},{6,4},{7,5},{8,10},{9,11},{10,... | collective-permute-start | bytes 2949128 | tf_op jit(solution)/shard_map/ppermute | solution.py:21
  71.0 26.7 %collective-permute-start.4 = (bf16[768,640]{1,0:T(8,128)(2,1)S(1)}, bf16[768,640]{1,0:T(8,128)(2,1)S(1)}, u32[]{:S(2)}, u32[]{:S(2)}) collective-permute-start(bf16[768,640]{1,0:T(8,128)(2,1)S(1)} %slice.57), channel_id=1, source_target_pairs={{0,1},{1,0},{2,3},{3,2},{4,5},{5,4},{6,7},{7,6},{8,9},{9,8},{10,11... | collective-permute-start | bytes 2949128 | tf_op jit(solution)/shard_map/ppermute | solution.py:23
  71.0 20.4 %collective-permute-start = (f32[2,768]{1,0:T(2,128)S(1)}, f32[2,768]{1,0:T(2,128)S(1)}, u32[]{:S(2)}, u32[]{:S(2)}) collective-permute-start(f32[2,768]{1,0:T(2,128)S(1)} %pad_maximum_fusion), channel_id=1, source_target_pairs={{0,2},{1,3},{2,0},{3,1},{4,6},{5,7},{6,4},{7,5},{8,10},{9,11},{10,... | collective-permute-start | bytes 18440 | tf_op jit(solution)/shard_map/ppermute | solution.py:21
  71.6 19.8 %collective-permute-start.3 = (f32[2,768]{1,0:T(2,128)S(1)}, f32[2,768]{1,0:T(2,128)S(1)}, u32[]{:S(2)}, u32[]{:S(2)}) collective-permute-start(f32[2,768]{1,0:T(2,128)S(1)} %pad_maximum_fusion), channel_id=1, source_target_pairs={{0,1},{1,0},{2,3},{3,2},{4,5},{5,4},{6,7},{7,6},{8,9},{9,8},{10,11... | collective-permute-start | bytes 18440 | tf_op jit(solution)/shard_map/ppermute | solution.py:23
  76.9 18.0 %copy-start.2 = (f32[768,768]{0,1:T(8,128)S(1)}, f32[768,768]{0,1:T(8,128)}, u32[]{:S(2)}) copy-start(f32[768,768]{0,1:T(8,128)} %fusion.18) | copy-start | bytes 7077892
  91.4 1.2 %collective-permute-start.6 = (f32[2,768]{1,0:T(2,128)S(1)}, f32[2,768]{1,0:T(2,128)S(1)}, u32[]{:S(2)}, u32[]{:S(2)}) collective-permute-start(f32[2,768]{1,0:T(2,128)S(1)} %collective-permute-done), channel_id=1, source_target_pairs={{0,1},{1,0},{2,3},{3,2},{4,5},{5,4},{6,7},{7,6},{8,9},{9,8},{10,11... | collective-permute-start | bytes 18440 | tf_op jit(solution)/shard_map/ppermute | solution.py:23
  92.7 7.7 %collective-permute-start.7 = (bf16[768,640]{1,0:T(8,128)(2,1)S(1)}, bf16[768,640]{1,0:T(8,128)(2,1)S(1)}, u32[]{:S(2)}, u32[]{:S(2)}) collective-permute-start(bf16[768,640]{1,0:T(8,128)(2,1)S(1)} %collective-permute-done.1), channel_id=1, source_target_pairs={{0,1},{1,0},{2,3},{3,2},{4,5},{5,4},{6,7},{7,6},{8,9},{9,8},{10,11... | collective-permute-start | bytes 2949128 | tf_op jit(solution)/shard_map/ppermute | solution.py:23
  94.9 2.8 %copy-start.1 = (f32[768,768]{0,1:T(8,128)S(1)}, f32[768,768]{0,1:T(8,128)}, u32[]{:S(2)}) copy-start(f32[768,768]{0,1:T(8,128)} %fusion.19) | copy-start | bytes 7077892

commit v6 on v4

--- a/solution.py
+++ b/solution.py
@@ -69,12 +69,35 @@
         got = lax.all_to_all(send, "grp", split_axis=0, concat_axis=0, tiled=True)
         return got.reshape(n_slot, -1)
 
-    got_a = route(jnp.concatenate([embeds[:, :half], meta], axis=1))
-    q_emb, q_lab, q_ord = unpack(got_a, half, n_all)
-    keys_a = gather_split(q_emb, n_split)
-    keys_m = gather_split(jnp.stack([q_lab, q_ord]), n_split)
-    got_b = route(embeds[:, half:])
-    keys_b = gather_split(got_b, n_split)
+    if n_split == 4:
+        half = emb_w - 3 * emb_w // 8
+        cross = [(0, 2), (2, 0), (1, 3), (3, 1)]
+        pair = [(0, 1), (1, 0), (2, 3), (3, 2)]
+        raw_b = embeds[:, half:]
+        par_b = lax.ppermute(raw_b, "split", cross)
+        par_place = lax.ppermute(place, "split", cross)
+        got_a = route(jnp.concatenate([embeds[:, :half], meta], axis=1))
+        q_emb, q_lab, q_ord = unpack(got_a, half, n_all)
+        keys_a = gather_split(q_emb, n_split)
+        keys_m = gather_split(jnp.stack([q_lab, q_ord]), n_split)
+        pick_par = par_place[None, :] == jnp.arange(n_slot, dtype=jnp.int32)[:, None]
+        send_own = jnp.dot(pick.astype(jnp.bfloat16), raw_b, preferred_element_type=jnp.float32)
+        send_par = jnp.dot(pick_par.astype(jnp.bfloat16), par_b, preferred_element_type=jnp.float32)
+        send = jnp.concatenate(
+            [send_own.reshape(n_grp, cap, -1), send_par.reshape(n_grp, cap, -1)], axis=1
+        ).astype(jnp.bfloat16)
+        got = lax.all_to_all(send, "grp", split_axis=0, concat_axis=0, tiled=True)
+        got_b = got[:, :cap].reshape(n_slot, -1)
+        cross_b = got[:, cap:].reshape(n_slot, -1)
+        keys_b = [cross_b, lax.ppermute(got_b, "split", pair), lax.ppermute(cross_b, "split", pair)]
+    else:
+        half = emb_w // 2
+        got_a = route(jnp.concatenate([embeds[:, :half], meta], axis=1))
+        q_emb, q_lab, q_ord = unpack(got_a, half, n_all)
+        keys_a = gather_split(q_emb, n_split)
+        keys_m = gather_split(jnp.stack([q_lab, q_ord]), n_split)
+        got_b = route(embeds[:, half:])
+        keys_b = gather_split(got_b, n_split)
 
     def dots(k_a, k_b):
         s = jnp.einsum("qe,ke->qk", q_emb, k_a, preferred_element_type=jnp.float32)

time: 115 us -> 112 us (0.974)
  waiting for transfers between devices: 46.1 us -> 40.2 us
  local copies, waits for them, and re-layouts: 9.22 us -> 12.2 us
  matrix products: 28.1 us -> 26.8 us
    all_to_all x2 -> x1, waiting for transfers between devices: 34.6 us -> 17.5 us  [route(): got = lax.all_to_all(send, 'grp', split_axis=0, concat_axis=0, tiled=True)]
    dot_general x4, matrix products: 8.74 us -> 3.48 us  [dots(): jnp.einsum('qe,ke->qk', got_b, k_b, preferred_element_type=jnp.float32)]
    ppermute x0 -> x4, waiting for transfers between devices: none -> 5.03 us  [the longest x1 5.02 us: local(): par_place = lax.ppermute(place, 'split', cross)]
    ppermute x3 -> x2, waiting for transfers between devices: 9.91 us -> 14.8 us  [gather_split(): cross = lax.ppermute(rows, 'split', [(0, 2), (1, 3), (2, 0), (3, 1)])]
    all_to_all x0 -> x1, starting transfers between devices: none -> 4.45 us  [local(): got = lax.all_to_all(send, 'grp', split_axis=0, concat_axis=0, tiled=True)]
    all_to_all x2 -> x1, starting transfers between devices: 11.6 us -> 7.25 us  [route(): got = lax.all_to_all(send, 'grp', split_axis=0, concat_axis=0, tiled=True)]
    dot_general x4, matrix products: 9.04 us -> 12.4 us  [dots(): s = jnp.einsum('qe,ke->qk', q_emb, k_a, preferred_element_type=jnp.float32)]
    ppermute x0 -> x4, starting transfers between devices: none -> 2.66 us  [the longest x1 1.59 us: local(): par_b = lax.ppermute(raw_b, 'split', cross)]
  transfers between devices with their start and end apart: 11 -> 12, of which waited for: 4 -> 5; matrix products, arithmetic and copies ran while one was open for 24% -> 21% of each run, Pallas kernels for 0% -> 0%
where the time goes in v6:
time: 112 us; the launch traced here: 111 us
  waiting for transfers between devices  40.2 us (36%)
  matrix products  26.8 us (24%)
  starting transfers between devices  16.8 us (15%)
  local copies, waits for them, and re-layouts  12.2 us (11%)
  blocking collectives  10.3 us (9%)
  other arithmetic  4.67 us (4%)
    all_to_all x1, waiting for transfers between devices, route(): got = lax.all_to_all(send, 'grp', split_axis=0, concat_axis=0, tiled=True)  17.5 us
    ppermute x2, waiting for transfers between devices, gather_split(): cross = lax.ppermute(rows, 'split', [(0, 2), (1, 3), (2, 0), (3, 1)])  14.8 us
    dot_general x4, matrix products, dots(): s = jnp.einsum('qe,ke->qk', q_emb, k_a, preferred_element_type=jnp.float32)  12.4 us
    all_to_all x1, blocking collectives, local(): lax.all_to_all(best.reshape(n_grp, cap), 'grp', split_axis=0, concat_axis...  10.3 us
    all_to_all x1, starting transfers between devices, route(): got = lax.all_to_all(send, 'grp', split_axis=0, concat_axis=0, tiled=True)  7.25 us
    dot_general x1, matrix products, embed_rows(): jnp.einsum('...h,he->...e', rows, weight, preferred_element_type=jnp.floa...  5.94 us
    ppermute x1, waiting for transfers between devices, local(): par_place = lax.ppermute(place, 'split', cross)  5.02 us
    all_to_all x1, starting transfers between devices, local(): got = lax.all_to_all(send, 'grp', split_axis=0, concat_axis=0, tiled=True)  4.45 us
  transfers between devices with their start and end apart: 12, of which 5 were waited for; matrix products, arithmetic and copies ran while one was open for 21% of the time, Pallas kernels for 0%

profile of v6, /device:TPU:0, one launch (start us, length us, event | category | flops | bytes accessed | tf_op | source)
XLA Modules:
  0.0 111.2 jit_solution(11223365336966744790)
XLA Ops:
  0.0 1.9 %copy-done = bf16[384,4096]{1,0:T(8,128)(2,1)S(1)} copy-done((bf16[384,4096]{1,0:T(8,128)(2,1)S(1)}, bf16[384,4096]{1,0:T(8,128)(2,1)}, u32[]{:S(2)}) %copy-start) | copy-done | bytes 3145752
  1.9 5.9 %multiply_reduce_fusion = (f32[384]{0:T(512)S(1)}, f32[384,1024]{1,0:T(8,128)S(1)}) fusion(bf16[384,4096]{1,0:T(8,128)(2,1)S(1)} %copy-done, bf16[4096,1024]{1,0:T(8,128)(2,1)} %param.6), kind=kOutput, calls=%fused_computation.5 | convolution fusion | flops 3222011392 | bytes 13108736 | tf_op jit(solution)/shard_map/...h,he->...e/dot_general | solution.py:14
  8.3 0.9 copy-done.1
  9.2 0.8 slice.60
  11.2 1.9 %concatenate.10 = bf16[384,768]{1,0:T(8,128)(2,1)} concatenate(bf16[384,640]{1,0:T(8,128)(2,1)} %slice.60, bf16[384,1]{1,0:T(8,128)(2,1)S(1)} %stack.26, bf16[384,1]{1,0:T(8,128)(2,1)S(1)} %stack.27, bf16[384,1]{1,0:T(8,128)(2,1)S(1)} %stack.28, bf16[384,1]{1,0:T(8,128)(2,1)S(1)} %stack.29, bf16[384,124]{1,0:T(8,128)(2,1)} %broadcast_in_dim.19), dimensions={1} | concatenate | bytes 1179648 | tf_op jit(solution)/shard_map/concatenate | solution.py:79
  13.1 2.8 %convolution_convert_fusion = bf16[768,768]{1,0:T(8,128)(2,1)} fusion(bf16[384,768]{1,0:T(8,128)(2,1)} %concatenate.10, s32[384]{0:T(512)S(1)} %convert_add_fusion), kind=kOutput, calls=%fused_computation.6 | convolution fusion | flops 453869568 | bytes 1771008 | tf_op jit(solution)/shard_map/dot_general | solution.py:67
  16.0 7.3 %all-to-all-start = ((bf16[8,96,768]{2,1,0:T(8,128)(2,1)}), bf16[8,96,768]{2,1,0:T(8,128)(2,1)}, u32[]{:S(2)}, u32[]{:S(2)}) async-start(bf16[8,96,768]{2,1,0:T(8,128)(2,1)} %bitcast.28), calls=%async_computation | async-start | bytes 2359296 | tf_op jit(solution)/shard_map/all_to_all | solution.py:69
  23.2 1.0 slice.66
  24.2 1.6 %collective-permute-start.1 = (bf16[384,384]{1,0:T(8,128)(2,1)S(1)}, bf16[384,384]{1,0:T(8,128)(2,1)S(1)}, u32[]{:S(2)}, u32[]{:S(2)}) collective-permute-start(bf16[384,384]{1,0:T(8,128)(2,1)S(1)} %slice.66), channel_id=1, source_target_pairs={{0,2},{2,0},{1,3},{3,1},{4,6},{6,4},{5,7},{7,5},{8,10},{10,8},{9,1... | collective-permute-start | bytes 884744 | tf_op jit(solution)/shard_map/ppermute | solution.py:77
  26.3 1.5 %convolution_convert_fusion.2 = bf16[768,384]{1,0:T(8,128)(2,1)S(1)} fusion(s32[384]{0:T(512)S(1)} %convert_add_fusion, bf16[384,1024]{1,0:T(8,128)(2,1)} %copy-done.1), kind=kOutput, calls=%fused_computation.8 | convolution fusion | flops 227082240 | bytes 886272 | tf_op jit(solution)/shard_map/dot_general | solution.py:84
  27.8 5.0 %collective-permute-done = s32[384]{0:T(512)S(1)} collective-permute-done((s32[384]{0:T(512)S(1)}, s32[384]{0:T(512)S(1)}, u32[]{:S(2)}, u32[]{:S(2)}) %collective-permute-start) | collective-permute-done | bytes 1568 | tf_op jit(solution)/shard_map/ppermute | solution.py:78
  33.3 1.1 %pad_maximum_fusion = bf16[8,192,384]{2,1,0:T(8,128)(2,1)} fusion(bf16[8,96,384]{2,1,0:T(8,128)(2,1)S(1)} %bitcast.30, bf16[8,96,384]{2,1,0:T(8,128)(2,1)S(1)} %bitcast.29), kind=kLoop, calls=%fused_computation.9 | loop fusion | flops 2359296 | bytes 2359296 | tf_op jit(solution)/shard_map/concatenate | solution.py:86
  34.4 17.5 %all-to-all-done = bf16[8,96,768]{2,1,0:T(8,128)(2,1)} async-done(((bf16[8,96,768]{2,1,0:T(8,128)(2,1)}), bf16[8,96,768]{2,1,0:T(8,128)(2,1)}, u32[]{:S(2)}, u32[]{:S(2)}) %all-to-all-start) | async-done | bytes 1179680 | tf_op jit(solution)/shard_map/all_to_all | solution.py:69
  51.9 4.4 %all-to-all-start.1 = ((bf16[8,192,384]{2,1,0:T(8,128)(2,1)}), bf16[8,192,384]{2,1,0:T(8,128)(2,1)}, u32[]{:S(2)}, u32[]{:S(2)}) async-start(bf16[8,192,384]{2,1,0:T(8,128)(2,1)} %pad_maximum_fusion), calls=%async_computation.1 | async-start | bytes 2359296 | tf_op jit(solution)/shard_map/all_to_all | solution.py:89
  56.4 2.2 %slice.65 = bf16[768,640]{1,0:T(8,128)(2,1)} slice(bf16[768,768]{1,0:T(8,128)(2,1)} %bitcast.1), slice={[0:768], [0:640]} | slice | bytes 1966080 | tf_op jit(solution)/shard_map/slice | solution.py:31
  58.6 1.5 %collective-permute-start.3 = (bf16[768,640]{1,0:T(8,128)(2,1)}, bf16[768,640]{1,0:T(8,128)(2,1)}, u32[]{:S(2)}, u32[]{:S(2)}) collective-permute-start(bf16[768,640]{1,0:T(8,128)(2,1)} %slice.65), channel_id=1, source_target_pairs={{0,2},{1,3},{2,0},{3,1},{4,6},{5,7},{6,4},{7,5},{8,10},{9,11},{10,... | collective-permute-start | bytes 2949128 | tf_op jit(solution)/shard_map/ppermute | solution.py:21
  60.1 1.8 %convert_reduce_fusion = (f32[768]{0:T(1024)S(1)}, f32[768]{0:T(1024)S(1)}) fusion(bf16[768,768]{1,0:T(8,128)(2,1)} %bitcast.1), kind=kLoop, calls=%fused_computation.19 | loop fusion | flops 6144 | bytes 12288 | tf_op jit(solution)/shard_map/eq | solution.py:107
  62.8 4.0 %fusion.17 = f32[768,768]{0,1:T(8,128)} fusion(bf16[768,768]{1,0:T(8,128)(2,1)} %bitcast.1), kind=kOutput, calls=%fused_computation.63 | convolution fusion | flops 754974720 | bytes 3342336 | tf_op jit(solution)/shard_map/qe,ke->qk/dot_general | solution.py:103
  66.8 14.8 %collective-permute-done.2 = f32[2,768]{1,0:T(2,128)S(1)} collective-permute-done((f32[2,768]{1,0:T(2,128)S(1)}, f32[2,768]{1,0:T(2,128)S(1)}, u32[]{:S(2)}, u32[]{:S(2)}) %collective-permute-start.2) | collective-permute-done | bytes 6176 | tf_op jit(solution)/shard_map/ppermute | solution.py:21
  81.7 1.1 collective-permute-done.7
  82.8 1.8 %all-to-all-done.1 = bf16[8,192,384]{2,1,0:T(8,128)(2,1)} async-done(((bf16[8,192,384]{2,1,0:T(8,128)(2,1)}), bf16[8,192,384]{2,1,0:T(8,128)(2,1)}, u32[]{:S(2)}, u32[]{:S(2)}) %all-to-all-start.1) | async-done | bytes 1179680 | tf_op jit(solution)/shard_map/all_to_all | solution.py:89
  84.6 1.5 %fusion.19 = (bf16[8,96,384]{2,1,0:T(8,128)(2,1)S(1)}, bf16[8,96,384]{2,1,0:T(8,128)(2,1)S(1)}) fusion(bf16[8,192,384]{2,1,0:T(8,128)(2,1)} %all-to-all-done.1), kind=kLoop, calls=%fused_computation.65 | loop fusion | bytes 2359296 | tf_op jit(solution)/shard_map/slice | solution.py:91
  86.7 1.1 select_reduce_fusion.3
  87.8 0.8 fusion.20
  88.6 0.8 fusion.22
  89.6 0.8 fusion.21
  90.4 2.9 %select_reduce_fusion.2 = f32[768]{0:T(1024)S(1)} fusion(f32[768,768]{0,1:T(8,128)S(1)} %fusion.20, bf16[768,640]{1,0:T(8,128)(2,1)} %collective-permute-done.3, f32[768]{0:T(1024)S(1)} %get-tuple-element.6, f32[768]{0:T(1024)S(1)} %get-tuple-element.5, f32[768]{0:T(1024)S(1)} %get-tuple-element.8, f32[768]{0:T(1024)S(1)} %get-tuple-element.7, ...), kind=kOutput, calls=%fused_computation.2 | convolution fusion | flops 759102720 | bytes 4341504 | tf_op jit(solution)/shard_map/qe,ke->qk/dot_general | solution.py:103
  93.3 2.9 %select_reduce_fusion.1 = f32[768]{0:T(1024)S(1)} fusion(f32[768,768]{0,1:T(8,128)S(1)} %fusion.21, bf16[768,640]{1,0:T(8,128)(2,1)} %collective-permute-done.5, f32[768]{0:T(1024)S(1)} %get-tuple-element.6, f32[768]{0:T(1024)S(1)} %get-tuple-element.5, f32[768]{0:T(1024)S(1)} %get-tuple-element.10, f32[768]{0:T(1024)S(1)} %get-tuple-element.9, ...), kind=kOutput, calls=%fused_computation.1 | convolution fusion | flops 759102720 | bytes 4341504 | tf_op jit(solution)/shard_map/qe,ke->qk/dot_general | solution.py:103
  96.2 2.6 %select_reduce_fusion = f32[768]{0:T(1024)S(1)} fusion(f32[768,768]{0,1:T(8,128)S(1)} %fusion.22, bf16[768,640]{1,0:T(8,128)(2,1)S(1)} %collective-permute-done.8, f32[768]{0:T(1024)S(1)} %get-tuple-element.6, f32[768]{0:T(1024)S(1)} %get-tuple-element.5, f32[768]{0:T(1024)S(1)} %get-tuple-element.12, f32[768]{0:T(1024)S(1)} %get-tuple-element.11, ...), kind=kOutput, calls=%fused_computation | convolution fusion | flops 759102720 | bytes 4341504 | tf_op jit(solution)/shard_map/qe,ke->qk/dot_general | solution.py:103
  98.9 10.3 %all_to_all.16 = f32[8,1,96]{2,1,0:T(1,128)S(1)} all-to-all(f32[8,1,96]{2,1,0:T(1,128)S(1)} %max.41), channel_id=1, replica_groups=mesh['grp'=8,'split'=4] {'grp'}, dimensions={0} | all-to-all | bytes 6144 | tf_op jit(solution)/shard_map/all_to_all | solution.py:115
  109.7 0.7 reduce.27
  110.4 0.8 select_reduce_fusion.4
  (52 shorter events, 4.9 us)
Async XLA Ops:
  0.0 1.9 %copy-start = (bf16[384,4096]{1,0:T(8,128)(2,1)S(1)}, bf16[384,4096]{1,0:T(8,128)(2,1)}, u32[]{:S(2)}) copy-start(bf16[384,4096]{1,0:T(8,128)(2,1)} %param.5) | copy-start | bytes 9437188
  0.0 7.9 %copy-start.3 = (s32[384]{0:T(512)S(1)}, s32[384]{0:T(512)}, u32[]{:S(2)}) copy-start(s32[384]{0:T(512)} %param.7) | copy-start | bytes 4612
  7.8 2.3 %copy-start.2 = (s32[384]{0:T(512)S(1)}, s32[384]{0:T(512)}, u32[]{:S(2)}) copy-start(s32[384]{0:T(512)} %param.8) | copy-start | bytes 4612
  7.8 2.4 %copy-start.4 = (s32[384]{0:T(512)S(1)}, s32[384]{0:T(512)}, u32[]{:S(2)}) copy-start(s32[384]{0:T(512)} %param.9) | copy-start | bytes 4612
  8.3 0.9 copy-start.1
  16.0 35.9 %all-to-all-start = ((bf16[8,96,768]{2,1,0:T(8,128)(2,1)}), bf16[8,96,768]{2,1,0:T(8,128)(2,1)}, u32[]{:S(2)}, u32[]{:S(2)}) async-start(bf16[8,96,768]{2,1,0:T(8,128)(2,1)} %bitcast.28), calls=%async_computation | async-start | bytes 2359296 | tf_op jit(solution)/shard_map/all_to_all | solution.py:69
  24.2 8.6 %collective-permute-start.1 = (bf16[384,384]{1,0:T(8,128)(2,1)S(1)}, bf16[384,384]{1,0:T(8,128)(2,1)S(1)}, u32[]{:S(2)}, u32[]{:S(2)}) collective-permute-start(bf16[384,384]{1,0:T(8,128)(2,1)S(1)} %slice.66), channel_id=1, source_target_pairs={{0,2},{2,0},{1,3},{3,1},{4,6},{6,4},{5,7},{7,5},{8,10},{10,8},{9,1... | collective-permute-start | bytes 884744 | tf_op jit(solution)/shard_map/ppermute | solution.py:77
  25.8 7.0 %collective-permute-start = (s32[384]{0:T(512)S(1)}, s32[384]{0:T(512)S(1)}, u32[]{:S(2)}, u32[]{:S(2)}) collective-permute-start(s32[384]{0:T(512)S(1)} %convert_add_fusion), channel_id=1, source_target_pairs={{0,2},{2,0},{1,3},{3,1},{4,6},{6,4},{5,7},{7,5},{8,10},{10,8},{9,1... | collective-permute-start | bytes 4616 | tf_op jit(solution)/shard_map/ppermute | solution.py:78
  51.9 32.7 %all-to-all-start.1 = ((bf16[8,192,384]{2,1,0:T(8,128)(2,1)}), bf16[8,192,384]{2,1,0:T(8,128)(2,1)}, u32[]{:S(2)}, u32[]{:S(2)}) async-start(bf16[8,192,384]{2,1,0:T(8,128)(2,1)} %pad_maximum_fusion), calls=%async_computation.1 | async-start | bytes 2359296 | tf_op jit(solution)/shard_map/all_to_all | solution.py:89
  58.6 30.8 %collective-permute-start.3 = (bf16[768,640]{1,0:T(8,128)(2,1)}, bf16[768,640]{1,0:T(8,128)(2,1)}, u32[]{:S(2)}, u32[]{:S(2)}) collective-permute-start(bf16[768,640]{1,0:T(8,128)(2,1)} %slice.65), channel_id=1, source_target_pairs={{0,2},{1,3},{2,0},{3,1},{4,6},{5,7},{6,4},{7,5},{8,10},{9,11},{10,... | collective-permute-start | bytes 2949128 | tf_op jit(solution)/shard_map/ppermute | solution.py:21
  60.1 33.2 %collective-permute-start.5 = (bf16[768,640]{1,0:T(8,128)(2,1)}, bf16[768,640]{1,0:T(8,128)(2,1)}, u32[]{:S(2)}, u32[]{:S(2)}) collective-permute-start(bf16[768,640]{1,0:T(8,128)(2,1)} %slice.65), channel_id=1, source_target_pairs={{0,1},{1,0},{2,3},{3,2},{4,5},{5,4},{6,7},{7,6},{8,9},{9,8},{10,11... | collective-permute-start | bytes 2949128 | tf_op jit(solution)/shard_map/ppermute | solution.py:23
  62.0 19.6 %collective-permute-start.2 = (f32[2,768]{1,0:T(2,128)S(1)}, f32[2,768]{1,0:T(2,128)S(1)}, u32[]{:S(2)}, u32[]{:S(2)}) collective-permute-start(f32[2,768]{1,0:T(2,128)S(1)} %pad_maximum_fusion.1), channel_id=1, source_target_pairs={{0,2},{1,3},{2,0},{3,1},{4,6},{5,7},{6,4},{7,5},{8,10},{9,11},{10,... | collective-permute-start | bytes 18440 | tf_op jit(solution)/shard_map/ppermute | solution.py:21
  62.5 19.0 %collective-permute-start.4 = (f32[2,768]{1,0:T(2,128)S(1)}, f32[2,768]{1,0:T(2,128)S(1)}, u32[]{:S(2)}, u32[]{:S(2)}) collective-permute-start(f32[2,768]{1,0:T(2,128)S(1)} %pad_maximum_fusion.1), channel_id=1, source_target_pairs={{0,1},{1,0},{2,3},{3,2},{4,5},{5,4},{6,7},{7,6},{8,9},{9,8},{10,11... | collective-permute-start | bytes 18440 | tf_op jit(solution)/shard_map/ppermute | solution.py:23
  81.6 1.2 %collective-permute-start.7 = (f32[2,768]{1,0:T(2,128)S(1)}, f32[2,768]{1,0:T(2,128)S(1)}, u32[]{:S(2)}, u32[]{:S(2)}) collective-permute-start(f32[2,768]{1,0:T(2,128)S(1)} %collective-permute-done.2), channel_id=1, source_target_pairs={{0,1},{1,0},{2,3},{3,2},{4,5},{5,4},{6,7},{7,6},{8,9},{9,8},{10,11... | collective-permute-start | bytes 18440 | tf_op jit(solution)/shard_map/ppermute | solution.py:23
  84.6 2.1 %copy-start.5 = (f32[768,768]{0,1:T(8,128)S(1)}, f32[768,768]{0,1:T(8,128)}, u32[]{:S(2)}) copy-start(f32[768,768]{0,1:T(8,128)} %fusion.17) | copy-start | bytes 7077892
  86.1 2.5 %collective-permute-start.9 = (bf16[768,384]{1,0:T(8,128)(2,1)S(1)}, bf16[768,384]{1,0:T(8,128)(2,1)S(1)}, u32[]{:S(2)}, u32[]{:S(2)}) collective-permute-start(bf16[768,384]{1,0:T(8,128)(2,1)S(1)} %bitcast.26), channel_id=1, source_target_pairs={{0,1},{1,0},{2,3},{3,2},{4,5},{5,4},{6,7},{7,6},{8,9},{9,8},{10,11... | collective-permute-start | bytes 1769480 | tf_op jit(solution)/shard_map/ppermute | solution.py:92
  86.2 3.4 %collective-permute-start.6 = (bf16[768,384]{1,0:T(8,128)(2,1)S(1)}, bf16[768,384]{1,0:T(8,128)(2,1)S(1)}, u32[]{:S(2)}, u32[]{:S(2)}) collective-permute-start(bf16[768,384]{1,0:T(8,128)(2,1)S(1)} %bitcast.21), channel_id=1, source_target_pairs={{0,1},{1,0},{2,3},{3,2},{4,5},{5,4},{6,7},{7,6},{8,9},{9,8},{10,11... | collective-permute-start | bytes 1769480 | tf_op jit(solution)/shard_map/ppermute | solution.py:92
  89.4 6.8 %collective-permute-start.8 = (bf16[768,640]{1,0:T(8,128)(2,1)}, bf16[768,640]{1,0:T(8,128)(2,1)S(1)}, u32[]{:S(2)}, u32[]{:S(2)}) collective-permute-start(bf16[768,640]{1,0:T(8,128)(2,1)} %collective-permute-done.3), channel_id=1, source_target_pairs={{0,1},{1,0},{2,3},{3,2},{4,5},{5,4},{6,7},{7,6},{8,9},{9,8},{10,11... | collective-permute-start | bytes 2949128 | tf_op jit(solution)/shard_map/ppermute | solution.py:23

commit v7 on v6

--- a/solution.py
+++ b/solution.py
@@ -99,18 +99,18 @@
         got_b = route(embeds[:, half:])
         keys_b = gather_split(got_b, n_split)
 
-    def dots(k_a, k_b):
+    def part(k_a, hits):
         s = jnp.einsum("qe,ke->qk", q_emb, k_a, preferred_element_type=jnp.float32)
-        return s + jnp.einsum("qe,ke->qk", got_b, k_b, preferred_element_type=jnp.float32)
+        return jnp.where(hits, s, -jnp.inf)
 
-    scores = dots(q_emb, got_b)
-    hits = (q_lab[:, None] == q_lab[None, :]) & (q_lab[None, :] > 0) & (q_ord[None, :] < q_ord[:, None])
-    best = jnp.max(jnp.where(hits, scores, jnp.float32(-1.0)), axis=1)
-    for k_a, k_b, k_m in zip(keys_a, keys_b, keys_m):
+    parts = [part(q_emb, (q_lab[:, None] == q_lab[None, :]) & (q_lab[None, :] > 0) & (q_ord[None, :] < q_ord[:, None]))]
+    for k_a, k_m in zip(keys_a, keys_m):
         k_lab, k_ord = k_m[0], k_m[1]
-        scores = dots(k_a, k_b)
-        hits = (q_lab[:, None] == k_lab[None, :]) & (k_lab[None, :] > 0) & (k_ord[None, :] < q_ord[:, None])
-        best = jnp.maximum(best, jnp.max(jnp.where(hits, scores, jnp.float32(-1.0)), axis=1))
+        parts.append(part(k_a, (q_lab[:, None] == k_lab[None, :]) & (k_lab[None, :] > 0) & (k_ord[None, :] < q_ord[:, None])))
+    best = jnp.full((n_slot,), -1.0, jnp.float32)
+    for masked, k_b in zip(parts, [got_b] + list(keys_b)):
+        s = masked + jnp.einsum("qe,ke->qk", got_b, k_b, preferred_element_type=jnp.float32)
+        best = jnp.maximum(best, jnp.max(s, axis=1))
 
     returned = lax.all_to_all(
         best.reshape(n_grp, cap), "grp", split_axis=0, concat_axis=0, tiled=True

time: 112 us -> 114 us (1.018)
  blocking collectives: 10.3 us -> 11.9 us
    ppermute x2, waiting for transfers between devices: 14.8 us -> 0.86 us  [gather_split(): cross = lax.ppermute(rows, 'split', [(0, 2), (1, 3), (2, 0), (3, 1)])]
    all_to_all x1, waiting for transfers between devices: 1.84 us -> 15.4 us  [local(): got = lax.all_to_all(send, 'grp', split_axis=0, concat_axis=0, tiled=True)]
    all_to_all x1, blocking collectives: 10.3 us -> 11.9 us  [local(): lax.all_to_all(best.reshape(n_grp, cap), 'grp', split_axis=0, concat_axis...]
    unnamed x12 -> x10, local copies, waits for them, and re-layouts: 2.82 us -> 2.06 us
  transfers between devices with their start and end apart: 12 -> 12, of which waited for: 5 -> 6; matrix products, arithmetic and copies ran while one was open for 21% -> 20% of each run, Pallas kernels for 0% -> 0%
where the time goes in v7:
time: 114 us
  waiting for transfers between devices  40.9 us (36%)
  matrix products  26.8 us (24%)
  starting transfers between devices  17 us (15%)
  blocking collectives  11.9 us (10%)
  local copies, waits for them, and re-layouts  11.2 us (10%)
  other arithmetic  5.51 us (5%)
    all_to_all x1, waiting for transfers between devices, route(): got = lax.all_to_all(send, 'grp', split_axis=0, concat_axis=0, tiled=True)  17.5 us
    all_to_all x1, waiting for transfers between devices, local(): got = lax.all_to_all(send, 'grp', split_axis=0, concat_axis=0, tiled=True)  15.4 us
    dot_general x4, matrix products, part(): s = jnp.einsum('qe,ke->qk', q_emb, k_a, preferred_element_type=jnp.float32)  12.2 us
    all_to_all x1, blocking collectives, local(): lax.all_to_all(best.reshape(n_grp, cap), 'grp', split_axis=0, concat_axis...  11.9 us
    all_to_all x1, starting transfers between devices, route(): got = lax.all_to_all(send, 'grp', split_axis=0, concat_axis=0, tiled=True)  7.25 us
    dot_general x1, matrix products, embed_rows(): jnp.einsum('...h,he->...e', rows, weight, preferred_element_type=jnp.floa...  5.94 us
    ppermute x1, waiting for transfers between devices, local(): par_place = lax.ppermute(place, 'split', cross)  5.02 us
    all_to_all x1, starting transfers between devices, local(): got = lax.all_to_all(send, 'grp', split_axis=0, concat_axis=0, tiled=True)  4.45 us
  transfers between devices with their start and end apart: 12, of which 6 were waited for; matrix products, arithmetic and copies ran while one was open for 20% of the time, Pallas kernels for 0%

profile of v7, /device:TPU:0, one launch (start us, length us, event | category | flops | bytes accessed | tf_op | source)
XLA Modules:
  0.0 113.7 jit_solution(9991846189942785741)
XLA Ops:
  0.0 0.8 convert_convert_fusion.1
  1.1 0.8 copy-done
  1.9 5.9 %multiply_reduce_fusion = (f32[384]{0:T(512)S(1)}, f32[384,1024]{1,0:T(8,128)S(1)}) fusion(bf16[384,4096]{1,0:T(8,128)(2,1)S(1)} %copy-done, bf16[4096,1024]{1,0:T(8,128)(2,1)} %param.6), kind=kOutput, calls=%fused_computation.5 | convolution fusion | flops 3222011392 | bytes 13108736 | tf_op jit(solution)/shard_map/...h,he->...e/dot_general | solution.py:14
  8.1 0.9 copy-done.1
  9.0 0.8 slice.60
  11.0 1.9 %concatenate.10 = bf16[384,768]{1,0:T(8,128)(2,1)} concatenate(bf16[384,640]{1,0:T(8,128)(2,1)} %slice.60, bf16[384,1]{1,0:T(8,128)(2,1)S(1)} %stack.26, bf16[384,1]{1,0:T(8,128)(2,1)S(1)} %stack.27, bf16[384,1]{1,0:T(8,128)(2,1)S(1)} %stack.28, bf16[384,1]{1,0:T(8,128)(2,1)S(1)} %stack.29, bf16[384,124]{1,0:T(8,128)(2,1)} %broadcast_in_dim.21), dimensions={1} | concatenate | bytes 1179648 | tf_op jit(solution)/shard_map/concatenate | solution.py:79
  12.9 2.8 %convolution_convert_fusion = bf16[768,768]{1,0:T(8,128)(2,1)} fusion(bf16[384,768]{1,0:T(8,128)(2,1)} %concatenate.10, s32[384]{0:T(512)S(1)} %convert_add_fusion), kind=kOutput, calls=%fused_computation.6 | convolution fusion | flops 453869568 | bytes 1771008 | tf_op jit(solution)/shard_map/dot_general | solution.py:67
  15.7 7.3 %all-to-all-start = ((bf16[8,96,768]{2,1,0:T(8,128)(2,1)}), bf16[8,96,768]{2,1,0:T(8,128)(2,1)}, u32[]{:S(2)}, u32[]{:S(2)}) async-start(bf16[8,96,768]{2,1,0:T(8,128)(2,1)} %bitcast.28), calls=%async_computation | async-start | bytes 2359296 | tf_op jit(solution)/shard_map/all_to_all | solution.py:69
  23.0 1.0 slice.66
  24.0 1.6 %collective-permute-start.1 = (bf16[384,384]{1,0:T(8,128)(2,1)S(1)}, bf16[384,384]{1,0:T(8,128)(2,1)S(1)}, u32[]{:S(2)}, u32[]{:S(2)}) collective-permute-start(bf16[384,384]{1,0:T(8,128)(2,1)S(1)} %slice.66), channel_id=1, source_target_pairs={{0,2},{2,0},{1,3},{3,1},{4,6},{6,4},{5,7},{7,5},{8,10},{10,8},{9,1... | collective-permute-start | bytes 884744 | tf_op jit(solution)/shard_map/ppermute | solution.py:77
  26.1 1.5 %convolution_convert_fusion.2 = bf16[768,384]{1,0:T(8,128)(2,1)S(1)} fusion(s32[384]{0:T(512)S(1)} %convert_add_fusion, bf16[384,1024]{1,0:T(8,128)(2,1)} %copy-done.1), kind=kOutput, calls=%fused_computation.8 | convolution fusion | flops 227082240 | bytes 886272 | tf_op jit(solution)/shard_map/dot_general | solution.py:84
  27.5 5.0 %collective-permute-done = s32[384]{0:T(512)S(1)} collective-permute-done((s32[384]{0:T(512)S(1)}, s32[384]{0:T(512)S(1)}, u32[]{:S(2)}, u32[]{:S(2)}) %collective-permute-start) | collective-permute-done | bytes 1568 | tf_op jit(solution)/shard_map/ppermute | solution.py:78
  33.1 1.1 pad_maximum_fusion
  34.2 17.5 %all-to-all-done = bf16[8,96,768]{2,1,0:T(8,128)(2,1)} async-done(((bf16[8,96,768]{2,1,0:T(8,128)(2,1)}), bf16[8,96,768]{2,1,0:T(8,128)(2,1)}, u32[]{:S(2)}, u32[]{:S(2)}) %all-to-all-start) | async-done | bytes 1179680 | tf_op jit(solution)/shard_map/all_to_all | solution.py:69
  51.7 4.4 %all-to-all-start.1 = ((bf16[8,192,384]{2,1,0:T(8,128)(2,1)}), bf16[8,192,384]{2,1,0:T(8,128)(2,1)}, u32[]{:S(2)}, u32[]{:S(2)}) async-start(bf16[8,192,384]{2,1,0:T(8,128)(2,1)} %pad_maximum_fusion), calls=%async_computation.1 | async-start | bytes 2359296 | tf_op jit(solution)/shard_map/all_to_all | solution.py:89
  56.1 1.8 %convert_reduce_fusion = (f32[768]{0:T(1024)S(1)}, f32[768]{0:T(1024)S(1)}) fusion(bf16[768,768]{1,0:T(8,128)(2,1)} %bitcast.1), kind=kLoop, calls=%fused_computation.19 | loop fusion | flops 6144 | bytes 12288 | tf_op jit(solution)/shard_map/eq | solution.py:106
  58.0 1.6 %collective-permute-start.2 = (f32[2,768]{1,0:T(2,128)S(1)}, f32[2,768]{1,0:T(2,128)S(1)}, u32[]{:S(2)}, u32[]{:S(2)}) collective-permute-start(f32[2,768]{1,0:T(2,128)S(1)} %pad_maximum_fusion.1), channel_id=1, source_target_pairs={{0,2},{1,3},{2,0},{3,1},{4,6},{5,7},{6,4},{7,5},{8,10},{9,11},{10,... | collective-permute-start | bytes 18440 | tf_op jit(solution)/shard_map/ppermute | solution.py:21
  59.6 4.0 %fusion.20 = f32[768,768]{0,1:T(8,128)} fusion(bf16[768,768]{1,0:T(8,128)(2,1)} %bitcast.1), kind=kOutput, calls=%fused_computation.66 | convolution fusion | flops 754974720 | bytes 3342336 | tf_op jit(solution)/shard_map/qe,ke->qk/dot_general | solution.py:103
  63.6 2.2 %slice.65 = bf16[768,640]{1,0:T(8,128)(2,1)} slice(bf16[768,768]{1,0:T(8,128)(2,1)} %bitcast.1), slice={[0:768], [0:640]} | slice | bytes 1966080 | tf_op jit(solution)/shard_map/slice | solution.py:31
  67.1 1.9 %collective-permute-done.7 = f32[2,768]{1,0:T(2,128)S(1)} collective-permute-done((f32[2,768]{1,0:T(2,128)S(1)}, f32[2,768]{1,0:T(2,128)S(1)}, u32[]{:S(2)}, u32[]{:S(2)}) %collective-permute-start.7) | collective-permute-done | bytes 6176 | tf_op jit(solution)/shard_map/ppermute | solution.py:23
  69.0 15.4 %all-to-all-done.1 = bf16[8,192,384]{2,1,0:T(8,128)(2,1)} async-done(((bf16[8,192,384]{2,1,0:T(8,128)(2,1)}), bf16[8,192,384]{2,1,0:T(8,128)(2,1)}, u32[]{:S(2)}, u32[]{:S(2)}) %all-to-all-start.1) | async-done | bytes 1179680 | tf_op jit(solution)/shard_map/all_to_all | solution.py:89
  84.4 1.4 %fusion.26 = (bf16[8,96,384]{2,1,0:T(8,128)(2,1)S(1)}, bf16[8,96,384]{2,1,0:T(8,128)(2,1)S(1)}) fusion(bf16[8,192,384]{2,1,0:T(8,128)(2,1)} %all-to-all-done.1), kind=kLoop, calls=%fused_computation.68 | loop fusion | bytes 2359296 | tf_op jit(solution)/shard_map/slice | solution.py:91
  86.3 0.8 fusion.27
  87.4 1.0 add_reduce_fusion.3
  88.7 0.8 fusion.28
  89.5 0.9 collective-permute-done.3
  90.3 2.6 %fusion.16 = f32[768,768]{0,1:T(8,128)S(1)} fusion(bf16[768,640]{1,0:T(8,128)(2,1)} %collective-permute-done.5, bf16[768,768]{1,0:T(8,128)(2,1)} %bitcast.1), kind=kOutput, calls=%fused_computation.62 | convolution fusion | flops 754974720 | bytes 4325376 | tf_op jit(solution)/shard_map/qe,ke->qk/dot_general | solution.py:103
  93.0 1.0 add_reduce_fusion.1
  94.0 2.9 %add_reduce_fusion.2 = f32[768]{0:T(1024)S(1)} fusion(f32[768,768]{0,1:T(8,128)S(1)} %fusion.27, f32[768]{0:T(1024)S(1)} %get-tuple-element.6, f32[768]{0:T(1024)S(1)} %get-tuple-element.5, f32[768]{0:T(1024)S(1)} %get-tuple-element.8, f32[768]{0:T(1024)S(1)} %get-tuple-element.7, pred[768]{0:T(1024)(128)(4,1)S(1)} %compare_reduce_fusion.2, ...), kind=kOutput, calls=%fused_computation.2 | convolution fusion | flops 759102720 | bytes 4341504 | tf_op jit(solution)/shard_map/qe,ke->qk/dot_general | solution.py:103
  97.0 2.6 %add_reduce_fusion = f32[768]{0:T(1024)S(1)} fusion(f32[768,768]{0,1:T(8,128)S(1)} %fusion.28, f32[768]{0:T(1024)S(1)} %get-tuple-element.6, f32[768]{0:T(1024)S(1)} %get-tuple-element.5, f32[768]{0:T(1024)S(1)} %get-tuple-element.12, f32[768]{0:T(1024)S(1)} %get-tuple-element.11, pred[768]{0:T(1024)(128)(4,1)S(1)} %compare_reduce_fusion, ...), kind=kOutput, calls=%fused_computation | convolution fusion | flops 759102720 | bytes 4341504 | tf_op jit(solution)/shard_map/qe,ke->qk/dot_general | solution.py:103
  99.7 11.9 %all_to_all.16 = f32[8,1,96]{2,1,0:T(1,128)S(1)} all-to-all(f32[8,1,96]{2,1,0:T(1,128)S(1)} %max.41), channel_id=1, replica_groups=mesh['grp'=8,'split'=4] {'grp'}, dimensions={0} | all-to-all | bytes 6144 | tf_op jit(solution)/shard_map/all_to_all | solution.py:115
  112.9 0.8 select_reduce_fusion
  (50 shorter events, 6.2 us)
Async XLA Ops:
  0.0 1.9 %copy-start = (bf16[384,4096]{1,0:T(8,128)(2,1)S(1)}, bf16[384,4096]{1,0:T(8,128)(2,1)}, u32[]{:S(2)}) copy-start(bf16[384,4096]{1,0:T(8,128)(2,1)} %param.5) | copy-start | bytes 9437188
  7.9 2.1 %copy-start.3 = (s32[384]{0:T(512)S(1)}, s32[384]{0:T(512)}, u32[]{:S(2)}) copy-start(s32[384]{0:T(512)} %param.9) | copy-start | bytes 4612
  7.9 2.3 %copy-start.2 = (s32[384]{0:T(512)S(1)}, s32[384]{0:T(512)}, u32[]{:S(2)}) copy-start(s32[384]{0:T(512)} %param.8) | copy-start | bytes 4612
  8.0 0.9 copy-start.1
  15.7 35.9 %all-to-all-start = ((bf16[8,96,768]{2,1,0:T(8,128)(2,1)}), bf16[8,96,768]{2,1,0:T(8,128)(2,1)}, u32[]{:S(2)}, u32[]{:S(2)}) async-start(bf16[8,96,768]{2,1,0:T(8,128)(2,1)} %bitcast.28), calls=%async_computation | async-start | bytes 2359296 | tf_op jit(solution)/shard_map/all_to_all | solution.py:69
  24.0 8.6 %collective-permute-start.1 = (bf16[384,384]{1,0:T(8,128)(2,1)S(1)}, bf16[384,384]{1,0:T(8,128)(2,1)S(1)}, u32[]{:S(2)}, u32[]{:S(2)}) collective-permute-start(bf16[384,384]{1,0:T(8,128)(2,1)S(1)} %slice.66), channel_id=1, source_target_pairs={{0,2},{2,0},{1,3},{3,1},{4,6},{6,4},{5,7},{7,5},{8,10},{10,8},{9,1... | collective-permute-start | bytes 884744 | tf_op jit(solution)/shard_map/ppermute | solution.py:77
  25.6 7.0 %collective-permute-start = (s32[384]{0:T(512)S(1)}, s32[384]{0:T(512)S(1)}, u32[]{:S(2)}, u32[]{:S(2)}) collective-permute-start(s32[384]{0:T(512)S(1)} %convert_add_fusion), channel_id=1, source_target_pairs={{0,2},{2,0},{1,3},{3,1},{4,6},{6,4},{5,7},{7,5},{8,10},{10,8},{9,1... | collective-permute-start | bytes 4616 | tf_op jit(solution)/shard_map/ppermute | solution.py:78
  51.7 32.7 %all-to-all-start.1 = ((bf16[8,192,384]{2,1,0:T(8,128)(2,1)}), bf16[8,192,384]{2,1,0:T(8,128)(2,1)}, u32[]{:S(2)}, u32[]{:S(2)}) async-start(bf16[8,192,384]{2,1,0:T(8,128)(2,1)} %pad_maximum_fusion), calls=%async_computation.1 | async-start | bytes 2359296 | tf_op jit(solution)/shard_map/all_to_all | solution.py:89
  58.0 8.6 %collective-permute-start.2 = (f32[2,768]{1,0:T(2,128)S(1)}, f32[2,768]{1,0:T(2,128)S(1)}, u32[]{:S(2)}, u32[]{:S(2)}) collective-permute-start(f32[2,768]{1,0:T(2,128)S(1)} %pad_maximum_fusion.1), channel_id=1, source_target_pairs={{0,2},{1,3},{2,0},{3,1},{4,6},{5,7},{6,4},{7,5},{8,10},{9,11},{10,... | collective-permute-start | bytes 18440 | tf_op jit(solution)/shard_map/ppermute | solution.py:21
  65.8 1.2 %collective-permute-start.4 = (f32[2,768]{1,0:T(2,128)S(1)}, f32[2,768]{1,0:T(2,128)S(1)}, u32[]{:S(2)}, u32[]{:S(2)}) collective-permute-start(f32[2,768]{1,0:T(2,128)S(1)} %pad_maximum_fusion.1), channel_id=1, source_target_pairs={{0,1},{1,0},{2,3},{3,2},{4,5},{5,4},{6,7},{7,6},{8,9},{9,8},{10,11... | collective-permute-start | bytes 18440 | tf_op jit(solution)/shard_map/ppermute | solution.py:23
  65.8 24.5 %collective-permute-start.3 = (bf16[768,640]{1,0:T(8,128)(2,1)}, bf16[768,640]{1,0:T(8,128)(2,1)}, u32[]{:S(2)}, u32[]{:S(2)}) collective-permute-start(bf16[768,640]{1,0:T(8,128)(2,1)} %slice.65), channel_id=1, source_target_pairs={{0,2},{1,3},{2,0},{3,1},{4,6},{5,7},{6,4},{7,5},{8,10},{9,11},{10,... | collective-permute-start | bytes 2949128 | tf_op jit(solution)/shard_map/ppermute | solution.py:21
  66.4 24.0 %collective-permute-start.5 = (bf16[768,640]{1,0:T(8,128)(2,1)}, bf16[768,640]{1,0:T(8,128)(2,1)}, u32[]{:S(2)}, u32[]{:S(2)}) collective-permute-start(bf16[768,640]{1,0:T(8,128)(2,1)} %slice.65), channel_id=1, source_target_pairs={{0,1},{1,0},{2,3},{3,2},{4,5},{5,4},{6,7},{7,6},{8,9},{9,8},{10,11... | collective-permute-start | bytes 2949128 | tf_op jit(solution)/shard_map/ppermute | solution.py:23
  66.6 2.3 %collective-permute-start.7 = (f32[2,768]{1,0:T(2,128)S(1)}, f32[2,768]{1,0:T(2,128)S(1)}, u32[]{:S(2)}, u32[]{:S(2)}) collective-permute-start(f32[2,768]{1,0:T(2,128)S(1)} %collective-permute-done.2), channel_id=1, source_target_pairs={{0,1},{1,0},{2,3},{3,2},{4,5},{5,4},{6,7},{7,6},{8,9},{9,8},{10,11... | collective-permute-start | bytes 18440 | tf_op jit(solution)/shard_map/ppermute | solution.py:23
  85.8 1.7 %copy-start.4 = (f32[768,768]{0,1:T(8,128)S(1)}, f32[768,768]{0,1:T(8,128)}, u32[]{:S(2)}) copy-start(f32[768,768]{0,1:T(8,128)} %fusion.20) | copy-start | bytes 7077892
  85.8 7.2 %collective-permute-start.6 = (bf16[768,384]{1,0:T(8,128)(2,1)S(1)}, bf16[768,384]{1,0:T(8,128)(2,1)S(1)}, u32[]{:S(2)}, u32[]{:S(2)}) collective-permute-start(bf16[768,384]{1,0:T(8,128)(2,1)S(1)} %bitcast.21), channel_id=1, source_target_pairs={{0,1},{1,0},{2,3},{3,2},{4,5},{5,4},{6,7},{7,6},{8,9},{9,8},{10,11... | collective-permute-start | bytes 1769480 | tf_op jit(solution)/shard_map/ppermute | solution.py:92
  85.8 2.8 %collective-permute-start.9 = (bf16[768,384]{1,0:T(8,128)(2,1)S(1)}, bf16[768,384]{1,0:T(8,128)(2,1)S(1)}, u32[]{:S(2)}, u32[]{:S(2)}) collective-permute-start(bf16[768,384]{1,0:T(8,128)(2,1)S(1)} %bitcast.26), channel_id=1, source_target_pairs={{0,1},{1,0},{2,3},{3,2},{4,5},{5,4},{6,7},{7,6},{8,9},{9,8},{10,11... | collective-permute-start | bytes 1769480 | tf_op jit(solution)/shard_map/ppermute | solution.py:92
  90.3 6.6 %collective-permute-start.8 = (bf16[768,640]{1,0:T(8,128)(2,1)}, bf16[768,640]{1,0:T(8,128)(2,1)S(1)}, u32[]{:S(2)}, u32[]{:S(2)}) collective-permute-start(bf16[768,640]{1,0:T(8,128)(2,1)} %collective-permute-done.3), channel_id=1, source_target_pairs={{0,1},{1,0},{2,3},{3,2},{4,5},{5,4},{6,7},{7,6},{8,9},{9,8},{10,11... | collective-permute-start | bytes 2949128 | tf_op jit(solution)/shard_map/ppermute | solution.py:23

commit v8 on v7

--- a/solution.py
+++ b/solution.py
@@ -2,6 +2,7 @@
 import jax.numpy as jnp
 from jax import lax
 from jax.sharding import PartitionSpec as P
+from jax.experimental import pallas as pl
 
 CL_GRP = 4
 
@@ -14,6 +15,43 @@
     proj = jnp.einsum("...h,he->...e", rows, weight, preferred_element_type=jnp.float32)
     scale = lax.rsqrt(jnp.sum(proj * proj, axis=-1, keepdims=True) + EPS)
     return (proj * scale).astype(jnp.bfloat16)
+
+
+def _block_max_kernel(qa_ref, qb_ref, ka_ref, kb_ref, qm_ref, km_ref, o_ref):
+    nt = (((1,), (1,)), ((), ()))
+    s = lax.dot_general(qa_ref[...], ka_ref[...], nt, preferred_element_type=jnp.float32)
+    s = s + lax.dot_general(qb_ref[...], kb_ref[...], nt, preferred_element_type=jnp.float32)
+    q_lab, q_ord = qm_ref[:, 0:1], qm_ref[:, 1:2]
+    k_lab, k_ord = km_ref[0:1, :], km_ref[1:2, :]
+    hits = (q_lab == k_lab) & (k_lab > 0) & (k_ord < q_ord)
+    o_ref[...] = jnp.max(jnp.where(hits, s, jnp.float32(-1.0)), axis=1, keepdims=True)
+
+
+def block_max(qa, qb, ka, kb, qm, km):
+    n_q, n_k = qa.shape[0], ka.shape[0]
+    tq = 256 if n_q % 256 == 0 else n_q
+    wa, wb = qa.shape[1], qb.shape[1]
+    cost = pl.CostEstimate(
+        flops=2 * n_q * n_k * (wa + wb),
+        bytes_accessed=2 * (n_q + n_k) * (wa + wb) + 4 * n_q * n_k // 64,
+        transcendentals=0,
+    )
+    out = pl.pallas_call(
+        _block_max_kernel,
+        out_shape=jax.ShapeDtypeStruct((n_q, 1), jnp.float32),
+        grid=(n_q // tq,),
+        in_specs=[
+            pl.BlockSpec((tq, wa), lambda i: (i, 0)),
+            pl.BlockSpec((tq, wb), lambda i: (i, 0)),
+            pl.BlockSpec((n_k, wa), lambda i: (0, 0)),
+            pl.BlockSpec((n_k, wb), lambda i: (0, 0)),
+            pl.BlockSpec((tq, qm.shape[1]), lambda i: (i, 0)),
+            pl.BlockSpec((km.shape[0], n_k), lambda i: (0, 0)),
+        ],
+        out_specs=pl.BlockSpec((tq, 1), lambda i: (i, 0)),
+        cost_estimate=cost,
+    )(qa, qb, ka, kb, qm, km)
+    return out[:, 0]
 
 
 def gather_split(rows, n_split):
@@ -99,18 +137,13 @@
         got_b = route(embeds[:, half:])
         keys_b = gather_split(got_b, n_split)
 
-    def part(k_a, hits):
-        s = jnp.einsum("qe,ke->qk", q_emb, k_a, preferred_element_type=jnp.float32)
-        return jnp.where(hits, s, -jnp.inf)
-
-    parts = [part(q_emb, (q_lab[:, None] == q_lab[None, :]) & (q_lab[None, :] > 0) & (q_ord[None, :] < q_ord[:, None]))]
-    for k_a, k_m in zip(keys_a, keys_m):
-        k_lab, k_ord = k_m[0], k_m[1]
-        parts.append(part(k_a, (q_lab[:, None] == k_lab[None, :]) & (k_lab[None, :] > 0) & (k_ord[None, :] < q_ord[:, None])))
+    own_m = jnp.stack([q_lab, q_ord])
+    pad_m = jnp.zeros((6, n_slot), jnp.float32)
+    qm = jnp.concatenate([own_m, pad_m], axis=0).T
     best = jnp.full((n_slot,), -1.0, jnp.float32)
-    for masked, k_b in zip(parts, [got_b] + list(keys_b)):
-        s = masked + jnp.einsum("qe,ke->qk", got_b, k_b, preferred_element_type=jnp.float32)
-        best = jnp.maximum(best, jnp.max(s, axis=1))
+    for k_a, k_b, k_m in zip([q_emb] + list(keys_a), [got_b] + list(keys_b), [own_m] + list(keys_m)):
+        km = jnp.concatenate([k_m, pad_m], axis=0)
+        best = jnp.maximum(best, block_max(q_emb, got_b, k_a, k_b, qm, km))
 
     returned = lax.all_to_all(
         best.reshape(n_grp, cap), "grp", split_axis=0, concat_axis=0, tiled=True

time: 114 us -> 133 us (1.17)
  Pallas kernels: 0 us -> 20.5 us
  matrix products: 26.8 us -> 11 us
  waiting for transfers between devices: 40.9 us -> 50.6 us
  other arithmetic: 5.51 us -> 8.66 us
  local copies, waits for them, and re-layouts: 11.2 us -> 13.9 us
  blocking collectives: 11.9 us -> 9.74 us
    ppermute x2, waiting for transfers between devices: 0.86 us -> 23.6 us  [gather_split(): cross = lax.ppermute(rows, 'split', [(0, 2), (1, 3), (2, 0), (3, 1)])]
    pallas_call x0 -> x4, Pallas kernels: none -> 20.5 us  [block_max(): pl.pallas_call(_block_max_kernel, out_shape=jax.ShapeDtypeStruct((n_q, 1)...]
    dot_general x8 -> x0, matrix products: 15.9 us -> none  [the longest x4 12.2 us: part(): s = jnp.einsum('qe,ke->qk', q_emb, k_a, preferred_element_type=jnp.float32)]
    all_to_all x1, waiting for transfers between devices: 15.4 us -> 3.02 us  [local(): got = lax.all_to_all(send, 'grp', split_axis=0, concat_axis=0, tiled=True)]
    concatenate x0 -> x5, local copies, waits for them, and re-layouts: none -> 2.81 us  [the longest x3 1.82 us: local(): km = jnp.concatenate([k_m, pad_m], axis=0)]
    all_to_all x1, blocking collectives: 11.9 us -> 9.74 us  [local(): lax.all_to_all(best.reshape(n_grp, cap), 'grp', split_axis=0, concat_axis...]
    convert_element_type x0 -> x1, other arithmetic: none -> 2.06 us  [unpack(): lab = buf[:, emb_w].astype(jnp.float32)]
    ppermute x2, waiting for transfers between devices: 1.87 us -> 0.01 us  [gather_split(): lax.ppermute(cross, 'split', pair)]
  transfers between devices with their start and end apart: 12 -> 12, of which waited for: 6 -> 6; matrix products, arithmetic and copies ran while one was open for 20% -> 10% of each run, Pallas kernels for 0% -> 12%
where the time goes in v8:
time: 133 us; the launch traced here: 132 us
  waiting for transfers between devices  50.6 us (38%)
  Pallas kernels  20.5 us (15%)
  starting transfers between devices  17.3 us (13%)
  local copies, waits for them, and re-layouts  13.9 us (10%)
  matrix products  11 us (8%)
  blocking collectives  9.74 us (7%)
  other arithmetic  8.66 us (7%)
    ppermute x2, waiting for transfers between devices, gather_split(): cross = lax.ppermute(rows, 'split', [(0, 2), (1, 3), (2, 0), (3, 1)])  23.6 us
    pallas_call x4, Pallas kernels, block_max(): pl.pallas_call(_block_max_kernel, out_shape=jax.ShapeDtypeStruct((n_q, 1)...  20.5 us
    all_to_all x1, waiting for transfers between devices, route(): got = lax.all_to_all(send, 'grp', split_axis=0, concat_axis=0, tiled=True)  17.4 us
    all_to_all x1, blocking collectives, local(): lax.all_to_all(best.reshape(n_grp, cap), 'grp', split_axis=0, concat_axis...  9.74 us
    all_to_all x1, starting transfers between devices, route(): got = lax.all_to_all(send, 'grp', split_axis=0, concat_axis=0, tiled=True)  7.25 us
    dot_general x1, matrix products, embed_rows(): jnp.einsum('...h,he->...e', rows, weight, preferred_element_type=jnp.floa...  5.95 us
    ppermute x1, waiting for transfers between devices, local(): par_place = lax.ppermute(place, 'split', cross)  5.02 us
    all_to_all x1, starting transfers between devices, local(): got = lax.all_to_all(send, 'grp', split_axis=0, concat_axis=0, tiled=True)  4.25 us
  transfers between devices with their start and end apart: 12, of which 6 were waited for; matrix products, arithmetic and copies ran while one was open for 10% of the time, Pallas kernels for 12%

profile of v8, /device:TPU:0, one launch (start us, length us, event | category | flops | bytes accessed | tf_op | source)
XLA Modules:
  0.0 131.9 jit_solution(11702888879563165028)
XLA Ops:
  0.0 0.8 convert_convert_fusion
  0.8 0.8 fusion.10
  3.1 5.9 %multiply_reduce_fusion = (f32[384]{0:T(512)S(1)}, f32[384,1024]{1,0:T(8,128)S(1)}) fusion(bf16[384,4096]{1,0:T(8,128)(2,1)S(1)} %copy-done, bf16[4096,1024]{1,0:T(8,128)(2,1)} %param.6), kind=kOutput, calls=%fused_computation.1 | convolution fusion | flops 3222011392 | bytes 13108736 | tf_op jit(solution)/shard_map/...h,he->...e/dot_general | solution.py:15
  9.2 0.9 copy-done.1
  10.1 0.8 slice.36
  11.6 1.9 %concatenate.25 = bf16[384,768]{1,0:T(8,128)(2,1)} concatenate(bf16[384,640]{1,0:T(8,128)(2,1)} %slice.36, bf16[384,1]{1,0:T(8,128)(2,1)S(1)} %stack.29, bf16[384,1]{1,0:T(8,128)(2,1)S(1)} %stack.30, bf16[384,1]{1,0:T(8,128)(2,1)S(1)} %stack.31, bf16[384,1]{1,0:T(8,128)(2,1)S(1)} %stack.32, bf16[384,124]{1,0:T(8,128)(2,1)} %broadcast_in_dim.32), dimensions={1} | concatenate | bytes 1179648 | tf_op jit(solution)/shard_map/concatenate | solution.py:117
  13.5 2.9 %convolution_convert_fusion = bf16[768,768]{1,0:T(8,128)(2,1)} fusion(bf16[384,768]{1,0:T(8,128)(2,1)} %concatenate.25, s32[384]{0:T(512)S(1)} %convert_add_fusion), kind=kOutput, calls=%fused_computation.2 | convolution fusion | flops 453869568 | bytes 1771008 | tf_op jit(solution)/shard_map/dot_general | solution.py:105
  16.4 7.3 %all-to-all-start = ((bf16[8,96,768]{2,1,0:T(8,128)(2,1)}), bf16[8,96,768]{2,1,0:T(8,128)(2,1)}, u32[]{:S(2)}, u32[]{:S(2)}) async-start(bf16[8,96,768]{2,1,0:T(8,128)(2,1)} %bitcast.12), calls=%async_computation | async-start | bytes 2359296 | tf_op jit(solution)/shard_map/all_to_all | solution.py:107
  23.6 1.0 slice.38
  24.6 1.6 %collective-permute-start.1 = (bf16[384,384]{1,0:T(8,128)(2,1)S(1)}, bf16[384,384]{1,0:T(8,128)(2,1)S(1)}, u32[]{:S(2)}, u32[]{:S(2)}) collective-permute-start(bf16[384,384]{1,0:T(8,128)(2,1)S(1)} %slice.38), channel_id=1, source_target_pairs={{0,2},{2,0},{1,3},{3,1},{4,6},{6,4},{5,7},{7,5},{8,10},{10,8},{9,1... | collective-permute-start | bytes 884744 | tf_op jit(solution)/shard_map/ppermute | solution.py:115
  26.7 1.5 %convolution_convert_fusion.2 = bf16[768,384]{1,0:T(8,128)(2,1)S(1)} fusion(s32[384]{0:T(512)S(1)} %convert_add_fusion, bf16[384,1024]{1,0:T(8,128)(2,1)} %copy-done.1), kind=kOutput, calls=%fused_computation.4 | convolution fusion | flops 227082240 | bytes 886272 | tf_op jit(solution)/shard_map/dot_general | solution.py:122
  28.2 5.0 %collective-permute-done = s32[384]{0:T(512)S(1)} collective-permute-done((s32[384]{0:T(512)S(1)}, s32[384]{0:T(512)S(1)}, u32[]{:S(2)}, u32[]{:S(2)}) %collective-permute-start) | collective-permute-done | bytes 1568 | tf_op jit(solution)/shard_map/ppermute | solution.py:116
  33.7 1.1 pad_maximum_fusion
  34.9 17.4 %all-to-all-done = bf16[8,96,768]{2,1,0:T(8,128)(2,1)} async-done(((bf16[8,96,768]{2,1,0:T(8,128)(2,1)}), bf16[8,96,768]{2,1,0:T(8,128)(2,1)}, u32[]{:S(2)}, u32[]{:S(2)}) %all-to-all-start) | async-done | bytes 1179680 | tf_op jit(solution)/shard_map/all_to_all | solution.py:107
  52.3 4.3 %all-to-all-start.1 = ((bf16[8,192,384]{2,1,0:T(8,128)(2,1)}), bf16[8,192,384]{2,1,0:T(8,128)(2,1)}, u32[]{:S(2)}, u32[]{:S(2)}) async-start(bf16[8,192,384]{2,1,0:T(8,128)(2,1)} %pad_maximum_fusion), calls=%async_computation.1 | async-start | bytes 2359296 | tf_op jit(solution)/shard_map/all_to_all | solution.py:127
  56.6 2.2 %slice.37.qa_ref.ka_ref = bf16[768,640]{1,0:T(8,128)(2,1)} slice(bf16[768,768]{1,0:T(8,128)(2,1)} %bitcast.1), slice={[0:768], [0:640]} | slice | bytes 1966080 | tf_op jit(solution)/shard_map/slice | solution.py:69
  58.8 1.5 %collective-permute-start.2 = (bf16[768,640]{1,0:T(8,128)(2,1)}, bf16[768,640]{1,0:T(8,128)(2,1)}, u32[]{:S(2)}, u32[]{:S(2)}) collective-permute-start(bf16[768,640]{1,0:T(8,128)(2,1)} %slice.37.qa_ref.ka_ref), channel_id=1, source_target_pairs={{0,2},{1,3},{2,0},{3,1},{4,6},{5,7},{6,4},{7,5},{8,10},{9,11},{10,... | collective-permute-start | bytes 2949128 | tf_op jit(solution)/shard_map/ppermute | solution.py:59
  60.3 21.6 %collective-permute-done.2.ka_ref = bf16[768,640]{1,0:T(8,128)(2,1)} collective-permute-done((bf16[768,640]{1,0:T(8,128)(2,1)}, bf16[768,640]{1,0:T(8,128)(2,1)}, u32[]{:S(2)}, u32[]{:S(2)}) %collective-permute-start.2) | collective-permute-done | bytes 983072 | tf_op jit(solution)/shard_map/ppermute | solution.py:59
  81.9 3.0 %all-to-all-done.1 = bf16[8,192,384]{2,1,0:T(8,128)(2,1)} async-done(((bf16[8,192,384]{2,1,0:T(8,128)(2,1)}), bf16[8,192,384]{2,1,0:T(8,128)(2,1)}, u32[]{:S(2)}, u32[]{:S(2)}) %all-to-all-start.1) | async-done | bytes 1179680 | tf_op jit(solution)/shard_map/all_to_all | solution.py:127
  84.9 2.4 %fusion.14 = (bf16[8,96,384]{2,1,0:T(8,128)(2,1)}, bf16[8,96,384]{2,1,0:T(8,128)(2,1)}) fusion(bf16[8,192,384]{2,1,0:T(8,128)(2,1)} %all-to-all-done.1), kind=kLoop, calls=%fused_computation.47 | loop fusion | bytes 2359296 | tf_op jit(solution)/shard_map/slice | solution.py:129
  87.3 2.1 %convert_reduce_fusion = (f32[768]{0:T(1024)S(1)}, f32[768]{0:T(1024)S(1)}) fusion(bf16[768,768]{1,0:T(8,128)(2,1)} %bitcast.1), kind=kLoop, calls=%fused_computation.15 | loop fusion | flops 6144 | bytes 12288 | tf_op jit(solution)/shard_map/convert_element_type | solution.py:70
  90.1 1.5 %collective-permute-done.6 = f32[2,768]{1,0:T(2,128)S(1)} collective-permute-done((f32[2,768]{1,0:T(2,128)S(1)}, f32[2,768]{1,0:T(2,128)S(1)}, u32[]{:S(2)}, u32[]{:S(2)}) %collective-permute-start.6) | collective-permute-done | bytes 6176 | tf_op jit(solution)/shard_map/ppermute | solution.py:61
  91.6 1.5 %collective-permute-start.3 = (f32[2,768]{1,0:T(2,128)S(1)}, f32[2,768]{1,0:T(2,128)S(1)}, u32[]{:S(2)}, u32[]{:S(2)}) collective-permute-start(f32[2,768]{1,0:T(2,128)S(1)} %pad_maximum_fusion.1), channel_id=1, source_target_pairs={{0,2},{1,3},{2,0},{3,1},{4,6},{5,7},{6,4},{7,5},{8,10},{9,11},{10,... | collective-permute-start | bytes 18440 | tf_op jit(solution)/shard_map/ppermute | solution.py:59
  93.2 2.0 %collective-permute-done.3 = f32[2,768]{1,0:T(2,128)S(1)} collective-permute-done((f32[2,768]{1,0:T(2,128)S(1)}, f32[2,768]{1,0:T(2,128)S(1)}, u32[]{:S(2)}, u32[]{:S(2)}) %collective-permute-start.3) | collective-permute-done | bytes 6176 | tf_op jit(solution)/shard_map/ppermute | solution.py:59
  95.3 0.9 copy.32
  98.1 5.1 %shard_map.55 = f32[768,1]{1,0:T(8,128)} custom-call(bf16[768,640]{1,0:T(8,128)(2,1)} %slice.37.qa_ref.ka_ref, bf16[768,384]{1,0:T(8,128)(2,1)} %bitcast.4.qb_ref.kb_ref, bf16[768,640]{1,0:T(8,128)(2,1)} %slice.37.qa_ref.ka_ref, bf16[768,384]{1,0:T(8,128)(2,1)} %bitcast.4.qb_ref.kb_ref, f32[768,8]{1,0:T(8,128)} %bitcast.15, f32[8,768]{1,0:T(8,128)} %copy-done.3), custom_call_target="tpu_custom_call" | custom-call | flops 1207959552 | bytes 3182592 | tf_op jit(solution)/shard_map/pallas_call | solution.py:39
  103.2 5.1 %shard_map.56 = f32[768,1]{1,0:T(8,128)} custom-call(bf16[768,640]{1,0:T(8,128)(2,1)} %slice.37.qa_ref.ka_ref, bf16[768,384]{1,0:T(8,128)(2,1)} %bitcast.4.qb_ref.kb_ref, bf16[768,640]{1,0:T(8,128)(2,1)} %collective-permute-done.2.ka_ref, bf16[768,384]{1,0:T(8,128)(2,1)} %bitcast.6.kb_ref, f32[768,8]{1,0:T(8,128)} %bitcast.16, f32[8,768]{1,0:T(8,128)} %concatenate.28.km_ref), custom_call_target="tpu_custom_call" | custom-call | flops 1207959552 | bytes 3182592 | tf_op jit(solution)/shard_map/pallas_call | solution.py:39
  108.3 5.1 %shard_map.57 = f32[768,1]{1,0:T(8,128)} custom-call(bf16[768,640]{1,0:T(8,128)(2,1)} %slice.37.qa_ref.ka_ref, bf16[768,384]{1,0:T(8,128)(2,1)} %bitcast.4.qb_ref.kb_ref, bf16[768,640]{1,0:T(8,128)(2,1)} %collective-permute-done.4.ka_ref, bf16[768,384]{1,0:T(8,128)(2,1)} %collective-permute-done.5.kb_ref, f32[768,8]{1,0:T(8,128)} %bitcast.17, ...), custom_call_target="tpu_custom_call" | custom-call | flops 1207959552 | bytes 3182592 | tf_op jit(solution)/shard_map/pallas_call | solution.py:39
  113.5 5.2 %shard_map.58 = f32[768,1]{1,0:T(8,128)} custom-call(bf16[768,640]{1,0:T(8,128)(2,1)} %slice.37.qa_ref.ka_ref, bf16[768,384]{1,0:T(8,128)(2,1)} %bitcast.4.qb_ref.kb_ref, bf16[768,640]{1,0:T(8,128)(2,1)} %collective-permute-done.7.ka_ref, bf16[768,384]{1,0:T(8,128)(2,1)} %collective-permute-done.8.kb_ref, f32[768,8]{1,0:T(8,128)} %bitcast.18, ...), custom_call_target="tpu_custom_call" | custom-call | flops 1207959552 | bytes 3182592 | tf_op jit(solution)/shard_map/pallas_call | solution.py:39
  118.6 1.4 %maximum_reduce_fusion = f32[768]{0:T(1024)S(1)} fusion(f32[768,1]{1,0:T(8,128)} %shard_map.58, f32[768,1]{1,0:T(8,128)} %shard_map.57, f32[768,1]{1,0:T(8,128)} %shard_map.56, f32[768,1]{1,0:T(8,128)S(1)} %copy-done.2), kind=kLoop, calls=%fused_computation.16 | loop fusion | flops 3072 | bytes 15360 | tf_op jit(solution)/shard_map/max | solution.py:146
  120.1 9.7 %all_to_all.16 = f32[8,1,96]{2,1,0:T(1,128)S(1)} all-to-all(f32[8,1,96]{2,1,0:T(1,128)S(1)} %bitcast.19), channel_id=1, replica_groups=mesh['grp'=8,'split'=4] {'grp'}, dimensions={0} | all-to-all | bytes 6144 | tf_op jit(solution)/shard_map/all_to_all | solution.py:148
  131.1 0.8 select_reduce_fusion
  (44 shorter events, 7.2 us)
Async XLA Ops:
  0.0 3.0 %copy-start = (bf16[384,4096]{1,0:T(8,128)(2,1)S(1)}, bf16[384,4096]{1,0:T(8,128)(2,1)}, u32[]{:S(2)}) copy-start(bf16[384,4096]{1,0:T(8,128)(2,1)} %param.5) | copy-start | bytes 9437188
  9.2 0.9 copy-start.1
  16.4 35.9 %all-to-all-start = ((bf16[8,96,768]{2,1,0:T(8,128)(2,1)}), bf16[8,96,768]{2,1,0:T(8,128)(2,1)}, u32[]{:S(2)}, u32[]{:S(2)}) async-start(bf16[8,96,768]{2,1,0:T(8,128)(2,1)} %bitcast.12), calls=%async_computation | async-start | bytes 2359296 | tf_op jit(solution)/shard_map/all_to_all | solution.py:107
  24.6 8.6 %collective-permute-start.1 = (bf16[384,384]{1,0:T(8,128)(2,1)S(1)}, bf16[384,384]{1,0:T(8,128)(2,1)S(1)}, u32[]{:S(2)}, u32[]{:S(2)}) collective-permute-start(bf16[384,384]{1,0:T(8,128)(2,1)S(1)} %slice.38), channel_id=1, source_target_pairs={{0,2},{2,0},{1,3},{3,1},{4,6},{6,4},{5,7},{7,5},{8,10},{10,8},{9,1... | collective-permute-start | bytes 884744 | tf_op jit(solution)/shard_map/ppermute | solution.py:115
  26.2 7.0 %collective-permute-start = (s32[384]{0:T(512)S(1)}, s32[384]{0:T(512)S(1)}, u32[]{:S(2)}, u32[]{:S(2)}) collective-permute-start(s32[384]{0:T(512)S(1)} %convert_add_fusion), channel_id=1, source_target_pairs={{0,2},{2,0},{1,3},{3,1},{4,6},{6,4},{5,7},{7,5},{8,10},{10,8},{9,1... | collective-permute-start | bytes 4616 | tf_op jit(solution)/shard_map/ppermute | solution.py:116
  52.3 32.6 %all-to-all-start.1 = ((bf16[8,192,384]{2,1,0:T(8,128)(2,1)}), bf16[8,192,384]{2,1,0:T(8,128)(2,1)}, u32[]{:S(2)}, u32[]{:S(2)}) async-start(bf16[8,192,384]{2,1,0:T(8,128)(2,1)} %pad_maximum_fusion), calls=%async_computation.1 | async-start | bytes 2359296 | tf_op jit(solution)/shard_map/all_to_all | solution.py:127
  58.8 23.1 %collective-permute-start.2 = (bf16[768,640]{1,0:T(8,128)(2,1)}, bf16[768,640]{1,0:T(8,128)(2,1)}, u32[]{:S(2)}, u32[]{:S(2)}) collective-permute-start(bf16[768,640]{1,0:T(8,128)(2,1)} %slice.37.qa_ref.ka_ref), channel_id=1, source_target_pairs={{0,2},{1,3},{2,0},{3,1},{4,6},{5,7},{6,4},{7,5},{8,10},{9,11},{10,... | collective-permute-start | bytes 2949128 | tf_op jit(solution)/shard_map/ppermute | solution.py:59
  60.3 48.0 %collective-permute-start.4 = (bf16[768,640]{1,0:T(8,128)(2,1)}, bf16[768,640]{1,0:T(8,128)(2,1)}, u32[]{:S(2)}, u32[]{:S(2)}) collective-permute-start(bf16[768,640]{1,0:T(8,128)(2,1)} %slice.37.qa_ref.ka_ref), channel_id=1, source_target_pairs={{0,1},{1,0},{2,3},{3,2},{4,5},{5,4},{6,7},{7,6},{8,9},{9,8},{10,11... | collective-permute-start | bytes 2949128 | tf_op jit(solution)/shard_map/ppermute | solution.py:61
  81.9 31.6 %collective-permute-start.7 = (bf16[768,640]{1,0:T(8,128)(2,1)}, bf16[768,640]{1,0:T(8,128)(2,1)}, u32[]{:S(2)}, u32[]{:S(2)}) collective-permute-start(bf16[768,640]{1,0:T(8,128)(2,1)} %collective-permute-done.2.ka_ref), channel_id=1, source_target_pairs={{0,1},{1,0},{2,3},{3,2},{4,5},{5,4},{6,7},{7,6},{8,9},{9,8},{10,11... | collective-permute-start | bytes 2949128 | tf_op jit(solution)/shard_map/ppermute | solution.py:61
  87.3 21.0 %collective-permute-start.5 = (bf16[768,384]{1,0:T(8,128)(2,1)}, bf16[768,384]{1,0:T(8,128)(2,1)}, u32[]{:S(2)}, u32[]{:S(2)}) collective-permute-start(bf16[768,384]{1,0:T(8,128)(2,1)} %bitcast.4.qb_ref.kb_ref), channel_id=1, source_target_pairs={{0,1},{1,0},{2,3},{3,2},{4,5},{5,4},{6,7},{7,6},{8,9},{9,8},{10,11... | collective-permute-start | bytes 1769480 | tf_op jit(solution)/shard_map/ppermute | solution.py:130
  89.4 24.1 %collective-permute-start.8 = (bf16[768,384]{1,0:T(8,128)(2,1)}, bf16[768,384]{1,0:T(8,128)(2,1)}, u32[]{:S(2)}, u32[]{:S(2)}) collective-permute-start(bf16[768,384]{1,0:T(8,128)(2,1)} %bitcast.6.kb_ref), channel_id=1, source_target_pairs={{0,1},{1,0},{2,3},{3,2},{4,5},{5,4},{6,7},{7,6},{8,9},{9,8},{10,11... | collective-permute-start | bytes 1769480 | tf_op jit(solution)/shard_map/ppermute | solution.py:130
  90.0 1.6 %collective-permute-start.6 = (f32[2,768]{1,0:T(2,128)S(1)}, f32[2,768]{1,0:T(2,128)S(1)}, u32[]{:S(2)}, u32[]{:S(2)}) collective-permute-start(f32[2,768]{1,0:T(2,128)S(1)} %pad_maximum_fusion.1), channel_id=1, source_target_pairs={{0,1},{1,0},{2,3},{3,2},{4,5},{5,4},{6,7},{7,6},{8,9},{9,8},{10,11... | collective-permute-start | bytes 18440 | tf_op jit(solution)/shard_map/ppermute | solution.py:61
  91.6 3.6 %collective-permute-start.3 = (f32[2,768]{1,0:T(2,128)S(1)}, f32[2,768]{1,0:T(2,128)S(1)}, u32[]{:S(2)}, u32[]{:S(2)}) collective-permute-start(f32[2,768]{1,0:T(2,128)S(1)} %pad_maximum_fusion.1), channel_id=1, source_target_pairs={{0,2},{1,3},{2,0},{3,1},{4,6},{5,7},{6,4},{7,5},{8,10},{9,11},{10,... | collective-permute-start | bytes 18440 | tf_op jit(solution)/shard_map/ppermute | solution.py:59
  95.3 2.2 %collective-permute-start.9 = (f32[2,768]{1,0:T(2,128)S(1)}, f32[2,768]{1,0:T(2,128)S(1)}, u32[]{:S(2)}, u32[]{:S(2)}) collective-permute-start(f32[2,768]{1,0:T(2,128)S(1)} %collective-permute-done.3), channel_id=1, source_target_pairs={{0,1},{1,0},{2,3},{3,2},{4,5},{5,4},{6,7},{7,6},{8,9},{9,8},{10,11... | collective-permute-start | bytes 18440 | tf_op jit(solution)/shard_map/ppermute | solution.py:61
  95.3 2.7 %copy-start.3 = (f32[8,768]{1,0:T(8,128)}, f32[8,768]{1,0:T(8,128)S(1)}, u32[]{:S(2)}) copy-start(f32[8,768]{1,0:T(8,128)S(1)} %maximum_maximum_fusion.km_ref) | copy-start | bytes 73732
  113.5 5.2 %copy-start.2 = (f32[768,1]{1,0:T(8,128)S(1)}, f32[768,1]{1,0:T(8,128)}, u32[]{:S(2)}) copy-start(f32[768,1]{1,0:T(8,128)} %shard_map.55) | copy-start | bytes 9220

commit v9 on v7

--- a/solution.py
+++ b/solution.py
@@ -99,18 +99,22 @@
         got_b = route(embeds[:, half:])
         keys_b = gather_split(got_b, n_split)
 
-    def part(k_a, hits):
-        s = jnp.einsum("qe,ke->qk", q_emb, k_a, preferred_element_type=jnp.float32)
+    def part(q, k, hits):
+        s = jnp.einsum("qe,ke->qk", q, k, preferred_element_type=jnp.float32)
         return jnp.where(hits, s, -jnp.inf)
 
-    parts = [part(q_emb, (q_lab[:, None] == q_lab[None, :]) & (q_lab[None, :] > 0) & (q_ord[None, :] < q_ord[:, None]))]
+    own_hits = (q_lab[:, None] == q_lab[None, :]) & (q_lab[None, :] > 0) & (q_ord[None, :] < q_ord[:, None])
+    parts = [lax.optimization_barrier(part(q_emb, q_emb, own_hits))]
     for k_a, k_m in zip(keys_a, keys_m):
         k_lab, k_ord = k_m[0], k_m[1]
-        parts.append(part(k_a, (q_lab[:, None] == k_lab[None, :]) & (k_lab[None, :] > 0) & (k_ord[None, :] < q_ord[:, None])))
+        hits = (q_lab[:, None] == k_lab[None, :]) & (k_lab[None, :] > 0) & (k_ord[None, :] < q_ord[:, None])
+        parts.append(lax.optimization_barrier(part(q_emb, k_a, hits)))
     best = jnp.full((n_slot,), -1.0, jnp.float32)
     for masked, k_b in zip(parts, [got_b] + list(keys_b)):
-        s = masked + jnp.einsum("qe,ke->qk", got_b, k_b, preferred_element_type=jnp.float32)
-        best = jnp.maximum(best, jnp.max(s, axis=1))
+        second = lax.optimization_barrier(
+            jnp.einsum("qe,ke->qk", got_b, k_b, preferred_element_type=jnp.float32)
+        )
+        best = jnp.maximum(best, jnp.max(masked + second, axis=1))
 
     returned = lax.all_to_all(
         best.reshape(n_grp, cap), "grp", split_axis=0, concat_axis=0, tiled=True

time: 114 us -> 112 us (0.982)
  blocking collectives: 11.9 us -> 9.64 us
  waiting for transfers between devices: 40.9 us -> 39.7 us
    all_to_all x1, blocking collectives: 11.9 us -> 9.64 us  [local(): lax.all_to_all(best.reshape(n_grp, cap), 'grp', split_axis=0, concat_axis...]
    unnamed x10 -> x12, local copies, waits for them, and re-layouts: 2.06 us -> 2.83 us
  transfers between devices with their start and end apart: 12 -> 12, of which waited for: 6 -> 4; matrix products, arithmetic and copies ran while one was open for 20% -> 21% of each run, Pallas kernels for 0% -> 0%
where the time goes in v9:
time: 112 us; the launch traced here: 111 us
  waiting for transfers between devices  39.7 us (35%)
  matrix products  26.6 us (24%)
  starting transfers between devices  17.1 us (15%)
  local copies, waits for them, and re-layouts  12 us (11%)
  blocking collectives  9.64 us (9%)
  other arithmetic  5.64 us (5%)
    all_to_all x1, waiting for transfers between devices, route(): got = lax.all_to_all(send, 'grp', split_axis=0, concat_axis=0, tiled=True)  17.5 us
    all_to_all x1, waiting for transfers between devices, local(): got = lax.all_to_all(send, 'grp', split_axis=0, concat_axis=0, tiled=True)  16.4 us
    dot_general x4, matrix products, part(): s = jnp.einsum('qe,ke->qk', q, k, preferred_element_type=jnp.float32)  12.5 us
    all_to_all x1, blocking collectives, local(): lax.all_to_all(best.reshape(n_grp, cap), 'grp', split_axis=0, concat_axis...  9.64 us
    all_to_all x1, starting transfers between devices, route(): got = lax.all_to_all(send, 'grp', split_axis=0, concat_axis=0, tiled=True)  7.25 us
    dot_general x1, matrix products, embed_rows(): jnp.einsum('...h,he->...e', rows, weight, preferred_element_type=jnp.floa...  5.94 us
    ppermute x1, waiting for transfers between devices, local(): par_place = lax.ppermute(place, 'split', cross)  5.02 us
    all_to_all x1, starting transfers between devices, local(): got = lax.all_to_all(send, 'grp', split_axis=0, concat_axis=0, tiled=True)  4.45 us
  transfers between devices with their start and end apart: 12, of which 4 were waited for; matrix products, arithmetic and copies ran while one was open for 21% of the time, Pallas kernels for 0%

profile of v9, /device:TPU:0, one launch (start us, length us, event | category | flops | bytes accessed | tf_op | source)
XLA Modules:
  0.0 111.0 jit_solution(3677529005241758181)
XLA Ops:
  0.0 1.9 %copy-done = bf16[384,4096]{1,0:T(8,128)(2,1)S(1)} copy-done((bf16[384,4096]{1,0:T(8,128)(2,1)S(1)}, bf16[384,4096]{1,0:T(8,128)(2,1)}, u32[]{:S(2)}) %copy-start) | copy-done | bytes 3145752
  1.9 5.9 %multiply_reduce_fusion = (f32[384]{0:T(512)S(1)}, f32[384,1024]{1,0:T(8,128)S(1)}) fusion(bf16[384,4096]{1,0:T(8,128)(2,1)S(1)} %copy-done, bf16[4096,1024]{1,0:T(8,128)(2,1)} %param.6), kind=kOutput, calls=%fused_computation.9 | convolution fusion | flops 3222011392 | bytes 13108736 | tf_op jit(solution)/shard_map/...h,he->...e/dot_general | solution.py:14
  8.1 0.9 copy-done.1
  9.0 0.8 slice.60
  10.6 0.6 broadcast_in_dim.21
  11.2 1.9 %concatenate.10 = bf16[384,768]{1,0:T(8,128)(2,1)} concatenate(bf16[384,640]{1,0:T(8,128)(2,1)} %slice.60, bf16[384,1]{1,0:T(8,128)(2,1)S(1)} %stack.26, bf16[384,1]{1,0:T(8,128)(2,1)S(1)} %stack.27, bf16[384,1]{1,0:T(8,128)(2,1)S(1)} %stack.28, bf16[384,1]{1,0:T(8,128)(2,1)S(1)} %stack.29, bf16[384,124]{1,0:T(8,128)(2,1)} %broadcast_in_dim.21), dimensions={1} | concatenate | bytes 1179648 | tf_op jit(solution)/shard_map/concatenate | solution.py:79
  13.1 2.8 %convolution_convert_fusion = bf16[768,768]{1,0:T(8,128)(2,1)} fusion(bf16[384,768]{1,0:T(8,128)(2,1)} %concatenate.10, s32[384]{0:T(512)S(1)} %convert_add_fusion), kind=kOutput, calls=%fused_computation.10 | convolution fusion | flops 453869568 | bytes 1771008 | tf_op jit(solution)/shard_map/dot_general | solution.py:67
  16.0 7.3 %all-to-all-start = ((bf16[8,96,768]{2,1,0:T(8,128)(2,1)}), bf16[8,96,768]{2,1,0:T(8,128)(2,1)}, u32[]{:S(2)}, u32[]{:S(2)}) async-start(bf16[8,96,768]{2,1,0:T(8,128)(2,1)} %bitcast.28), calls=%async_computation | async-start | bytes 2359296 | tf_op jit(solution)/shard_map/all_to_all | solution.py:69
  23.2 1.0 slice.66
  24.2 1.6 %collective-permute-start.1 = (bf16[384,384]{1,0:T(8,128)(2,1)S(1)}, bf16[384,384]{1,0:T(8,128)(2,1)S(1)}, u32[]{:S(2)}, u32[]{:S(2)}) collective-permute-start(bf16[384,384]{1,0:T(8,128)(2,1)S(1)} %slice.66), channel_id=1, source_target_pairs={{0,2},{2,0},{1,3},{3,1},{4,6},{6,4},{5,7},{7,5},{8,10},{10,8},{9,1... | collective-permute-start | bytes 884744 | tf_op jit(solution)/shard_map/ppermute | solution.py:77
  26.3 1.5 %convolution_convert_fusion.2 = bf16[768,384]{1,0:T(8,128)(2,1)S(1)} fusion(s32[384]{0:T(512)S(1)} %convert_add_fusion, bf16[384,1024]{1,0:T(8,128)(2,1)} %copy-done.1), kind=kOutput, calls=%fused_computation.12 | convolution fusion | flops 227082240 | bytes 886272 | tf_op jit(solution)/shard_map/dot_general | solution.py:84
  27.8 5.0 %collective-permute-done = s32[384]{0:T(512)S(1)} collective-permute-done((s32[384]{0:T(512)S(1)}, s32[384]{0:T(512)S(1)}, u32[]{:S(2)}, u32[]{:S(2)}) %collective-permute-start) | collective-permute-done | bytes 1568 | tf_op jit(solution)/shard_map/ppermute | solution.py:78
  33.3 1.1 %pad_maximum_fusion = bf16[8,192,384]{2,1,0:T(8,128)(2,1)} fusion(bf16[8,96,384]{2,1,0:T(8,128)(2,1)S(1)} %bitcast.30, bf16[8,96,384]{2,1,0:T(8,128)(2,1)S(1)} %bitcast.29), kind=kLoop, calls=%fused_computation.13 | loop fusion | flops 2359296 | bytes 2359296 | tf_op jit(solution)/shard_map/concatenate | solution.py:86
  34.4 17.5 %all-to-all-done = bf16[8,96,768]{2,1,0:T(8,128)(2,1)} async-done(((bf16[8,96,768]{2,1,0:T(8,128)(2,1)}), bf16[8,96,768]{2,1,0:T(8,128)(2,1)}, u32[]{:S(2)}, u32[]{:S(2)}) %all-to-all-start) | async-done | bytes 1179680 | tf_op jit(solution)/shard_map/all_to_all | solution.py:69
  51.9 4.4 %all-to-all-start.1 = ((bf16[8,192,384]{2,1,0:T(8,128)(2,1)}), bf16[8,192,384]{2,1,0:T(8,128)(2,1)}, u32[]{:S(2)}, u32[]{:S(2)}) async-start(bf16[8,192,384]{2,1,0:T(8,128)(2,1)} %pad_maximum_fusion), calls=%async_computation.1 | async-start | bytes 2359296 | tf_op jit(solution)/shard_map/all_to_all | solution.py:89
  56.4 2.2 %slice.65 = bf16[768,640]{1,0:T(8,128)(2,1)} slice(bf16[768,768]{1,0:T(8,128)(2,1)} %bitcast.1), slice={[0:768], [0:640]} | slice | bytes 1966080 | tf_op jit(solution)/shard_map/slice | solution.py:31
  58.6 1.8 %convert_reduce_fusion = (f32[768]{0:T(1024)S(1)}, f32[768]{0:T(1024)S(1)}) fusion(bf16[768,768]{1,0:T(8,128)(2,1)} %bitcast.1), kind=kLoop, calls=%fused_computation.23 | loop fusion | flops 6144 | bytes 12288 | tf_op jit(solution)/shard_map/eq | solution.py:106
  60.5 1.6 %collective-permute-start.2 = (f32[2,768]{1,0:T(2,128)S(1)}, f32[2,768]{1,0:T(2,128)S(1)}, u32[]{:S(2)}, u32[]{:S(2)}) collective-permute-start(f32[2,768]{1,0:T(2,128)S(1)} %pad_maximum_fusion.1), channel_id=1, source_target_pairs={{0,2},{1,3},{2,0},{3,1},{4,6},{5,7},{6,4},{7,5},{8,10},{9,11},{10,... | collective-permute-start | bytes 18440 | tf_op jit(solution)/shard_map/ppermute | solution.py:21
  62.8 4.2 %and_select_fusion.3 = f32[768,768]{1,0:T(8,128)} fusion(f32[768]{0:T(1024)S(1)} %get-tuple-element.6, f32[768]{0:T(1024)S(1)} %get-tuple-element.5, pred[768]{0:T(1024)(128)(4,1)S(1)} %broadcast_compare_fusion, bf16[768,768]{1,0:T(8,128)(2,1)} %bitcast.1), kind=kOutput, calls=%fused_computation.7 | convolution fusion | flops 757923840 | bytes 3359744 | tf_op jit(solution)/shard_map/qe,ke->qk/dot_general | solution.py:103
  67.4 0.8 collective-permute-done.7
  68.2 16.4 %all-to-all-done.1 = bf16[8,192,384]{2,1,0:T(8,128)(2,1)} async-done(((bf16[8,192,384]{2,1,0:T(8,128)(2,1)}), bf16[8,192,384]{2,1,0:T(8,128)(2,1)}, u32[]{:S(2)}, u32[]{:S(2)}) %all-to-all-start.1) | async-done | bytes 1179680 | tf_op jit(solution)/shard_map/all_to_all | solution.py:89
  84.6 1.4 %fusion.27 = (bf16[8,96,384]{2,1,0:T(8,128)(2,1)S(1)}, bf16[8,96,384]{2,1,0:T(8,128)(2,1)S(1)}) fusion(bf16[8,192,384]{2,1,0:T(8,128)(2,1)} %all-to-all-done.1), kind=kLoop, calls=%fused_computation.71 | loop fusion | bytes 2359296 | tf_op jit(solution)/shard_map/slice | solution.py:91
  86.6 0.8 fusion.29
  87.4 0.8 fusion.28
  88.2 0.8 fusion.31
  89.0 0.8 fusion.30
  89.9 2.8 %and_select_fusion.1 = f32[768,768]{1,0:T(8,128)S(1)} fusion(f32[768]{0:T(1024)S(1)} %get-tuple-element.10, f32[768]{0:T(1024)S(1)} %get-tuple-element.9, pred[768]{0:T(1024)(128)(4,1)S(1)} %compare_reduce_fusion.1, f32[768]{0:T(1024)S(1)} %get-tuple-element.6, f32[768]{0:T(1024)S(1)} %get-tuple-element.5, bf16[768,640]{1,0:T(8,128)(2,1)} %collective-permute-done.5, ...), kind=kOutput, calls=%fused_computation.5 | convolution fusion | flops 757923840 | bytes 4338432 | tf_op jit(solution)/shard_map/qe,ke->qk/dot_general | solution.py:103
  92.8 3.0 %and_select_fusion.2 = f32[768,768]{1,0:T(8,128)S(1)} fusion(f32[768]{0:T(1024)S(1)} %get-tuple-element.8, f32[768]{0:T(1024)S(1)} %get-tuple-element.7, pred[768]{0:T(1024)(128)(4,1)S(1)} %compare_reduce_fusion.2, f32[768]{0:T(1024)S(1)} %get-tuple-element.6, f32[768]{0:T(1024)S(1)} %get-tuple-element.5, bf16[768,640]{1,0:T(8,128)(2,1)} %collective-permute-done.3, ...), kind=kOutput, calls=%fused_computation.6 | convolution fusion | flops 757923840 | bytes 4338432 | tf_op jit(solution)/shard_map/qe,ke->qk/dot_general | solution.py:103
  96.2 2.5 %and_select_fusion = f32[768,768]{1,0:T(8,128)S(1)} fusion(f32[768]{0:T(1024)S(1)} %get-tuple-element.12, f32[768]{0:T(1024)S(1)} %get-tuple-element.11, pred[768]{0:T(1024)(128)(4,1)S(1)} %compare_reduce_fusion, f32[768]{0:T(1024)S(1)} %get-tuple-element.6, f32[768]{0:T(1024)S(1)} %get-tuple-element.5, bf16[768,640]{1,0:T(8,128)(2,1)S(1)} %collective-permute-done.8, ...), kind=kOutput, calls=%fused_computation.4 | convolution fusion | flops 757923840 | bytes 4338432 | tf_op jit(solution)/shard_map/qe,ke->qk/dot_general | solution.py:103
  99.3 9.6 %all_to_all.16 = f32[8,1,96]{2,1,0:T(1,128)S(1)} all-to-all(f32[8,1,96]{2,1,0:T(1,128)S(1)} %max.41), channel_id=1, replica_groups=mesh['grp'=8,'split'=4] {'grp'}, dimensions={0} | all-to-all | bytes 6144 | tf_op jit(solution)/shard_map/all_to_all | solution.py:119
  109.5 0.7 reduce.27
  110.2 0.8 select_reduce_fusion
  (54 shorter events, 5.4 us)
Async XLA Ops:
  0.0 1.9 %copy-start = (bf16[384,4096]{1,0:T(8,128)(2,1)S(1)}, bf16[384,4096]{1,0:T(8,128)(2,1)}, u32[]{:S(2)}) copy-start(bf16[384,4096]{1,0:T(8,128)(2,1)} %param.5) | copy-start | bytes 9437188
  7.8 2.0 %copy-start.4 = (s32[384]{0:T(512)S(1)}, s32[384]{0:T(512)}, u32[]{:S(2)}) copy-start(s32[384]{0:T(512)} %param.7) | copy-start | bytes 4612
  7.8 2.1 %copy-start.3 = (s32[384]{0:T(512)S(1)}, s32[384]{0:T(512)}, u32[]{:S(2)}) copy-start(s32[384]{0:T(512)} %param.8) | copy-start | bytes 4612
  7.9 2.2 %copy-start.5 = (s32[384]{0:T(512)S(1)}, s32[384]{0:T(512)}, u32[]{:S(2)}) copy-start(s32[384]{0:T(512)} %param.9) | copy-start | bytes 4612
  8.0 0.9 copy-start.1
  16.0 35.9 %all-to-all-start = ((bf16[8,96,768]{2,1,0:T(8,128)(2,1)}), bf16[8,96,768]{2,1,0:T(8,128)(2,1)}, u32[]{:S(2)}, u32[]{:S(2)}) async-start(bf16[8,96,768]{2,1,0:T(8,128)(2,1)} %bitcast.28), calls=%async_computation | async-start | bytes 2359296 | tf_op jit(solution)/shard_map/all_to_all | solution.py:69
  24.2 8.6 %collective-permute-start.1 = (bf16[384,384]{1,0:T(8,128)(2,1)S(1)}, bf16[384,384]{1,0:T(8,128)(2,1)S(1)}, u32[]{:S(2)}, u32[]{:S(2)}) collective-permute-start(bf16[384,384]{1,0:T(8,128)(2,1)S(1)} %slice.66), channel_id=1, source_target_pairs={{0,2},{2,0},{1,3},{3,1},{4,6},{6,4},{5,7},{7,5},{8,10},{10,8},{9,1... | collective-permute-start | bytes 884744 | tf_op jit(solution)/shard_map/ppermute | solution.py:77
  25.8 7.0 %collective-permute-start = (s32[384]{0:T(512)S(1)}, s32[384]{0:T(512)S(1)}, u32[]{:S(2)}, u32[]{:S(2)}) collective-permute-start(s32[384]{0:T(512)S(1)} %convert_add_fusion), channel_id=1, source_target_pairs={{0,2},{2,0},{1,3},{3,1},{4,6},{6,4},{5,7},{7,5},{8,10},{10,8},{9,1... | collective-permute-start | bytes 4616 | tf_op jit(solution)/shard_map/ppermute | solution.py:78
  51.9 32.7 %all-to-all-start.1 = ((bf16[8,192,384]{2,1,0:T(8,128)(2,1)}), bf16[8,192,384]{2,1,0:T(8,128)(2,1)}, u32[]{:S(2)}, u32[]{:S(2)}) async-start(bf16[8,192,384]{2,1,0:T(8,128)(2,1)} %pad_maximum_fusion), calls=%async_computation.1 | async-start | bytes 2359296 | tf_op jit(solution)/shard_map/all_to_all | solution.py:89
  60.5 6.5 %collective-permute-start.2 = (f32[2,768]{1,0:T(2,128)S(1)}, f32[2,768]{1,0:T(2,128)S(1)}, u32[]{:S(2)}, u32[]{:S(2)}) collective-permute-start(f32[2,768]{1,0:T(2,128)S(1)} %pad_maximum_fusion.1), channel_id=1, source_target_pairs={{0,2},{1,3},{2,0},{3,1},{4,6},{5,7},{6,4},{7,5},{8,10},{9,11},{10,... | collective-permute-start | bytes 18440 | tf_op jit(solution)/shard_map/ppermute | solution.py:21
  62.0 5.2 %collective-permute-start.4 = (f32[2,768]{1,0:T(2,128)S(1)}, f32[2,768]{1,0:T(2,128)S(1)}, u32[]{:S(2)}, u32[]{:S(2)}) collective-permute-start(f32[2,768]{1,0:T(2,128)S(1)} %pad_maximum_fusion.1), channel_id=1, source_target_pairs={{0,1},{1,0},{2,3},{3,2},{4,5},{5,4},{6,7},{7,6},{8,9},{9,8},{10,11... | collective-permute-start | bytes 18440 | tf_op jit(solution)/shard_map/ppermute | solution.py:23
  62.0 27.7 %collective-permute-start.3 = (bf16[768,640]{1,0:T(8,128)(2,1)}, bf16[768,640]{1,0:T(8,128)(2,1)}, u32[]{:S(2)}, u32[]{:S(2)}) collective-permute-start(bf16[768,640]{1,0:T(8,128)(2,1)} %slice.65), channel_id=1, source_target_pairs={{0,2},{1,3},{2,0},{3,1},{4,6},{5,7},{6,4},{7,5},{8,10},{9,11},{10,... | collective-permute-start | bytes 2949128 | tf_op jit(solution)/shard_map/ppermute | solution.py:21
  62.5 27.4 %collective-permute-start.5 = (bf16[768,640]{1,0:T(8,128)(2,1)}, bf16[768,640]{1,0:T(8,128)(2,1)}, u32[]{:S(2)}, u32[]{:S(2)}) collective-permute-start(bf16[768,640]{1,0:T(8,128)(2,1)} %slice.65), channel_id=1, source_target_pairs={{0,1},{1,0},{2,3},{3,2},{4,5},{5,4},{6,7},{7,6},{8,9},{9,8},{10,11... | collective-permute-start | bytes 2949128 | tf_op jit(solution)/shard_map/ppermute | solution.py:23
  67.0 1.2 %collective-permute-start.7 = (f32[2,768]{1,0:T(2,128)S(1)}, f32[2,768]{1,0:T(2,128)S(1)}, u32[]{:S(2)}, u32[]{:S(2)}) collective-permute-start(f32[2,768]{1,0:T(2,128)S(1)} %collective-permute-done.2), channel_id=1, source_target_pairs={{0,1},{1,0},{2,3},{3,2},{4,5},{5,4},{6,7},{7,6},{8,9},{9,8},{10,11... | collective-permute-start | bytes 18440 | tf_op jit(solution)/shard_map/ppermute | solution.py:23
  86.0 2.2 %collective-permute-start.9 = (bf16[768,384]{1,0:T(8,128)(2,1)S(1)}, bf16[768,384]{1,0:T(8,128)(2,1)S(1)}, u32[]{:S(2)}, u32[]{:S(2)}) collective-permute-start(bf16[768,384]{1,0:T(8,128)(2,1)S(1)} %bitcast.26), channel_id=1, source_target_pairs={{0,1},{1,0},{2,3},{3,2},{4,5},{5,4},{6,7},{7,6},{8,9},{9,8},{10,11... | collective-permute-start | bytes 1769480 | tf_op jit(solution)/shard_map/ppermute | solution.py:92
  86.1 2.9 %collective-permute-start.6 = (bf16[768,384]{1,0:T(8,128)(2,1)S(1)}, bf16[768,384]{1,0:T(8,128)(2,1)S(1)}, u32[]{:S(2)}, u32[]{:S(2)}) collective-permute-start(bf16[768,384]{1,0:T(8,128)(2,1)S(1)} %bitcast.21), channel_id=1, source_target_pairs={{0,1},{1,0},{2,3},{3,2},{4,5},{5,4},{6,7},{7,6},{8,9},{9,8},{10,11... | collective-permute-start | bytes 1769480 | tf_op jit(solution)/shard_map/ppermute | solution.py:92
  89.8 6.4 %collective-permute-start.8 = (bf16[768,640]{1,0:T(8,128)(2,1)}, bf16[768,640]{1,0:T(8,128)(2,1)S(1)}, u32[]{:S(2)}, u32[]{:S(2)}) collective-permute-start(bf16[768,640]{1,0:T(8,128)(2,1)} %collective-permute-done.3), channel_id=1, source_target_pairs={{0,1},{1,0},{2,3},{3,2},{4,5},{5,4},{6,7},{7,6},{8,9},{9,8},{10,11... | collective-permute-start | bytes 2949128 | tf_op jit(solution)/shard_map/ppermute | solution.py:23
  92.7 3.0 %copy-start.2 = (f32[768,768]{1,0:T(8,128)S(1)}, f32[768,768]{1,0:T(8,128)}, u32[]{:S(2)}) copy-start(f32[768,768]{1,0:T(8,128)} %and_select_fusion.3) | copy-start | bytes 7077892

commit v10 on v9

--- a/solution.py
+++ b/solution.py
@@ -70,7 +70,7 @@
         return got.reshape(n_slot, -1)
 
     if n_split == 4:
-        half = emb_w - 3 * emb_w // 8
+        half = emb_w // 2
         cross = [(0, 2), (2, 0), (1, 3), (3, 1)]
         pair = [(0, 1), (1, 0), (2, 3), (3, 2)]
         raw_b = embeds[:, half:]
@@ -103,12 +103,16 @@
         s = jnp.einsum("qe,ke->qk", q, k, preferred_element_type=jnp.float32)
         return jnp.where(hits, s, -jnp.inf)
 
-    own_hits = (q_lab[:, None] == q_lab[None, :]) & (q_lab[None, :] > 0) & (q_ord[None, :] < q_ord[:, None])
-    parts = [lax.optimization_barrier(part(q_emb, q_emb, own_hits))]
+    q_base = q_lab * 1048576.0
+    q_code = q_base + q_ord
+
+    def hits_of(k_lab, k_ord):
+        k_code = k_lab * 1048576.0 + k_ord
+        return (k_code[None, :] >= q_base[:, None]) & (k_code[None, :] < q_code[:, None])
+
+    parts = [lax.optimization_barrier(part(q_emb, q_emb, hits_of(q_lab, q_ord)))]
     for k_a, k_m in zip(keys_a, keys_m):
-        k_lab, k_ord = k_m[0], k_m[1]
-        hits = (q_lab[:, None] == k_lab[None, :]) & (k_lab[None, :] > 0) & (k_ord[None, :] < q_ord[:, None])
-        parts.append(lax.optimization_barrier(part(q_emb, k_a, hits)))
+        parts.append(lax.optimization_barrier(part(q_emb, k_a, hits_of(k_m[0], k_m[1]))))
     best = jnp.full((n_slot,), -1.0, jnp.float32)
     for masked, k_b in zip(parts, [got_b] + list(keys_b)):
         second = lax.optimization_barrier(

time: 112 us -> 114 us (1.018)
  other arithmetic: 5.64 us -> 8.3 us
    ppermute x2, waiting for transfers between devices: 0.01 us -> 10.6 us  [gather_split(): cross = lax.ppermute(rows, 'split', [(0, 2), (1, 3), (2, 0), (3, 1)])]
    all_to_all x1, waiting for transfers between devices: 16.4 us -> 8.24 us  [local(): got = lax.all_to_all(send, 'grp', split_axis=0, concat_axis=0, tiled=True)]
    all_to_all x1, waiting for transfers between devices: 17.5 us -> 11.9 us  [route(): got = lax.all_to_all(send, 'grp', split_axis=0, concat_axis=0, tiled=True)]
    another operation x4, local copies, waits for them, and re-layouts: 0.46 us -> 3 us  [local(): jnp.stack([label, block.astype(jnp.float32), (order // 256).astype(jnp.fl...]
    another operation x3, other arithmetic: 0.03 us -> 2.35 us
    ppermute x1, waiting for transfers between devices: 5.02 us -> 7.01 us  [local(): par_place = lax.ppermute(place, 'split', cross)]
    mul x0 -> x1, other arithmetic: none -> 1.94 us  [hits_of(): k_code = k_lab * 1048576.0 + k_ord]
    eq x1 -> x0, other arithmetic: 1.81 us -> none  [local(): q_lab[:, None] == q_lab[None, :]]
  transfers between devices with their start and end apart: 12 -> 12, of which waited for: 4 -> 5; matrix products, arithmetic and copies ran while one was open for 21% -> 21% of each run, Pallas kernels for 0% -> 0%
where the time goes in v10:
time: 114 us
  waiting for transfers between devices  38.8 us (34%)
  matrix products  27.2 us (24%)
  starting transfers between devices  16.9 us (15%)
  local copies, waits for them, and re-layouts  12.4 us (11%)
  blocking collectives  9.86 us (9%)
  other arithmetic  8.3 us (7%)
    dot_general x4, matrix products, part(): s = jnp.einsum('qe,ke->qk', q, k, preferred_element_type=jnp.float32)  12.8 us
    all_to_all x1, waiting for transfers between devices, route(): got = lax.all_to_all(send, 'grp', split_axis=0, concat_axis=0, tiled=True)  11.9 us
    ppermute x2, waiting for transfers between devices, gather_split(): cross = lax.ppermute(rows, 'split', [(0, 2), (1, 3), (2, 0), (3, 1)])  10.6 us
    all_to_all x1, blocking collectives, local(): lax.all_to_all(best.reshape(n_grp, cap), 'grp', split_axis=0, concat_axis...  9.86 us
    all_to_all x1, waiting for transfers between devices, local(): got = lax.all_to_all(send, 'grp', split_axis=0, concat_axis=0, tiled=True)  8.24 us
    all_to_all x1, starting transfers between devices, route(): got = lax.all_to_all(send, 'grp', split_axis=0, concat_axis=0, tiled=True)  7.25 us
    ppermute x1, waiting for transfers between devices, local(): par_place = lax.ppermute(place, 'split', cross)  7.01 us
    dot_general x1, matrix products, embed_rows(): jnp.einsum('...h,he->...e', rows, weight, preferred_element_type=jnp.floa...  5.94 us
  transfers between devices with their start and end apart: 12, of which 5 were waited for; matrix products, arithmetic and copies ran while one was open for 21% of the time, Pallas kernels for 0%

profile of v10, /device:TPU:0, one launch (start us, length us, event | category | flops | bytes accessed | tf_op | source)
XLA Modules:
  0.0 113.7 jit_solution(12178678773934762618)
XLA Ops:
  0.0 0.8 convert_convert_fusion
  0.8 0.8 fusion.17
  5.6 5.9 %multiply_reduce_fusion = (f32[384]{0:T(512)S(1)}, f32[384,1024]{1,0:T(8,128)S(1)}) fusion(bf16[384,4096]{1,0:T(8,128)(2,1)S(1)} %copy-done, bf16[4096,1024]{1,0:T(8,128)(2,1)} %param.6), kind=kOutput, calls=%fused_computation.10 | convolution fusion | flops 3222011392 | bytes 13108736 | tf_op jit(solution)/shard_map/...h,he->...e/dot_general | solution.py:14
  11.7 0.9 copy-done.1
  14.0 1.9 %concatenate.10 = bf16[384,640]{1,0:T(8,128)(2,1)} concatenate(bf16[384,512]{1,0:T(8,128)(2,1)S(1)} %get-tuple-element.14, bf16[384,1]{1,0:T(8,128)(2,1)} %stack.26, bf16[384,1]{1,0:T(8,128)(2,1)} %stack.27, bf16[384,1]{1,0:T(8,128)(2,1)} %stack.28, bf16[384,1]{1,0:T(8,128)(2,1)} %stack.29, bf16[384,124]{1,0:T(8,128)(2,1)} %broadcast_in_dim.21), dimensions={1} | concatenate | bytes 983040 | tf_op jit(solution)/shard_map/concatenate | solution.py:79
  15.9 2.8 %convolution_convert_fusion = bf16[768,640]{1,0:T(8,128)(2,1)} fusion(bf16[384,640]{1,0:T(8,128)(2,1)} %concatenate.10, s32[384]{0:T(512)S(1)} %convert_add_fusion.1), kind=kOutput, calls=%fused_computation.11 | convolution fusion | flops 378273792 | bytes 1476096 | tf_op jit(solution)/shard_map/dot_general | solution.py:67
  18.7 7.3 %all-to-all-start = ((bf16[8,96,640]{2,1,0:T(8,128)(2,1)}), bf16[8,96,640]{2,1,0:T(8,128)(2,1)}, u32[]{:S(2)}, u32[]{:S(2)}) async-start(bf16[8,96,640]{2,1,0:T(8,128)(2,1)} %bitcast.28), calls=%async_computation | async-start | bytes 1966080 | tf_op jit(solution)/shard_map/all_to_all | solution.py:69
  26.0 1.6 %collective-permute-start.1 = (bf16[384,512]{1,0:T(8,128)(2,1)S(1)}, bf16[384,512]{1,0:T(8,128)(2,1)S(1)}, u32[]{:S(2)}, u32[]{:S(2)}) collective-permute-start(bf16[384,512]{1,0:T(8,128)(2,1)S(1)} %copy-done.5), channel_id=1, source_target_pairs={{0,2},{2,0},{1,3},{3,1},{4,6},{6,4},{5,7},{7,5},{8,10},{10,8},{9,1... | collective-permute-start | bytes 1179656 | tf_op jit(solution)/shard_map/ppermute | solution.py:77
  28.1 1.6 %convolution_convert_fusion.2 = bf16[768,512]{1,0:T(8,128)(2,1)S(1)} fusion(s32[384]{0:T(512)S(1)} %convert_add_fusion.1, bf16[384,1024]{1,0:T(8,128)(2,1)} %copy-done.1), kind=kOutput, calls=%fused_computation.13 | convolution fusion | flops 302678016 | bytes 1181184 | tf_op jit(solution)/shard_map/dot_general | solution.py:84
  29.6 7.0 %collective-permute-done = s32[384]{0:T(512)S(1)} collective-permute-done((s32[384]{0:T(512)S(1)}, s32[384]{0:T(512)S(1)}, u32[]{:S(2)}, u32[]{:S(2)}) %collective-permute-start) | collective-permute-done | bytes 1568 | tf_op jit(solution)/shard_map/ppermute | solution.py:78
  37.2 1.4 %pad_maximum_fusion = bf16[8,192,512]{2,1,0:T(8,128)(2,1)} fusion(bf16[8,96,512]{2,1,0:T(8,128)(2,1)S(1)} %bitcast.30, bf16[8,96,512]{2,1,0:T(8,128)(2,1)S(1)} %bitcast.29), kind=kLoop, calls=%fused_computation.8 | loop fusion | flops 3145728 | bytes 3145728 | tf_op jit(solution)/shard_map/concatenate | solution.py:86
  38.6 11.9 %all-to-all-done = bf16[8,96,640]{2,1,0:T(8,128)(2,1)} async-done(((bf16[8,96,640]{2,1,0:T(8,128)(2,1)}), bf16[8,96,640]{2,1,0:T(8,128)(2,1)}, u32[]{:S(2)}, u32[]{:S(2)}) %all-to-all-start) | async-done | bytes 983072 | tf_op jit(solution)/shard_map/all_to_all | solution.py:69
  50.5 4.3 %all-to-all-start.1 = ((bf16[8,192,512]{2,1,0:T(8,128)(2,1)}), bf16[8,192,512]{2,1,0:T(8,128)(2,1)}, u32[]{:S(2)}, u32[]{:S(2)}) async-start(bf16[8,192,512]{2,1,0:T(8,128)(2,1)} %pad_maximum_fusion), calls=%async_computation.1 | async-start | bytes 3145728 | tf_op jit(solution)/shard_map/all_to_all | solution.py:89
  54.8 1.2 %slice.65 = bf16[768,512]{1,0:T(8,128)(2,1)S(1)} slice(bf16[768,640]{1,0:T(8,128)(2,1)} %bitcast.1), slice={[0:768], [0:512]} | slice | bytes 1572864 | tf_op jit(solution)/shard_map/slice | solution.py:31
  56.0 1.9 %fusion.5 = (f32[768]{0:T(1024)S(1)}, f32[768]{0:T(1024)S(1)}, f32[768]{0:T(1024)S(1)}, f32[768]{0:T(1024)S(1)}) fusion(bf16[768,640]{1,0:T(8,128)(2,1)} %bitcast.1), kind=kLoop, calls=%fused_computation.26 | loop fusion | flops 7680 | bytes 18432 | tf_op jit(solution)/shard_map/mul | solution.py:110
  58.6 1.5 %collective-permute-start.2 = (f32[2,768]{1,0:T(2,128)S(1)}, f32[2,768]{1,0:T(2,128)S(1)}, u32[]{:S(2)}, u32[]{:S(2)}) collective-permute-start(f32[2,768]{1,0:T(2,128)S(1)} %pad_maximum_fusion.1), channel_id=1, source_target_pairs={{0,2},{1,3},{2,0},{3,1},{4,6},{5,7},{6,4},{7,5},{8,10},{9,11},{10,... | collective-permute-start | bytes 18440 | tf_op jit(solution)/shard_map/ppermute | solution.py:21
  60.6 3.6 %and_select_fusion.3 = f32[768,768]{1,0:T(8,128)} fusion(f32[768]{0:T(1024)S(1)} %add.105, f32[768]{0:T(1024)S(1)} %get-tuple-element.8, f32[768]{0:T(1024)S(1)} %get-tuple-element.5, bf16[768,640]{1,0:T(8,128)(2,1)} %bitcast.1), kind=kOutput, calls=%fused_computation.7 | convolution fusion | flops 606339072 | bytes 3154944 | tf_op jit(solution)/shard_map/qe,ke->qk/dot_general | solution.py:103
  64.3 1.1 collective-permute-done.7
  65.5 3.4 %and_select_fusion.1 = f32[768,768]{1,0:T(8,128)} fusion(bf16[768,512]{1,0:T(8,128)(2,1)S(1)} %collective-permute-done.5, f32[768]{0:T(1024)S(1)} %fusion.11, f32[768]{0:T(1024)S(1)} %get-tuple-element.8, f32[768]{0:T(1024)S(1)} %get-tuple-element.5, bf16[768,640]{1,0:T(8,128)(2,1)} %bitcast.1), kind=kOutput, calls=%fused_computation.5 | convolution fusion | flops 606339072 | bytes 3941376 | tf_op jit(solution)/shard_map/qe,ke->qk/dot_general | solution.py:103
  68.9 10.6 %collective-permute-done.3 = bf16[768,512]{1,0:T(8,128)(2,1)} collective-permute-done((bf16[768,512]{1,0:T(8,128)(2,1)S(1)}, bf16[768,512]{1,0:T(8,128)(2,1)}, u32[]{:S(2)}, u32[]{:S(2)}) %collective-permute-start.3) | collective-permute-done | bytes 786464 | tf_op jit(solution)/shard_map/ppermute | solution.py:21
  79.5 3.6 %and_select_fusion.2 = f32[768,768]{1,0:T(8,128)} fusion(bf16[768,512]{1,0:T(8,128)(2,1)} %collective-permute-done.3, f32[768]{0:T(1024)S(1)} %fusion.12, f32[768]{0:T(1024)S(1)} %get-tuple-element.8, f32[768]{0:T(1024)S(1)} %get-tuple-element.5, bf16[768,640]{1,0:T(8,128)(2,1)} %bitcast.1), kind=kOutput, calls=%fused_computation.6 | convolution fusion | flops 606339072 | bytes 3941376 | tf_op jit(solution)/shard_map/qe,ke->qk/dot_general | solution.py:103
  83.1 8.2 %all-to-all-done.1 = bf16[8,192,512]{2,1,0:T(8,128)(2,1)} async-done(((bf16[8,192,512]{2,1,0:T(8,128)(2,1)}), bf16[8,192,512]{2,1,0:T(8,128)(2,1)}, u32[]{:S(2)}, u32[]{:S(2)}) %all-to-all-start.1) | async-done | bytes 1572896 | tf_op jit(solution)/shard_map/all_to_all | solution.py:89
  91.3 1.5 %fusion.25 = (bf16[8,96,512]{2,1,0:T(8,128)(2,1)S(1)}, bf16[8,96,512]{2,1,0:T(8,128)(2,1)S(1)}) fusion(bf16[8,192,512]{2,1,0:T(8,128)(2,1)} %all-to-all-done.1), kind=kLoop, calls=%fused_computation.72 | loop fusion | bytes 3145728 | tf_op jit(solution)/shard_map/slice | solution.py:91
  93.4 0.8 fusion.28
  94.2 0.8 fusion.27
  95.0 1.0 copy-done.3
  96.5 2.2 %and_select_fusion = f32[768,768]{1,0:T(8,128)S(1)} fusion(bf16[768,512]{1,0:T(8,128)(2,1)} %collective-permute-done.8, f32[768]{0:T(1024)S(1)} %fusion.10, f32[768]{0:T(1024)S(1)} %get-tuple-element.8, f32[768]{0:T(1024)S(1)} %get-tuple-element.5, bf16[768,640]{1,0:T(8,128)(2,1)} %bitcast.1), kind=kOutput, calls=%fused_computation.4 | convolution fusion | flops 606339072 | bytes 3941376 | tf_op jit(solution)/shard_map/qe,ke->qk/dot_general | solution.py:103
  98.7 0.8 fusion.29
  99.6 0.8 fusion.30
  100.4 0.8 copy-done.2
  101.8 9.9 %all_to_all.16 = f32[8,1,96]{2,1,0:T(1,128)S(1)} all-to-all(f32[8,1,96]{2,1,0:T(1,128)S(1)} %max.41), channel_id=1, replica_groups=mesh['grp'=8,'split'=4] {'grp'}, dimensions={0} | all-to-all | bytes 6144 | tf_op jit(solution)/shard_map/all_to_all | solution.py:123
  112.9 0.8 select_reduce_fusion
  (50 shorter events, 10.8 us)
Async XLA Ops:
  0.0 5.6 %copy-start = (bf16[384,4096]{1,0:T(8,128)(2,1)S(1)}, bf16[384,4096]{1,0:T(8,128)(2,1)}, u32[]{:S(2)}) copy-start(bf16[384,4096]{1,0:T(8,128)(2,1)} %param.5) | copy-start | bytes 9437188
  11.7 0.9 copy-start.1
  15.9 10.1 %copy-start.5 = (bf16[384,512]{1,0:T(8,128)(2,1)S(1)}, bf16[384,512]{1,0:T(8,128)(2,1)}, u32[]{:S(2)}) copy-start(bf16[384,512]{1,0:T(8,128)(2,1)} %get-tuple-element.13) | copy-start | bytes 1179652
  18.7 31.7 %all-to-all-start = ((bf16[8,96,640]{2,1,0:T(8,128)(2,1)}), bf16[8,96,640]{2,1,0:T(8,128)(2,1)}, u32[]{:S(2)}, u32[]{:S(2)}) async-start(bf16[8,96,640]{2,1,0:T(8,128)(2,1)} %bitcast.28), calls=%async_computation | async-start | bytes 1966080 | tf_op jit(solution)/shard_map/all_to_all | solution.py:69
  26.0 10.7 %collective-permute-start.1 = (bf16[384,512]{1,0:T(8,128)(2,1)S(1)}, bf16[384,512]{1,0:T(8,128)(2,1)S(1)}, u32[]{:S(2)}, u32[]{:S(2)}) collective-permute-start(bf16[384,512]{1,0:T(8,128)(2,1)S(1)} %copy-done.5), channel_id=1, source_target_pairs={{0,2},{2,0},{1,3},{3,1},{4,6},{6,4},{5,7},{7,5},{8,10},{10,8},{9,1... | collective-permute-start | bytes 1179656 | tf_op jit(solution)/shard_map/ppermute | solution.py:77
  27.6 9.1 %collective-permute-start = (s32[384]{0:T(512)S(1)}, s32[384]{0:T(512)S(1)}, u32[]{:S(2)}, u32[]{:S(2)}) collective-permute-start(s32[384]{0:T(512)S(1)} %convert_add_fusion.1), channel_id=1, source_target_pairs={{0,2},{2,0},{1,3},{3,1},{4,6},{6,4},{5,7},{7,5},{8,10},{10,8},{9,1... | collective-permute-start | bytes 4616 | tf_op jit(solution)/shard_map/ppermute | solution.py:78
  50.5 40.9 %all-to-all-start.1 = ((bf16[8,192,512]{2,1,0:T(8,128)(2,1)}), bf16[8,192,512]{2,1,0:T(8,128)(2,1)}, u32[]{:S(2)}, u32[]{:S(2)}) async-start(bf16[8,192,512]{2,1,0:T(8,128)(2,1)} %pad_maximum_fusion), calls=%async_computation.1 | async-start | bytes 3145728 | tf_op jit(solution)/shard_map/all_to_all | solution.py:89
  56.0 9.5 %collective-permute-start.5 = (bf16[768,512]{1,0:T(8,128)(2,1)S(1)}, bf16[768,512]{1,0:T(8,128)(2,1)S(1)}, u32[]{:S(2)}, u32[]{:S(2)}) collective-permute-start(bf16[768,512]{1,0:T(8,128)(2,1)S(1)} %slice.65), channel_id=1, source_target_pairs={{0,1},{1,0},{2,3},{3,2},{4,5},{5,4},{6,7},{7,6},{8,9},{9,8},{10,11... | collective-permute-start | bytes 2359304 | tf_op jit(solution)/shard_map/ppermute | solution.py:23
  58.0 6.3 %collective-permute-start.4 = (f32[2,768]{1,0:T(2,128)S(1)}, f32[2,768]{1,0:T(2,128)S(1)}, u32[]{:S(2)}, u32[]{:S(2)}) collective-permute-start(f32[2,768]{1,0:T(2,128)S(1)} %pad_maximum_fusion.1), channel_id=1, source_target_pairs={{0,1},{1,0},{2,3},{3,2},{4,5},{5,4},{6,7},{7,6},{8,9},{9,8},{10,11... | collective-permute-start | bytes 18440 | tf_op jit(solution)/shard_map/ppermute | solution.py:23
  58.6 5.6 %collective-permute-start.2 = (f32[2,768]{1,0:T(2,128)S(1)}, f32[2,768]{1,0:T(2,128)S(1)}, u32[]{:S(2)}, u32[]{:S(2)}) collective-permute-start(f32[2,768]{1,0:T(2,128)S(1)} %pad_maximum_fusion.1), channel_id=1, source_target_pairs={{0,2},{1,3},{2,0},{3,1},{4,6},{5,7},{6,4},{7,5},{8,10},{9,11},{10,... | collective-permute-start | bytes 18440 | tf_op jit(solution)/shard_map/ppermute | solution.py:21
  60.1 19.4 %collective-permute-start.3 = (bf16[768,512]{1,0:T(8,128)(2,1)S(1)}, bf16[768,512]{1,0:T(8,128)(2,1)}, u32[]{:S(2)}, u32[]{:S(2)}) collective-permute-start(bf16[768,512]{1,0:T(8,128)(2,1)S(1)} %slice.65), channel_id=1, source_target_pairs={{0,2},{1,3},{2,0},{3,1},{4,6},{5,7},{6,4},{7,5},{8,10},{9,11},{10,... | collective-permute-start | bytes 2359304 | tf_op jit(solution)/shard_map/ppermute | solution.py:21
  64.2 1.2 %collective-permute-start.7 = (f32[2,768]{1,0:T(2,128)S(1)}, f32[2,768]{1,0:T(2,128)S(1)}, u32[]{:S(2)}, u32[]{:S(2)}) collective-permute-start(f32[2,768]{1,0:T(2,128)S(1)} %collective-permute-done.2), channel_id=1, source_target_pairs={{0,1},{1,0},{2,3},{3,2},{4,5},{5,4},{6,7},{7,6},{8,9},{9,8},{10,11... | collective-permute-start | bytes 18440 | tf_op jit(solution)/shard_map/ppermute | solution.py:23
  83.1 13.4 %collective-permute-start.8 = (bf16[768,512]{1,0:T(8,128)(2,1)}, bf16[768,512]{1,0:T(8,128)(2,1)}, u32[]{:S(2)}, u32[]{:S(2)}) collective-permute-start(bf16[768,512]{1,0:T(8,128)(2,1)} %collective-permute-done.3), channel_id=1, source_target_pairs={{0,1},{1,0},{2,3},{3,2},{4,5},{5,4},{6,7},{7,6},{8,9},{9,8},{10,11... | collective-permute-start | bytes 2359304 | tf_op jit(solution)/shard_map/ppermute | solution.py:23
  92.8 6.8 %collective-permute-start.9 = (bf16[768,512]{1,0:T(8,128)(2,1)S(1)}, bf16[768,512]{1,0:T(8,128)(2,1)S(1)}, u32[]{:S(2)}, u32[]{:S(2)}) collective-permute-start(bf16[768,512]{1,0:T(8,128)(2,1)S(1)} %bitcast.26), channel_id=1, source_target_pairs={{0,1},{1,0},{2,3},{3,2},{4,5},{5,4},{6,7},{7,6},{8,9},{9,8},{10,11... | collective-permute-start | bytes 2359304 | tf_op jit(solution)/shard_map/ppermute | solution.py:92
  92.9 5.9 %collective-permute-start.6 = (bf16[768,512]{1,0:T(8,128)(2,1)S(1)}, bf16[768,512]{1,0:T(8,128)(2,1)S(1)}, u32[]{:S(2)}, u32[]{:S(2)}) collective-permute-start(bf16[768,512]{1,0:T(8,128)(2,1)S(1)} %bitcast.21), channel_id=1, source_target_pairs={{0,1},{1,0},{2,3},{3,2},{4,5},{5,4},{6,7},{7,6},{8,9},{9,8},{10,11... | collective-permute-start | bytes 2359304 | tf_op jit(solution)/shard_map/ppermute | solution.py:92
  93.4 1.7 %copy-start.4 = (f32[768,768]{1,0:T(8,128)S(1)}, f32[768,768]{1,0:T(8,128)}, u32[]{:S(2)}) copy-start(f32[768,768]{1,0:T(8,128)} %and_select_fusion.2) | copy-start | bytes 7077892
  94.2 1.8 %copy-start.3 = (f32[768,768]{1,0:T(8,128)S(1)}, f32[768,768]{1,0:T(8,128)}, u32[]{:S(2)}) copy-start(f32[768,768]{1,0:T(8,128)} %and_select_fusion.3) | copy-start | bytes 7077892
  99.6 1.7 %copy-start.2 = (f32[768,768]{1,0:T(8,128)S(1)}, f32[768,768]{1,0:T(8,128)}, u32[]{:S(2)}) copy-start(f32[768,768]{1,0:T(8,128)} %and_select_fusion.1) | copy-start | bytes 7077892

commit v11 on v6

--- a/solution.py
+++ b/solution.py
@@ -76,7 +76,13 @@
         raw_b = embeds[:, half:]
         par_b = lax.ppermute(raw_b, "split", cross)
         par_place = lax.ppermute(place, "split", cross)
-        got_a = route(jnp.concatenate([embeds[:, :half], meta], axis=1))
+        col = jnp.arange(half + META, dtype=jnp.int32)[None, :]
+        rows_a = jnp.where(
+            col < half,
+            jnp.pad(embeds[:, :half], ((0, 0), (0, META))),
+            jnp.pad(meta, ((0, 0), (half, 0))),
+        )
+        got_a = route(rows_a)
         q_emb, q_lab, q_ord = unpack(got_a, half, n_all)
         keys_a = gather_split(q_emb, n_split)
         keys_m = gather_split(jnp.stack([q_lab, q_ord]), n_split)

time: 112 us -> 111 us (level)
  local copies, waits for them, and re-layouts: 12.2 us -> 10.2 us
where the time goes in v11:
time: 111 us; the launch traced here: 110 us
  waiting for transfers between devices  40.2 us (36%)
  matrix products  26.9 us (24%)
  starting transfers between devices  16.8 us (15%)
  blocking collectives  10.3 us (9%)
  local copies, waits for them, and re-layouts  10.2 us (9%)
  other arithmetic  5.6 us (5%)
    all_to_all x1, waiting for transfers between devices, route(): got = lax.all_to_all(send, 'grp', split_axis=0, concat_axis=0, tiled=True)  17.5 us
    ppermute x2, waiting for transfers between devices, gather_split(): cross = lax.ppermute(rows, 'split', [(0, 2), (1, 3), (2, 0), (3, 1)])  14.8 us
    dot_general x4, matrix products, dots(): s = jnp.einsum('qe,ke->qk', q_emb, k_a, preferred_element_type=jnp.float32)  12.4 us
    all_to_all x1, blocking collectives, local(): lax.all_to_all(best.reshape(n_grp, cap), 'grp', split_axis=0, concat_axis...  10.3 us
    all_to_all x1, starting transfers between devices, route(): got = lax.all_to_all(send, 'grp', split_axis=0, concat_axis=0, tiled=True)  7.25 us
    dot_general x1, matrix products, embed_rows(): jnp.einsum('...h,he->...e', rows, weight, preferred_element_type=jnp.floa...  5.98 us
    ppermute x1, waiting for transfers between devices, local(): par_place = lax.ppermute(place, 'split', cross)  5.02 us
    all_to_all x1, starting transfers between devices, local(): got = lax.all_to_all(send, 'grp', split_axis=0, concat_axis=0, tiled=True)  4.45 us
  transfers between devices with their start and end apart: 12, of which 5 were waited for; matrix products, arithmetic and copies ran while one was open for 21% of the time, Pallas kernels for 0%

profile of v11, /device:TPU:0, one launch (start us, length us, event | category | flops | bytes accessed | tf_op | source)
XLA Modules:
  0.0 110.3 jit_solution(3938607834440693958)
XLA Ops:
  0.0 1.9 %copy-done = bf16[384,4096]{1,0:T(8,128)(2,1)S(1)} copy-done((bf16[384,4096]{1,0:T(8,128)(2,1)S(1)}, bf16[384,4096]{1,0:T(8,128)(2,1)}, u32[]{:S(2)}) %copy-start) | copy-done | bytes 3145752
  1.9 6.0 %multiply_reduce_fusion = (f32[384]{0:T(512)S(1)}, f32[384,1024]{1,0:T(8,128)S(1)}) fusion(bf16[384,4096]{1,0:T(8,128)(2,1)S(1)} %copy-done, bf16[4096,1024]{1,0:T(8,128)(2,1)} %param.6), kind=kOutput, calls=%fused_computation.5 | convolution fusion | flops 3222011392 | bytes 13108736 | tf_op jit(solution)/shard_map/...h,he->...e/dot_general | solution.py:14
  8.7 1.1 multiply_convert_fusion
  9.8 0.6 broadcast_in_dim.28
  10.4 1.8 %concatenate.8 = bf16[384,128]{1,0:T(8,128)(2,1)} concatenate(bf16[384,1]{1,0:T(8,128)(2,1)S(1)} %stack.26, bf16[384,1]{1,0:T(8,128)(2,1)S(1)} %stack.27, bf16[384,1]{1,0:T(8,128)(2,1)S(1)} %stack.28, bf16[384,1]{1,0:T(8,128)(2,1)S(1)} %stack.29, bf16[384,124]{1,0:T(8,128)(2,1)} %broadcast_in_dim.28), dimensions={1} | concatenate | bytes 196608 | tf_op jit(solution)/shard_map/concatenate | solution.py:61
  12.2 2.9 %convolution_convert_fusion = bf16[768,768]{1,0:T(8,128)(2,1)} fusion(bf16[384,1024]{1,0:T(8,128)(2,1)} %multiply_convert_fusion, bf16[384,128]{1,0:T(8,128)(2,1)} %concatenate.8, s32[384]{0:T(512)S(1)} %convert_add_fusion, pred[768]{0:T(1024)(128)(4,1)S(1)} %copy-done.4, pred[768]{0:T(1024)(128)(4,1)S(1)} %iota_compare_fusion.9), kind=kOutput, calls=%fused_computation.6 | convolution fusion | flops 454459392 | bytes 1870848 | tf_op jit(solution)/shard_map/dot_general | solution.py:67
  15.1 7.3 %all-to-all-start = ((bf16[8,96,768]{2,1,0:T(8,128)(2,1)}), bf16[8,96,768]{2,1,0:T(8,128)(2,1)}, u32[]{:S(2)}, u32[]{:S(2)}) async-start(bf16[8,96,768]{2,1,0:T(8,128)(2,1)} %bitcast.27), calls=%async_computation | async-start | bytes 2359296 | tf_op jit(solution)/shard_map/all_to_all | solution.py:69
  22.3 1.0 slice.67
  23.3 1.6 %collective-permute-start.1 = (bf16[384,384]{1,0:T(8,128)(2,1)S(1)}, bf16[384,384]{1,0:T(8,128)(2,1)S(1)}, u32[]{:S(2)}, u32[]{:S(2)}) collective-permute-start(bf16[384,384]{1,0:T(8,128)(2,1)S(1)} %slice.67), channel_id=1, source_target_pairs={{0,2},{2,0},{1,3},{3,1},{4,6},{6,4},{5,7},{7,5},{8,10},{10,8},{9,1... | collective-permute-start | bytes 884744 | tf_op jit(solution)/shard_map/ppermute | solution.py:77
  25.4 1.5 %convolution_convert_fusion.2 = bf16[768,384]{1,0:T(8,128)(2,1)S(1)} fusion(s32[384]{0:T(512)S(1)} %convert_add_fusion, bf16[384,1024]{1,0:T(8,128)(2,1)} %multiply_convert_fusion), kind=kOutput, calls=%fused_computation.8 | convolution fusion | flops 227082240 | bytes 886272 | tf_op jit(solution)/shard_map/dot_general | solution.py:90
  26.9 5.0 %collective-permute-done = s32[384]{0:T(512)S(1)} collective-permute-done((s32[384]{0:T(512)S(1)}, s32[384]{0:T(512)S(1)}, u32[]{:S(2)}, u32[]{:S(2)}) %collective-permute-start) | collective-permute-done | bytes 1568 | tf_op jit(solution)/shard_map/ppermute | solution.py:78
  32.4 1.1 %pad_maximum_fusion = bf16[8,192,384]{2,1,0:T(8,128)(2,1)} fusion(bf16[8,96,384]{2,1,0:T(8,128)(2,1)S(1)} %bitcast.29, bf16[8,96,384]{2,1,0:T(8,128)(2,1)S(1)} %bitcast.28), kind=kLoop, calls=%fused_computation.9 | loop fusion | flops 2359296 | bytes 2359296 | tf_op jit(solution)/shard_map/concatenate | solution.py:92
  33.5 17.5 %all-to-all-done = bf16[8,96,768]{2,1,0:T(8,128)(2,1)} async-done(((bf16[8,96,768]{2,1,0:T(8,128)(2,1)}), bf16[8,96,768]{2,1,0:T(8,128)(2,1)}, u32[]{:S(2)}, u32[]{:S(2)}) %all-to-all-start) | async-done | bytes 1179680 | tf_op jit(solution)/shard_map/all_to_all | solution.py:69
  51.0 4.4 %all-to-all-start.1 = ((bf16[8,192,384]{2,1,0:T(8,128)(2,1)}), bf16[8,192,384]{2,1,0:T(8,128)(2,1)}, u32[]{:S(2)}, u32[]{:S(2)}) async-start(bf16[8,192,384]{2,1,0:T(8,128)(2,1)} %pad_maximum_fusion), calls=%async_computation.1 | async-start | bytes 2359296 | tf_op jit(solution)/shard_map/all_to_all | solution.py:95
  55.4 2.2 %slice.66 = bf16[768,640]{1,0:T(8,128)(2,1)} slice(bf16[768,768]{1,0:T(8,128)(2,1)} %bitcast.1), slice={[0:768], [0:640]} | slice | bytes 1966080 | tf_op jit(solution)/shard_map/slice | solution.py:31
  57.7 1.5 %collective-permute-start.3 = (bf16[768,640]{1,0:T(8,128)(2,1)}, bf16[768,640]{1,0:T(8,128)(2,1)}, u32[]{:S(2)}, u32[]{:S(2)}) collective-permute-start(bf16[768,640]{1,0:T(8,128)(2,1)} %slice.66), channel_id=1, source_target_pairs={{0,2},{1,3},{2,0},{3,1},{4,6},{5,7},{6,4},{7,5},{8,10},{9,11},{10,... | collective-permute-start | bytes 2949128 | tf_op jit(solution)/shard_map/ppermute | solution.py:21
  59.2 1.8 %convert_reduce_fusion = (f32[768]{0:T(1024)S(1)}, f32[768]{0:T(1024)S(1)}) fusion(bf16[768,768]{1,0:T(8,128)(2,1)} %bitcast.1), kind=kLoop, calls=%fused_computation.24 | loop fusion | flops 6144 | bytes 12288 | tf_op jit(solution)/shard_map/eq | solution.py:113
  61.9 4.0 %fusion.24 = f32[768,768]{0,1:T(8,128)} fusion(bf16[768,768]{1,0:T(8,128)(2,1)} %bitcast.1), kind=kOutput, calls=%fused_computation.71 | convolution fusion | flops 754974720 | bytes 3342336 | tf_op jit(solution)/shard_map/qe,ke->qk/dot_general | solution.py:109
  65.9 14.8 %collective-permute-done.2 = f32[2,768]{1,0:T(2,128)S(1)} collective-permute-done((f32[2,768]{1,0:T(2,128)S(1)}, f32[2,768]{1,0:T(2,128)S(1)}, u32[]{:S(2)}, u32[]{:S(2)}) %collective-permute-start.2) | collective-permute-done | bytes 6176 | tf_op jit(solution)/shard_map/ppermute | solution.py:21
  80.8 1.1 collective-permute-done.7
  81.9 1.8 %all-to-all-done.1 = bf16[8,192,384]{2,1,0:T(8,128)(2,1)} async-done(((bf16[8,192,384]{2,1,0:T(8,128)(2,1)}), bf16[8,192,384]{2,1,0:T(8,128)(2,1)}, u32[]{:S(2)}, u32[]{:S(2)}) %all-to-all-start.1) | async-done | bytes 1179680 | tf_op jit(solution)/shard_map/all_to_all | solution.py:95
  83.7 1.5 %fusion.26 = (bf16[8,96,384]{2,1,0:T(8,128)(2,1)S(1)}, bf16[8,96,384]{2,1,0:T(8,128)(2,1)S(1)}) fusion(bf16[8,192,384]{2,1,0:T(8,128)(2,1)} %all-to-all-done.1), kind=kLoop, calls=%fused_computation.73 | loop fusion | bytes 2359296 | tf_op jit(solution)/shard_map/slice | solution.py:97
  85.8 1.1 select_reduce_fusion.3
  86.9 0.8 fusion.27
  87.7 0.8 fusion.29
  88.7 0.8 fusion.28
  89.5 2.9 %select_reduce_fusion.2 = f32[768]{0:T(1024)S(1)} fusion(f32[768,768]{0,1:T(8,128)S(1)} %fusion.27, bf16[768,640]{1,0:T(8,128)(2,1)} %collective-permute-done.3, f32[768]{0:T(1024)S(1)} %get-tuple-element.6, f32[768]{0:T(1024)S(1)} %get-tuple-element.5, f32[768]{0:T(1024)S(1)} %get-tuple-element.8, f32[768]{0:T(1024)S(1)} %get-tuple-element.7, ...), kind=kOutput, calls=%fused_computation.2 | convolution fusion | flops 759102720 | bytes 4341504 | tf_op jit(solution)/shard_map/qe,ke->qk/dot_general | solution.py:109
  92.4 2.9 %select_reduce_fusion.1 = f32[768]{0:T(1024)S(1)} fusion(f32[768,768]{0,1:T(8,128)S(1)} %fusion.28, bf16[768,640]{1,0:T(8,128)(2,1)} %collective-permute-done.5, f32[768]{0:T(1024)S(1)} %get-tuple-element.6, f32[768]{0:T(1024)S(1)} %get-tuple-element.5, f32[768]{0:T(1024)S(1)} %get-tuple-element.10, f32[768]{0:T(1024)S(1)} %get-tuple-element.9, ...), kind=kOutput, calls=%fused_computation.1 | convolution fusion | flops 759102720 | bytes 4341504 | tf_op jit(solution)/shard_map/qe,ke->qk/dot_general | solution.py:109
  95.3 2.6 %select_reduce_fusion = f32[768]{0:T(1024)S(1)} fusion(f32[768,768]{0,1:T(8,128)S(1)} %fusion.29, bf16[768,640]{1,0:T(8,128)(2,1)S(1)} %collective-permute-done.8, f32[768]{0:T(1024)S(1)} %get-tuple-element.6, f32[768]{0:T(1024)S(1)} %get-tuple-element.5, f32[768]{0:T(1024)S(1)} %get-tuple-element.12, f32[768]{0:T(1024)S(1)} %get-tuple-element.11, ...), kind=kOutput, calls=%fused_computation | convolution fusion | flops 759102720 | bytes 4341504 | tf_op jit(solution)/shard_map/qe,ke->qk/dot_general | solution.py:109
  98.0 10.3 %all_to_all.16 = f32[8,1,96]{2,1,0:T(1,128)S(1)} all-to-all(f32[8,1,96]{2,1,0:T(1,128)S(1)} %max.41), channel_id=1, replica_groups=mesh['grp'=8,'split'=4] {'grp'}, dimensions={0} | all-to-all | bytes 6144 | tf_op jit(solution)/shard_map/all_to_all | solution.py:121
  108.8 0.7 reduce.27
  109.5 0.8 select_reduce_fusion.4
  (52 shorter events, 4.1 us)
Async XLA Ops:
  0.0 1.9 %copy-start = (bf16[384,4096]{1,0:T(8,128)(2,1)S(1)}, bf16[384,4096]{1,0:T(8,128)(2,1)}, u32[]{:S(2)}) copy-start(bf16[384,4096]{1,0:T(8,128)(2,1)} %param.5) | copy-start | bytes 9437188
  1.9 6.0 %copy-start.2 = (s32[384]{0:T(512)S(1)}, s32[384]{0:T(512)}, u32[]{:S(2)}) copy-start(s32[384]{0:T(512)} %param.7) | copy-start | bytes 4612
  1.9 6.4 %copy-start.1 = (s32[384]{0:T(512)S(1)}, s32[384]{0:T(512)}, u32[]{:S(2)}) copy-start(s32[384]{0:T(512)} %param.8) | copy-start | bytes 4612
  1.9 6.5 %copy-start.3 = (s32[384]{0:T(512)S(1)}, s32[384]{0:T(512)}, u32[]{:S(2)}) copy-start(s32[384]{0:T(512)} %param.9) | copy-start | bytes 4612
  7.9 4.3 %copy-start.4 = (pred[768]{0:T(1024)(128)(4,1)S(1)}, pred[768]{0:T(1024)(128)(4,1)}, u32[]{:S(2)}) copy-start(pred[768]{0:T(1024)(128)(4,1)} %constant.55.clone.1) | copy-start | bytes 2308
  15.1 35.9 %all-to-all-start = ((bf16[8,96,768]{2,1,0:T(8,128)(2,1)}), bf16[8,96,768]{2,1,0:T(8,128)(2,1)}, u32[]{:S(2)}, u32[]{:S(2)}) async-start(bf16[8,96,768]{2,1,0:T(8,128)(2,1)} %bitcast.27), calls=%async_computation | async-start | bytes 2359296 | tf_op jit(solution)/shard_map/all_to_all | solution.py:69
  23.3 8.6 %collective-permute-start.1 = (bf16[384,384]{1,0:T(8,128)(2,1)S(1)}, bf16[384,384]{1,0:T(8,128)(2,1)S(1)}, u32[]{:S(2)}, u32[]{:S(2)}) collective-permute-start(bf16[384,384]{1,0:T(8,128)(2,1)S(1)} %slice.67), channel_id=1, source_target_pairs={{0,2},{2,0},{1,3},{3,1},{4,6},{6,4},{5,7},{7,5},{8,10},{10,8},{9,1... | collective-permute-start | bytes 884744 | tf_op jit(solution)/shard_map/ppermute | solution.py:77
  24.9 7.0 %collective-permute-start = (s32[384]{0:T(512)S(1)}, s32[384]{0:T(512)S(1)}, u32[]{:S(2)}, u32[]{:S(2)}) collective-permute-start(s32[384]{0:T(512)S(1)} %convert_add_fusion), channel_id=1, source_target_pairs={{0,2},{2,0},{1,3},{3,1},{4,6},{6,4},{5,7},{7,5},{8,10},{10,8},{9,1... | collective-permute-start | bytes 4616 | tf_op jit(solution)/shard_map/ppermute | solution.py:78
  51.0 32.7 %all-to-all-start.1 = ((bf16[8,192,384]{2,1,0:T(8,128)(2,1)}), bf16[8,192,384]{2,1,0:T(8,128)(2,1)}, u32[]{:S(2)}, u32[]{:S(2)}) async-start(bf16[8,192,384]{2,1,0:T(8,128)(2,1)} %pad_maximum_fusion), calls=%async_computation.1 | async-start | bytes 2359296 | tf_op jit(solution)/shard_map/all_to_all | solution.py:95
  57.7 30.8 %collective-permute-start.3 = (bf16[768,640]{1,0:T(8,128)(2,1)}, bf16[768,640]{1,0:T(8,128)(2,1)}, u32[]{:S(2)}, u32[]{:S(2)}) collective-permute-start(bf16[768,640]{1,0:T(8,128)(2,1)} %slice.66), channel_id=1, source_target_pairs={{0,2},{1,3},{2,0},{3,1},{4,6},{5,7},{6,4},{7,5},{8,10},{9,11},{10,... | collective-permute-start | bytes 2949128 | tf_op jit(solution)/shard_map/ppermute | solution.py:21
  59.2 33.2 %collective-permute-start.5 = (bf16[768,640]{1,0:T(8,128)(2,1)}, bf16[768,640]{1,0:T(8,128)(2,1)}, u32[]{:S(2)}, u32[]{:S(2)}) collective-permute-start(bf16[768,640]{1,0:T(8,128)(2,1)} %slice.66), channel_id=1, source_target_pairs={{0,1},{1,0},{2,3},{3,2},{4,5},{5,4},{6,7},{7,6},{8,9},{9,8},{10,11... | collective-permute-start | bytes 2949128 | tf_op jit(solution)/shard_map/ppermute | solution.py:23
  61.1 19.6 %collective-permute-start.2 = (f32[2,768]{1,0:T(2,128)S(1)}, f32[2,768]{1,0:T(2,128)S(1)}, u32[]{:S(2)}, u32[]{:S(2)}) collective-permute-start(f32[2,768]{1,0:T(2,128)S(1)} %pad_maximum_fusion.1), channel_id=1, source_target_pairs={{0,2},{1,3},{2,0},{3,1},{4,6},{5,7},{6,4},{7,5},{8,10},{9,11},{10,... | collective-permute-start | bytes 18440 | tf_op jit(solution)/shard_map/ppermute | solution.py:21
  61.6 19.0 %collective-permute-start.4 = (f32[2,768]{1,0:T(2,128)S(1)}, f32[2,768]{1,0:T(2,128)S(1)}, u32[]{:S(2)}, u32[]{:S(2)}) collective-permute-start(f32[2,768]{1,0:T(2,128)S(1)} %pad_maximum_fusion.1), channel_id=1, source_target_pairs={{0,1},{1,0},{2,3},{3,2},{4,5},{5,4},{6,7},{7,6},{8,9},{9,8},{10,11... | collective-permute-start | bytes 18440 | tf_op jit(solution)/shard_map/ppermute | solution.py:23
  80.6 1.2 %collective-permute-start.7 = (f32[2,768]{1,0:T(2,128)S(1)}, f32[2,768]{1,0:T(2,128)S(1)}, u32[]{:S(2)}, u32[]{:S(2)}) collective-permute-start(f32[2,768]{1,0:T(2,128)S(1)} %collective-permute-done.2), channel_id=1, source_target_pairs={{0,1},{1,0},{2,3},{3,2},{4,5},{5,4},{6,7},{7,6},{8,9},{9,8},{10,11... | collective-permute-start | bytes 18440 | tf_op jit(solution)/shard_map/ppermute | solution.py:23
  83.7 2.1 %copy-start.5 = (f32[768,768]{0,1:T(8,128)S(1)}, f32[768,768]{0,1:T(8,128)}, u32[]{:S(2)}) copy-start(f32[768,768]{0,1:T(8,128)} %fusion.24) | copy-start | bytes 7077892
  85.2 2.5 %collective-permute-start.9 = (bf16[768,384]{1,0:T(8,128)(2,1)S(1)}, bf16[768,384]{1,0:T(8,128)(2,1)S(1)}, u32[]{:S(2)}, u32[]{:S(2)}) collective-permute-start(bf16[768,384]{1,0:T(8,128)(2,1)S(1)} %bitcast.25), channel_id=1, source_target_pairs={{0,1},{1,0},{2,3},{3,2},{4,5},{5,4},{6,7},{7,6},{8,9},{9,8},{10,11... | collective-permute-start | bytes 1769480 | tf_op jit(solution)/shard_map/ppermute | solution.py:98
  85.3 3.4 %collective-permute-start.6 = (bf16[768,384]{1,0:T(8,128)(2,1)S(1)}, bf16[768,384]{1,0:T(8,128)(2,1)S(1)}, u32[]{:S(2)}, u32[]{:S(2)}) collective-permute-start(bf16[768,384]{1,0:T(8,128)(2,1)S(1)} %bitcast.20), channel_id=1, source_target_pairs={{0,1},{1,0},{2,3},{3,2},{4,5},{5,4},{6,7},{7,6},{8,9},{9,8},{10,11... | collective-permute-start | bytes 1769480 | tf_op jit(solution)/shard_map/ppermute | solution.py:98
  88.5 6.8 %collective-permute-start.8 = (bf16[768,640]{1,0:T(8,128)(2,1)}, bf16[768,640]{1,0:T(8,128)(2,1)S(1)}, u32[]{:S(2)}, u32[]{:S(2)}) collective-permute-start(bf16[768,640]{1,0:T(8,128)(2,1)} %collective-permute-done.3), channel_id=1, source_target_pairs={{0,1},{1,0},{2,3},{3,2},{4,5},{5,4},{6,7},{7,6},{8,9},{9,8},{10,11... | collective-permute-start | bytes 2949128 | tf_op jit(solution)/shard_map/ppermute | solution.py:23

commit v12 on v11

--- a/solution.py
+++ b/solution.py
@@ -53,14 +53,12 @@
     emb_w = embeds.shape[1]
     half = emb_w // 2
     label = (cluster_id - owner_of * CL_GRP + 1).astype(jnp.float32)
-    meta_cols = jnp.stack(
-        [label, block.astype(jnp.float32), (order // 256).astype(jnp.float32),
-         (order % 256).astype(jnp.float32)],
-        axis=1,
-    )
-    meta = jnp.concatenate(
-        [meta_cols, jnp.zeros((n_doc, META - meta_cols.shape[1]), jnp.float32)], axis=1
-    ).astype(jnp.bfloat16)
+    digits = [label, block.astype(jnp.float32), (order // 256).astype(jnp.float32), (order % 256).astype(jnp.float32)]
+    mcol = jnp.arange(META, dtype=jnp.int32)[None, :]
+    meta = jnp.zeros((n_doc, META), jnp.float32)
+    for i, d in enumerate(digits):
+        meta = jnp.where(mcol == i, d[:, None], meta)
+    meta = meta.astype(jnp.bfloat16)
     pick = place[None, :] == jnp.arange(n_slot, dtype=jnp.int32)[:, None]
 
     def route(rows):

time: 111 us -> 107 us (0.964)
  local copies, waits for them, and re-layouts: 10.2 us -> 8 us
    concatenate x1 -> x0, local copies, waits for them, and re-layouts: 1.75 us -> none  [local(): jnp.concatenate([meta_cols, jnp.zeros((n_doc, META - meta_cols.shape[1]),...]
    unnamed x12 -> x14, local copies, waits for them, and re-layouts: 1.91 us -> 2.52 us
  transfers between devices with their start and end apart: 12 -> 12, of which waited for: 5 -> 5; matrix products, arithmetic and copies ran while one was open for 21% -> 22% of each run, Pallas kernels for 0% -> 0%
where the time goes in v12:
time: 107 us; the launch traced here: 106 us
  waiting for transfers between devices  40.2 us (38%)
  matrix products  25.9 us (24%)
  starting transfers between devices  16.8 us (16%)
  blocking collectives  10.3 us (10%)
  local copies, waits for them, and re-layouts  8 us (7%)
  other arithmetic  4.95 us (5%)
    all_to_all x1, waiting for transfers between devices, route(): got = lax.all_to_all(send, 'grp', split_axis=0, concat_axis=0, tiled=True)  17.5 us
    ppermute x2, waiting for transfers between devices, gather_split(): cross = lax.ppermute(rows, 'split', [(0, 2), (1, 3), (2, 0), (3, 1)])  14.8 us
    dot_general x4, matrix products, dots(): s = jnp.einsum('qe,ke->qk', q_emb, k_a, preferred_element_type=jnp.float32)  12.4 us
    all_to_all x1, blocking collectives, local(): lax.all_to_all(best.reshape(n_grp, cap), 'grp', split_axis=0, concat_axis...  10.3 us
    all_to_all x1, starting transfers between devices, route(): got = lax.all_to_all(send, 'grp', split_axis=0, concat_axis=0, tiled=True)  7.25 us
    dot_general x1, matrix products, embed_rows(): jnp.einsum('...h,he->...e', rows, weight, preferred_element_type=jnp.floa...  5.98 us
    ppermute x1, waiting for transfers between devices, local(): par_place = lax.ppermute(place, 'split', cross)  5.02 us
    all_to_all x1, starting transfers between devices, local(): got = lax.all_to_all(send, 'grp', split_axis=0, concat_axis=0, tiled=True)  4.45 us
  transfers between devices with their start and end apart: 12, of which 5 were waited for; matrix products, arithmetic and copies ran while one was open for 22% of the time, Pallas kernels for 0%

profile of v12, /device:TPU:0, one launch (start us, length us, event | category | flops | bytes accessed | tf_op | source)
XLA Modules:
  0.0 106.3 jit_solution(12695131512112053921)
XLA Ops:
  0.0 1.9 %copy-done = bf16[384,4096]{1,0:T(8,128)(2,1)S(1)} copy-done((bf16[384,4096]{1,0:T(8,128)(2,1)S(1)}, bf16[384,4096]{1,0:T(8,128)(2,1)}, u32[]{:S(2)}) %copy-start) | copy-done | bytes 3145752
  1.9 6.0 %multiply_reduce_fusion = (f32[384]{0:T(512)S(1)}, f32[384,1024]{1,0:T(8,128)S(1)}) fusion(bf16[384,4096]{1,0:T(8,128)(2,1)S(1)} %copy-done, bf16[4096,1024]{1,0:T(8,128)(2,1)} %param.6), kind=kOutput, calls=%fused_computation.5 | convolution fusion | flops 3222011392 | bytes 13108736 | tf_op jit(solution)/shard_map/...h,he->...e/dot_general | solution.py:14
  8.6 0.6 copy-done.1
  9.3 1.8 %convolution_convert_fusion = bf16[768,768]{1,0:T(8,128)(2,1)} fusion(bf16[384,1024]{1,0:T(8,128)(2,1)S(1)} %multiply_convert_fusion, bf16[384,128]{1,0:T(8,128)(2,1)S(1)} %select_convert_fusion, s32[384]{0:T(512)S(1)} %convert_add_fusion, pred[768]{0:T(1024)(128)(4,1)S(1)} %copy-done.5, pred[768]{0:T(1024)(128)(4,1)S(1)} %iota_compare_fusion.9), kind=kOutput, calls=%fused_computation.6 | convolution fusion | flops 454459392 | bytes 1871872 | tf_op jit(solution)/shard_map/dot_general | solution.py:65
  11.1 7.3 %all-to-all-start = ((bf16[8,96,768]{2,1,0:T(8,128)(2,1)}), bf16[8,96,768]{2,1,0:T(8,128)(2,1)}, u32[]{:S(2)}, u32[]{:S(2)}) async-start(bf16[8,96,768]{2,1,0:T(8,128)(2,1)} %bitcast.27), calls=%async_computation | async-start | bytes 2359296 | tf_op jit(solution)/shard_map/all_to_all | solution.py:67
  18.4 1.0 slice.67
  19.4 1.6 %collective-permute-start.1 = (bf16[384,384]{1,0:T(8,128)(2,1)S(1)}, bf16[384,384]{1,0:T(8,128)(2,1)S(1)}, u32[]{:S(2)}, u32[]{:S(2)}) collective-permute-start(bf16[384,384]{1,0:T(8,128)(2,1)S(1)} %slice.67), channel_id=1, source_target_pairs={{0,2},{2,0},{1,3},{3,1},{4,6},{6,4},{5,7},{7,5},{8,10},{10,8},{9,1... | collective-permute-start | bytes 884744 | tf_op jit(solution)/shard_map/ppermute | solution.py:75
  21.5 1.5 %convolution_convert_fusion.2 = bf16[768,384]{1,0:T(8,128)(2,1)S(1)} fusion(s32[384]{0:T(512)S(1)} %convert_add_fusion, bf16[384,1024]{1,0:T(8,128)(2,1)} %copy-done.1), kind=kOutput, calls=%fused_computation.8 | convolution fusion | flops 227082240 | bytes 886272 | tf_op jit(solution)/shard_map/dot_general | solution.py:88
  22.9 5.0 %collective-permute-done = s32[384]{0:T(512)S(1)} collective-permute-done((s32[384]{0:T(512)S(1)}, s32[384]{0:T(512)S(1)}, u32[]{:S(2)}, u32[]{:S(2)}) %collective-permute-start) | collective-permute-done | bytes 1568 | tf_op jit(solution)/shard_map/ppermute | solution.py:76
  28.4 1.1 %pad_maximum_fusion = bf16[8,192,384]{2,1,0:T(8,128)(2,1)} fusion(bf16[8,96,384]{2,1,0:T(8,128)(2,1)S(1)} %bitcast.29, bf16[8,96,384]{2,1,0:T(8,128)(2,1)S(1)} %bitcast.28), kind=kLoop, calls=%fused_computation.9 | loop fusion | flops 2359296 | bytes 2359296 | tf_op jit(solution)/shard_map/concatenate | solution.py:90
  29.6 17.5 %all-to-all-done = bf16[8,96,768]{2,1,0:T(8,128)(2,1)} async-done(((bf16[8,96,768]{2,1,0:T(8,128)(2,1)}), bf16[8,96,768]{2,1,0:T(8,128)(2,1)}, u32[]{:S(2)}, u32[]{:S(2)}) %all-to-all-start) | async-done | bytes 1179680 | tf_op jit(solution)/shard_map/all_to_all | solution.py:67
  47.0 4.4 %all-to-all-start.1 = ((bf16[8,192,384]{2,1,0:T(8,128)(2,1)}), bf16[8,192,384]{2,1,0:T(8,128)(2,1)}, u32[]{:S(2)}, u32[]{:S(2)}) async-start(bf16[8,192,384]{2,1,0:T(8,128)(2,1)} %pad_maximum_fusion), calls=%async_computation.1 | async-start | bytes 2359296 | tf_op jit(solution)/shard_map/all_to_all | solution.py:93
  51.5 2.2 %slice.66 = bf16[768,640]{1,0:T(8,128)(2,1)} slice(bf16[768,768]{1,0:T(8,128)(2,1)} %bitcast.1), slice={[0:768], [0:640]} | slice | bytes 1966080 | tf_op jit(solution)/shard_map/slice | solution.py:31
  53.7 1.5 %collective-permute-start.3 = (bf16[768,640]{1,0:T(8,128)(2,1)}, bf16[768,640]{1,0:T(8,128)(2,1)}, u32[]{:S(2)}, u32[]{:S(2)}) collective-permute-start(bf16[768,640]{1,0:T(8,128)(2,1)} %slice.66), channel_id=1, source_target_pairs={{0,2},{1,3},{2,0},{3,1},{4,6},{5,7},{6,4},{7,5},{8,10},{9,11},{10,... | collective-permute-start | bytes 2949128 | tf_op jit(solution)/shard_map/ppermute | solution.py:21
  55.3 1.8 %convert_reduce_fusion = (f32[768]{0:T(1024)S(1)}, f32[768]{0:T(1024)S(1)}) fusion(bf16[768,768]{1,0:T(8,128)(2,1)} %bitcast.1), kind=kLoop, calls=%fused_computation.24 | loop fusion | flops 6144 | bytes 12288 | tf_op jit(solution)/shard_map/eq | solution.py:111
  57.1 0.6 collective-permute-start.2
  57.9 4.0 %fusion.22 = f32[768,768]{0,1:T(8,128)} fusion(bf16[768,768]{1,0:T(8,128)(2,1)} %bitcast.1), kind=kOutput, calls=%fused_computation.73 | convolution fusion | flops 754974720 | bytes 3342336 | tf_op jit(solution)/shard_map/qe,ke->qk/dot_general | solution.py:107
  61.9 14.8 %collective-permute-done.2 = f32[2,768]{1,0:T(2,128)S(1)} collective-permute-done((f32[2,768]{1,0:T(2,128)S(1)}, f32[2,768]{1,0:T(2,128)S(1)}, u32[]{:S(2)}, u32[]{:S(2)}) %collective-permute-start.2) | collective-permute-done | bytes 6176 | tf_op jit(solution)/shard_map/ppermute | solution.py:21
  76.8 1.1 collective-permute-done.7
  77.9 1.8 %all-to-all-done.1 = bf16[8,192,384]{2,1,0:T(8,128)(2,1)} async-done(((bf16[8,192,384]{2,1,0:T(8,128)(2,1)}), bf16[8,192,384]{2,1,0:T(8,128)(2,1)}, u32[]{:S(2)}, u32[]{:S(2)}) %all-to-all-start.1) | async-done | bytes 1179680 | tf_op jit(solution)/shard_map/all_to_all | solution.py:93
  79.8 1.5 %fusion.24 = (bf16[8,96,384]{2,1,0:T(8,128)(2,1)S(1)}, bf16[8,96,384]{2,1,0:T(8,128)(2,1)S(1)}) fusion(bf16[8,192,384]{2,1,0:T(8,128)(2,1)} %all-to-all-done.1), kind=kLoop, calls=%fused_computation.75 | loop fusion | bytes 2359296 | tf_op jit(solution)/shard_map/slice | solution.py:95
  81.8 1.1 %select_reduce_fusion.3 = f32[768]{0:T(1024)S(1)} fusion(f32[768,768]{0,1:T(8,128)S(1)} %copy-done.6, bf16[768,384]{1,0:T(8,128)(2,1)S(1)} %bitcast.21, f32[768]{0:T(1024)S(1)} %get-tuple-element.6, f32[768]{0:T(1024)S(1)} %get-tuple-element.5, pred[768]{0:T(1024)(128)(4,1)S(1)} %broadcast_compare_fusion), kind=kOutput, calls=%fused_computation.3 | convolution fusion | flops 457112832 | bytes 2959104 | tf_op jit(solution)/shard_map/qe,ke->qk/dot_general | solution.py:108
  83.0 0.8 fusion.25
  83.8 0.8 fusion.27
  84.7 0.8 fusion.26
  85.5 2.9 %select_reduce_fusion.2 = f32[768]{0:T(1024)S(1)} fusion(f32[768,768]{0,1:T(8,128)S(1)} %fusion.25, bf16[768,640]{1,0:T(8,128)(2,1)} %collective-permute-done.3, f32[768]{0:T(1024)S(1)} %get-tuple-element.6, f32[768]{0:T(1024)S(1)} %get-tuple-element.5, f32[768]{0:T(1024)S(1)} %get-tuple-element.8, f32[768]{0:T(1024)S(1)} %get-tuple-element.7, ...), kind=kOutput, calls=%fused_computation.2 | convolution fusion | flops 759102720 | bytes 4341504 | tf_op jit(solution)/shard_map/qe,ke->qk/dot_general | solution.py:107
  88.4 2.9 %select_reduce_fusion.1 = f32[768]{0:T(1024)S(1)} fusion(f32[768,768]{0,1:T(8,128)S(1)} %fusion.26, bf16[768,640]{1,0:T(8,128)(2,1)} %collective-permute-done.5, f32[768]{0:T(1024)S(1)} %get-tuple-element.6, f32[768]{0:T(1024)S(1)} %get-tuple-element.5, f32[768]{0:T(1024)S(1)} %get-tuple-element.10, f32[768]{0:T(1024)S(1)} %get-tuple-element.9, ...), kind=kOutput, calls=%fused_computation.1 | convolution fusion | flops 759102720 | bytes 4341504 | tf_op jit(solution)/shard_map/qe,ke->qk/dot_general | solution.py:107
  91.3 2.6 %select_reduce_fusion = f32[768]{0:T(1024)S(1)} fusion(f32[768,768]{0,1:T(8,128)S(1)} %fusion.27, bf16[768,640]{1,0:T(8,128)(2,1)S(1)} %collective-permute-done.8, f32[768]{0:T(1024)S(1)} %get-tuple-element.6, f32[768]{0:T(1024)S(1)} %get-tuple-element.5, f32[768]{0:T(1024)S(1)} %get-tuple-element.12, f32[768]{0:T(1024)S(1)} %get-tuple-element.11, ...), kind=kOutput, calls=%fused_computation | convolution fusion | flops 759102720 | bytes 4341504 | tf_op jit(solution)/shard_map/qe,ke->qk/dot_general | solution.py:107
  94.0 10.3 %all_to_all.16 = f32[8,1,96]{2,1,0:T(1,128)S(1)} all-to-all(f32[8,1,96]{2,1,0:T(1,128)S(1)} %max.41), channel_id=1, replica_groups=mesh['grp'=8,'split'=4] {'grp'}, dimensions={0} | all-to-all | bytes 6144 | tf_op jit(solution)/shard_map/all_to_all | solution.py:119
  104.3 0.5 broadcast.148
  104.8 0.7 reduce.27
  105.5 0.8 select_reduce_fusion.4
  (50 shorter events, 3.0 us)
Async XLA Ops:
  0.0 1.9 %copy-start = (bf16[384,4096]{1,0:T(8,128)(2,1)S(1)}, bf16[384,4096]{1,0:T(8,128)(2,1)}, u32[]{:S(2)}) copy-start(bf16[384,4096]{1,0:T(8,128)(2,1)} %param.5) | copy-start | bytes 9437188
  1.9 6.0 %copy-start.3 = (s32[384]{0:T(512)S(1)}, s32[384]{0:T(512)}, u32[]{:S(2)}) copy-start(s32[384]{0:T(512)} %param.9) | copy-start | bytes 4612
  1.9 6.0 %copy-start.4 = (s32[384]{0:T(512)S(1)}, s32[384]{0:T(512)}, u32[]{:S(2)}) copy-start(s32[384]{0:T(512)} %param.7) | copy-start | bytes 4612
  1.9 6.3 %copy-start.2 = (s32[384]{0:T(512)S(1)}, s32[384]{0:T(512)}, u32[]{:S(2)}) copy-start(s32[384]{0:T(512)} %param.8) | copy-start | bytes 4612
  7.9 1.4 %copy-start.5 = (pred[768]{0:T(1024)(128)(4,1)S(1)}, pred[768]{0:T(1024)(128)(4,1)}, u32[]{:S(2)}) copy-start(pred[768]{0:T(1024)(128)(4,1)} %constant.58.clone.1) | copy-start | bytes 2308
  8.3 0.9 copy-start.1
  11.1 35.9 %all-to-all-start = ((bf16[8,96,768]{2,1,0:T(8,128)(2,1)}), bf16[8,96,768]{2,1,0:T(8,128)(2,1)}, u32[]{:S(2)}, u32[]{:S(2)}) async-start(bf16[8,96,768]{2,1,0:T(8,128)(2,1)} %bitcast.27), calls=%async_computation | async-start | bytes 2359296 | tf_op jit(solution)/shard_map/all_to_all | solution.py:67
  19.4 8.6 %collective-permute-start.1 = (bf16[384,384]{1,0:T(8,128)(2,1)S(1)}, bf16[384,384]{1,0:T(8,128)(2,1)S(1)}, u32[]{:S(2)}, u32[]{:S(2)}) collective-permute-start(bf16[384,384]{1,0:T(8,128)(2,1)S(1)} %slice.67), channel_id=1, source_target_pairs={{0,2},{2,0},{1,3},{3,1},{4,6},{6,4},{5,7},{7,5},{8,10},{10,8},{9,1... | collective-permute-start | bytes 884744 | tf_op jit(solution)/shard_map/ppermute | solution.py:75
  20.9 7.0 %collective-permute-start = (s32[384]{0:T(512)S(1)}, s32[384]{0:T(512)S(1)}, u32[]{:S(2)}, u32[]{:S(2)}) collective-permute-start(s32[384]{0:T(512)S(1)} %convert_add_fusion), channel_id=1, source_target_pairs={{0,2},{2,0},{1,3},{3,1},{4,6},{6,4},{5,7},{7,5},{8,10},{10,8},{9,1... | collective-permute-start | bytes 4616 | tf_op jit(solution)/shard_map/ppermute | solution.py:76
  47.0 32.7 %all-to-all-start.1 = ((bf16[8,192,384]{2,1,0:T(8,128)(2,1)}), bf16[8,192,384]{2,1,0:T(8,128)(2,1)}, u32[]{:S(2)}, u32[]{:S(2)}) async-start(bf16[8,192,384]{2,1,0:T(8,128)(2,1)} %pad_maximum_fusion), calls=%async_computation.1 | async-start | bytes 2359296 | tf_op jit(solution)/shard_map/all_to_all | solution.py:93
  53.7 30.8 %collective-permute-start.3 = (bf16[768,640]{1,0:T(8,128)(2,1)}, bf16[768,640]{1,0:T(8,128)(2,1)}, u32[]{:S(2)}, u32[]{:S(2)}) collective-permute-start(bf16[768,640]{1,0:T(8,128)(2,1)} %slice.66), channel_id=1, source_target_pairs={{0,2},{1,3},{2,0},{3,1},{4,6},{5,7},{6,4},{7,5},{8,10},{9,11},{10,... | collective-permute-start | bytes 2949128 | tf_op jit(solution)/shard_map/ppermute | solution.py:21
  55.3 33.2 %collective-permute-start.5 = (bf16[768,640]{1,0:T(8,128)(2,1)}, bf16[768,640]{1,0:T(8,128)(2,1)}, u32[]{:S(2)}, u32[]{:S(2)}) collective-permute-start(bf16[768,640]{1,0:T(8,128)(2,1)} %slice.66), channel_id=1, source_target_pairs={{0,1},{1,0},{2,3},{3,2},{4,5},{5,4},{6,7},{7,6},{8,9},{9,8},{10,11... | collective-permute-start | bytes 2949128 | tf_op jit(solution)/shard_map/ppermute | solution.py:23
  57.1 19.6 %collective-permute-start.2 = (f32[2,768]{1,0:T(2,128)S(1)}, f32[2,768]{1,0:T(2,128)S(1)}, u32[]{:S(2)}, u32[]{:S(2)}) collective-permute-start(f32[2,768]{1,0:T(2,128)S(1)} %pad_maximum_fusion.1), channel_id=1, source_target_pairs={{0,2},{1,3},{2,0},{3,1},{4,6},{5,7},{6,4},{7,5},{8,10},{9,11},{10,... | collective-permute-start | bytes 18440 | tf_op jit(solution)/shard_map/ppermute | solution.py:21
  57.7 19.0 %collective-permute-start.4 = (f32[2,768]{1,0:T(2,128)S(1)}, f32[2,768]{1,0:T(2,128)S(1)}, u32[]{:S(2)}, u32[]{:S(2)}) collective-permute-start(f32[2,768]{1,0:T(2,128)S(1)} %pad_maximum_fusion.1), channel_id=1, source_target_pairs={{0,1},{1,0},{2,3},{3,2},{4,5},{5,4},{6,7},{7,6},{8,9},{9,8},{10,11... | collective-permute-start | bytes 18440 | tf_op jit(solution)/shard_map/ppermute | solution.py:23
  76.7 1.2 %collective-permute-start.7 = (f32[2,768]{1,0:T(2,128)S(1)}, f32[2,768]{1,0:T(2,128)S(1)}, u32[]{:S(2)}, u32[]{:S(2)}) collective-permute-start(f32[2,768]{1,0:T(2,128)S(1)} %collective-permute-done.2), channel_id=1, source_target_pairs={{0,1},{1,0},{2,3},{3,2},{4,5},{5,4},{6,7},{7,6},{8,9},{9,8},{10,11... | collective-permute-start | bytes 18440 | tf_op jit(solution)/shard_map/ppermute | solution.py:23
  79.8 2.1 %copy-start.6 = (f32[768,768]{0,1:T(8,128)S(1)}, f32[768,768]{0,1:T(8,128)}, u32[]{:S(2)}) copy-start(f32[768,768]{0,1:T(8,128)} %fusion.22) | copy-start | bytes 7077892
  81.3 2.5 %collective-permute-start.9 = (bf16[768,384]{1,0:T(8,128)(2,1)S(1)}, bf16[768,384]{1,0:T(8,128)(2,1)S(1)}, u32[]{:S(2)}, u32[]{:S(2)}) collective-permute-start(bf16[768,384]{1,0:T(8,128)(2,1)S(1)} %bitcast.25), channel_id=1, source_target_pairs={{0,1},{1,0},{2,3},{3,2},{4,5},{5,4},{6,7},{7,6},{8,9},{9,8},{10,11... | collective-permute-start | bytes 1769480 | tf_op jit(solution)/shard_map/ppermute | solution.py:96
  81.3 3.4 %collective-permute-start.6 = (bf16[768,384]{1,0:T(8,128)(2,1)S(1)}, bf16[768,384]{1,0:T(8,128)(2,1)S(1)}, u32[]{:S(2)}, u32[]{:S(2)}) collective-permute-start(bf16[768,384]{1,0:T(8,128)(2,1)S(1)} %bitcast.20), channel_id=1, source_target_pairs={{0,1},{1,0},{2,3},{3,2},{4,5},{5,4},{6,7},{7,6},{8,9},{9,8},{10,11... | collective-permute-start | bytes 1769480 | tf_op jit(solution)/shard_map/ppermute | solution.py:96
  84.6 6.8 %collective-permute-start.8 = (bf16[768,640]{1,0:T(8,128)(2,1)}, bf16[768,640]{1,0:T(8,128)(2,1)S(1)}, u32[]{:S(2)}, u32[]{:S(2)}) collective-permute-start(bf16[768,640]{1,0:T(8,128)(2,1)} %collective-permute-done.3), channel_id=1, source_target_pairs={{0,1},{1,0},{2,3},{3,2},{4,5},{5,4},{6,7},{7,6},{8,9},{9,8},{10,11... | collective-permute-start | bytes 2949128 | tf_op jit(solution)/shard_map/ppermute | solution.py:23

commit v13 on v12

--- a/solution.py
+++ b/solution.py
@@ -119,7 +119,12 @@
     returned = lax.all_to_all(
         best.reshape(n_grp, cap), "grp", split_axis=0, concat_axis=0, tiled=True
     ).reshape(n_slot)
-    return jnp.max(jnp.where(pick, returned[:, None], -jnp.inf), axis=0)
+    hi = lax.reduce_precision(returned, exponent_bits=8, mantissa_bits=7)
+    rest = returned - hi
+    mid = lax.reduce_precision(rest, exponent_bits=8, mantissa_bits=7)
+    pieces = jnp.stack([hi, mid, rest - mid], axis=1).astype(jnp.bfloat16)
+    got = jnp.einsum("sd,sp->dp", pick.astype(jnp.bfloat16), pieces, preferred_element_type=jnp.float32)
+    return (got[:, 0] + got[:, 1]) + got[:, 2]
 
 
 def solution(mesh):

time: 107 us -> 107 us (level)
    unnamed x14 -> x10, local copies, waits for them, and re-layouts: 2.52 us -> 1.47 us
where the time goes in v13:
time: 107 us; the launch traced here: 106 us
  waiting for transfers between devices  40.2 us (38%)
  matrix products  26.2 us (24%)
  starting transfers between devices  16.8 us (16%)
  blocking collectives  10.2 us (10%)
  local copies, waits for them, and re-layouts  6.95 us (6%)
  other arithmetic  5.62 us (5%)
    all_to_all x1, waiting for transfers between devices, route(): got = lax.all_to_all(send, 'grp', split_axis=0, concat_axis=0, tiled=True)  17.5 us
    ppermute x2, waiting for transfers between devices, gather_split(): cross = lax.ppermute(rows, 'split', [(0, 2), (1, 3), (2, 0), (3, 1)])  14.8 us
    dot_general x4, matrix products, dots(): s = jnp.einsum('qe,ke->qk', q_emb, k_a, preferred_element_type=jnp.float32)  12.4 us
    all_to_all x1, blocking collectives, local(): lax.all_to_all(best.reshape(n_grp, cap), 'grp', split_axis=0, concat_axis...  10.2 us
    all_to_all x1, starting transfers between devices, route(): got = lax.all_to_all(send, 'grp', split_axis=0, concat_axis=0, tiled=True)  7.25 us
    dot_general x1, matrix products, embed_rows(): jnp.einsum('...h,he->...e', rows, weight, preferred_element_type=jnp.floa...  5.95 us
    ppermute x1, waiting for transfers between devices, local(): par_place = lax.ppermute(place, 'split', cross)  5.02 us
    all_to_all x1, starting transfers between devices, local(): got = lax.all_to_all(send, 'grp', split_axis=0, concat_axis=0, tiled=True)  4.45 us
  transfers between devices with their start and end apart: 12, of which 5 were waited for; matrix products, arithmetic and copies ran while one was open for 22% of the time, Pallas kernels for 0%

profile of v13, /device:TPU:0, one launch (start us, length us, event | category | flops | bytes accessed | tf_op | source)
XLA Modules:
  0.0 106.2 jit_solution(3127243725793971824)
XLA Ops:
  0.0 0.9 fusion.21
  1.1 0.8 copy-done
  1.9 5.9 %multiply_reduce_fusion = (f32[384]{0:T(512)S(1)}, f32[384,1024]{1,0:T(8,128)S(1)}) fusion(bf16[384,4096]{1,0:T(8,128)(2,1)S(1)} %copy-done, bf16[4096,1024]{1,0:T(8,128)(2,1)} %param.6), kind=kOutput, calls=%fused_computation.5 | convolution fusion | flops 3222011392 | bytes 13108736 | tf_op jit(solution)/shard_map/...h,he->...e/dot_general | solution.py:14
  8.4 0.6 copy-done.1
  9.0 1.8 %convolution_convert_fusion = bf16[768,768]{1,0:T(8,128)(2,1)} fusion(bf16[384,1024]{1,0:T(8,128)(2,1)S(1)} %multiply_convert_fusion, bf16[384,128]{1,0:T(8,128)(2,1)S(1)} %select_convert_fusion, s32[384]{0:T(512)S(1)} %convert_add_fusion, pred[768]{0:T(1024)(128)(4,1)S(1)} %copy-done.3, pred[768]{0:T(1024)(128)(4,1)S(1)} %iota_compare_fusion.10), kind=kOutput, calls=%fused_computation.6 | convolution fusion | flops 454459392 | bytes 1871872 | tf_op jit(solution)/shard_map/dot_general | solution.py:65
  10.9 7.3 %all-to-all-start = ((bf16[8,96,768]{2,1,0:T(8,128)(2,1)}), bf16[8,96,768]{2,1,0:T(8,128)(2,1)}, u32[]{:S(2)}, u32[]{:S(2)}) async-start(bf16[8,96,768]{2,1,0:T(8,128)(2,1)} %bitcast.27), calls=%async_computation | async-start | bytes 2359296 | tf_op jit(solution)/shard_map/all_to_all | solution.py:67
  18.1 1.0 slice.79
  19.1 1.6 %collective-permute-start.1 = (bf16[384,384]{1,0:T(8,128)(2,1)S(1)}, bf16[384,384]{1,0:T(8,128)(2,1)S(1)}, u32[]{:S(2)}, u32[]{:S(2)}) collective-permute-start(bf16[384,384]{1,0:T(8,128)(2,1)S(1)} %slice.79), channel_id=1, source_target_pairs={{0,2},{2,0},{1,3},{3,1},{4,6},{6,4},{5,7},{7,5},{8,10},{10,8},{9,1... | collective-permute-start | bytes 884744 | tf_op jit(solution)/shard_map/ppermute | solution.py:75
  21.2 1.5 %convolution_convert_fusion.2 = bf16[768,384]{1,0:T(8,128)(2,1)S(1)} fusion(s32[384]{0:T(512)S(1)} %convert_add_fusion, bf16[384,1024]{1,0:T(8,128)(2,1)} %copy-done.1), kind=kOutput, calls=%fused_computation.8 | convolution fusion | flops 227082240 | bytes 886272 | tf_op jit(solution)/shard_map/dot_general | solution.py:88
  22.7 5.0 %collective-permute-done = s32[384]{0:T(512)S(1)} collective-permute-done((s32[384]{0:T(512)S(1)}, s32[384]{0:T(512)S(1)}, u32[]{:S(2)}, u32[]{:S(2)}) %collective-permute-start) | collective-permute-done | bytes 1568 | tf_op jit(solution)/shard_map/ppermute | solution.py:76
  28.2 1.1 %pad_maximum_fusion = bf16[8,192,384]{2,1,0:T(8,128)(2,1)} fusion(bf16[8,96,384]{2,1,0:T(8,128)(2,1)S(1)} %bitcast.29, bf16[8,96,384]{2,1,0:T(8,128)(2,1)S(1)} %bitcast.28), kind=kLoop, calls=%fused_computation.9 | loop fusion | flops 2359296 | bytes 2359296 | tf_op jit(solution)/shard_map/concatenate | solution.py:90
  29.3 17.5 %all-to-all-done = bf16[8,96,768]{2,1,0:T(8,128)(2,1)} async-done(((bf16[8,96,768]{2,1,0:T(8,128)(2,1)}), bf16[8,96,768]{2,1,0:T(8,128)(2,1)}, u32[]{:S(2)}, u32[]{:S(2)}) %all-to-all-start) | async-done | bytes 1179680 | tf_op jit(solution)/shard_map/all_to_all | solution.py:67
  46.8 4.4 %all-to-all-start.1 = ((bf16[8,192,384]{2,1,0:T(8,128)(2,1)}), bf16[8,192,384]{2,1,0:T(8,128)(2,1)}, u32[]{:S(2)}, u32[]{:S(2)}) async-start(bf16[8,192,384]{2,1,0:T(8,128)(2,1)} %pad_maximum_fusion), calls=%async_computation.1 | async-start | bytes 2359296 | tf_op jit(solution)/shard_map/all_to_all | solution.py:93
  51.2 2.2 %slice.78 = bf16[768,640]{1,0:T(8,128)(2,1)} slice(bf16[768,768]{1,0:T(8,128)(2,1)} %bitcast.1), slice={[0:768], [0:640]} | slice | bytes 1966080 | tf_op jit(solution)/shard_map/slice | solution.py:31
  53.5 1.5 %collective-permute-start.3 = (bf16[768,640]{1,0:T(8,128)(2,1)}, bf16[768,640]{1,0:T(8,128)(2,1)}, u32[]{:S(2)}, u32[]{:S(2)}) collective-permute-start(bf16[768,640]{1,0:T(8,128)(2,1)} %slice.78), channel_id=1, source_target_pairs={{0,2},{1,3},{2,0},{3,1},{4,6},{5,7},{6,4},{7,5},{8,10},{9,11},{10,... | collective-permute-start | bytes 2949128 | tf_op jit(solution)/shard_map/ppermute | solution.py:21
  55.0 1.8 %convert_reduce_fusion = (f32[768]{0:T(1024)S(1)}, f32[768]{0:T(1024)S(1)}) fusion(bf16[768,768]{1,0:T(8,128)(2,1)} %bitcast.1), kind=kLoop, calls=%fused_computation.25 | loop fusion | flops 6144 | bytes 12288 | tf_op jit(solution)/shard_map/eq | solution.py:111
  56.9 0.6 collective-permute-start.2
  57.7 4.0 %fusion.32 = f32[768,768]{0,1:T(8,128)} fusion(bf16[768,768]{1,0:T(8,128)(2,1)} %bitcast.1), kind=kOutput, calls=%fused_computation.88 | convolution fusion | flops 754974720 | bytes 3342336 | tf_op jit(solution)/shard_map/qe,ke->qk/dot_general | solution.py:107
  61.7 14.8 %collective-permute-done.2 = f32[2,768]{1,0:T(2,128)S(1)} collective-permute-done((f32[2,768]{1,0:T(2,128)S(1)}, f32[2,768]{1,0:T(2,128)S(1)}, u32[]{:S(2)}, u32[]{:S(2)}) %collective-permute-start.2) | collective-permute-done | bytes 6176 | tf_op jit(solution)/shard_map/ppermute | solution.py:21
  76.6 1.1 collective-permute-done.7
  77.7 1.8 %all-to-all-done.1 = bf16[8,192,384]{2,1,0:T(8,128)(2,1)} async-done(((bf16[8,192,384]{2,1,0:T(8,128)(2,1)}), bf16[8,192,384]{2,1,0:T(8,128)(2,1)}, u32[]{:S(2)}, u32[]{:S(2)}) %all-to-all-start.1) | async-done | bytes 1179680 | tf_op jit(solution)/shard_map/all_to_all | solution.py:93
  79.5 1.5 %fusion.34 = (bf16[8,96,384]{2,1,0:T(8,128)(2,1)S(1)}, bf16[8,96,384]{2,1,0:T(8,128)(2,1)S(1)}) fusion(bf16[8,192,384]{2,1,0:T(8,128)(2,1)} %all-to-all-done.1), kind=kLoop, calls=%fused_computation.90 | loop fusion | bytes 2359296 | tf_op jit(solution)/shard_map/slice | solution.py:95
  81.6 1.1 %select_reduce_fusion.3 = f32[768]{0:T(1024)S(1)} fusion(f32[768,768]{0,1:T(8,128)S(1)} %copy-done.4, bf16[768,384]{1,0:T(8,128)(2,1)S(1)} %bitcast.21, f32[768]{0:T(1024)S(1)} %get-tuple-element.6, f32[768]{0:T(1024)S(1)} %get-tuple-element.5, pred[768]{0:T(1024)(128)(4,1)S(1)} %broadcast_compare_fusion), kind=kOutput, calls=%fused_computation.3 | convolution fusion | flops 457112832 | bytes 2959104 | tf_op jit(solution)/shard_map/qe,ke->qk/dot_general | solution.py:108
  82.7 0.8 fusion.35
  83.5 0.8 fusion.37
  84.5 0.8 fusion.36
  85.3 2.9 %select_reduce_fusion.2 = f32[768]{0:T(1024)S(1)} fusion(f32[768,768]{0,1:T(8,128)S(1)} %fusion.35, bf16[768,640]{1,0:T(8,128)(2,1)} %collective-permute-done.3, f32[768]{0:T(1024)S(1)} %get-tuple-element.6, f32[768]{0:T(1024)S(1)} %get-tuple-element.5, f32[768]{0:T(1024)S(1)} %get-tuple-element.8, f32[768]{0:T(1024)S(1)} %get-tuple-element.7, ...), kind=kOutput, calls=%fused_computation.2 | convolution fusion | flops 759102720 | bytes 4341504 | tf_op jit(solution)/shard_map/qe,ke->qk/dot_general | solution.py:107
  88.2 2.9 %select_reduce_fusion.1 = f32[768]{0:T(1024)S(1)} fusion(f32[768,768]{0,1:T(8,128)S(1)} %fusion.36, bf16[768,640]{1,0:T(8,128)(2,1)} %collective-permute-done.5, f32[768]{0:T(1024)S(1)} %get-tuple-element.6, f32[768]{0:T(1024)S(1)} %get-tuple-element.5, f32[768]{0:T(1024)S(1)} %get-tuple-element.10, f32[768]{0:T(1024)S(1)} %get-tuple-element.9, ...), kind=kOutput, calls=%fused_computation.1 | convolution fusion | flops 759102720 | bytes 4341504 | tf_op jit(solution)/shard_map/qe,ke->qk/dot_general | solution.py:107
  91.1 2.6 %select_reduce_fusion = f32[768]{0:T(1024)S(1)} fusion(f32[768,768]{0,1:T(8,128)S(1)} %fusion.37, bf16[768,640]{1,0:T(8,128)(2,1)S(1)} %collective-permute-done.8, f32[768]{0:T(1024)S(1)} %get-tuple-element.6, f32[768]{0:T(1024)S(1)} %get-tuple-element.5, f32[768]{0:T(1024)S(1)} %get-tuple-element.12, f32[768]{0:T(1024)S(1)} %get-tuple-element.11, ...), kind=kOutput, calls=%fused_computation | convolution fusion | flops 759102720 | bytes 4341504 | tf_op jit(solution)/shard_map/qe,ke->qk/dot_general | solution.py:107
  93.8 10.2 %all_to_all.16 = f32[8,1,96]{2,1,0:T(1,128)S(1)} all-to-all(f32[8,1,96]{2,1,0:T(1,128)S(1)} %max.41), channel_id=1, replica_groups=mesh['grp'=8,'split'=4] {'grp'}, dimensions={0} | all-to-all | bytes 6144 | tf_op jit(solution)/shard_map/all_to_all | solution.py:119
  104.5 0.7 reduce.29
  105.6 0.6 fusion.25
  (48 shorter events, 3.8 us)
Async XLA Ops:
  0.0 1.9 %copy-start = (bf16[384,4096]{1,0:T(8,128)(2,1)S(1)}, bf16[384,4096]{1,0:T(8,128)(2,1)}, u32[]{:S(2)}) copy-start(bf16[384,4096]{1,0:T(8,128)(2,1)} %param.5) | copy-start | bytes 9437188
  1.9 6.0 %copy-start.2 = (s32[384]{0:T(512)S(1)}, s32[384]{0:T(512)}, u32[]{:S(2)}) copy-start(s32[384]{0:T(512)} %param.8) | copy-start | bytes 4612
  7.9 1.1 %copy-start.3 = (pred[768]{0:T(1024)(128)(4,1)S(1)}, pred[768]{0:T(1024)(128)(4,1)}, u32[]{:S(2)}) copy-start(pred[768]{0:T(1024)(128)(4,1)} %constant.58.clone.1) | copy-start | bytes 2308
  8.1 0.9 copy-start.1
  10.9 35.9 %all-to-all-start = ((bf16[8,96,768]{2,1,0:T(8,128)(2,1)}), bf16[8,96,768]{2,1,0:T(8,128)(2,1)}, u32[]{:S(2)}, u32[]{:S(2)}) async-start(bf16[8,96,768]{2,1,0:T(8,128)(2,1)} %bitcast.27), calls=%async_computation | async-start | bytes 2359296 | tf_op jit(solution)/shard_map/all_to_all | solution.py:67
  19.1 8.6 %collective-permute-start.1 = (bf16[384,384]{1,0:T(8,128)(2,1)S(1)}, bf16[384,384]{1,0:T(8,128)(2,1)S(1)}, u32[]{:S(2)}, u32[]{:S(2)}) collective-permute-start(bf16[384,384]{1,0:T(8,128)(2,1)S(1)} %slice.79), channel_id=1, source_target_pairs={{0,2},{2,0},{1,3},{3,1},{4,6},{6,4},{5,7},{7,5},{8,10},{10,8},{9,1... | collective-permute-start | bytes 884744 | tf_op jit(solution)/shard_map/ppermute | solution.py:75
  20.7 7.0 %collective-permute-start = (s32[384]{0:T(512)S(1)}, s32[384]{0:T(512)S(1)}, u32[]{:S(2)}, u32[]{:S(2)}) collective-permute-start(s32[384]{0:T(512)S(1)} %convert_add_fusion), channel_id=1, source_target_pairs={{0,2},{2,0},{1,3},{3,1},{4,6},{6,4},{5,7},{7,5},{8,10},{10,8},{9,1... | collective-permute-start | bytes 4616 | tf_op jit(solution)/shard_map/ppermute | solution.py:76
  46.8 32.7 %all-to-all-start.1 = ((bf16[8,192,384]{2,1,0:T(8,128)(2,1)}), bf16[8,192,384]{2,1,0:T(8,128)(2,1)}, u32[]{:S(2)}, u32[]{:S(2)}) async-start(bf16[8,192,384]{2,1,0:T(8,128)(2,1)} %pad_maximum_fusion), calls=%async_computation.1 | async-start | bytes 2359296 | tf_op jit(solution)/shard_map/all_to_all | solution.py:93
  53.5 30.8 %collective-permute-start.3 = (bf16[768,640]{1,0:T(8,128)(2,1)}, bf16[768,640]{1,0:T(8,128)(2,1)}, u32[]{:S(2)}, u32[]{:S(2)}) collective-permute-start(bf16[768,640]{1,0:T(8,128)(2,1)} %slice.78), channel_id=1, source_target_pairs={{0,2},{1,3},{2,0},{3,1},{4,6},{5,7},{6,4},{7,5},{8,10},{9,11},{10,... | collective-permute-start | bytes 2949128 | tf_op jit(solution)/shard_map/ppermute | solution.py:21
  55.0 33.2 %collective-permute-start.5 = (bf16[768,640]{1,0:T(8,128)(2,1)}, bf16[768,640]{1,0:T(8,128)(2,1)}, u32[]{:S(2)}, u32[]{:S(2)}) collective-permute-start(bf16[768,640]{1,0:T(8,128)(2,1)} %slice.78), channel_id=1, source_target_pairs={{0,1},{1,0},{2,3},{3,2},{4,5},{5,4},{6,7},{7,6},{8,9},{9,8},{10,11... | collective-permute-start | bytes 2949128 | tf_op jit(solution)/shard_map/ppermute | solution.py:23
  56.9 19.6 %collective-permute-start.2 = (f32[2,768]{1,0:T(2,128)S(1)}, f32[2,768]{1,0:T(2,128)S(1)}, u32[]{:S(2)}, u32[]{:S(2)}) collective-permute-start(f32[2,768]{1,0:T(2,128)S(1)} %pad_maximum_fusion.1), channel_id=1, source_target_pairs={{0,2},{1,3},{2,0},{3,1},{4,6},{5,7},{6,4},{7,5},{8,10},{9,11},{10,... | collective-permute-start | bytes 18440 | tf_op jit(solution)/shard_map/ppermute | solution.py:21
  57.4 19.0 %collective-permute-start.4 = (f32[2,768]{1,0:T(2,128)S(1)}, f32[2,768]{1,0:T(2,128)S(1)}, u32[]{:S(2)}, u32[]{:S(2)}) collective-permute-start(f32[2,768]{1,0:T(2,128)S(1)} %pad_maximum_fusion.1), channel_id=1, source_target_pairs={{0,1},{1,0},{2,3},{3,2},{4,5},{5,4},{6,7},{7,6},{8,9},{9,8},{10,11... | collective-permute-start | bytes 18440 | tf_op jit(solution)/shard_map/ppermute | solution.py:23
  76.4 1.2 %collective-permute-start.7 = (f32[2,768]{1,0:T(2,128)S(1)}, f32[2,768]{1,0:T(2,128)S(1)}, u32[]{:S(2)}, u32[]{:S(2)}) collective-permute-start(f32[2,768]{1,0:T(2,128)S(1)} %collective-permute-done.2), channel_id=1, source_target_pairs={{0,1},{1,0},{2,3},{3,2},{4,5},{5,4},{6,7},{7,6},{8,9},{9,8},{10,11... | collective-permute-start | bytes 18440 | tf_op jit(solution)/shard_map/ppermute | solution.py:23
  79.5 2.1 %copy-start.4 = (f32[768,768]{0,1:T(8,128)S(1)}, f32[768,768]{0,1:T(8,128)}, u32[]{:S(2)}) copy-start(f32[768,768]{0,1:T(8,128)} %fusion.32) | copy-start | bytes 7077892
  81.0 2.5 %collective-permute-start.9 = (bf16[768,384]{1,0:T(8,128)(2,1)S(1)}, bf16[768,384]{1,0:T(8,128)(2,1)S(1)}, u32[]{:S(2)}, u32[]{:S(2)}) collective-permute-start(bf16[768,384]{1,0:T(8,128)(2,1)S(1)} %bitcast.25), channel_id=1, source_target_pairs={{0,1},{1,0},{2,3},{3,2},{4,5},{5,4},{6,7},{7,6},{8,9},{9,8},{10,11... | collective-permute-start | bytes 1769480 | tf_op jit(solution)/shard_map/ppermute | solution.py:96
  81.1 3.4 %collective-permute-start.6 = (bf16[768,384]{1,0:T(8,128)(2,1)S(1)}, bf16[768,384]{1,0:T(8,128)(2,1)S(1)}, u32[]{:S(2)}, u32[]{:S(2)}) collective-permute-start(bf16[768,384]{1,0:T(8,128)(2,1)S(1)} %bitcast.20), channel_id=1, source_target_pairs={{0,1},{1,0},{2,3},{3,2},{4,5},{5,4},{6,7},{7,6},{8,9},{9,8},{10,11... | collective-permute-start | bytes 1769480 | tf_op jit(solution)/shard_map/ppermute | solution.py:96
  84.3 6.8 %collective-permute-start.8 = (bf16[768,640]{1,0:T(8,128)(2,1)}, bf16[768,640]{1,0:T(8,128)(2,1)S(1)}, u32[]{:S(2)}, u32[]{:S(2)}) collective-permute-start(bf16[768,640]{1,0:T(8,128)(2,1)} %collective-permute-done.3), channel_id=1, source_target_pairs={{0,1},{1,0},{2,3},{3,2},{4,5},{5,4},{6,7},{7,6},{8,9},{9,8},{10,11... | collective-permute-start | bytes 2949128 | tf_op jit(solution)/shard_map/ppermute | solution.py:23

commit v14 on v13

--- a/solution.py
+++ b/solution.py
@@ -82,7 +82,6 @@
         )
         got_a = route(rows_a)
         q_emb, q_lab, q_ord = unpack(got_a, half, n_all)
-        keys_a = gather_split(q_emb, n_split)
         keys_m = gather_split(jnp.stack([q_lab, q_ord]), n_split)
         pick_par = par_place[None, :] == jnp.arange(n_slot, dtype=jnp.int32)[:, None]
         send_own = jnp.dot(pick.astype(jnp.bfloat16), raw_b, preferred_element_type=jnp.float32)
@@ -90,6 +89,8 @@
         send = jnp.concatenate(
             [send_own.reshape(n_grp, cap, -1), send_par.reshape(n_grp, cap, -1)], axis=1
         ).astype(jnp.bfloat16)
+        q_emb, send = lax.optimization_barrier((q_emb, send))
+        keys_a = gather_split(q_emb, n_split)
         got = lax.all_to_all(send, "grp", split_axis=0, concat_axis=0, tiled=True)
         got_b = got[:, :cap].reshape(n_slot, -1)
         cross_b = got[:, cap:].reshape(n_slot, -1)

time: 107 us -> 109 us (1.019)
  waiting for transfers between devices: 40.2 us -> 41.4 us
    ppermute x2, waiting for transfers between devices: 14.8 us -> 16.3 us  [gather_split(): cross = lax.ppermute(rows, 'split', [(0, 2), (1, 3), (2, 0), (3, 1)])]
  transfers between devices with their start and end apart: 12 -> 12, of which waited for: 5 -> 5; matrix products, arithmetic and copies ran while one was open for 22% -> 19% of each run, Pallas kernels for 0% -> 0%
where the time goes in v14:
time: 109 us
  waiting for transfers between devices  41.4 us (38%)
  matrix products  26.7 us (24%)
  starting transfers between devices  17.4 us (16%)
  blocking collectives  10.4 us (10%)
  local copies, waits for them, and re-layouts  6.81 us (6%)
  other arithmetic  5.89 us (5%)
    all_to_all x1, waiting for transfers between devices, route(): got = lax.all_to_all(send, 'grp', split_axis=0, concat_axis=0, tiled=True)  17.5 us
    ppermute x2, waiting for transfers between devices, gather_split(): cross = lax.ppermute(rows, 'split', [(0, 2), (1, 3), (2, 0), (3, 1)])  16.3 us
    dot_general x4, matrix products, dots(): s = jnp.einsum('qe,ke->qk', q_emb, k_a, preferred_element_type=jnp.float32)  12.9 us
    all_to_all x1, blocking collectives, local(): lax.all_to_all(best.reshape(n_grp, cap), 'grp', split_axis=0, concat_axis...  10.4 us
    all_to_all x1, starting transfers between devices, route(): got = lax.all_to_all(send, 'grp', split_axis=0, concat_axis=0, tiled=True)  7.25 us
    dot_general x1, matrix products, embed_rows(): jnp.einsum('...h,he->...e', rows, weight, preferred_element_type=jnp.floa...  5.95 us
    ppermute x1, waiting for transfers between devices, local(): par_place = lax.ppermute(place, 'split', cross)  5.02 us
    all_to_all x1, starting transfers between devices, local(): got = lax.all_to_all(send, 'grp', split_axis=0, concat_axis=0, tiled=True)  4.43 us
  transfers between devices with their start and end apart: 12, of which 5 were waited for; matrix products, arithmetic and copies ran while one was open for 19% of the time, Pallas kernels for 0%

profile of v14, /device:TPU:0, one launch (start us, length us, event | category | flops | bytes accessed | tf_op | source)
XLA Modules:
  0.0 108.9 jit_solution(15858984279237302833)
XLA Ops:
  0.0 0.9 fusion.21
  1.1 0.8 copy-done
  1.9 5.9 %multiply_reduce_fusion = (f32[384]{0:T(512)S(1)}, f32[384,1024]{1,0:T(8,128)S(1)}) fusion(bf16[384,4096]{1,0:T(8,128)(2,1)S(1)} %copy-done, bf16[4096,1024]{1,0:T(8,128)(2,1)} %param.6), kind=kOutput, calls=%fused_computation.5 | convolution fusion | flops 3222011392 | bytes 13108736 | tf_op jit(solution)/shard_map/...h,he->...e/dot_general | solution.py:14
  8.4 0.6 copy-done.1
  9.0 1.9 %convolution_convert_fusion = bf16[768,768]{1,0:T(8,128)(2,1)} fusion(bf16[384,1024]{1,0:T(8,128)(2,1)S(1)} %multiply_convert_fusion, bf16[384,128]{1,0:T(8,128)(2,1)S(1)} %select_convert_fusion, s32[384]{0:T(512)S(1)} %convert_add_fusion, pred[768]{0:T(1024)(128)(4,1)S(1)} %copy-done.3, pred[768]{0:T(1024)(128)(4,1)S(1)} %iota_compare_fusion.10), kind=kOutput, calls=%fused_computation.6 | convolution fusion | flops 454459392 | bytes 1871872 | tf_op jit(solution)/shard_map/dot_general | solution.py:65
  10.9 7.3 %all-to-all-start = ((bf16[8,96,768]{2,1,0:T(8,128)(2,1)}), bf16[8,96,768]{2,1,0:T(8,128)(2,1)}, u32[]{:S(2)}, u32[]{:S(2)}) async-start(bf16[8,96,768]{2,1,0:T(8,128)(2,1)} %bitcast.32), calls=%async_computation | async-start | bytes 2359296 | tf_op jit(solution)/shard_map/all_to_all | solution.py:67
  18.1 1.0 slice.79
  19.1 1.6 %collective-permute-start.1 = (bf16[384,384]{1,0:T(8,128)(2,1)S(1)}, bf16[384,384]{1,0:T(8,128)(2,1)S(1)}, u32[]{:S(2)}, u32[]{:S(2)}) collective-permute-start(bf16[384,384]{1,0:T(8,128)(2,1)S(1)} %slice.79), channel_id=1, source_target_pairs={{0,2},{2,0},{1,3},{3,1},{4,6},{6,4},{5,7},{7,5},{8,10},{10,8},{9,1... | collective-permute-start | bytes 884744 | tf_op jit(solution)/shard_map/ppermute | solution.py:75
  21.2 1.5 %convolution_convert_fusion.2 = bf16[768,384]{1,0:T(8,128)(2,1)S(1)} fusion(s32[384]{0:T(512)S(1)} %convert_add_fusion, bf16[384,1024]{1,0:T(8,128)(2,1)} %copy-done.1), kind=kOutput, calls=%fused_computation.8 | convolution fusion | flops 227082240 | bytes 886272 | tf_op jit(solution)/shard_map/dot_general | solution.py:87
  22.7 5.0 %collective-permute-done = s32[384]{0:T(512)S(1)} collective-permute-done((s32[384]{0:T(512)S(1)}, s32[384]{0:T(512)S(1)}, u32[]{:S(2)}, u32[]{:S(2)}) %collective-permute-start) | collective-permute-done | bytes 1568 | tf_op jit(solution)/shard_map/ppermute | solution.py:76
  28.2 1.1 %pad_maximum_fusion = bf16[8,192,384]{2,1,0:T(8,128)(2,1)} fusion(bf16[8,96,384]{2,1,0:T(8,128)(2,1)S(1)} %bitcast.34, bf16[8,96,384]{2,1,0:T(8,128)(2,1)S(1)} %bitcast.33), kind=kLoop, calls=%fused_computation.9 | loop fusion | flops 2359296 | bytes 2359296 | tf_op jit(solution)/shard_map/concatenate | solution.py:89
  29.4 17.5 %all-to-all-done = bf16[8,96,768]{2,1,0:T(8,128)(2,1)} async-done(((bf16[8,96,768]{2,1,0:T(8,128)(2,1)}), bf16[8,96,768]{2,1,0:T(8,128)(2,1)}, u32[]{:S(2)}, u32[]{:S(2)}) %all-to-all-start) | async-done | bytes 1179680 | tf_op jit(solution)/shard_map/all_to_all | solution.py:67
  46.8 2.3 %slice.78 = bf16[768,640]{1,0:T(8,128)(2,1)} slice(bf16[768,768]{1,0:T(8,128)(2,1)} %bitcast.1), slice={[0:768], [0:640]} | slice | bytes 1966080 | tf_op jit(solution)/shard_map/slice | solution.py:31
  49.1 4.4 %all-to-all-start.1 = ((bf16[8,192,384]{2,1,0:T(8,128)(2,1)}), bf16[8,192,384]{2,1,0:T(8,128)(2,1)}, u32[]{:S(2)}, u32[]{:S(2)}) async-start(bf16[8,192,384]{2,1,0:T(8,128)(2,1)} %pad_maximum_fusion), calls=%async_computation.1 | async-start | bytes 2359296 | tf_op jit(solution)/shard_map/all_to_all | solution.py:94
  53.5 2.1 %convert_reduce_fusion = (f32[768]{0:T(1024)S(1)}, f32[768]{0:T(1024)S(1)}) fusion(bf16[768,768]{1,0:T(8,128)(2,1)} %bitcast.1), kind=kLoop, calls=%fused_computation.25 | loop fusion | flops 6144 | bytes 12288 | tf_op jit(solution)/shard_map/eq | solution.py:112
  55.6 1.6 %collective-permute-start.3 = (bf16[768,640]{1,0:T(8,128)(2,1)}, bf16[768,640]{1,0:T(8,128)(2,1)}, u32[]{:S(2)}, u32[]{:S(2)}) collective-permute-start(bf16[768,640]{1,0:T(8,128)(2,1)} %slice.78), channel_id=1, source_target_pairs={{0,2},{1,3},{2,0},{3,1},{4,6},{5,7},{6,4},{7,5},{8,10},{9,11},{10,... | collective-permute-start | bytes 2949128 | tf_op jit(solution)/shard_map/ppermute | solution.py:21
  57.2 4.1 %fusion.30 = f32[768,768]{0,1:T(8,128)} fusion(bf16[768,640]{1,0:T(8,128)(2,1)} %slice.78), kind=kOutput, calls=%fused_computation.86 | convolution fusion | flops 754974720 | bytes 3342336 | tf_op jit(solution)/shard_map/qe,ke->qk/dot_general | solution.py:108
  61.2 0.6 collective-permute-start.2
  62.3 16.3 %collective-permute-done.2 = f32[2,768]{1,0:T(2,128)S(1)} collective-permute-done((f32[2,768]{1,0:T(2,128)S(1)}, f32[2,768]{1,0:T(2,128)S(1)}, u32[]{:S(2)}, u32[]{:S(2)}) %collective-permute-start.2) | collective-permute-done | bytes 6176 | tf_op jit(solution)/shard_map/ppermute | solution.py:21
  78.8 1.1 %collective-permute-done.7 = f32[2,768]{1,0:T(2,128)S(1)} collective-permute-done((f32[2,768]{1,0:T(2,128)S(1)}, f32[2,768]{1,0:T(2,128)S(1)}, u32[]{:S(2)}, u32[]{:S(2)}) %collective-permute-start.7) | collective-permute-done | bytes 6176 | tf_op jit(solution)/shard_map/ppermute | solution.py:23
  80.2 1.5 %all-to-all-done.1 = bf16[8,192,384]{2,1,0:T(8,128)(2,1)} async-done(((bf16[8,192,384]{2,1,0:T(8,128)(2,1)}), bf16[8,192,384]{2,1,0:T(8,128)(2,1)}, u32[]{:S(2)}, u32[]{:S(2)}) %all-to-all-start.1) | async-done | bytes 1179680 | tf_op jit(solution)/shard_map/all_to_all | solution.py:94
  81.8 1.4 %fusion.29 = (bf16[8,96,384]{2,1,0:T(8,128)(2,1)S(1)}, bf16[8,96,384]{2,1,0:T(8,128)(2,1)S(1)}) fusion(bf16[8,192,384]{2,1,0:T(8,128)(2,1)} %all-to-all-done.1), kind=kLoop, calls=%fused_computation.85 | loop fusion | bytes 2359296 | tf_op jit(solution)/shard_map/slice | solution.py:96
  83.2 0.8 fusion.31
  84.6 3.0 %select_reduce_fusion.2 = f32[768]{0:T(1024)S(1)} fusion(f32[768,768]{0,1:T(8,128)S(1)} %fusion.31, bf16[768,640]{1,0:T(8,128)(2,1)} %slice.78, bf16[768,640]{1,0:T(8,128)(2,1)} %collective-permute-done.3, f32[768]{0:T(1024)S(1)} %get-tuple-element.10, f32[768]{0:T(1024)S(1)} %get-tuple-element.9, f32[768]{0:T(1024)S(1)} %get-tuple-element.12, ...), kind=kOutput, calls=%fused_computation.2 | convolution fusion | flops 759102720 | bytes 4341504 | tf_op jit(solution)/shard_map/qe,ke->qk/dot_general | solution.py:108
  87.6 1.1 %select_reduce_fusion.3 = f32[768]{0:T(1024)S(1)} fusion(f32[768,768]{0,1:T(8,128)S(1)} %copy-done.4, bf16[768,384]{1,0:T(8,128)(2,1)S(1)} %bitcast.27, f32[768]{0:T(1024)S(1)} %get-tuple-element.10, f32[768]{0:T(1024)S(1)} %get-tuple-element.9, pred[768]{0:T(1024)(128)(4,1)S(1)} %broadcast_compare_fusion), kind=kOutput, calls=%fused_computation.3 | convolution fusion | flops 457112832 | bytes 2959104 | tf_op jit(solution)/shard_map/qe,ke->qk/dot_general | solution.py:109
  88.8 0.8 fusion.32
  89.6 0.8 fusion.33
  90.4 2.9 %select_reduce_fusion.1 = f32[768]{0:T(1024)S(1)} fusion(f32[768,768]{0,1:T(8,128)S(1)} %fusion.32, bf16[768,640]{1,0:T(8,128)(2,1)} %slice.78, bf16[768,640]{1,0:T(8,128)(2,1)} %collective-permute-done.5, f32[768]{0:T(1024)S(1)} %get-tuple-element.10, f32[768]{0:T(1024)S(1)} %get-tuple-element.9, f32[768]{0:T(1024)S(1)} %get-tuple-element.14, ...), kind=kOutput, calls=%fused_computation.1 | convolution fusion | flops 759102720 | bytes 4341504 | tf_op jit(solution)/shard_map/qe,ke->qk/dot_general | solution.py:108
  93.3 2.9 %select_reduce_fusion = f32[768]{0:T(1024)S(1)} fusion(f32[768,768]{0,1:T(8,128)S(1)} %fusion.33, bf16[768,640]{1,0:T(8,128)(2,1)} %slice.78, bf16[768,640]{1,0:T(8,128)(2,1)} %collective-permute-done.8, f32[768]{0:T(1024)S(1)} %get-tuple-element.10, f32[768]{0:T(1024)S(1)} %get-tuple-element.9, f32[768]{0:T(1024)S(1)} %get-tuple-element.16, ...), kind=kOutput, calls=%fused_computation | convolution fusion | flops 759102720 | bytes 4341504 | tf_op jit(solution)/shard_map/qe,ke->qk/dot_general | solution.py:108
  96.3 10.4 %all_to_all.16 = f32[8,1,96]{2,1,0:T(1,128)S(1)} all-to-all(f32[8,1,96]{2,1,0:T(1,128)S(1)} %max.41), channel_id=1, replica_groups=mesh['grp'=8,'split'=4] {'grp'}, dimensions={0} | all-to-all | bytes 6144 | tf_op jit(solution)/shard_map/all_to_all | solution.py:120
  107.2 0.7 reduce.29
  108.3 0.6 fusion.25
  (48 shorter events, 4.3 us)
Async XLA Ops:
  0.0 1.9 %copy-start = (bf16[384,4096]{1,0:T(8,128)(2,1)S(1)}, bf16[384,4096]{1,0:T(8,128)(2,1)}, u32[]{:S(2)}) copy-start(bf16[384,4096]{1,0:T(8,128)(2,1)} %param.5) | copy-start | bytes 9437188
  1.9 6.0 %copy-start.2 = (s32[384]{0:T(512)S(1)}, s32[384]{0:T(512)}, u32[]{:S(2)}) copy-start(s32[384]{0:T(512)} %param.8) | copy-start | bytes 4612
  7.9 1.1 %copy-start.3 = (pred[768]{0:T(1024)(128)(4,1)S(1)}, pred[768]{0:T(1024)(128)(4,1)}, u32[]{:S(2)}) copy-start(pred[768]{0:T(1024)(128)(4,1)} %constant.58.clone.1) | copy-start | bytes 2308
  8.1 0.9 copy-start.1
  10.9 35.9 %all-to-all-start = ((bf16[8,96,768]{2,1,0:T(8,128)(2,1)}), bf16[8,96,768]{2,1,0:T(8,128)(2,1)}, u32[]{:S(2)}, u32[]{:S(2)}) async-start(bf16[8,96,768]{2,1,0:T(8,128)(2,1)} %bitcast.32), calls=%async_computation | async-start | bytes 2359296 | tf_op jit(solution)/shard_map/all_to_all | solution.py:67
  19.1 8.6 %collective-permute-start.1 = (bf16[384,384]{1,0:T(8,128)(2,1)S(1)}, bf16[384,384]{1,0:T(8,128)(2,1)S(1)}, u32[]{:S(2)}, u32[]{:S(2)}) collective-permute-start(bf16[384,384]{1,0:T(8,128)(2,1)S(1)} %slice.79), channel_id=1, source_target_pairs={{0,2},{2,0},{1,3},{3,1},{4,6},{6,4},{5,7},{7,5},{8,10},{10,8},{9,1... | collective-permute-start | bytes 884744 | tf_op jit(solution)/shard_map/ppermute | solution.py:75
  20.7 7.0 %collective-permute-start = (s32[384]{0:T(512)S(1)}, s32[384]{0:T(512)S(1)}, u32[]{:S(2)}, u32[]{:S(2)}) collective-permute-start(s32[384]{0:T(512)S(1)} %convert_add_fusion), channel_id=1, source_target_pairs={{0,2},{2,0},{1,3},{3,1},{4,6},{6,4},{5,7},{7,5},{8,10},{10,8},{9,1... | collective-permute-start | bytes 4616 | tf_op jit(solution)/shard_map/ppermute | solution.py:76
  49.1 32.7 %all-to-all-start.1 = ((bf16[8,192,384]{2,1,0:T(8,128)(2,1)}), bf16[8,192,384]{2,1,0:T(8,128)(2,1)}, u32[]{:S(2)}, u32[]{:S(2)}) async-start(bf16[8,192,384]{2,1,0:T(8,128)(2,1)} %pad_maximum_fusion), calls=%async_computation.1 | async-start | bytes 2359296 | tf_op jit(solution)/shard_map/all_to_all | solution.py:94
  55.6 24.4 %collective-permute-start.3 = (bf16[768,640]{1,0:T(8,128)(2,1)}, bf16[768,640]{1,0:T(8,128)(2,1)}, u32[]{:S(2)}, u32[]{:S(2)}) collective-permute-start(bf16[768,640]{1,0:T(8,128)(2,1)} %slice.78), channel_id=1, source_target_pairs={{0,2},{1,3},{2,0},{3,1},{4,6},{5,7},{6,4},{7,5},{8,10},{9,11},{10,... | collective-permute-start | bytes 2949128 | tf_op jit(solution)/shard_map/ppermute | solution.py:21
  61.2 17.4 %collective-permute-start.2 = (f32[2,768]{1,0:T(2,128)S(1)}, f32[2,768]{1,0:T(2,128)S(1)}, u32[]{:S(2)}, u32[]{:S(2)}) collective-permute-start(f32[2,768]{1,0:T(2,128)S(1)} %pad_maximum_fusion.1), channel_id=1, source_target_pairs={{0,2},{1,3},{2,0},{3,1},{4,6},{5,7},{6,4},{7,5},{8,10},{9,11},{10,... | collective-permute-start | bytes 18440 | tf_op jit(solution)/shard_map/ppermute | solution.py:21
  61.8 16.9 %collective-permute-start.4 = (f32[2,768]{1,0:T(2,128)S(1)}, f32[2,768]{1,0:T(2,128)S(1)}, u32[]{:S(2)}, u32[]{:S(2)}) collective-permute-start(f32[2,768]{1,0:T(2,128)S(1)} %pad_maximum_fusion.1), channel_id=1, source_target_pairs={{0,1},{1,0},{2,3},{3,2},{4,5},{5,4},{6,7},{7,6},{8,9},{9,8},{10,11... | collective-permute-start | bytes 18440 | tf_op jit(solution)/shard_map/ppermute | solution.py:23
  61.8 28.5 %collective-permute-start.5 = (bf16[768,640]{1,0:T(8,128)(2,1)}, bf16[768,640]{1,0:T(8,128)(2,1)}, u32[]{:S(2)}, u32[]{:S(2)}) collective-permute-start(bf16[768,640]{1,0:T(8,128)(2,1)} %slice.78), channel_id=1, source_target_pairs={{0,1},{1,0},{2,3},{3,2},{4,5},{5,4},{6,7},{7,6},{8,9},{9,8},{10,11... | collective-permute-start | bytes 2949128 | tf_op jit(solution)/shard_map/ppermute | solution.py:23
  78.7 1.2 %collective-permute-start.7 = (f32[2,768]{1,0:T(2,128)S(1)}, f32[2,768]{1,0:T(2,128)S(1)}, u32[]{:S(2)}, u32[]{:S(2)}) collective-permute-start(f32[2,768]{1,0:T(2,128)S(1)} %collective-permute-done.2), channel_id=1, source_target_pairs={{0,1},{1,0},{2,3},{3,2},{4,5},{5,4},{6,7},{7,6},{8,9},{9,8},{10,11... | collective-permute-start | bytes 18440 | tf_op jit(solution)/shard_map/ppermute | solution.py:23
  80.0 13.3 %collective-permute-start.8 = (bf16[768,640]{1,0:T(8,128)(2,1)}, bf16[768,640]{1,0:T(8,128)(2,1)}, u32[]{:S(2)}, u32[]{:S(2)}) collective-permute-start(bf16[768,640]{1,0:T(8,128)(2,1)} %collective-permute-done.3), channel_id=1, source_target_pairs={{0,1},{1,0},{2,3},{3,2},{4,5},{5,4},{6,7},{7,6},{8,9},{9,8},{10,11... | collective-permute-start | bytes 2949128 | tf_op jit(solution)/shard_map/ppermute | solution.py:23
  83.1 5.6 %collective-permute-start.6 = (bf16[768,384]{1,0:T(8,128)(2,1)S(1)}, bf16[768,384]{1,0:T(8,128)(2,1)S(1)}, u32[]{:S(2)}, u32[]{:S(2)}) collective-permute-start(bf16[768,384]{1,0:T(8,128)(2,1)S(1)} %bitcast.25), channel_id=1, source_target_pairs={{0,1},{1,0},{2,3},{3,2},{4,5},{5,4},{6,7},{7,6},{8,9},{9,8},{10,11... | collective-permute-start | bytes 1769480 | tf_op jit(solution)/shard_map/ppermute | solution.py:97
  84.0 5.5 %collective-permute-start.9 = (bf16[768,384]{1,0:T(8,128)(2,1)S(1)}, bf16[768,384]{1,0:T(8,128)(2,1)S(1)}, u32[]{:S(2)}, u32[]{:S(2)}) collective-permute-start(bf16[768,384]{1,0:T(8,128)(2,1)S(1)} %bitcast.31), channel_id=1, source_target_pairs={{0,1},{1,0},{2,3},{3,2},{4,5},{5,4},{6,7},{7,6},{8,9},{9,8},{10,11... | collective-permute-start | bytes 1769480 | tf_op jit(solution)/shard_map/ppermute | solution.py:97
  84.6 3.0 %copy-start.4 = (f32[768,768]{0,1:T(8,128)S(1)}, f32[768,768]{0,1:T(8,128)}, u32[]{:S(2)}) copy-start(f32[768,768]{0,1:T(8,128)} %fusion.30) | copy-start | bytes 7077892

commit v15 on v12

--- a/solution.py
+++ b/solution.py
@@ -107,14 +107,17 @@
         s = jnp.einsum("qe,ke->qk", q_emb, k_a, preferred_element_type=jnp.float32)
         return s + jnp.einsum("qe,ke->qk", got_b, k_b, preferred_element_type=jnp.float32)
 
-    scores = dots(q_emb, got_b)
-    hits = (q_lab[:, None] == q_lab[None, :]) & (q_lab[None, :] > 0) & (q_ord[None, :] < q_ord[:, None])
-    best = jnp.max(jnp.where(hits, scores, jnp.float32(-1.0)), axis=1)
+    q_base = q_lab * 1048576.0
+    q_code = q_base + q_ord
+
+    def block_best(scores, k_lab, k_ord):
+        k_code = k_lab * 1048576.0 + k_ord
+        hits = (k_code[None, :] >= q_base[:, None]) & (k_code[None, :] < q_code[:, None])
+        return jnp.max(jnp.where(hits, scores, jnp.float32(-1.0)), axis=1)
+
+    best = block_best(dots(q_emb, got_b), q_lab, q_ord)
     for k_a, k_b, k_m in zip(keys_a, keys_b, keys_m):
-        k_lab, k_ord = k_m[0], k_m[1]
-        scores = dots(k_a, k_b)
-        hits = (q_lab[:, None] == k_lab[None, :]) & (k_lab[None, :] > 0) & (k_ord[None, :] < q_ord[:, None])
-        best = jnp.maximum(best, jnp.max(jnp.where(hits, scores, jnp.float32(-1.0)), axis=1))
+        best = jnp.maximum(best, block_best(dots(k_a, k_b), k_m[0], k_m[1]))
 
     returned = lax.all_to_all(
         best.reshape(n_grp, cap), "grp", split_axis=0, concat_axis=0, tiled=True

time: 107 us -> 109 us (1.019)
  local copies, waits for them, and re-layouts: 8 us -> 6.07 us
  blocking collectives: 10.3 us -> 12.2 us
  other arithmetic: 4.95 us -> 6.76 us
    all_to_all x1, waiting for transfers between devices: 1.84 us -> 15.3 us  [local(): got = lax.all_to_all(send, 'grp', split_axis=0, concat_axis=0, tiled=True)]
    ppermute x2, waiting for transfers between devices: 14.8 us -> 1.44 us  [gather_split(): cross = lax.ppermute(rows, 'split', [(0, 2), (1, 3), (2, 0), (3, 1)])]
    convert_element_type x0 -> x1, other arithmetic: none -> 2.02 us  [unpack(): lab = buf[:, emb_w].astype(jnp.float32)]
    all_to_all x1, blocking collectives: 10.3 us -> 12.2 us  [local(): lax.all_to_all(best.reshape(n_grp, cap), 'grp', split_axis=0, concat_axis...]
    unnamed x14 -> x8, local copies, waits for them, and re-layouts: 2.52 us -> 0.67 us
    eq x1 -> x0, other arithmetic: 1.81 us -> none  [local(): q_lab[:, None] == q_lab[None, :]]
  transfers between devices with their start and end apart: 12 -> 12, of which waited for: 5 -> 6; matrix products, arithmetic and copies ran while one was open for 22% -> 21% of each run, Pallas kernels for 0% -> 0%
where the time goes in v15:
time: 109 us
  waiting for transfers between devices  41.2 us (38%)
  matrix products  25.2 us (23%)
  starting transfers between devices  16.9 us (16%)
  blocking collectives  12.2 us (11%)
  other arithmetic  6.76 us (6%)
  local copies, waits for them, and re-layouts  6.07 us (6%)
    all_to_all x1, waiting for transfers between devices, route(): got = lax.all_to_all(send, 'grp', split_axis=0, concat_axis=0, tiled=True)  17.5 us
    all_to_all x1, waiting for transfers between devices, local(): got = lax.all_to_all(send, 'grp', split_axis=0, concat_axis=0, tiled=True)  15.3 us
    all_to_all x1, blocking collectives, local(): lax.all_to_all(best.reshape(n_grp, cap), 'grp', split_axis=0, concat_axis...  12.2 us
    dot_general x4, matrix products, dots(): s = jnp.einsum('qe,ke->qk', q_emb, k_a, preferred_element_type=jnp.float32)  12 us
    all_to_all x1, starting transfers between devices, route(): got = lax.all_to_all(send, 'grp', split_axis=0, concat_axis=0, tiled=True)  7.25 us
    dot_general x1, matrix products, embed_rows(): jnp.einsum('...h,he->...e', rows, weight, preferred_element_type=jnp.floa...  5.94 us
    ppermute x1, waiting for transfers between devices, local(): par_place = lax.ppermute(place, 'split', cross)  5.02 us
    all_to_all x1, starting transfers between devices, local(): got = lax.all_to_all(send, 'grp', split_axis=0, concat_axis=0, tiled=True)  4.27 us
  transfers between devices with their start and end apart: 12, of which 6 were waited for; matrix products, arithmetic and copies ran while one was open for 21% of the time, Pallas kernels for 0%

profile of v15, /device:TPU:0, one launch (start us, length us, event | category | flops | bytes accessed | tf_op | source)
XLA Modules:
  0.0 108.5 jit_solution(6718938782611019326)
XLA Ops:
  0.0 0.8 convert_element_type.114
  0.9 0.8 fusion.20
  1.9 5.9 %multiply_reduce_fusion = (f32[384]{0:T(512)S(1)}, f32[384,1024]{1,0:T(8,128)S(1)}) fusion(bf16[384,4096]{1,0:T(8,128)(2,1)S(1)} %copy-done, bf16[4096,1024]{1,0:T(8,128)(2,1)} %param.6), kind=kOutput, calls=%fused_computation.5 | convolution fusion | flops 3222011392 | bytes 13108736 | tf_op jit(solution)/shard_map/...h,he->...e/dot_general | solution.py:14
  8.3 0.6 copy-done.1
  9.0 1.8 %convolution_convert_fusion = bf16[768,768]{1,0:T(8,128)(2,1)} fusion(bf16[384,1024]{1,0:T(8,128)(2,1)S(1)} %multiply_convert_fusion, bf16[384,128]{1,0:T(8,128)(2,1)S(1)} %select_convert_fusion, s32[384]{0:T(512)S(1)} %convert_add_fusion.1, pred[768]{0:T(1024)(128)(4,1)S(1)} %copy-done.2, pred[768]{0:T(1024)(128)(4,1)S(1)} %iota_compare_fusion.9), kind=kOutput, calls=%fused_computation.6 | convolution fusion | flops 454459392 | bytes 1871872 | tf_op jit(solution)/shard_map/dot_general | solution.py:65
  10.8 7.3 %all-to-all-start = ((bf16[8,96,768]{2,1,0:T(8,128)(2,1)}), bf16[8,96,768]{2,1,0:T(8,128)(2,1)}, u32[]{:S(2)}, u32[]{:S(2)}) async-start(bf16[8,96,768]{2,1,0:T(8,128)(2,1)} %bitcast.27), calls=%async_computation | async-start | bytes 2359296 | tf_op jit(solution)/shard_map/all_to_all | solution.py:67
  18.1 1.0 slice.67
  19.1 1.6 %collective-permute-start.1 = (bf16[384,384]{1,0:T(8,128)(2,1)S(1)}, bf16[384,384]{1,0:T(8,128)(2,1)S(1)}, u32[]{:S(2)}, u32[]{:S(2)}) collective-permute-start(bf16[384,384]{1,0:T(8,128)(2,1)S(1)} %slice.67), channel_id=1, source_target_pairs={{0,2},{2,0},{1,3},{3,1},{4,6},{6,4},{5,7},{7,5},{8,10},{10,8},{9,1... | collective-permute-start | bytes 884744 | tf_op jit(solution)/shard_map/ppermute | solution.py:75
  21.1 1.5 %convolution_convert_fusion.2 = bf16[768,384]{1,0:T(8,128)(2,1)S(1)} fusion(s32[384]{0:T(512)S(1)} %convert_add_fusion.1, bf16[384,1024]{1,0:T(8,128)(2,1)} %copy-done.1), kind=kOutput, calls=%fused_computation.8 | convolution fusion | flops 227082240 | bytes 886272 | tf_op jit(solution)/shard_map/dot_general | solution.py:88
  22.6 5.0 %collective-permute-done = s32[384]{0:T(512)S(1)} collective-permute-done((s32[384]{0:T(512)S(1)}, s32[384]{0:T(512)S(1)}, u32[]{:S(2)}, u32[]{:S(2)}) %collective-permute-start) | collective-permute-done | bytes 1568 | tf_op jit(solution)/shard_map/ppermute | solution.py:76
  28.1 1.1 %pad_maximum_fusion = bf16[8,192,384]{2,1,0:T(8,128)(2,1)} fusion(bf16[8,96,384]{2,1,0:T(8,128)(2,1)S(1)} %bitcast.29, bf16[8,96,384]{2,1,0:T(8,128)(2,1)S(1)} %bitcast.28), kind=kLoop, calls=%fused_computation.9 | loop fusion | flops 2359296 | bytes 2359296 | tf_op jit(solution)/shard_map/concatenate | solution.py:90
  29.3 17.5 %all-to-all-done = bf16[8,96,768]{2,1,0:T(8,128)(2,1)} async-done(((bf16[8,96,768]{2,1,0:T(8,128)(2,1)}), bf16[8,96,768]{2,1,0:T(8,128)(2,1)}, u32[]{:S(2)}, u32[]{:S(2)}) %all-to-all-start) | async-done | bytes 1179680 | tf_op jit(solution)/shard_map/all_to_all | solution.py:67
  46.7 4.3 %all-to-all-start.1 = ((bf16[8,192,384]{2,1,0:T(8,128)(2,1)}), bf16[8,192,384]{2,1,0:T(8,128)(2,1)}, u32[]{:S(2)}, u32[]{:S(2)}) async-start(bf16[8,192,384]{2,1,0:T(8,128)(2,1)} %pad_maximum_fusion), calls=%async_computation.1 | async-start | bytes 2359296 | tf_op jit(solution)/shard_map/all_to_all | solution.py:93
  51.0 2.0 %convert_reduce_fusion = (f32[768]{0:T(1024)S(1)}, f32[768]{0:T(1024)S(1)}, f32[768]{0:T(1024)S(1)}, f32[768]{0:T(1024)S(1)}) fusion(bf16[768,768]{1,0:T(8,128)(2,1)} %bitcast.1), kind=kLoop, calls=%fused_computation.24 | loop fusion | flops 7680 | bytes 18432 | tf_op jit(solution)/shard_map/convert_element_type | solution.py:32
  53.1 1.6 %collective-permute-start.2 = (f32[2,768]{1,0:T(2,128)S(1)}, f32[2,768]{1,0:T(2,128)S(1)}, u32[]{:S(2)}, u32[]{:S(2)}) collective-permute-start(f32[2,768]{1,0:T(2,128)S(1)} %pad_maximum_fusion.1), channel_id=1, source_target_pairs={{0,2},{1,3},{2,0},{3,1},{4,6},{5,7},{6,4},{7,5},{8,10},{9,11},{10,... | collective-permute-start | bytes 18440 | tf_op jit(solution)/shard_map/ppermute | solution.py:21
  54.7 4.0 %fusion.29 = f32[768,768]{0,1:T(8,128)} fusion(bf16[768,768]{1,0:T(8,128)(2,1)} %bitcast.1), kind=kOutput, calls=%fused_computation.77 | convolution fusion | flops 754974720 | bytes 3342336 | tf_op jit(solution)/shard_map/qe,ke->qk/dot_general | solution.py:107
  58.7 2.2 %slice.66 = bf16[768,640]{1,0:T(8,128)(2,1)} slice(bf16[768,768]{1,0:T(8,128)(2,1)} %bitcast.1), slice={[0:768], [0:640]} | slice | bytes 1966080 | tf_op jit(solution)/shard_map/slice | solution.py:31
  62.1 1.9 %collective-permute-done.7 = f32[2,768]{1,0:T(2,128)S(1)} collective-permute-done((f32[2,768]{1,0:T(2,128)S(1)}, f32[2,768]{1,0:T(2,128)S(1)}, u32[]{:S(2)}, u32[]{:S(2)}) %collective-permute-start.7) | collective-permute-done | bytes 6176 | tf_op jit(solution)/shard_map/ppermute | solution.py:23
  64.0 15.3 %all-to-all-done.1 = bf16[8,192,384]{2,1,0:T(8,128)(2,1)} async-done(((bf16[8,192,384]{2,1,0:T(8,128)(2,1)}), bf16[8,192,384]{2,1,0:T(8,128)(2,1)}, u32[]{:S(2)}, u32[]{:S(2)}) %all-to-all-start.1) | async-done | bytes 1179680 | tf_op jit(solution)/shard_map/all_to_all | solution.py:93
  79.4 1.5 %fusion.31 = (bf16[8,96,384]{2,1,0:T(8,128)(2,1)S(1)}, bf16[8,96,384]{2,1,0:T(8,128)(2,1)S(1)}) fusion(bf16[8,192,384]{2,1,0:T(8,128)(2,1)} %all-to-all-done.1), kind=kLoop, calls=%fused_computation.79 | loop fusion | bytes 2359296 | tf_op jit(solution)/shard_map/slice | solution.py:95
  81.4 0.9 select_reduce_fusion.3
  82.4 0.8 fusion.32
  83.2 0.8 fusion.33
  84.0 1.4 %collective-permute-done.3 = bf16[768,640]{1,0:T(8,128)(2,1)} collective-permute-done((bf16[768,640]{1,0:T(8,128)(2,1)}, bf16[768,640]{1,0:T(8,128)(2,1)}, u32[]{:S(2)}, u32[]{:S(2)}) %collective-permute-start.3) | collective-permute-done | bytes 983072 | tf_op jit(solution)/shard_map/ppermute | solution.py:21
  85.4 0.8 fusion.34
  86.2 2.8 %select_reduce_fusion.2 = f32[768]{0:T(1024)S(1)} fusion(f32[768,768]{0,1:T(8,128)S(1)} %fusion.32, bf16[768,640]{1,0:T(8,128)(2,1)} %collective-permute-done.3, f32[768]{0:T(1024)S(1)} %get-tuple-element.7, f32[768]{0:T(1024)S(1)} %get-tuple-element.8, f32[768]{0:T(1024)S(1)} %fusion.18, bf16[768,768]{1,0:T(8,128)(2,1)} %bitcast.1), kind=kOutput, calls=%fused_computation.2 | convolution fusion | flops 758512896 | bytes 4337664 | tf_op jit(solution)/shard_map/qe,ke->qk/dot_general | solution.py:107
  89.0 2.8 %select_reduce_fusion.1 = f32[768]{0:T(1024)S(1)} fusion(f32[768,768]{0,1:T(8,128)S(1)} %fusion.33, bf16[768,640]{1,0:T(8,128)(2,1)} %collective-permute-done.5, f32[768]{0:T(1024)S(1)} %get-tuple-element.7, f32[768]{0:T(1024)S(1)} %get-tuple-element.8, f32[768]{0:T(1024)S(1)} %fusion.17, bf16[768,768]{1,0:T(8,128)(2,1)} %bitcast.1), kind=kOutput, calls=%fused_computation.1 | convolution fusion | flops 758512896 | bytes 4337664 | tf_op jit(solution)/shard_map/qe,ke->qk/dot_general | solution.py:107
  91.8 2.5 %select_reduce_fusion = f32[768]{0:T(1024)S(1)} fusion(f32[768,768]{0,1:T(8,128)S(1)} %fusion.34, bf16[768,640]{1,0:T(8,128)(2,1)S(1)} %collective-permute-done.8, f32[768]{0:T(1024)S(1)} %get-tuple-element.7, f32[768]{0:T(1024)S(1)} %get-tuple-element.8, f32[768]{0:T(1024)S(1)} %fusion.16, bf16[768,768]{1,0:T(8,128)(2,1)} %bitcast.1), kind=kOutput, calls=%fused_computation | convolution fusion | flops 758512896 | bytes 4337664 | tf_op jit(solution)/shard_map/qe,ke->qk/dot_general | solution.py:107
  94.3 12.2 %all_to_all.16 = f32[8,1,96]{2,1,0:T(1,128)S(1)} all-to-all(f32[8,1,96]{2,1,0:T(1,128)S(1)} %max.41), channel_id=1, replica_groups=mesh['grp'=8,'split'=4] {'grp'}, dimensions={0} | all-to-all | bytes 6144 | tf_op jit(solution)/shard_map/all_to_all | solution.py:122
  106.5 0.5 broadcast.154
  107.0 0.7 reduce.18
  107.7 0.8 select_reduce_fusion.4
  (41 shorter events, 3.6 us)
Async XLA Ops:
  0.0 1.9 %copy-start = (bf16[384,4096]{1,0:T(8,128)(2,1)S(1)}, bf16[384,4096]{1,0:T(8,128)(2,1)}, u32[]{:S(2)}) copy-start(bf16[384,4096]{1,0:T(8,128)(2,1)} %param.5) | copy-start | bytes 9437188
  7.9 1.1 %copy-start.2 = (pred[768]{0:T(1024)(128)(4,1)S(1)}, pred[768]{0:T(1024)(128)(4,1)}, u32[]{:S(2)}) copy-start(pred[768]{0:T(1024)(128)(4,1)} %constant.58.clone.1) | copy-start | bytes 2308
  8.0 0.9 copy-start.1
  10.8 35.9 %all-to-all-start = ((bf16[8,96,768]{2,1,0:T(8,128)(2,1)}), bf16[8,96,768]{2,1,0:T(8,128)(2,1)}, u32[]{:S(2)}, u32[]{:S(2)}) async-start(bf16[8,96,768]{2,1,0:T(8,128)(2,1)} %bitcast.27), calls=%async_computation | async-start | bytes 2359296 | tf_op jit(solution)/shard_map/all_to_all | solution.py:67
  19.1 8.6 %collective-permute-start.1 = (bf16[384,384]{1,0:T(8,128)(2,1)S(1)}, bf16[384,384]{1,0:T(8,128)(2,1)S(1)}, u32[]{:S(2)}, u32[]{:S(2)}) collective-permute-start(bf16[384,384]{1,0:T(8,128)(2,1)S(1)} %slice.67), channel_id=1, source_target_pairs={{0,2},{2,0},{1,3},{3,1},{4,6},{6,4},{5,7},{7,5},{8,10},{10,8},{9,1... | collective-permute-start | bytes 884744 | tf_op jit(solution)/shard_map/ppermute | solution.py:75
  20.6 7.0 %collective-permute-start = (s32[384]{0:T(512)S(1)}, s32[384]{0:T(512)S(1)}, u32[]{:S(2)}, u32[]{:S(2)}) collective-permute-start(s32[384]{0:T(512)S(1)} %convert_add_fusion.1), channel_id=1, source_target_pairs={{0,2},{2,0},{1,3},{3,1},{4,6},{6,4},{5,7},{7,5},{8,10},{10,8},{9,1... | collective-permute-start | bytes 4616 | tf_op jit(solution)/shard_map/ppermute | solution.py:76
  46.7 32.6 %all-to-all-start.1 = ((bf16[8,192,384]{2,1,0:T(8,128)(2,1)}), bf16[8,192,384]{2,1,0:T(8,128)(2,1)}, u32[]{:S(2)}, u32[]{:S(2)}) async-start(bf16[8,192,384]{2,1,0:T(8,128)(2,1)} %pad_maximum_fusion), calls=%async_computation.1 | async-start | bytes 2359296 | tf_op jit(solution)/shard_map/all_to_all | solution.py:93
  53.1 8.6 %collective-permute-start.2 = (f32[2,768]{1,0:T(2,128)S(1)}, f32[2,768]{1,0:T(2,128)S(1)}, u32[]{:S(2)}, u32[]{:S(2)}) collective-permute-start(f32[2,768]{1,0:T(2,128)S(1)} %pad_maximum_fusion.1), channel_id=1, source_target_pairs={{0,2},{1,3},{2,0},{3,1},{4,6},{5,7},{6,4},{7,5},{8,10},{9,11},{10,... | collective-permute-start | bytes 18440 | tf_op jit(solution)/shard_map/ppermute | solution.py:21
  60.9 1.2 %collective-permute-start.4 = (f32[2,768]{1,0:T(2,128)S(1)}, f32[2,768]{1,0:T(2,128)S(1)}, u32[]{:S(2)}, u32[]{:S(2)}) collective-permute-start(f32[2,768]{1,0:T(2,128)S(1)} %pad_maximum_fusion.1), channel_id=1, source_target_pairs={{0,1},{1,0},{2,3},{3,2},{4,5},{5,4},{6,7},{7,6},{8,9},{9,8},{10,11... | collective-permute-start | bytes 18440 | tf_op jit(solution)/shard_map/ppermute | solution.py:23
  60.9 24.5 %collective-permute-start.3 = (bf16[768,640]{1,0:T(8,128)(2,1)}, bf16[768,640]{1,0:T(8,128)(2,1)}, u32[]{:S(2)}, u32[]{:S(2)}) collective-permute-start(bf16[768,640]{1,0:T(8,128)(2,1)} %slice.66), channel_id=1, source_target_pairs={{0,2},{1,3},{2,0},{3,1},{4,6},{5,7},{6,4},{7,5},{8,10},{9,11},{10,... | collective-permute-start | bytes 2949128 | tf_op jit(solution)/shard_map/ppermute | solution.py:21
  61.4 27.6 %collective-permute-start.5 = (bf16[768,640]{1,0:T(8,128)(2,1)}, bf16[768,640]{1,0:T(8,128)(2,1)}, u32[]{:S(2)}, u32[]{:S(2)}) collective-permute-start(bf16[768,640]{1,0:T(8,128)(2,1)} %slice.66), channel_id=1, source_target_pairs={{0,1},{1,0},{2,3},{3,2},{4,5},{5,4},{6,7},{7,6},{8,9},{9,8},{10,11... | collective-permute-start | bytes 2949128 | tf_op jit(solution)/shard_map/ppermute | solution.py:23
  61.7 2.3 %collective-permute-start.7 = (f32[2,768]{1,0:T(2,128)S(1)}, f32[2,768]{1,0:T(2,128)S(1)}, u32[]{:S(2)}, u32[]{:S(2)}) collective-permute-start(f32[2,768]{1,0:T(2,128)S(1)} %collective-permute-done.2), channel_id=1, source_target_pairs={{0,1},{1,0},{2,3},{3,2},{4,5},{5,4},{6,7},{7,6},{8,9},{9,8},{10,11... | collective-permute-start | bytes 18440 | tf_op jit(solution)/shard_map/ppermute | solution.py:23
  79.4 2.1 %copy-start.3 = (f32[768,768]{0,1:T(8,128)S(1)}, f32[768,768]{0,1:T(8,128)}, u32[]{:S(2)}) copy-start(f32[768,768]{0,1:T(8,128)} %fusion.29) | copy-start | bytes 7077892
  80.9 2.3 %collective-permute-start.6 = (bf16[768,384]{1,0:T(8,128)(2,1)S(1)}, bf16[768,384]{1,0:T(8,128)(2,1)S(1)}, u32[]{:S(2)}, u32[]{:S(2)}) collective-permute-start(bf16[768,384]{1,0:T(8,128)(2,1)S(1)} %bitcast.20), channel_id=1, source_target_pairs={{0,1},{1,0},{2,3},{3,2},{4,5},{5,4},{6,7},{7,6},{8,9},{9,8},{10,11... | collective-permute-start | bytes 1769480 | tf_op jit(solution)/shard_map/ppermute | solution.py:96
  80.9 4.5 %collective-permute-start.9 = (bf16[768,384]{1,0:T(8,128)(2,1)S(1)}, bf16[768,384]{1,0:T(8,128)(2,1)S(1)}, u32[]{:S(2)}, u32[]{:S(2)}) collective-permute-start(bf16[768,384]{1,0:T(8,128)(2,1)S(1)} %bitcast.25), channel_id=1, source_target_pairs={{0,1},{1,0},{2,3},{3,2},{4,5},{5,4},{6,7},{7,6},{8,9},{9,8},{10,11... | collective-permute-start | bytes 1769480 | tf_op jit(solution)/shard_map/ppermute | solution.py:96
  85.4 6.4 %collective-permute-start.8 = (bf16[768,640]{1,0:T(8,128)(2,1)}, bf16[768,640]{1,0:T(8,128)(2,1)S(1)}, u32[]{:S(2)}, u32[]{:S(2)}) collective-permute-start(bf16[768,640]{1,0:T(8,128)(2,1)} %collective-permute-done.3), channel_id=1, source_target_pairs={{0,1},{1,0},{2,3},{3,2},{4,5},{5,4},{6,7},{7,6},{8,9},{9,8},{10,11... | collective-permute-start | bytes 2949128 | tf_op jit(solution)/shard_map/ppermute | solution.py:23

commit v16 on v15

--- a/solution.py
+++ b/solution.py
@@ -82,8 +82,9 @@
         )
         got_a = route(rows_a)
         q_emb, q_lab, q_ord = unpack(got_a, half, n_all)
-        keys_a = gather_split(q_emb, n_split)
-        keys_m = gather_split(jnp.stack([q_lab, q_ord]), n_split)
+        own_m = jnp.stack([q_lab, q_ord])
+        keys_a = [lax.ppermute(q_emb, "split", cross), lax.ppermute(q_emb, "split", pair)]
+        keys_m = [lax.ppermute(own_m, "split", cross), lax.ppermute(own_m, "split", pair)]
         pick_par = par_place[None, :] == jnp.arange(n_slot, dtype=jnp.int32)[:, None]
         send_own = jnp.dot(pick.astype(jnp.bfloat16), raw_b, preferred_element_type=jnp.float32)
         send_par = jnp.dot(pick_par.astype(jnp.bfloat16), par_b, preferred_element_type=jnp.float32)
@@ -93,7 +94,7 @@
         got = lax.all_to_all(send, "grp", split_axis=0, concat_axis=0, tiled=True)
         got_b = got[:, :cap].reshape(n_slot, -1)
         cross_b = got[:, cap:].reshape(n_slot, -1)
-        keys_b = [cross_b, lax.ppermute(got_b, "split", pair), lax.ppermute(cross_b, "split", pair)]
+        keys_b = [cross_b, lax.ppermute(got_b, "split", pair)]
     else:
         half = emb_w // 2
         got_a = route(jnp.concatenate([embeds[:, :half], meta], axis=1))
@@ -103,21 +104,20 @@
         got_b = route(embeds[:, half:])
         keys_b = gather_split(got_b, n_split)
 
-    def dots(k_a, k_b):
-        s = jnp.einsum("qe,ke->qk", q_emb, k_a, preferred_element_type=jnp.float32)
-        return s + jnp.einsum("qe,ke->qk", got_b, k_b, preferred_element_type=jnp.float32)
-
-    q_base = q_lab * 1048576.0
-    q_code = q_base + q_ord
-
-    def block_best(scores, k_lab, k_ord):
-        k_code = k_lab * 1048576.0 + k_ord
-        hits = (k_code[None, :] >= q_base[:, None]) & (k_code[None, :] < q_code[:, None])
+    def block_best(qa, qb, qm, ka, kb, km):
+        scores = jnp.einsum("qe,ke->qk", qa, ka, preferred_element_type=jnp.float32)
+        scores = scores + jnp.einsum("qe,ke->qk", qb, kb, preferred_element_type=jnp.float32)
+        hits = (qm[0][:, None] == km[0][None, :]) & (km[0][None, :] > 0) & (km[1][None, :] < qm[1][:, None])
         return jnp.max(jnp.where(hits, scores, jnp.float32(-1.0)), axis=1)
 
-    best = block_best(dots(q_emb, got_b), q_lab, q_ord)
+    mine = (q_emb, got_b, jnp.stack([q_lab, q_ord]))
+    best = block_best(*mine, *mine)
     for k_a, k_b, k_m in zip(keys_a, keys_b, keys_m):
-        best = jnp.maximum(best, block_best(dots(k_a, k_b), k_m[0], k_m[1]))
+        best = jnp.maximum(best, block_best(*mine, k_a, k_b, k_m))
+    if n_split == 4:
+        near = (keys_a[1], keys_b[1], keys_m[1])
+        far = (keys_a[0], keys_b[0], keys_m[0])
+        best = jnp.maximum(best, lax.ppermute(block_best(*near, *far), "split", pair))
 
     returned = lax.all_to_all(
         best.reshape(n_grp, cap), "grp", split_axis=0, concat_axis=0, tiled=True

time: 109 us -> 106 us (0.972)
  blocking collectives: 12.2 us -> 9.64 us
    ppermute x8 -> x6, waiting for transfers between devices: 3.4 us -> 0.02 us  [the longest x1 0.01 us: local(): lax.ppermute(own_m, 'split', cross)]
    all_to_all x1, blocking collectives: 12.2 us -> 9.64 us  [local(): lax.all_to_all(best.reshape(n_grp, cap), 'grp', split_axis=0, concat_axis...]
    all_to_all x1, waiting for transfers between devices: 15.3 us -> 17.8 us  [local(): got = lax.all_to_all(send, 'grp', split_axis=0, concat_axis=0, tiled=True)]
    convert_element_type x1 -> x0, other arithmetic: 2.02 us -> none  [unpack(): lab = buf[:, emb_w].astype(jnp.float32)]
    eq x0 -> x1, other arithmetic: none -> 1.81 us  [block_best(): qm[0][:, None] == km[0][None, :]]
    ppermute x8 -> x6, starting transfers between devices: 3.24 us -> 2.31 us  [the longest x1 1.59 us: local(): lax.ppermute(own_m, 'split', cross)]
  transfers between devices with their start and end apart: 12 -> 10, of which waited for: 6 -> 3; matrix products, arithmetic and copies ran while one was open for 21% -> 22% of each run, Pallas kernels for 0% -> 0%
where the time goes in v16:
time: 106 us
  waiting for transfers between devices  40.3 us (38%)
  matrix products  26.2 us (25%)
  starting transfers between devices  16.1 us (15%)
  blocking collectives  9.64 us (9%)
  local copies, waits for them, and re-layouts  6.75 us (6%)
  other arithmetic  6.55 us (6%)
    all_to_all x1, waiting for transfers between devices, local(): got = lax.all_to_all(send, 'grp', split_axis=0, concat_axis=0, tiled=True)  17.8 us
    all_to_all x1, waiting for transfers between devices, route(): got = lax.all_to_all(send, 'grp', split_axis=0, concat_axis=0, tiled=True)  17.5 us
    dot_general x4, matrix products, block_best(): scores = jnp.einsum('qe,ke->qk', qa, ka, preferred_element_type=jnp.float32)  12.7 us
    all_to_all x1, blocking collectives, local(): lax.all_to_all(best.reshape(n_grp, cap), 'grp', split_axis=0, concat_axis...  9.64 us
    all_to_all x1, starting transfers between devices, route(): got = lax.all_to_all(send, 'grp', split_axis=0, concat_axis=0, tiled=True)  7.25 us
    dot_general x1, matrix products, embed_rows(): jnp.einsum('...h,he->...e', rows, weight, preferred_element_type=jnp.floa...  5.94 us
    ppermute x1, waiting for transfers between devices, local(): par_place = lax.ppermute(place, 'split', cross)  5.02 us
    all_to_all x1, starting transfers between devices, local(): got = lax.all_to_all(send, 'grp', split_axis=0, concat_axis=0, tiled=True)  4.45 us
  transfers between devices with their start and end apart: 10, of which 3 were waited for; matrix products, arithmetic and copies ran while one was open for 22% of the time, Pallas kernels for 0%

profile of v16, /device:TPU:0, one launch (start us, length us, event | category | flops | bytes accessed | tf_op | source)
XLA Modules:
  0.0 105.8 jit_solution(14801905145818810352)
XLA Ops:
  0.0 0.8 convert_element_type.106
  0.9 0.8 fusion.13
  1.9 5.9 %multiply_reduce_fusion = (f32[384]{0:T(512)S(1)}, f32[384,1024]{1,0:T(8,128)S(1)}) fusion(bf16[384,4096]{1,0:T(8,128)(2,1)S(1)} %copy-done, bf16[4096,1024]{1,0:T(8,128)(2,1)} %param.6), kind=kOutput, calls=%fused_computation.5 | convolution fusion | flops 3222011392 | bytes 13108736 | tf_op jit(solution)/shard_map/...h,he->...e/dot_general | solution.py:14
  8.3 0.6 copy-done.1
  9.0 1.8 %convolution_convert_fusion = bf16[768,768]{1,0:T(8,128)(2,1)} fusion(bf16[384,1024]{1,0:T(8,128)(2,1)S(1)} %multiply_convert_fusion, bf16[384,128]{1,0:T(8,128)(2,1)S(1)} %select_convert_fusion, s32[384]{0:T(512)S(1)} %convert_add_fusion, pred[768]{0:T(1024)(128)(4,1)S(1)} %copy-done.2, pred[768]{0:T(1024)(128)(4,1)S(1)} %iota_compare_fusion.9), kind=kOutput, calls=%fused_computation.6 | convolution fusion | flops 454459392 | bytes 1871872 | tf_op jit(solution)/shard_map/dot_general | solution.py:65
  10.8 7.2 %all-to-all-start = ((bf16[8,96,768]{2,1,0:T(8,128)(2,1)}), bf16[8,96,768]{2,1,0:T(8,128)(2,1)}, u32[]{:S(2)}, u32[]{:S(2)}) async-start(bf16[8,96,768]{2,1,0:T(8,128)(2,1)} %bitcast.27), calls=%async_computation | async-start | bytes 2359296 | tf_op jit(solution)/shard_map/all_to_all | solution.py:67
  18.1 1.0 slice.66
  19.1 1.6 %collective-permute-start.1 = (bf16[384,384]{1,0:T(8,128)(2,1)S(1)}, bf16[384,384]{1,0:T(8,128)(2,1)S(1)}, u32[]{:S(2)}, u32[]{:S(2)}) collective-permute-start(bf16[384,384]{1,0:T(8,128)(2,1)S(1)} %slice.66), channel_id=1, source_target_pairs={{0,2},{2,0},{1,3},{3,1},{4,6},{6,4},{5,7},{7,5},{8,10},{10,8},{9,1... | collective-permute-start | bytes 884744 | tf_op jit(solution)/shard_map/ppermute | solution.py:75
  21.1 1.5 %convolution_convert_fusion.2 = bf16[768,384]{1,0:T(8,128)(2,1)S(1)} fusion(s32[384]{0:T(512)S(1)} %convert_add_fusion, bf16[384,1024]{1,0:T(8,128)(2,1)} %copy-done.1), kind=kOutput, calls=%fused_computation.8 | convolution fusion | flops 227082240 | bytes 886272 | tf_op jit(solution)/shard_map/dot_general | solution.py:89
  22.6 5.0 %collective-permute-done = s32[384]{0:T(512)S(1)} collective-permute-done((s32[384]{0:T(512)S(1)}, s32[384]{0:T(512)S(1)}, u32[]{:S(2)}, u32[]{:S(2)}) %collective-permute-start) | collective-permute-done | bytes 1568 | tf_op jit(solution)/shard_map/ppermute | solution.py:76
  28.1 1.1 %pad_maximum_fusion = bf16[8,192,384]{2,1,0:T(8,128)(2,1)} fusion(bf16[8,96,384]{2,1,0:T(8,128)(2,1)S(1)} %bitcast.29, bf16[8,96,384]{2,1,0:T(8,128)(2,1)S(1)} %bitcast.28), kind=kLoop, calls=%fused_computation.9 | loop fusion | flops 2359296 | bytes 2359296 | tf_op jit(solution)/shard_map/concatenate | solution.py:91
  29.3 17.5 %all-to-all-done = bf16[8,96,768]{2,1,0:T(8,128)(2,1)} async-done(((bf16[8,96,768]{2,1,0:T(8,128)(2,1)}), bf16[8,96,768]{2,1,0:T(8,128)(2,1)}, u32[]{:S(2)}, u32[]{:S(2)}) %all-to-all-start) | async-done | bytes 1179680 | tf_op jit(solution)/shard_map/all_to_all | solution.py:67
  46.7 4.4 %all-to-all-start.1 = ((bf16[8,192,384]{2,1,0:T(8,128)(2,1)}), bf16[8,192,384]{2,1,0:T(8,128)(2,1)}, u32[]{:S(2)}, u32[]{:S(2)}) async-start(bf16[8,192,384]{2,1,0:T(8,128)(2,1)} %pad_maximum_fusion), calls=%async_computation.1 | async-start | bytes 2359296 | tf_op jit(solution)/shard_map/all_to_all | solution.py:94
  51.2 1.8 %convert_reduce_fusion = (f32[768]{0:T(1024)S(1)}, f32[768]{0:T(1024)S(1)}) fusion(bf16[768,768]{1,0:T(8,128)(2,1)} %bitcast.1), kind=kLoop, calls=%fused_computation.24 | loop fusion | flops 6144 | bytes 12288 | tf_op jit(solution)/shard_map/eq | solution.py:110
  53.1 1.6 %collective-permute-start.2 = (f32[2,768]{1,0:T(2,128)S(1)}, f32[2,768]{1,0:T(2,128)S(1)}, u32[]{:S(2)}, u32[]{:S(2)}) collective-permute-start(f32[2,768]{1,0:T(2,128)S(1)} %pad_maximum_fusion.1), channel_id=1, source_target_pairs={{0,2},{2,0},{1,3},{3,1},{4,6},{6,4},{5,7},{7,5},{8,10},{10,8},{9,1... | collective-permute-start | bytes 18440 | tf_op jit(solution)/shard_map/ppermute | solution.py:87
  54.7 2.2 %slice.65 = bf16[768,640]{1,0:T(8,128)(2,1)} slice(bf16[768,768]{1,0:T(8,128)(2,1)} %bitcast.1), slice={[0:768], [0:640]} | slice | bytes 1966080 | tf_op jit(solution)/shard_map/slice | solution.py:31
  56.9 0.5 collective-permute-start.3
  57.5 4.0 %fusion.21 = f32[768,768]{0,1:T(8,128)} fusion(bf16[768,768]{1,0:T(8,128)(2,1)} %bitcast.1), kind=kOutput, calls=%fused_computation.69 | convolution fusion | flops 754974720 | bytes 3342336 | tf_op jit(solution)/shard_map/qe,ke->qk/dot_general | solution.py:108
  61.6 17.8 %all-to-all-done.1 = bf16[8,192,384]{2,1,0:T(8,128)(2,1)} async-done(((bf16[8,192,384]{2,1,0:T(8,128)(2,1)}), bf16[8,192,384]{2,1,0:T(8,128)(2,1)}, u32[]{:S(2)}, u32[]{:S(2)}) %all-to-all-start.1) | async-done | bytes 1179680 | tf_op jit(solution)/shard_map/all_to_all | solution.py:94
  79.4 1.4 %fusion.23 = (bf16[8,96,384]{2,1,0:T(8,128)(2,1)S(1)}, bf16[8,96,384]{2,1,0:T(8,128)(2,1)S(1)}) fusion(bf16[8,192,384]{2,1,0:T(8,128)(2,1)} %all-to-all-done.1), kind=kLoop, calls=%fused_computation.71 | loop fusion | bytes 2359296 | tf_op jit(solution)/shard_map/slice | solution.py:96
  80.9 0.8 fusion.24
  81.7 0.8 copy-done.3
  82.5 1.1 %select_reduce_fusion.3 = f32[768]{0:T(1024)S(1)} fusion(f32[768,768]{0,1:T(8,128)S(1)} %copy-done.3, bf16[768,384]{1,0:T(8,128)(2,1)S(1)} %bitcast.23, f32[768]{0:T(1024)S(1)} %get-tuple-element.6, f32[768]{0:T(1024)S(1)} %get-tuple-element.5, pred[768]{0:T(1024)(128)(4,1)S(1)} %broadcast_compare_fusion), kind=kOutput, calls=%fused_computation.3 | convolution fusion | flops 457112832 | bytes 2959104 | tf_op jit(solution)/shard_map/qe,ke->qk/dot_general | solution.py:109
  83.6 0.8 fusion.26
  84.4 0.8 fusion.25
  85.2 2.9 %select_reduce_fusion = f32[768]{0:T(1024)S(1)} fusion(f32[768,768]{0,1:T(8,128)S(1)} %fusion.26, bf16[768,640]{1,0:T(8,128)(2,1)} %collective-permute-done.5, bf16[768,640]{1,0:T(8,128)(2,1)} %collective-permute-done.3, f32[768]{0:T(1024)S(1)} %get-tuple-element.10, f32[768]{0:T(1024)S(1)} %get-tuple-element.9, f32[768]{0:T(1024)S(1)} %get-tuple-element.8, ...), kind=kOutput, calls=%fused_computation | convolution fusion | flops 759102720 | bytes 4341504 | tf_op jit(solution)/shard_map/qe,ke->qk/dot_general | solution.py:108
  88.2 2.9 %select_reduce_fusion.2 = f32[768]{0:T(1024)S(1)} fusion(f32[768,768]{0,1:T(8,128)S(1)} %fusion.24, bf16[768,640]{1,0:T(8,128)(2,1)} %collective-permute-done.3, f32[768]{0:T(1024)S(1)} %get-tuple-element.6, f32[768]{0:T(1024)S(1)} %get-tuple-element.5, f32[768]{0:T(1024)S(1)} %get-tuple-element.8, f32[768]{0:T(1024)S(1)} %get-tuple-element.7, ...), kind=kOutput, calls=%fused_computation.2 | convolution fusion | flops 759102720 | bytes 4341504 | tf_op jit(solution)/shard_map/qe,ke->qk/dot_general | solution.py:108
  91.1 2.9 %select_reduce_fusion.1 = f32[768]{0:T(1024)S(1)} fusion(f32[768,768]{0,1:T(8,128)S(1)} %fusion.25, bf16[768,640]{1,0:T(8,128)(2,1)} %collective-permute-done.5, f32[768]{0:T(1024)S(1)} %get-tuple-element.6, f32[768]{0:T(1024)S(1)} %get-tuple-element.5, f32[768]{0:T(1024)S(1)} %get-tuple-element.10, f32[768]{0:T(1024)S(1)} %get-tuple-element.9, ...), kind=kOutput, calls=%fused_computation.1 | convolution fusion | flops 759102720 | bytes 4341504 | tf_op jit(solution)/shard_map/qe,ke->qk/dot_general | solution.py:108
  94.1 9.6 %all_to_all.19 = f32[8,1,96]{2,1,0:T(1,128)S(1)} all-to-all(f32[8,1,96]{2,1,0:T(1,128)S(1)} %all_to_all.14), channel_id=1, replica_groups=mesh['grp'=8,'split'=4] {'grp'}, dimensions={0} | all-to-all | bytes 6144 | tf_op jit(solution)/shard_map/all_to_all | solution.py:122
  103.7 0.5 broadcast.144
  104.3 0.7 reduce.21
  105.0 0.8 select_reduce_fusion.4
  (38 shorter events, 2.2 us)
Async XLA Ops:
  0.0 1.9 %copy-start = (bf16[384,4096]{1,0:T(8,128)(2,1)S(1)}, bf16[384,4096]{1,0:T(8,128)(2,1)}, u32[]{:S(2)}) copy-start(bf16[384,4096]{1,0:T(8,128)(2,1)} %param.5) | copy-start | bytes 9437188
  7.9 1.1 %copy-start.2 = (pred[768]{0:T(1024)(128)(4,1)S(1)}, pred[768]{0:T(1024)(128)(4,1)}, u32[]{:S(2)}) copy-start(pred[768]{0:T(1024)(128)(4,1)} %constant.58.clone.1) | copy-start | bytes 2308
  8.0 0.9 copy-start.1
  10.8 35.9 %all-to-all-start = ((bf16[8,96,768]{2,1,0:T(8,128)(2,1)}), bf16[8,96,768]{2,1,0:T(8,128)(2,1)}, u32[]{:S(2)}, u32[]{:S(2)}) async-start(bf16[8,96,768]{2,1,0:T(8,128)(2,1)} %bitcast.27), calls=%async_computation | async-start | bytes 2359296 | tf_op jit(solution)/shard_map/all_to_all | solution.py:67
  19.1 8.6 %collective-permute-start.1 = (bf16[384,384]{1,0:T(8,128)(2,1)S(1)}, bf16[384,384]{1,0:T(8,128)(2,1)S(1)}, u32[]{:S(2)}, u32[]{:S(2)}) collective-permute-start(bf16[384,384]{1,0:T(8,128)(2,1)S(1)} %slice.66), channel_id=1, source_target_pairs={{0,2},{2,0},{1,3},{3,1},{4,6},{6,4},{5,7},{7,5},{8,10},{10,8},{9,1... | collective-permute-start | bytes 884744 | tf_op jit(solution)/shard_map/ppermute | solution.py:75
  20.6 7.0 %collective-permute-start = (s32[384]{0:T(512)S(1)}, s32[384]{0:T(512)S(1)}, u32[]{:S(2)}, u32[]{:S(2)}) collective-permute-start(s32[384]{0:T(512)S(1)} %convert_add_fusion), channel_id=1, source_target_pairs={{0,2},{2,0},{1,3},{3,1},{4,6},{6,4},{5,7},{7,5},{8,10},{10,8},{9,1... | collective-permute-start | bytes 4616 | tf_op jit(solution)/shard_map/ppermute | solution.py:76
  46.7 32.7 %all-to-all-start.1 = ((bf16[8,192,384]{2,1,0:T(8,128)(2,1)}), bf16[8,192,384]{2,1,0:T(8,128)(2,1)}, u32[]{:S(2)}, u32[]{:S(2)}) async-start(bf16[8,192,384]{2,1,0:T(8,128)(2,1)} %pad_maximum_fusion), calls=%async_computation.1 | async-start | bytes 2359296 | tf_op jit(solution)/shard_map/all_to_all | solution.py:94
  53.0 8.4 %collective-permute-start.4 = (f32[2,768]{1,0:T(2,128)S(1)}, f32[2,768]{1,0:T(2,128)S(1)}, u32[]{:S(2)}, u32[]{:S(2)}) collective-permute-start(f32[2,768]{1,0:T(2,128)S(1)} %pad_maximum_fusion.1), channel_id=1, source_target_pairs={{0,1},{1,0},{2,3},{3,2},{4,5},{5,4},{6,7},{7,6},{8,9},{9,8},{10,11... | collective-permute-start | bytes 18440 | tf_op jit(solution)/shard_map/ppermute | solution.py:87
  53.1 8.4 %collective-permute-start.2 = (f32[2,768]{1,0:T(2,128)S(1)}, f32[2,768]{1,0:T(2,128)S(1)}, u32[]{:S(2)}, u32[]{:S(2)}) collective-permute-start(f32[2,768]{1,0:T(2,128)S(1)} %pad_maximum_fusion.1), channel_id=1, source_target_pairs={{0,2},{2,0},{1,3},{3,1},{4,6},{6,4},{5,7},{7,5},{8,10},{10,8},{9,1... | collective-permute-start | bytes 18440 | tf_op jit(solution)/shard_map/ppermute | solution.py:87
  56.9 28.2 %collective-permute-start.3 = (bf16[768,640]{1,0:T(8,128)(2,1)}, bf16[768,640]{1,0:T(8,128)(2,1)}, u32[]{:S(2)}, u32[]{:S(2)}) collective-permute-start(bf16[768,640]{1,0:T(8,128)(2,1)} %slice.65), channel_id=1, source_target_pairs={{0,2},{2,0},{1,3},{3,1},{4,6},{6,4},{5,7},{7,5},{8,10},{10,8},{9,1... | collective-permute-start | bytes 2949128 | tf_op jit(solution)/shard_map/ppermute | solution.py:86
  57.4 27.8 %collective-permute-start.5 = (bf16[768,640]{1,0:T(8,128)(2,1)}, bf16[768,640]{1,0:T(8,128)(2,1)}, u32[]{:S(2)}, u32[]{:S(2)}) collective-permute-start(bf16[768,640]{1,0:T(8,128)(2,1)} %slice.65), channel_id=1, source_target_pairs={{0,1},{1,0},{2,3},{3,2},{4,5},{5,4},{6,7},{7,6},{8,9},{9,8},{10,11... | collective-permute-start | bytes 2949128 | tf_op jit(solution)/shard_map/ppermute | solution.py:86
  80.8 1.7 %copy-start.3 = (f32[768,768]{0,1:T(8,128)S(1)}, f32[768,768]{0,1:T(8,128)}, u32[]{:S(2)}) copy-start(f32[768,768]{0,1:T(8,128)} %fusion.21) | copy-start | bytes 7077892
  80.8 2.8 %collective-permute-start.6 = (bf16[768,384]{1,0:T(8,128)(2,1)S(1)}, bf16[768,384]{1,0:T(8,128)(2,1)S(1)}, u32[]{:S(2)}, u32[]{:S(2)}) collective-permute-start(bf16[768,384]{1,0:T(8,128)(2,1)S(1)} %bitcast.21), channel_id=1, source_target_pairs={{0,1},{1,0},{2,3},{3,2},{4,5},{5,4},{6,7},{7,6},{8,9},{9,8},{10,11... | collective-permute-start | bytes 1769480 | tf_op jit(solution)/shard_map/ppermute | solution.py:97
  88.1 5.9 %collective-permute-start.7 = (f32[768]{0:T(1024)S(1)}, f32[768]{0:T(1024)S(1)}, u32[]{:S(2)}, u32[]{:S(2)}) collective-permute-start(f32[768]{0:T(1024)S(1)} %select_reduce_fusion), channel_id=1, source_target_pairs={{0,1},{1,0},{2,3},{3,2},{4,5},{5,4},{6,7},{7,6},{8,9},{9,8},{10,11... | collective-permute-start | bytes 9224 | tf_op jit(solution)/shard_map/ppermute | solution.py:120

commit v17 on v16

--- a/solution.py
+++ b/solution.py
@@ -110,10 +110,22 @@
         hits = (qm[0][:, None] == km[0][None, :]) & (km[0][None, :] > 0) & (km[1][None, :] < qm[1][:, None])
         return jnp.max(jnp.where(hits, scores, jnp.float32(-1.0)), axis=1)
 
+    def early_best(qa, qb, qm, ka, kb, km):
+        scores = jnp.einsum("qe,ke->qk", qa, ka, preferred_element_type=jnp.float32)
+        hits = (qm[0][:, None] == km[0][None, :]) & (km[0][None, :] > 0) & (km[1][None, :] < qm[1][:, None])
+        masked = lax.optimization_barrier(jnp.where(hits, scores, -jnp.inf))
+        scores = masked + jnp.einsum("qe,ke->qk", qb, kb, preferred_element_type=jnp.float32)
+        return jnp.maximum(jnp.max(scores, axis=1), jnp.float32(-1.0))
+
     mine = (q_emb, got_b, jnp.stack([q_lab, q_ord]))
-    best = block_best(*mine, *mine)
-    for k_a, k_b, k_m in zip(keys_a, keys_b, keys_m):
-        best = jnp.maximum(best, block_best(*mine, k_a, k_b, k_m))
+    blocks = list(zip(keys_a, keys_b, keys_m))
+    if n_split == 4:
+        best = jnp.maximum(early_best(*mine, *mine), early_best(*mine, *blocks[1]))
+        best = jnp.maximum(best, block_best(*mine, *blocks[0]))
+    else:
+        best = block_best(*mine, *mine)
+        for k_a, k_b, k_m in blocks:
+            best = jnp.maximum(best, block_best(*mine, k_a, k_b, k_m))
     if n_split == 4:
         near = (keys_a[1], keys_b[1], keys_m[1])
         far = (keys_a[0], keys_b[0], keys_m[0])

time: 106 us -> 108 us (1.019)
  local copies, waits for them, and re-layouts: 6.75 us -> 8.4 us
  other arithmetic: 6.55 us -> 5.21 us
    all_to_all x1, waiting for transfers between devices: 17.8 us -> 1.35 us  [local(): got = lax.all_to_all(send, 'grp', split_axis=0, concat_axis=0, tiled=True)]
    ppermute x1, waiting for transfers between devices: 0.01 us -> 16.4 us  [local(): lax.ppermute(own_m, 'split', cross)]
    dot_general x0 -> x4, matrix products: none -> 8.68 us  [the longest x2 6.98 us: early_best(): scores = jnp.einsum('qe,ke->qk', qa, ka, preferred_element_type=jnp.float32)]
    dot_general x4 -> x2, matrix products: 12.7 us -> 5.97 us  [block_best(): scores = jnp.einsum('qe,ke->qk', qa, ka, preferred_element_type=jnp.float32)]
    dot_general x4 -> x2, matrix products: 3.49 us -> 1.59 us  [block_best(): jnp.einsum('qe,ke->qk', qb, kb, preferred_element_type=jnp.float32)]
    unnamed x8 -> x14, local copies, waits for them, and re-layouts: 1.44 us -> 2.95 us
  transfers between devices with their start and end apart: 10 -> 10, of which waited for: 3 -> 4; matrix products, arithmetic and copies ran while one was open for 22% -> 22% of each run, Pallas kernels for 0% -> 0%
where the time goes in v17:
time: 108 us; the launch traced here: 107 us
  waiting for transfers between devices  40.3 us (37%)
  matrix products  26.2 us (24%)
  starting transfers between devices  16.1 us (15%)
  blocking collectives  10.7 us (10%)
  local copies, waits for them, and re-layouts  8.4 us (8%)
  other arithmetic  5.21 us (5%)
    all_to_all x1, waiting for transfers between devices, route(): got = lax.all_to_all(send, 'grp', split_axis=0, concat_axis=0, tiled=True)  17.5 us
    ppermute x1, waiting for transfers between devices, local(): lax.ppermute(own_m, 'split', cross)  16.4 us
    all_to_all x1, blocking collectives, local(): lax.all_to_all(best.reshape(n_grp, cap), 'grp', split_axis=0, concat_axis...  10.7 us
    all_to_all x1, starting transfers between devices, route(): got = lax.all_to_all(send, 'grp', split_axis=0, concat_axis=0, tiled=True)  7.25 us
    dot_general x2, matrix products, early_best(): scores = jnp.einsum('qe,ke->qk', qa, ka, preferred_element_type=jnp.float32)  6.98 us
    dot_general x1, matrix products, embed_rows(): jnp.einsum('...h,he->...e', rows, weight, preferred_element_type=jnp.floa...  5.98 us
    dot_general x2, matrix products, block_best(): scores = jnp.einsum('qe,ke->qk', qa, ka, preferred_element_type=jnp.float32)  5.97 us
    ppermute x1, waiting for transfers between devices, local(): par_place = lax.ppermute(place, 'split', cross)  5.02 us
  transfers between devices with their start and end apart: 10, of which 4 were waited for; matrix products, arithmetic and copies ran while one was open for 22% of the time, Pallas kernels for 0%

profile of v17, /device:TPU:0, one launch (start us, length us, event | category | flops | bytes accessed | tf_op | source)
XLA Modules:
  0.0 107.1 jit_solution(8080805425350778118)
XLA Ops:
  0.0 1.9 %copy-done = bf16[384,4096]{1,0:T(8,128)(2,1)S(1)} copy-done((bf16[384,4096]{1,0:T(8,128)(2,1)S(1)}, bf16[384,4096]{1,0:T(8,128)(2,1)}, u32[]{:S(2)}) %copy-start) | copy-done | bytes 3145752
  1.9 6.0 %multiply_reduce_fusion = (f32[384]{0:T(512)S(1)}, f32[384,1024]{1,0:T(8,128)S(1)}) fusion(bf16[384,4096]{1,0:T(8,128)(2,1)S(1)} %copy-done, bf16[4096,1024]{1,0:T(8,128)(2,1)} %param.6), kind=kOutput, calls=%fused_computation.7 | convolution fusion | flops 3222011392 | bytes 13108736 | tf_op jit(solution)/shard_map/...h,he->...e/dot_general | solution.py:14
  8.6 0.6 copy-done.2
  9.3 1.8 %convolution_convert_fusion = bf16[768,768]{1,0:T(8,128)(2,1)} fusion(bf16[384,1024]{1,0:T(8,128)(2,1)S(1)} %multiply_convert_fusion, bf16[384,128]{1,0:T(8,128)(2,1)S(1)} %select_convert_fusion, s32[384]{0:T(512)S(1)} %convert_add_fusion, pred[768]{0:T(1024)(128)(4,1)S(1)} %copy-done.6, pred[768]{0:T(1024)(128)(4,1)S(1)} %iota_compare_fusion.9), kind=kOutput, calls=%fused_computation.8 | convolution fusion | flops 454459392 | bytes 1871872 | tf_op jit(solution)/shard_map/dot_general | solution.py:65
  11.1 7.3 %all-to-all-start = ((bf16[8,96,768]{2,1,0:T(8,128)(2,1)}), bf16[8,96,768]{2,1,0:T(8,128)(2,1)}, u32[]{:S(2)}, u32[]{:S(2)}) async-start(bf16[8,96,768]{2,1,0:T(8,128)(2,1)} %bitcast.27), calls=%async_computation | async-start | bytes 2359296 | tf_op jit(solution)/shard_map/all_to_all | solution.py:67
  18.4 1.0 slice.66
  19.4 1.6 %collective-permute-start.1 = (bf16[384,384]{1,0:T(8,128)(2,1)S(1)}, bf16[384,384]{1,0:T(8,128)(2,1)S(1)}, u32[]{:S(2)}, u32[]{:S(2)}) collective-permute-start(bf16[384,384]{1,0:T(8,128)(2,1)S(1)} %slice.66), channel_id=1, source_target_pairs={{0,2},{2,0},{1,3},{3,1},{4,6},{6,4},{5,7},{7,5},{8,10},{10,8},{9,1... | collective-permute-start | bytes 884744 | tf_op jit(solution)/shard_map/ppermute | solution.py:75
  20.9 0.5 collective-permute-start
  21.5 1.5 %convolution_convert_fusion.2 = bf16[768,384]{1,0:T(8,128)(2,1)S(1)} fusion(s32[384]{0:T(512)S(1)} %convert_add_fusion, bf16[384,1024]{1,0:T(8,128)(2,1)} %copy-done.2), kind=kOutput, calls=%fused_computation.10 | convolution fusion | flops 227082240 | bytes 886272 | tf_op jit(solution)/shard_map/dot_general | solution.py:89
  22.9 5.0 %collective-permute-done = s32[384]{0:T(512)S(1)} collective-permute-done((s32[384]{0:T(512)S(1)}, s32[384]{0:T(512)S(1)}, u32[]{:S(2)}, u32[]{:S(2)}) %collective-permute-start) | collective-permute-done | bytes 1568 | tf_op jit(solution)/shard_map/ppermute | solution.py:76
  28.4 1.1 %pad_maximum_fusion = bf16[8,192,384]{2,1,0:T(8,128)(2,1)} fusion(bf16[8,96,384]{2,1,0:T(8,128)(2,1)S(1)} %bitcast.29, bf16[8,96,384]{2,1,0:T(8,128)(2,1)S(1)} %bitcast.28), kind=kLoop, calls=%fused_computation.11 | loop fusion | flops 2359296 | bytes 2359296 | tf_op jit(solution)/shard_map/concatenate | solution.py:91
  29.6 17.5 %all-to-all-done = bf16[8,96,768]{2,1,0:T(8,128)(2,1)} async-done(((bf16[8,96,768]{2,1,0:T(8,128)(2,1)}), bf16[8,96,768]{2,1,0:T(8,128)(2,1)}, u32[]{:S(2)}, u32[]{:S(2)}) %all-to-all-start) | async-done | bytes 1179680 | tf_op jit(solution)/shard_map/all_to_all | solution.py:67
  47.0 4.4 %all-to-all-start.1 = ((bf16[8,192,384]{2,1,0:T(8,128)(2,1)}), bf16[8,192,384]{2,1,0:T(8,128)(2,1)}, u32[]{:S(2)}, u32[]{:S(2)}) async-start(bf16[8,192,384]{2,1,0:T(8,128)(2,1)} %pad_maximum_fusion), calls=%async_computation.1 | async-start | bytes 2359296 | tf_op jit(solution)/shard_map/all_to_all | solution.py:94
  51.5 2.2 %slice.65 = bf16[768,640]{1,0:T(8,128)(2,1)} slice(bf16[768,768]{1,0:T(8,128)(2,1)} %bitcast.1), slice={[0:768], [0:640]} | slice | bytes 1966080 | tf_op jit(solution)/shard_map/slice | solution.py:31
  53.7 1.5 %collective-permute-start.6 = (bf16[768,640]{1,0:T(8,128)(2,1)}, bf16[768,640]{1,0:T(8,128)(2,1)}, u32[]{:S(2)}, u32[]{:S(2)}) collective-permute-start(bf16[768,640]{1,0:T(8,128)(2,1)} %slice.65), channel_id=1, source_target_pairs={{0,2},{2,0},{1,3},{3,1},{4,6},{6,4},{5,7},{7,5},{8,10},{10,8},{9,1... | collective-permute-start | bytes 2949128 | tf_op jit(solution)/shard_map/ppermute | solution.py:86
  55.3 1.8 %convert_reduce_fusion = (f32[768]{0:T(1024)S(1)}, f32[768]{0:T(1024)S(1)}) fusion(bf16[768,768]{1,0:T(8,128)(2,1)} %bitcast.1), kind=kLoop, calls=%fused_computation.26 | loop fusion | flops 6144 | bytes 12288 | tf_op jit(solution)/shard_map/eq | solution.py:115
  57.1 0.6 collective-permute-start.5
  57.7 4.2 %and_select_fusion.1 = f32[768,768]{1,0:T(8,128)} fusion(f32[768]{0:T(1024)S(1)} %get-tuple-element.6, f32[768]{0:T(1024)S(1)} %get-tuple-element.5, pred[768]{0:T(1024)(128)(4,1)S(1)} %broadcast_compare_fusion, bf16[768,768]{1,0:T(8,128)(2,1)} %bitcast.1), kind=kOutput, calls=%fused_computation.5 | convolution fusion | flops 757923840 | bytes 3359744 | tf_op jit(solution)/shard_map/qe,ke->qk/dot_general | solution.py:114
  61.9 16.4 %collective-permute-done.5 = f32[2,768]{1,0:T(2,128)S(1)} collective-permute-done((f32[2,768]{1,0:T(2,128)S(1)}, f32[2,768]{1,0:T(2,128)S(1)}, u32[]{:S(2)}, u32[]{:S(2)}) %collective-permute-start.5) | collective-permute-done | bytes 6176 | tf_op jit(solution)/shard_map/ppermute | solution.py:87
  78.4 1.3 %all-to-all-done.1 = bf16[8,192,384]{2,1,0:T(8,128)(2,1)} async-done(((bf16[8,192,384]{2,1,0:T(8,128)(2,1)}), bf16[8,192,384]{2,1,0:T(8,128)(2,1)}, u32[]{:S(2)}, u32[]{:S(2)}) %all-to-all-start.1) | async-done | bytes 1179680 | tf_op jit(solution)/shard_map/all_to_all | solution.py:94
  79.8 1.5 %fusion.25 = (bf16[8,96,384]{2,1,0:T(8,128)(2,1)S(1)}, bf16[8,96,384]{2,1,0:T(8,128)(2,1)S(1)}) fusion(bf16[8,192,384]{2,1,0:T(8,128)(2,1)} %all-to-all-done.1), kind=kLoop, calls=%fused_computation.73 | loop fusion | bytes 2359296 | tf_op jit(solution)/shard_map/slice | solution.py:96
  81.8 0.9 add_reduce_fusion.1
  82.7 0.8 fusion.27
  83.5 0.8 fusion.28
  84.3 0.8 fusion.26
  85.1 3.0 %select_reduce_fusion = f32[768]{0:T(1024)S(1)} fusion(f32[768,768]{1,0:T(8,128)S(1)} %fusion.28, bf16[768,640]{1,0:T(8,128)(2,1)} %collective-permute-done.3, bf16[768,640]{1,0:T(8,128)(2,1)} %collective-permute-done.6, f32[768]{0:T(1024)S(1)} %get-tuple-element.10, f32[768]{0:T(1024)S(1)} %get-tuple-element.9, f32[768]{0:T(1024)S(1)} %get-tuple-element.8, ...), kind=kOutput, calls=%fused_computation | convolution fusion | flops 759102720 | bytes 4341504 | tf_op jit(solution)/shard_map/qe,ke->qk/dot_general | solution.py:108
  88.2 2.8 %and_select_fusion = f32[768,768]{1,0:T(8,128)S(1)} fusion(f32[768]{0:T(1024)S(1)} %get-tuple-element.8, f32[768]{0:T(1024)S(1)} %get-tuple-element.7, f32[768]{0:T(1024)S(1)} %get-tuple-element.6, f32[768]{0:T(1024)S(1)} %get-tuple-element.5, pred[768]{0:T(1024)(128)(4,1)S(1)} %compare_reduce_fusion.1, bf16[768,640]{1,0:T(8,128)(2,1)} %collective-permute-done.3, ...), kind=kOutput, calls=%fused_computation.4 | convolution fusion | flops 757923840 | bytes 4338432 | tf_op jit(solution)/shard_map/qe,ke->qk/dot_general | solution.py:114
  91.0 3.0 %select_reduce_fusion.1 = f32[768]{0:T(1024)S(1)} fusion(f32[768,768]{1,0:T(8,128)S(1)} %fusion.27, bf16[768,640]{1,0:T(8,128)(2,1)} %collective-permute-done.6, f32[768]{0:T(1024)S(1)} %get-tuple-element.10, f32[768]{0:T(1024)S(1)} %get-tuple-element.9, f32[768]{0:T(1024)S(1)} %get-tuple-element.6, f32[768]{0:T(1024)S(1)} %get-tuple-element.5, ...), kind=kOutput, calls=%fused_computation.1 | convolution fusion | flops 759102720 | bytes 4341504 | tf_op jit(solution)/shard_map/qe,ke->qk/dot_general | solution.py:108
  94.4 10.7 %all_to_all.19 = f32[8,1,96]{2,1,0:T(1,128)S(1)} all-to-all(f32[8,1,96]{2,1,0:T(1,128)S(1)} %all_to_all.14), channel_id=1, replica_groups=mesh['grp'=8,'split'=4] {'grp'}, dimensions={0} | all-to-all | bytes 6144 | tf_op jit(solution)/shard_map/all_to_all | solution.py:134
  105.1 0.5 broadcast.149
  105.6 0.7 reduce.21
  106.3 0.8 select_reduce_fusion.2
  (45 shorter events, 2.4 us)
Async XLA Ops:
  0.0 1.9 %copy-start = (bf16[384,4096]{1,0:T(8,128)(2,1)S(1)}, bf16[384,4096]{1,0:T(8,128)(2,1)}, u32[]{:S(2)}) copy-start(bf16[384,4096]{1,0:T(8,128)(2,1)} %param.5) | copy-start | bytes 9437188
  1.9 6.0 %copy-start.4 = (s32[384]{0:T(512)S(1)}, s32[384]{0:T(512)}, u32[]{:S(2)}) copy-start(s32[384]{0:T(512)} %param.9) | copy-start | bytes 4612
  1.9 6.0 %copy-start.5 = (s32[384]{0:T(512)S(1)}, s32[384]{0:T(512)}, u32[]{:S(2)}) copy-start(s32[384]{0:T(512)} %param.7) | copy-start | bytes 4612
  1.9 6.3 %copy-start.3 = (s32[384]{0:T(512)S(1)}, s32[384]{0:T(512)}, u32[]{:S(2)}) copy-start(s32[384]{0:T(512)} %param.8) | copy-start | bytes 4612
  7.9 1.4 %copy-start.6 = (pred[768]{0:T(1024)(128)(4,1)S(1)}, pred[768]{0:T(1024)(128)(4,1)}, u32[]{:S(2)}) copy-start(pred[768]{0:T(1024)(128)(4,1)} %constant.59.clone.1) | copy-start | bytes 2308
  8.3 0.9 copy-start.2
  11.1 35.9 %all-to-all-start = ((bf16[8,96,768]{2,1,0:T(8,128)(2,1)}), bf16[8,96,768]{2,1,0:T(8,128)(2,1)}, u32[]{:S(2)}, u32[]{:S(2)}) async-start(bf16[8,96,768]{2,1,0:T(8,128)(2,1)} %bitcast.27), calls=%async_computation | async-start | bytes 2359296 | tf_op jit(solution)/shard_map/all_to_all | solution.py:67
  19.4 8.6 %collective-permute-start.1 = (bf16[384,384]{1,0:T(8,128)(2,1)S(1)}, bf16[384,384]{1,0:T(8,128)(2,1)S(1)}, u32[]{:S(2)}, u32[]{:S(2)}) collective-permute-start(bf16[384,384]{1,0:T(8,128)(2,1)S(1)} %slice.66), channel_id=1, source_target_pairs={{0,2},{2,0},{1,3},{3,1},{4,6},{6,4},{5,7},{7,5},{8,10},{10,8},{9,1... | collective-permute-start | bytes 884744 | tf_op jit(solution)/shard_map/ppermute | solution.py:75
  20.9 7.0 %collective-permute-start = (s32[384]{0:T(512)S(1)}, s32[384]{0:T(512)S(1)}, u32[]{:S(2)}, u32[]{:S(2)}) collective-permute-start(s32[384]{0:T(512)S(1)} %convert_add_fusion), channel_id=1, source_target_pairs={{0,2},{2,0},{1,3},{3,1},{4,6},{6,4},{5,7},{7,5},{8,10},{10,8},{9,1... | collective-permute-start | bytes 4616 | tf_op jit(solution)/shard_map/ppermute | solution.py:76
  47.0 32.7 %all-to-all-start.1 = ((bf16[8,192,384]{2,1,0:T(8,128)(2,1)}), bf16[8,192,384]{2,1,0:T(8,128)(2,1)}, u32[]{:S(2)}, u32[]{:S(2)}) async-start(bf16[8,192,384]{2,1,0:T(8,128)(2,1)} %pad_maximum_fusion), calls=%async_computation.1 | async-start | bytes 2359296 | tf_op jit(solution)/shard_map/all_to_all | solution.py:94
  53.7 31.4 %collective-permute-start.3 = (bf16[768,640]{1,0:T(8,128)(2,1)}, bf16[768,640]{1,0:T(8,128)(2,1)}, u32[]{:S(2)}, u32[]{:S(2)}) collective-permute-start(bf16[768,640]{1,0:T(8,128)(2,1)} %slice.65), channel_id=1, source_target_pairs={{0,1},{1,0},{2,3},{3,2},{4,5},{5,4},{6,7},{7,6},{8,9},{9,8},{10,11... | collective-permute-start | bytes 2949128 | tf_op jit(solution)/shard_map/ppermute | solution.py:86
  53.7 31.4 %collective-permute-start.6 = (bf16[768,640]{1,0:T(8,128)(2,1)}, bf16[768,640]{1,0:T(8,128)(2,1)}, u32[]{:S(2)}, u32[]{:S(2)}) collective-permute-start(bf16[768,640]{1,0:T(8,128)(2,1)} %slice.65), channel_id=1, source_target_pairs={{0,2},{2,0},{1,3},{3,1},{4,6},{6,4},{5,7},{7,5},{8,10},{10,8},{9,1... | collective-permute-start | bytes 2949128 | tf_op jit(solution)/shard_map/ppermute | solution.py:86
  57.1 21.2 %collective-permute-start.5 = (f32[2,768]{1,0:T(2,128)S(1)}, f32[2,768]{1,0:T(2,128)S(1)}, u32[]{:S(2)}, u32[]{:S(2)}) collective-permute-start(f32[2,768]{1,0:T(2,128)S(1)} %pad_maximum_fusion.1), channel_id=1, source_target_pairs={{0,2},{2,0},{1,3},{3,1},{4,6},{6,4},{5,7},{7,5},{8,10},{10,8},{9,1... | collective-permute-start | bytes 18440 | tf_op jit(solution)/shard_map/ppermute | solution.py:87
  57.7 20.6 %collective-permute-start.2 = (f32[2,768]{1,0:T(2,128)S(1)}, f32[2,768]{1,0:T(2,128)S(1)}, u32[]{:S(2)}, u32[]{:S(2)}) collective-permute-start(f32[2,768]{1,0:T(2,128)S(1)} %pad_maximum_fusion.1), channel_id=1, source_target_pairs={{0,1},{1,0},{2,3},{3,2},{4,5},{5,4},{6,7},{7,6},{8,9},{9,8},{10,11... | collective-permute-start | bytes 18440 | tf_op jit(solution)/shard_map/ppermute | solution.py:87
  79.8 2.0 %copy-start.1 = (f32[768,768]{1,0:T(8,128)S(1)}, f32[768,768]{1,0:T(8,128)}, u32[]{:S(2)}) copy-start(f32[768,768]{1,0:T(8,128)} %and_select_fusion.1) | copy-start | bytes 7077892
  81.3 2.2 %collective-permute-start.4 = (bf16[768,384]{1,0:T(8,128)(2,1)S(1)}, bf16[768,384]{1,0:T(8,128)(2,1)S(1)}, u32[]{:S(2)}, u32[]{:S(2)}) collective-permute-start(bf16[768,384]{1,0:T(8,128)(2,1)S(1)} %bitcast.21), channel_id=1, source_target_pairs={{0,1},{1,0},{2,3},{3,2},{4,5},{5,4},{6,7},{7,6},{8,9},{9,8},{10,11... | collective-permute-start | bytes 1769480 | tf_op jit(solution)/shard_map/ppermute | solution.py:97
  88.1 6.2 %collective-permute-start.7 = (f32[768]{0:T(1024)S(1)}, f32[768]{0:T(1024)S(1)}, u32[]{:S(2)}, u32[]{:S(2)}) collective-permute-start(f32[768]{0:T(1024)S(1)} %select_reduce_fusion), channel_id=1, source_target_pairs={{0,1},{1,0},{2,3},{3,2},{4,5},{5,4},{6,7},{7,6},{8,9},{9,8},{10,11... | collective-permute-start | bytes 9224 | tf_op jit(solution)/shard_map/ppermute | solution.py:132

commit v18 on v16

--- a/solution.py
+++ b/solution.py
@@ -88,12 +88,12 @@
         pick_par = par_place[None, :] == jnp.arange(n_slot, dtype=jnp.int32)[:, None]
         send_own = jnp.dot(pick.astype(jnp.bfloat16), raw_b, preferred_element_type=jnp.float32)
         send_par = jnp.dot(pick_par.astype(jnp.bfloat16), par_b, preferred_element_type=jnp.float32)
-        send = jnp.concatenate(
-            [send_own.reshape(n_grp, cap, -1), send_par.reshape(n_grp, cap, -1)], axis=1
+        send = jnp.stack(
+            [send_own.reshape(n_grp, cap, -1), send_par.reshape(n_grp, cap, -1)], axis=0
         ).astype(jnp.bfloat16)
-        got = lax.all_to_all(send, "grp", split_axis=0, concat_axis=0, tiled=True)
-        got_b = got[:, :cap].reshape(n_slot, -1)
-        cross_b = got[:, cap:].reshape(n_slot, -1)
+        got = lax.all_to_all(send, "grp", split_axis=1, concat_axis=1, tiled=True)
+        got_b = got[0].reshape(n_slot, -1)
+        cross_b = got[1].reshape(n_slot, -1)
         keys_b = [cross_b, lax.ppermute(got_b, "split", pair)]
     else:
         half = emb_w // 2

time: 106 us -> 106 us (level)
    another operation x0 -> x1, other arithmetic: none -> 1.13 us  [local(): jnp.stack([send_own.reshape(n_grp, cap, -1), send_par.reshape(n_grp, cap,...]
    concatenate x1 -> x0, other arithmetic: 1.13 us -> none  [local(): jnp.concatenate([send_own.reshape(n_grp, cap, -1), send_par.reshape(n_grp...]
where the time goes in v18:
time: 106 us
  waiting for transfers between devices  40.3 us (38%)
  matrix products  26.2 us (25%)
  starting transfers between devices  16.1 us (15%)
  blocking collectives  9.64 us (9%)
  local copies, waits for them, and re-layouts  6.75 us (6%)
  other arithmetic  6.56 us (6%)
    all_to_all x1, waiting for transfers between devices, local(): got = lax.all_to_all(send, 'grp', split_axis=1, concat_axis=1, tiled=True)  17.8 us
    all_to_all x1, waiting for transfers between devices, route(): got = lax.all_to_all(send, 'grp', split_axis=0, concat_axis=0, tiled=True)  17.5 us
    dot_general x4, matrix products, block_best(): scores = jnp.einsum('qe,ke->qk', qa, ka, preferred_element_type=jnp.float32)  12.7 us
    all_to_all x1, blocking collectives, local(): lax.all_to_all(best.reshape(n_grp, cap), 'grp', split_axis=0, concat_axis...  9.64 us
    all_to_all x1, starting transfers between devices, route(): got = lax.all_to_all(send, 'grp', split_axis=0, concat_axis=0, tiled=True)  7.25 us
    dot_general x1, matrix products, embed_rows(): jnp.einsum('...h,he->...e', rows, weight, preferred_element_type=jnp.floa...  5.94 us
    ppermute x1, waiting for transfers between devices, local(): par_place = lax.ppermute(place, 'split', cross)  5.02 us
    all_to_all x1, starting transfers between devices, local(): got = lax.all_to_all(send, 'grp', split_axis=1, concat_axis=1, tiled=True)  4.45 us
  transfers between devices with their start and end apart: 10, of which 3 were waited for; matrix products, arithmetic and copies ran while one was open for 22% of the time, Pallas kernels for 0%

profile of v18, /device:TPU:0, one launch (start us, length us, event | category | flops | bytes accessed | tf_op | source)
XLA Modules:
  0.0 105.8 jit_solution(4683623332366857424)
XLA Ops:
  0.0 0.8 convert_element_type.106
  0.9 0.8 fusion.13
  1.9 5.9 %multiply_reduce_fusion = (f32[384]{0:T(512)S(1)}, f32[384,1024]{1,0:T(8,128)S(1)}) fusion(bf16[384,4096]{1,0:T(8,128)(2,1)S(1)} %copy-done, bf16[4096,1024]{1,0:T(8,128)(2,1)} %param.6), kind=kOutput, calls=%fused_computation.5 | convolution fusion | flops 3222011392 | bytes 13108736 | tf_op jit(solution)/shard_map/...h,he->...e/dot_general | solution.py:14
  8.3 0.6 copy-done.1
  9.0 1.8 %convolution_convert_fusion = bf16[768,768]{1,0:T(8,128)(2,1)} fusion(bf16[384,1024]{1,0:T(8,128)(2,1)S(1)} %multiply_convert_fusion, bf16[384,128]{1,0:T(8,128)(2,1)S(1)} %select_convert_fusion, s32[384]{0:T(512)S(1)} %convert_add_fusion, pred[768]{0:T(1024)(128)(4,1)S(1)} %copy-done.2, pred[768]{0:T(1024)(128)(4,1)S(1)} %iota_compare_fusion.9), kind=kOutput, calls=%fused_computation.6 | convolution fusion | flops 454459392 | bytes 1871872 | tf_op jit(solution)/shard_map/dot_general | solution.py:65
  10.8 7.2 %all-to-all-start = ((bf16[8,96,768]{2,1,0:T(8,128)(2,1)}), bf16[8,96,768]{2,1,0:T(8,128)(2,1)}, u32[]{:S(2)}, u32[]{:S(2)}) async-start(bf16[8,96,768]{2,1,0:T(8,128)(2,1)} %bitcast.31), calls=%async_computation | async-start | bytes 2359296 | tf_op jit(solution)/shard_map/all_to_all | solution.py:67
  18.1 1.0 slice.66
  19.1 1.6 %collective-permute-start.1 = (bf16[384,384]{1,0:T(8,128)(2,1)S(1)}, bf16[384,384]{1,0:T(8,128)(2,1)S(1)}, u32[]{:S(2)}, u32[]{:S(2)}) collective-permute-start(bf16[384,384]{1,0:T(8,128)(2,1)S(1)} %slice.66), channel_id=1, source_target_pairs={{0,2},{2,0},{1,3},{3,1},{4,6},{6,4},{5,7},{7,5},{8,10},{10,8},{9,1... | collective-permute-start | bytes 884744 | tf_op jit(solution)/shard_map/ppermute | solution.py:75
  21.1 1.5 %convolution_convert_fusion.2 = bf16[768,384]{1,0:T(8,128)(2,1)S(1)} fusion(s32[384]{0:T(512)S(1)} %convert_add_fusion, bf16[384,1024]{1,0:T(8,128)(2,1)} %copy-done.1), kind=kOutput, calls=%fused_computation.8 | convolution fusion | flops 227082240 | bytes 886272 | tf_op jit(solution)/shard_map/dot_general | solution.py:89
  22.6 5.0 %collective-permute-done = s32[384]{0:T(512)S(1)} collective-permute-done((s32[384]{0:T(512)S(1)}, s32[384]{0:T(512)S(1)}, u32[]{:S(2)}, u32[]{:S(2)}) %collective-permute-start) | collective-permute-done | bytes 1568 | tf_op jit(solution)/shard_map/ppermute | solution.py:76
  28.1 1.1 %pad_maximum_fusion = bf16[2,8,96,384]{3,2,0,1:T(8,128)(2,1)} fusion(bf16[1,8,96,384]{3,2,0,1:T(8,128)(2,1)S(1)} %bitcast.33, bf16[1,8,96,384]{3,2,0,1:T(8,128)(2,1)S(1)} %bitcast.32), kind=kLoop, calls=%fused_computation.9 | loop fusion | flops 589824 | bytes 2359296 | tf_op jit(solution)/shard_map/stack | solution.py:91
  29.3 17.5 %all-to-all-done = bf16[8,96,768]{2,1,0:T(8,128)(2,1)} async-done(((bf16[8,96,768]{2,1,0:T(8,128)(2,1)}), bf16[8,96,768]{2,1,0:T(8,128)(2,1)}, u32[]{:S(2)}, u32[]{:S(2)}) %all-to-all-start) | async-done | bytes 1179680 | tf_op jit(solution)/shard_map/all_to_all | solution.py:67
  46.7 4.4 %all-to-all-start.1 = ((bf16[2,8,96,384]{3,2,0,1:T(8,128)(2,1)}), bf16[2,8,96,384]{3,2,0,1:T(8,128)(2,1)}, u32[]{:S(2)}, u32[]{:S(2)}) async-start(bf16[2,8,96,384]{3,2,0,1:T(8,128)(2,1)} %pad_maximum_fusion), calls=%async_computation.1 | async-start | bytes 2359296 | tf_op jit(solution)/shard_map/all_to_all | solution.py:94
  51.2 1.8 %convert_reduce_fusion = (f32[768]{0:T(1024)S(1)}, f32[768]{0:T(1024)S(1)}) fusion(bf16[768,768]{1,0:T(8,128)(2,1)} %bitcast.1), kind=kLoop, calls=%fused_computation.24 | loop fusion | flops 6144 | bytes 12288 | tf_op jit(solution)/shard_map/eq | solution.py:110
  53.1 1.6 %collective-permute-start.2 = (f32[2,768]{1,0:T(2,128)S(1)}, f32[2,768]{1,0:T(2,128)S(1)}, u32[]{:S(2)}, u32[]{:S(2)}) collective-permute-start(f32[2,768]{1,0:T(2,128)S(1)} %pad_maximum_fusion.1), channel_id=1, source_target_pairs={{0,2},{2,0},{1,3},{3,1},{4,6},{6,4},{5,7},{7,5},{8,10},{10,8},{9,1... | collective-permute-start | bytes 18440 | tf_op jit(solution)/shard_map/ppermute | solution.py:87
  54.7 2.2 %slice.65 = bf16[768,640]{1,0:T(8,128)(2,1)} slice(bf16[768,768]{1,0:T(8,128)(2,1)} %bitcast.1), slice={[0:768], [0:640]} | slice | bytes 1966080 | tf_op jit(solution)/shard_map/slice | solution.py:31
  56.9 0.5 collective-permute-start.3
  57.5 4.0 %fusion.21 = f32[768,768]{0,1:T(8,128)} fusion(bf16[768,768]{1,0:T(8,128)(2,1)} %bitcast.1), kind=kOutput, calls=%fused_computation.69 | convolution fusion | flops 754974720 | bytes 3342336 | tf_op jit(solution)/shard_map/qe,ke->qk/dot_general | solution.py:108
  61.6 17.8 %all-to-all-done.1 = bf16[2,8,96,384]{3,2,0,1:T(8,128)(2,1)} async-done(((bf16[2,8,96,384]{3,2,0,1:T(8,128)(2,1)}), bf16[2,8,96,384]{3,2,0,1:T(8,128)(2,1)}, u32[]{:S(2)}, u32[]{:S(2)}) %all-to-all-start.1) | async-done | bytes 1179680 | tf_op jit(solution)/shard_map/all_to_all | solution.py:94
  79.4 1.4 %fusion.23 = (bf16[1,8,96,384]{3,2,0,1:T(8,128)(2,1)S(1)}, bf16[1,8,96,384]{3,2,0,1:T(8,128)(2,1)S(1)}) fusion(bf16[2,8,96,384]{3,2,0,1:T(8,128)(2,1)} %all-to-all-done.1), kind=kLoop, calls=%fused_computation.71 | loop fusion | bytes 2359296 | tf_op jit(solution)/shard_map/slice | solution.py:96
  80.9 0.8 fusion.24
  81.7 0.8 copy-done.3
  82.5 1.1 %select_reduce_fusion.3 = f32[768]{0:T(1024)S(1)} fusion(f32[768,768]{0,1:T(8,128)S(1)} %copy-done.3, bf16[768,384]{1,0:T(8,128)(2,1)S(1)} %bitcast.27, f32[768]{0:T(1024)S(1)} %get-tuple-element.6, f32[768]{0:T(1024)S(1)} %get-tuple-element.5, pred[768]{0:T(1024)(128)(4,1)S(1)} %broadcast_compare_fusion), kind=kOutput, calls=%fused_computation.3 | convolution fusion | flops 457112832 | bytes 2959104 | tf_op jit(solution)/shard_map/qe,ke->qk/dot_general | solution.py:109
  83.6 0.8 fusion.26
  84.4 0.8 fusion.25
  85.2 2.9 %select_reduce_fusion = f32[768]{0:T(1024)S(1)} fusion(f32[768,768]{0,1:T(8,128)S(1)} %fusion.26, bf16[768,640]{1,0:T(8,128)(2,1)} %collective-permute-done.5, bf16[768,640]{1,0:T(8,128)(2,1)} %collective-permute-done.3, f32[768]{0:T(1024)S(1)} %get-tuple-element.10, f32[768]{0:T(1024)S(1)} %get-tuple-element.9, f32[768]{0:T(1024)S(1)} %get-tuple-element.8, ...), kind=kOutput, calls=%fused_computation | convolution fusion | flops 759102720 | bytes 4341504 | tf_op jit(solution)/shard_map/qe,ke->qk/dot_general | solution.py:108
  88.2 2.9 %select_reduce_fusion.2 = f32[768]{0:T(1024)S(1)} fusion(f32[768,768]{0,1:T(8,128)S(1)} %fusion.24, bf16[768,640]{1,0:T(8,128)(2,1)} %collective-permute-done.3, f32[768]{0:T(1024)S(1)} %get-tuple-element.6, f32[768]{0:T(1024)S(1)} %get-tuple-element.5, f32[768]{0:T(1024)S(1)} %get-tuple-element.8, f32[768]{0:T(1024)S(1)} %get-tuple-element.7, ...), kind=kOutput, calls=%fused_computation.2 | convolution fusion | flops 759102720 | bytes 4341504 | tf_op jit(solution)/shard_map/qe,ke->qk/dot_general | solution.py:108
  91.1 2.9 %select_reduce_fusion.1 = f32[768]{0:T(1024)S(1)} fusion(f32[768,768]{0,1:T(8,128)S(1)} %fusion.25, bf16[768,640]{1,0:T(8,128)(2,1)} %collective-permute-done.5, f32[768]{0:T(1024)S(1)} %get-tuple-element.6, f32[768]{0:T(1024)S(1)} %get-tuple-element.5, f32[768]{0:T(1024)S(1)} %get-tuple-element.10, f32[768]{0:T(1024)S(1)} %get-tuple-element.9, ...), kind=kOutput, calls=%fused_computation.1 | convolution fusion | flops 759102720 | bytes 4341504 | tf_op jit(solution)/shard_map/qe,ke->qk/dot_general | solution.py:108
  94.1 9.6 %all_to_all.19 = f32[8,1,96]{2,1,0:T(1,128)S(1)} all-to-all(f32[8,1,96]{2,1,0:T(1,128)S(1)} %all_to_all.14), channel_id=1, replica_groups=mesh['grp'=8,'split'=4] {'grp'}, dimensions={0} | all-to-all | bytes 6144 | tf_op jit(solution)/shard_map/all_to_all | solution.py:122
  103.7 0.5 broadcast.144
  104.3 0.7 reduce.21
  105.0 0.8 select_reduce_fusion.4
  (38 shorter events, 2.2 us)
Async XLA Ops:
  0.0 1.9 %copy-start = (bf16[384,4096]{1,0:T(8,128)(2,1)S(1)}, bf16[384,4096]{1,0:T(8,128)(2,1)}, u32[]{:S(2)}) copy-start(bf16[384,4096]{1,0:T(8,128)(2,1)} %param.5) | copy-start | bytes 9437188
  7.9 1.1 %copy-start.2 = (pred[768]{0:T(1024)(128)(4,1)S(1)}, pred[768]{0:T(1024)(128)(4,1)}, u32[]{:S(2)}) copy-start(pred[768]{0:T(1024)(128)(4,1)} %constant.58.clone.1) | copy-start | bytes 2308
  8.0 0.9 copy-start.1
  10.8 35.9 %all-to-all-start = ((bf16[8,96,768]{2,1,0:T(8,128)(2,1)}), bf16[8,96,768]{2,1,0:T(8,128)(2,1)}, u32[]{:S(2)}, u32[]{:S(2)}) async-start(bf16[8,96,768]{2,1,0:T(8,128)(2,1)} %bitcast.31), calls=%async_computation | async-start | bytes 2359296 | tf_op jit(solution)/shard_map/all_to_all | solution.py:67
  19.1 8.6 %collective-permute-start.1 = (bf16[384,384]{1,0:T(8,128)(2,1)S(1)}, bf16[384,384]{1,0:T(8,128)(2,1)S(1)}, u32[]{:S(2)}, u32[]{:S(2)}) collective-permute-start(bf16[384,384]{1,0:T(8,128)(2,1)S(1)} %slice.66), channel_id=1, source_target_pairs={{0,2},{2,0},{1,3},{3,1},{4,6},{6,4},{5,7},{7,5},{8,10},{10,8},{9,1... | collective-permute-start | bytes 884744 | tf_op jit(solution)/shard_map/ppermute | solution.py:75
  20.6 7.0 %collective-permute-start = (s32[384]{0:T(512)S(1)}, s32[384]{0:T(512)S(1)}, u32[]{:S(2)}, u32[]{:S(2)}) collective-permute-start(s32[384]{0:T(512)S(1)} %convert_add_fusion), channel_id=1, source_target_pairs={{0,2},{2,0},{1,3},{3,1},{4,6},{6,4},{5,7},{7,5},{8,10},{10,8},{9,1... | collective-permute-start | bytes 4616 | tf_op jit(solution)/shard_map/ppermute | solution.py:76
  46.7 32.7 %all-to-all-start.1 = ((bf16[2,8,96,384]{3,2,0,1:T(8,128)(2,1)}), bf16[2,8,96,384]{3,2,0,1:T(8,128)(2,1)}, u32[]{:S(2)}, u32[]{:S(2)}) async-start(bf16[2,8,96,384]{3,2,0,1:T(8,128)(2,1)} %pad_maximum_fusion), calls=%async_computation.1 | async-start | bytes 2359296 | tf_op jit(solution)/shard_map/all_to_all | solution.py:94
  53.0 8.4 %collective-permute-start.4 = (f32[2,768]{1,0:T(2,128)S(1)}, f32[2,768]{1,0:T(2,128)S(1)}, u32[]{:S(2)}, u32[]{:S(2)}) collective-permute-start(f32[2,768]{1,0:T(2,128)S(1)} %pad_maximum_fusion.1), channel_id=1, source_target_pairs={{0,1},{1,0},{2,3},{3,2},{4,5},{5,4},{6,7},{7,6},{8,9},{9,8},{10,11... | collective-permute-start | bytes 18440 | tf_op jit(solution)/shard_map/ppermute | solution.py:87
  53.1 8.4 %collective-permute-start.2 = (f32[2,768]{1,0:T(2,128)S(1)}, f32[2,768]{1,0:T(2,128)S(1)}, u32[]{:S(2)}, u32[]{:S(2)}) collective-permute-start(f32[2,768]{1,0:T(2,128)S(1)} %pad_maximum_fusion.1), channel_id=1, source_target_pairs={{0,2},{2,0},{1,3},{3,1},{4,6},{6,4},{5,7},{7,5},{8,10},{10,8},{9,1... | collective-permute-start | bytes 18440 | tf_op jit(solution)/shard_map/ppermute | solution.py:87
  56.9 28.2 %collective-permute-start.3 = (bf16[768,640]{1,0:T(8,128)(2,1)}, bf16[768,640]{1,0:T(8,128)(2,1)}, u32[]{:S(2)}, u32[]{:S(2)}) collective-permute-start(bf16[768,640]{1,0:T(8,128)(2,1)} %slice.65), channel_id=1, source_target_pairs={{0,2},{2,0},{1,3},{3,1},{4,6},{6,4},{5,7},{7,5},{8,10},{10,8},{9,1... | collective-permute-start | bytes 2949128 | tf_op jit(solution)/shard_map/ppermute | solution.py:86
  57.4 27.8 %collective-permute-start.5 = (bf16[768,640]{1,0:T(8,128)(2,1)}, bf16[768,640]{1,0:T(8,128)(2,1)}, u32[]{:S(2)}, u32[]{:S(2)}) collective-permute-start(bf16[768,640]{1,0:T(8,128)(2,1)} %slice.65), channel_id=1, source_target_pairs={{0,1},{1,0},{2,3},{3,2},{4,5},{5,4},{6,7},{7,6},{8,9},{9,8},{10,11... | collective-permute-start | bytes 2949128 | tf_op jit(solution)/shard_map/ppermute | solution.py:86
  80.8 1.7 %copy-start.3 = (f32[768,768]{0,1:T(8,128)S(1)}, f32[768,768]{0,1:T(8,128)}, u32[]{:S(2)}) copy-start(f32[768,768]{0,1:T(8,128)} %fusion.21) | copy-start | bytes 7077892
  80.8 2.8 %collective-permute-start.6 = (bf16[768,384]{1,0:T(8,128)(2,1)S(1)}, bf16[768,384]{1,0:T(8,128)(2,1)S(1)}, u32[]{:S(2)}, u32[]{:S(2)}) collective-permute-start(bf16[768,384]{1,0:T(8,128)(2,1)S(1)} %bitcast.25), channel_id=1, source_target_pairs={{0,1},{1,0},{2,3},{3,2},{4,5},{5,4},{6,7},{7,6},{8,9},{9,8},{10,11... | collective-permute-start | bytes 1769480 | tf_op jit(solution)/shard_map/ppermute | solution.py:97
  88.1 5.9 %collective-permute-start.7 = (f32[768]{0:T(1024)S(1)}, f32[768]{0:T(1024)S(1)}, u32[]{:S(2)}, u32[]{:S(2)}) collective-permute-start(f32[768]{0:T(1024)S(1)} %select_reduce_fusion), channel_id=1, source_target_pairs={{0,1},{1,0},{2,3},{3,2},{4,5},{5,4},{6,7},{7,6},{8,9},{9,8},{10,11... | collective-permute-start | bytes 9224 | tf_op jit(solution)/shard_map/ppermute | solution.py:120

commit v19 on v16

--- a/solution.py
+++ b/solution.py
@@ -112,7 +112,7 @@
 
     mine = (q_emb, got_b, jnp.stack([q_lab, q_ord]))
     best = block_best(*mine, *mine)
-    for k_a, k_b, k_m in zip(keys_a, keys_b, keys_m):
+    for k_a, k_b, k_m in reversed(list(zip(keys_a, keys_b, keys_m))):
         best = jnp.maximum(best, block_best(*mine, k_a, k_b, k_m))
     if n_split == 4:
         near = (keys_a[1], keys_b[1], keys_m[1])

time: 106 us -> 106 us (level)
  no operation moved by 1% of the time
where the time goes in v19:
time: 106 us
  waiting for transfers between devices  39.9 us (38%)
  matrix products  26.2 us (25%)
  starting transfers between devices  16.5 us (16%)
  blocking collectives  9.64 us (9%)
  local copies, waits for them, and re-layouts  6.75 us (6%)
  other arithmetic  6.55 us (6%)
    all_to_all x1, waiting for transfers between devices, route(): got = lax.all_to_all(send, 'grp', split_axis=0, concat_axis=0, tiled=True)  17.5 us
    all_to_all x1, waiting for transfers between devices, local(): got = lax.all_to_all(send, 'grp', split_axis=0, concat_axis=0, tiled=True)  17.4 us
    dot_general x4, matrix products, block_best(): scores = jnp.einsum('qe,ke->qk', qa, ka, preferred_element_type=jnp.float32)  12.7 us
    all_to_all x1, blocking collectives, local(): lax.all_to_all(best.reshape(n_grp, cap), 'grp', split_axis=0, concat_axis...  9.64 us
    all_to_all x1, starting transfers between devices, route(): got = lax.all_to_all(send, 'grp', split_axis=0, concat_axis=0, tiled=True)  7.25 us
    dot_general x1, matrix products, embed_rows(): jnp.einsum('...h,he->...e', rows, weight, preferred_element_type=jnp.floa...  5.94 us
    ppermute x1, waiting for transfers between devices, local(): par_place = lax.ppermute(place, 'split', cross)  5.02 us
    all_to_all x1, starting transfers between devices, local(): got = lax.all_to_all(send, 'grp', split_axis=0, concat_axis=0, tiled=True)  4.45 us
  transfers between devices with their start and end apart: 10, of which 3 were waited for; matrix products, arithmetic and copies ran while one was open for 22% of the time, Pallas kernels for 0%

profile of v19, /device:TPU:0, one launch (start us, length us, event | category | flops | bytes accessed | tf_op | source)
XLA Modules:
  0.0 105.8 jit_solution(8911296033894902570)
XLA Ops:
  0.0 0.8 convert_element_type.106
  0.9 0.8 fusion.13
  1.9 5.9 %multiply_reduce_fusion = (f32[384]{0:T(512)S(1)}, f32[384,1024]{1,0:T(8,128)S(1)}) fusion(bf16[384,4096]{1,0:T(8,128)(2,1)S(1)} %copy-done, bf16[4096,1024]{1,0:T(8,128)(2,1)} %param.6), kind=kOutput, calls=%fused_computation.5 | convolution fusion | flops 3222011392 | bytes 13108736 | tf_op jit(solution)/shard_map/...h,he->...e/dot_general | solution.py:14
  8.3 0.6 copy-done.1
  9.0 1.8 %convolution_convert_fusion = bf16[768,768]{1,0:T(8,128)(2,1)} fusion(bf16[384,1024]{1,0:T(8,128)(2,1)S(1)} %multiply_convert_fusion, bf16[384,128]{1,0:T(8,128)(2,1)S(1)} %select_convert_fusion, s32[384]{0:T(512)S(1)} %convert_add_fusion, pred[768]{0:T(1024)(128)(4,1)S(1)} %copy-done.2, pred[768]{0:T(1024)(128)(4,1)S(1)} %iota_compare_fusion.9), kind=kOutput, calls=%fused_computation.6 | convolution fusion | flops 454459392 | bytes 1871872 | tf_op jit(solution)/shard_map/dot_general | solution.py:65
  10.8 7.2 %all-to-all-start = ((bf16[8,96,768]{2,1,0:T(8,128)(2,1)}), bf16[8,96,768]{2,1,0:T(8,128)(2,1)}, u32[]{:S(2)}, u32[]{:S(2)}) async-start(bf16[8,96,768]{2,1,0:T(8,128)(2,1)} %bitcast.27), calls=%async_computation | async-start | bytes 2359296 | tf_op jit(solution)/shard_map/all_to_all | solution.py:67
  18.1 1.0 slice.66
  19.1 1.6 %collective-permute-start.1 = (bf16[384,384]{1,0:T(8,128)(2,1)S(1)}, bf16[384,384]{1,0:T(8,128)(2,1)S(1)}, u32[]{:S(2)}, u32[]{:S(2)}) collective-permute-start(bf16[384,384]{1,0:T(8,128)(2,1)S(1)} %slice.66), channel_id=1, source_target_pairs={{0,2},{2,0},{1,3},{3,1},{4,6},{6,4},{5,7},{7,5},{8,10},{10,8},{9,1... | collective-permute-start | bytes 884744 | tf_op jit(solution)/shard_map/ppermute | solution.py:75
  21.1 1.5 %convolution_convert_fusion.2 = bf16[768,384]{1,0:T(8,128)(2,1)S(1)} fusion(s32[384]{0:T(512)S(1)} %convert_add_fusion, bf16[384,1024]{1,0:T(8,128)(2,1)} %copy-done.1), kind=kOutput, calls=%fused_computation.8 | convolution fusion | flops 227082240 | bytes 886272 | tf_op jit(solution)/shard_map/dot_general | solution.py:89
  22.6 5.0 %collective-permute-done = s32[384]{0:T(512)S(1)} collective-permute-done((s32[384]{0:T(512)S(1)}, s32[384]{0:T(512)S(1)}, u32[]{:S(2)}, u32[]{:S(2)}) %collective-permute-start) | collective-permute-done | bytes 1568 | tf_op jit(solution)/shard_map/ppermute | solution.py:76
  28.1 1.1 %pad_maximum_fusion = bf16[8,192,384]{2,1,0:T(8,128)(2,1)} fusion(bf16[8,96,384]{2,1,0:T(8,128)(2,1)S(1)} %bitcast.29, bf16[8,96,384]{2,1,0:T(8,128)(2,1)S(1)} %bitcast.28), kind=kLoop, calls=%fused_computation.9 | loop fusion | flops 2359296 | bytes 2359296 | tf_op jit(solution)/shard_map/concatenate | solution.py:91
  29.3 17.5 %all-to-all-done = bf16[8,96,768]{2,1,0:T(8,128)(2,1)} async-done(((bf16[8,96,768]{2,1,0:T(8,128)(2,1)}), bf16[8,96,768]{2,1,0:T(8,128)(2,1)}, u32[]{:S(2)}, u32[]{:S(2)}) %all-to-all-start) | async-done | bytes 1179680 | tf_op jit(solution)/shard_map/all_to_all | solution.py:67
  46.7 4.4 %all-to-all-start.1 = ((bf16[8,192,384]{2,1,0:T(8,128)(2,1)}), bf16[8,192,384]{2,1,0:T(8,128)(2,1)}, u32[]{:S(2)}, u32[]{:S(2)}) async-start(bf16[8,192,384]{2,1,0:T(8,128)(2,1)} %pad_maximum_fusion), calls=%async_computation.1 | async-start | bytes 2359296 | tf_op jit(solution)/shard_map/all_to_all | solution.py:94
  51.2 1.8 %convert_reduce_fusion = (f32[768]{0:T(1024)S(1)}, f32[768]{0:T(1024)S(1)}) fusion(bf16[768,768]{1,0:T(8,128)(2,1)} %bitcast.1), kind=kLoop, calls=%fused_computation.24 | loop fusion | flops 6144 | bytes 12288 | tf_op jit(solution)/shard_map/eq | solution.py:110
  53.0 1.6 %collective-permute-start.5 = (f32[2,768]{1,0:T(2,128)S(1)}, f32[2,768]{1,0:T(2,128)S(1)}, u32[]{:S(2)}, u32[]{:S(2)}) collective-permute-start(f32[2,768]{1,0:T(2,128)S(1)} %pad_maximum_fusion.1), channel_id=1, source_target_pairs={{0,2},{2,0},{1,3},{3,1},{4,6},{6,4},{5,7},{7,5},{8,10},{10,8},{9,1... | collective-permute-start | bytes 18440 | tf_op jit(solution)/shard_map/ppermute | solution.py:87
  54.6 2.2 %slice.65 = bf16[768,640]{1,0:T(8,128)(2,1)} slice(bf16[768,768]{1,0:T(8,128)(2,1)} %bitcast.1), slice={[0:768], [0:640]} | slice | bytes 1966080 | tf_op jit(solution)/shard_map/slice | solution.py:31
  56.9 0.5 collective-permute-start.3
  57.9 4.0 %fusion.21 = f32[768,768]{0,1:T(8,128)} fusion(bf16[768,768]{1,0:T(8,128)(2,1)} %bitcast.1), kind=kOutput, calls=%fused_computation.69 | convolution fusion | flops 754974720 | bytes 3342336 | tf_op jit(solution)/shard_map/qe,ke->qk/dot_general | solution.py:108
  62.0 17.4 %all-to-all-done.1 = bf16[8,192,384]{2,1,0:T(8,128)(2,1)} async-done(((bf16[8,192,384]{2,1,0:T(8,128)(2,1)}), bf16[8,192,384]{2,1,0:T(8,128)(2,1)}, u32[]{:S(2)}, u32[]{:S(2)}) %all-to-all-start.1) | async-done | bytes 1179680 | tf_op jit(solution)/shard_map/all_to_all | solution.py:94
  79.4 1.4 %fusion.23 = (bf16[8,96,384]{2,1,0:T(8,128)(2,1)S(1)}, bf16[8,96,384]{2,1,0:T(8,128)(2,1)S(1)}) fusion(bf16[8,192,384]{2,1,0:T(8,128)(2,1)} %all-to-all-done.1), kind=kLoop, calls=%fused_computation.71 | loop fusion | bytes 2359296 | tf_op jit(solution)/shard_map/slice | solution.py:96
  80.9 0.8 fusion.25
  81.7 0.8 copy-done.3
  82.5 1.1 %select_reduce_fusion.3 = f32[768]{0:T(1024)S(1)} fusion(f32[768,768]{0,1:T(8,128)S(1)} %copy-done.3, bf16[768,384]{1,0:T(8,128)(2,1)S(1)} %bitcast.23, f32[768]{0:T(1024)S(1)} %get-tuple-element.6, f32[768]{0:T(1024)S(1)} %get-tuple-element.5, pred[768]{0:T(1024)(128)(4,1)S(1)} %broadcast_compare_fusion), kind=kOutput, calls=%fused_computation.3 | convolution fusion | flops 457112832 | bytes 2959104 | tf_op jit(solution)/shard_map/qe,ke->qk/dot_general | solution.py:109
  83.6 0.8 fusion.26
  84.4 0.8 fusion.24
  85.2 2.9 %select_reduce_fusion = f32[768]{0:T(1024)S(1)} fusion(f32[768,768]{0,1:T(8,128)S(1)} %fusion.26, bf16[768,640]{1,0:T(8,128)(2,1)} %collective-permute-done.3, bf16[768,640]{1,0:T(8,128)(2,1)} %collective-permute-done.6, f32[768]{0:T(1024)S(1)} %get-tuple-element.10, f32[768]{0:T(1024)S(1)} %get-tuple-element.9, f32[768]{0:T(1024)S(1)} %get-tuple-element.8, ...), kind=kOutput, calls=%fused_computation | convolution fusion | flops 759102720 | bytes 4341504 | tf_op jit(solution)/shard_map/qe,ke->qk/dot_general | solution.py:108
  88.2 2.9 %select_reduce_fusion.1 = f32[768]{0:T(1024)S(1)} fusion(f32[768,768]{0,1:T(8,128)S(1)} %fusion.25, bf16[768,640]{1,0:T(8,128)(2,1)} %collective-permute-done.6, f32[768]{0:T(1024)S(1)} %get-tuple-element.6, f32[768]{0:T(1024)S(1)} %get-tuple-element.5, f32[768]{0:T(1024)S(1)} %get-tuple-element.8, f32[768]{0:T(1024)S(1)} %get-tuple-element.7, ...), kind=kOutput, calls=%fused_computation.1 | convolution fusion | flops 759102720 | bytes 4341504 | tf_op jit(solution)/shard_map/qe,ke->qk/dot_general | solution.py:108
  91.1 2.9 %select_reduce_fusion.2 = f32[768]{0:T(1024)S(1)} fusion(f32[768,768]{0,1:T(8,128)S(1)} %fusion.24, bf16[768,640]{1,0:T(8,128)(2,1)} %collective-permute-done.3, f32[768]{0:T(1024)S(1)} %get-tuple-element.6, f32[768]{0:T(1024)S(1)} %get-tuple-element.5, f32[768]{0:T(1024)S(1)} %get-tuple-element.10, f32[768]{0:T(1024)S(1)} %get-tuple-element.9, ...), kind=kOutput, calls=%fused_computation.2 | convolution fusion | flops 759102720 | bytes 4341504 | tf_op jit(solution)/shard_map/qe,ke->qk/dot_general | solution.py:108
  94.1 9.6 %all_to_all.19 = f32[8,1,96]{2,1,0:T(1,128)S(1)} all-to-all(f32[8,1,96]{2,1,0:T(1,128)S(1)} %all_to_all.14), channel_id=1, replica_groups=mesh['grp'=8,'split'=4] {'grp'}, dimensions={0} | all-to-all | bytes 6144 | tf_op jit(solution)/shard_map/all_to_all | solution.py:122
  103.7 0.5 broadcast.144
  104.3 0.7 reduce.21
  105.0 0.8 select_reduce_fusion.4
  (38 shorter events, 2.6 us)
Async XLA Ops:
  0.0 1.9 %copy-start = (bf16[384,4096]{1,0:T(8,128)(2,1)S(1)}, bf16[384,4096]{1,0:T(8,128)(2,1)}, u32[]{:S(2)}) copy-start(bf16[384,4096]{1,0:T(8,128)(2,1)} %param.5) | copy-start | bytes 9437188
  7.9 1.1 %copy-start.2 = (pred[768]{0:T(1024)(128)(4,1)S(1)}, pred[768]{0:T(1024)(128)(4,1)}, u32[]{:S(2)}) copy-start(pred[768]{0:T(1024)(128)(4,1)} %constant.58.clone.1) | copy-start | bytes 2308
  8.0 0.9 copy-start.1
  10.8 35.9 %all-to-all-start = ((bf16[8,96,768]{2,1,0:T(8,128)(2,1)}), bf16[8,96,768]{2,1,0:T(8,128)(2,1)}, u32[]{:S(2)}, u32[]{:S(2)}) async-start(bf16[8,96,768]{2,1,0:T(8,128)(2,1)} %bitcast.27), calls=%async_computation | async-start | bytes 2359296 | tf_op jit(solution)/shard_map/all_to_all | solution.py:67
  19.1 8.6 %collective-permute-start.1 = (bf16[384,384]{1,0:T(8,128)(2,1)S(1)}, bf16[384,384]{1,0:T(8,128)(2,1)S(1)}, u32[]{:S(2)}, u32[]{:S(2)}) collective-permute-start(bf16[384,384]{1,0:T(8,128)(2,1)S(1)} %slice.66), channel_id=1, source_target_pairs={{0,2},{2,0},{1,3},{3,1},{4,6},{6,4},{5,7},{7,5},{8,10},{10,8},{9,1... | collective-permute-start | bytes 884744 | tf_op jit(solution)/shard_map/ppermute | solution.py:75
  20.6 7.0 %collective-permute-start = (s32[384]{0:T(512)S(1)}, s32[384]{0:T(512)S(1)}, u32[]{:S(2)}, u32[]{:S(2)}) collective-permute-start(s32[384]{0:T(512)S(1)} %convert_add_fusion), channel_id=1, source_target_pairs={{0,2},{2,0},{1,3},{3,1},{4,6},{6,4},{5,7},{7,5},{8,10},{10,8},{9,1... | collective-permute-start | bytes 4616 | tf_op jit(solution)/shard_map/ppermute | solution.py:76
  46.7 32.7 %all-to-all-start.1 = ((bf16[8,192,384]{2,1,0:T(8,128)(2,1)}), bf16[8,192,384]{2,1,0:T(8,128)(2,1)}, u32[]{:S(2)}, u32[]{:S(2)}) async-start(bf16[8,192,384]{2,1,0:T(8,128)(2,1)} %pad_maximum_fusion), calls=%async_computation.1 | async-start | bytes 2359296 | tf_op jit(solution)/shard_map/all_to_all | solution.py:94
  53.0 8.9 %collective-permute-start.5 = (f32[2,768]{1,0:T(2,128)S(1)}, f32[2,768]{1,0:T(2,128)S(1)}, u32[]{:S(2)}, u32[]{:S(2)}) collective-permute-start(f32[2,768]{1,0:T(2,128)S(1)} %pad_maximum_fusion.1), channel_id=1, source_target_pairs={{0,2},{2,0},{1,3},{3,1},{4,6},{6,4},{5,7},{7,5},{8,10},{10,8},{9,1... | collective-permute-start | bytes 18440 | tf_op jit(solution)/shard_map/ppermute | solution.py:87
  54.6 7.3 %collective-permute-start.2 = (f32[2,768]{1,0:T(2,128)S(1)}, f32[2,768]{1,0:T(2,128)S(1)}, u32[]{:S(2)}, u32[]{:S(2)}) collective-permute-start(f32[2,768]{1,0:T(2,128)S(1)} %pad_maximum_fusion.1), channel_id=1, source_target_pairs={{0,1},{1,0},{2,3},{3,2},{4,5},{5,4},{6,7},{7,6},{8,9},{9,8},{10,11... | collective-permute-start | bytes 18440 | tf_op jit(solution)/shard_map/ppermute | solution.py:87
  56.9 28.3 %collective-permute-start.3 = (bf16[768,640]{1,0:T(8,128)(2,1)}, bf16[768,640]{1,0:T(8,128)(2,1)}, u32[]{:S(2)}, u32[]{:S(2)}) collective-permute-start(bf16[768,640]{1,0:T(8,128)(2,1)} %slice.65), channel_id=1, source_target_pairs={{0,1},{1,0},{2,3},{3,2},{4,5},{5,4},{6,7},{7,6},{8,9},{9,8},{10,11... | collective-permute-start | bytes 2949128 | tf_op jit(solution)/shard_map/ppermute | solution.py:86
  57.4 27.8 %collective-permute-start.6 = (bf16[768,640]{1,0:T(8,128)(2,1)}, bf16[768,640]{1,0:T(8,128)(2,1)}, u32[]{:S(2)}, u32[]{:S(2)}) collective-permute-start(bf16[768,640]{1,0:T(8,128)(2,1)} %slice.65), channel_id=1, source_target_pairs={{0,2},{2,0},{1,3},{3,1},{4,6},{6,4},{5,7},{7,5},{8,10},{10,8},{9,1... | collective-permute-start | bytes 2949128 | tf_op jit(solution)/shard_map/ppermute | solution.py:86
  80.8 1.7 %copy-start.3 = (f32[768,768]{0,1:T(8,128)S(1)}, f32[768,768]{0,1:T(8,128)}, u32[]{:S(2)}) copy-start(f32[768,768]{0,1:T(8,128)} %fusion.21) | copy-start | bytes 7077892
  80.8 2.8 %collective-permute-start.4 = (bf16[768,384]{1,0:T(8,128)(2,1)S(1)}, bf16[768,384]{1,0:T(8,128)(2,1)S(1)}, u32[]{:S(2)}, u32[]{:S(2)}) collective-permute-start(bf16[768,384]{1,0:T(8,128)(2,1)S(1)} %bitcast.21), channel_id=1, source_target_pairs={{0,1},{1,0},{2,3},{3,2},{4,5},{5,4},{6,7},{7,6},{8,9},{9,8},{10,11... | collective-permute-start | bytes 1769480 | tf_op jit(solution)/shard_map/ppermute | solution.py:97
  88.1 5.9 %collective-permute-start.7 = (f32[768]{0:T(1024)S(1)}, f32[768]{0:T(1024)S(1)}, u32[]{:S(2)}, u32[]{:S(2)}) collective-permute-start(f32[768]{0:T(1024)S(1)} %select_reduce_fusion), channel_id=1, source_target_pairs={{0,1},{1,0},{2,3},{3,2},{4,5},{5,4},{6,7},{7,6},{8,9},{9,8},{10,11... | collective-permute-start | bytes 9224 | tf_op jit(solution)/shard_map/ppermute | solution.py:120

commit v20 on v19

--- a/solution.py
+++ b/solution.py
@@ -112,12 +112,19 @@
 
     mine = (q_emb, got_b, jnp.stack([q_lab, q_ord]))
     best = block_best(*mine, *mine)
-    for k_a, k_b, k_m in reversed(list(zip(keys_a, keys_b, keys_m))):
-        best = jnp.maximum(best, block_best(*mine, k_a, k_b, k_m))
     if n_split == 4:
-        near = (keys_a[1], keys_b[1], keys_m[1])
-        far = (keys_a[0], keys_b[0], keys_m[0])
-        best = jnp.maximum(best, lax.ppermute(block_best(*near, *far), "split", pair))
+        best = jnp.maximum(best, block_best(*mine, keys_a[1], keys_b[1], keys_m[1]))
+        both = (
+            jnp.concatenate([q_emb, keys_a[1]], axis=0),
+            jnp.concatenate([got_b, keys_b[1]], axis=0),
+            jnp.concatenate([mine[2], keys_m[1]], axis=1),
+        )
+        far = block_best(*both, keys_a[0], keys_b[0], keys_m[0])
+        best = jnp.maximum(best, far[:n_slot])
+        best = jnp.maximum(best, lax.ppermute(far[n_slot:], "split", pair))
+    else:
+        for k_a, k_b, k_m in zip(keys_a, keys_b, keys_m):
+            best = jnp.maximum(best, block_best(*mine, k_a, k_b, k_m))
 
     returned = lax.all_to_all(
         best.reshape(n_grp, cap), "grp", split_axis=0, concat_axis=0, tiled=True

time: 106 us -> 107 us (level)
  blocking collectives: 9.64 us -> 12 us
  matrix products: 26.2 us -> 24.5 us
    all_to_all x1, blocking collectives: 9.64 us -> 12 us  [local(): lax.all_to_all(best.reshape(n_grp, cap), 'grp', split_axis=0, concat_axis...]
    dot_general x4 -> x3, matrix products: 12.7 us -> 11.2 us  [block_best(): scores = jnp.einsum('qe,ke->qk', qa, ka, preferred_element_type=jnp.float32)]
    dot_general x4 -> x3, matrix products: 3.49 us -> 3.31 us  [block_best(): jnp.einsum('qe,ke->qk', qb, kb, preferred_element_type=jnp.float32)]
  transfers between devices with their start and end apart: 10 -> 10, of which waited for: 3 -> 5; matrix products, arithmetic and copies ran while one was open for 22% -> 19% of each run, Pallas kernels for 0% -> 0%
where the time goes in v20:
time: 107 us
  waiting for transfers between devices  40.8 us (38%)
  matrix products  24.5 us (23%)
  starting transfers between devices  16.3 us (15%)
  blocking collectives  12 us (11%)
  other arithmetic  6.56 us (6%)
  local copies, waits for them, and re-layouts  6.47 us (6%)
    all_to_all x1, waiting for transfers between devices, local(): got = lax.all_to_all(send, 'grp', split_axis=0, concat_axis=0, tiled=True)  17.7 us
    all_to_all x1, waiting for transfers between devices, route(): got = lax.all_to_all(send, 'grp', split_axis=0, concat_axis=0, tiled=True)  17.5 us
    all_to_all x1, blocking collectives, local(): lax.all_to_all(best.reshape(n_grp, cap), 'grp', split_axis=0, concat_axis...  12 us
    dot_general x3, matrix products, block_best(): scores = jnp.einsum('qe,ke->qk', qa, ka, preferred_element_type=jnp.float32)  11.2 us
    all_to_all x1, starting transfers between devices, route(): got = lax.all_to_all(send, 'grp', split_axis=0, concat_axis=0, tiled=True)  7.25 us
    dot_general x1, matrix products, embed_rows(): jnp.einsum('...h,he->...e', rows, weight, preferred_element_type=jnp.floa...  5.94 us
    ppermute x1, waiting for transfers between devices, local(): par_place = lax.ppermute(place, 'split', cross)  5.02 us
    all_to_all x1, starting transfers between devices, local(): got = lax.all_to_all(send, 'grp', split_axis=0, concat_axis=0, tiled=True)  4.45 us
  transfers between devices with their start and end apart: 10, of which 5 were waited for; matrix products, arithmetic and copies ran while one was open for 19% of the time, Pallas kernels for 0%

profile of v20, /device:TPU:0, one launch (start us, length us, event | category | flops | bytes accessed | tf_op | source)
XLA Modules:
  0.0 106.9 jit_solution(15334634949183080345)
XLA Ops:
  0.0 0.8 convert_element_type.106
  0.9 0.8 fusion.21
  1.9 5.9 %multiply_reduce_fusion = (f32[384]{0:T(512)S(1)}, f32[384,1024]{1,0:T(8,128)S(1)}) fusion(bf16[384,4096]{1,0:T(8,128)(2,1)S(1)} %copy-done, bf16[4096,1024]{1,0:T(8,128)(2,1)} %param.6), kind=kOutput, calls=%fused_computation.7 | convolution fusion | flops 3222011392 | bytes 13108736 | tf_op jit(solution)/shard_map/...h,he->...e/dot_general | solution.py:14
  8.3 0.6 copy-done.1
  9.0 1.8 %convolution_convert_fusion = bf16[768,768]{1,0:T(8,128)(2,1)} fusion(bf16[384,1024]{1,0:T(8,128)(2,1)S(1)} %multiply_convert_fusion, bf16[384,128]{1,0:T(8,128)(2,1)S(1)} %select_convert_fusion, s32[384]{0:T(512)S(1)} %convert_add_fusion, pred[768]{0:T(1024)(128)(4,1)S(1)} %copy-done.2, pred[768]{0:T(1024)(128)(4,1)S(1)} %iota_compare_fusion.9), kind=kOutput, calls=%fused_computation.8 | convolution fusion | flops 454459392 | bytes 1871872 | tf_op jit(solution)/shard_map/dot_general | solution.py:65
  10.8 7.2 %all-to-all-start = ((bf16[8,96,768]{2,1,0:T(8,128)(2,1)}), bf16[8,96,768]{2,1,0:T(8,128)(2,1)}, u32[]{:S(2)}, u32[]{:S(2)}) async-start(bf16[8,96,768]{2,1,0:T(8,128)(2,1)} %bitcast.21), calls=%async_computation | async-start | bytes 2359296 | tf_op jit(solution)/shard_map/all_to_all | solution.py:67
  18.1 1.0 slice.77
  19.1 1.6 %collective-permute-start.1 = (bf16[384,384]{1,0:T(8,128)(2,1)S(1)}, bf16[384,384]{1,0:T(8,128)(2,1)S(1)}, u32[]{:S(2)}, u32[]{:S(2)}) collective-permute-start(bf16[384,384]{1,0:T(8,128)(2,1)S(1)} %slice.77), channel_id=1, source_target_pairs={{0,2},{2,0},{1,3},{3,1},{4,6},{6,4},{5,7},{7,5},{8,10},{10,8},{9,1... | collective-permute-start | bytes 884744 | tf_op jit(solution)/shard_map/ppermute | solution.py:75
  20.6 0.5 collective-permute-start
  21.1 1.5 %convolution_convert_fusion.2 = bf16[768,384]{1,0:T(8,128)(2,1)S(1)} fusion(s32[384]{0:T(512)S(1)} %convert_add_fusion, bf16[384,1024]{1,0:T(8,128)(2,1)} %copy-done.1), kind=kOutput, calls=%fused_computation.10 | convolution fusion | flops 227082240 | bytes 886272 | tf_op jit(solution)/shard_map/dot_general | solution.py:89
  22.6 5.0 %collective-permute-done = s32[384]{0:T(512)S(1)} collective-permute-done((s32[384]{0:T(512)S(1)}, s32[384]{0:T(512)S(1)}, u32[]{:S(2)}, u32[]{:S(2)}) %collective-permute-start) | collective-permute-done | bytes 1568 | tf_op jit(solution)/shard_map/ppermute | solution.py:76
  27.6 0.5 convolution_convert_fusion.1
  28.1 1.1 %pad_maximum_fusion = bf16[8,192,384]{2,1,0:T(8,128)(2,1)} fusion(bf16[8,96,384]{2,1,0:T(8,128)(2,1)S(1)} %bitcast.23, bf16[8,96,384]{2,1,0:T(8,128)(2,1)S(1)} %bitcast.22), kind=kLoop, calls=%fused_computation.11 | loop fusion | flops 2359296 | bytes 2359296 | tf_op jit(solution)/shard_map/concatenate | solution.py:91
  29.3 17.5 %all-to-all-done = bf16[8,96,768]{2,1,0:T(8,128)(2,1)} async-done(((bf16[8,96,768]{2,1,0:T(8,128)(2,1)}), bf16[8,96,768]{2,1,0:T(8,128)(2,1)}, u32[]{:S(2)}, u32[]{:S(2)}) %all-to-all-start) | async-done | bytes 1179680 | tf_op jit(solution)/shard_map/all_to_all | solution.py:67
  46.7 4.4 %all-to-all-start.1 = ((bf16[8,192,384]{2,1,0:T(8,128)(2,1)}), bf16[8,192,384]{2,1,0:T(8,128)(2,1)}, u32[]{:S(2)}, u32[]{:S(2)}) async-start(bf16[8,192,384]{2,1,0:T(8,128)(2,1)} %pad_maximum_fusion), calls=%async_computation.1 | async-start | bytes 2359296 | tf_op jit(solution)/shard_map/all_to_all | solution.py:94
  51.2 1.8 %convert_reduce_fusion = (f32[768]{0:T(1024)S(1)}, f32[768]{0:T(1024)S(1)}) fusion(bf16[768,768]{1,0:T(8,128)(2,1)} %bitcast.1), kind=kLoop, calls=%fused_computation.30 | loop fusion | flops 6144 | bytes 12288 | tf_op jit(solution)/shard_map/eq | solution.py:110
  53.1 4.0 %fusion.30 = f32[768,768]{0,1:T(8,128)} fusion(bf16[768,768]{1,0:T(8,128)(2,1)} %bitcast.1), kind=kOutput, calls=%fused_computation.80 | convolution fusion | flops 754974720 | bytes 3342336 | tf_op jit(solution)/shard_map/qe,ke->qk/dot_general | solution.py:108
  57.2 2.2 %slice.76 = bf16[768,640]{1,0:T(8,128)(2,1)} slice(bf16[768,768]{1,0:T(8,128)(2,1)} %bitcast.1), slice={[0:768], [0:640]} | slice | bytes 1966080 | tf_op jit(solution)/shard_map/slice | solution.py:31
  59.4 1.5 %collective-permute-start.5 = (f32[2,768]{1,0:T(2,128)S(1)}, f32[2,768]{1,0:T(2,128)S(1)}, u32[]{:S(2)}, u32[]{:S(2)}) collective-permute-start(f32[2,768]{1,0:T(2,128)S(1)} %pad_maximum_fusion.2), channel_id=1, source_target_pairs={{0,2},{2,0},{1,3},{3,1},{4,6},{6,4},{5,7},{7,5},{8,10},{10,8},{9,1... | collective-permute-start | bytes 18440 | tf_op jit(solution)/shard_map/ppermute | solution.py:87
  61.1 0.5 collective-permute-start.6
  61.7 17.7 %all-to-all-done.1 = bf16[8,192,384]{2,1,0:T(8,128)(2,1)} async-done(((bf16[8,192,384]{2,1,0:T(8,128)(2,1)}), bf16[8,192,384]{2,1,0:T(8,128)(2,1)}, u32[]{:S(2)}, u32[]{:S(2)}) %all-to-all-start.1) | async-done | bytes 1179680 | tf_op jit(solution)/shard_map/all_to_all | solution.py:94
  79.4 1.5 %fusion.32 = (bf16[8,96,384]{2,1,0:T(8,128)(2,1)S(1)}, bf16[8,96,384]{2,1,0:T(8,128)(2,1)S(1)}) fusion(bf16[8,192,384]{2,1,0:T(8,128)(2,1)} %all-to-all-done.1), kind=kLoop, calls=%fused_computation.82 | loop fusion | bytes 2359296 | tf_op jit(solution)/shard_map/slice | solution.py:95
  81.5 1.1 %select_reduce_fusion.2 = f32[768]{0:T(1024)S(1)} fusion(f32[768,768]{0,1:T(8,128)S(1)} %copy-done.3, bf16[768,384]{1,0:T(8,128)(2,1)S(1)} %bitcast.17, f32[768]{0:T(1024)S(1)} %get-tuple-element.6, f32[768]{0:T(1024)S(1)} %get-tuple-element.5, pred[768]{0:T(1024)(128)(4,1)S(1)} %broadcast_compare_fusion), kind=kOutput, calls=%fused_computation.2 | convolution fusion | flops 457112832 | bytes 2959104 | tf_op jit(solution)/shard_map/qe,ke->qk/dot_general | solution.py:109
  82.6 0.5 collective-permute-done.4
  83.0 0.8 fusion.33
  83.8 1.4 %fusion.3 = f32[1536,768]{0,1:T(8,128)S(1)} fusion(bf16[768,384]{1,0:T(8,128)(2,1)S(1)} %bitcast.20, bf16[768,384]{1,0:T(8,128)(2,1)S(1)} %collective-permute-done.4, bf16[768,384]{1,0:T(8,128)(2,1)S(1)} %bitcast.19), kind=kOutput, calls=%fused_computation.12 | convolution fusion | flops 908328960 | bytes 6488064 | tf_op jit(solution)/shard_map/qe,ke->qk/dot_general | solution.py:109
  85.4 4.4 %select_reduce_fusion = f32[1536]{0:T(1024)S(1)} fusion(f32[1536,768]{0,1:T(8,128)S(1)} %fusion.3, bf16[768,640]{1,0:T(8,128)(2,1)} %collective-permute-done.6, f32[1536]{0:T(1024)S(1)} %get-tuple-element.8, f32[1536]{0:T(1024)S(1)} %get-tuple-element.7, f32[768]{0:T(1024)S(1)} %get-tuple-element.12, f32[768]{0:T(1024)S(1)} %get-tuple-element.11, ...), kind=kOutput, calls=%fused_computation | convolution fusion | flops 1522137600 | bytes 7693056 | tf_op jit(solution)/shard_map/qe,ke->qk/dot_general | solution.py:108
  89.9 2.8 %select_reduce_fusion.1 = f32[768]{0:T(1024)S(1)} fusion(f32[768,768]{0,1:T(8,128)S(1)} %fusion.33, bf16[768,640]{1,0:T(8,128)(2,1)} %collective-permute-done.3, f32[768]{0:T(1024)S(1)} %get-tuple-element.6, f32[768]{0:T(1024)S(1)} %get-tuple-element.5, f32[768]{0:T(1024)S(1)} %get-tuple-element.10, f32[768]{0:T(1024)S(1)} %get-tuple-element.9, ...), kind=kOutput, calls=%fused_computation.1 | convolution fusion | flops 759102720 | bytes 4341504 | tf_op jit(solution)/shard_map/qe,ke->qk/dot_general | solution.py:108
  92.8 12.0 %all_to_all.19 = f32[8,1,96]{2,1,0:T(1,128)S(1)} all-to-all(f32[8,1,96]{2,1,0:T(1,128)S(1)} %all_to_all.14), channel_id=1, replica_groups=mesh['grp'=8,'split'=4] {'grp'}, dimensions={0} | all-to-all | bytes 6144 | tf_op jit(solution)/shard_map/all_to_all | solution.py:129
  104.8 0.5 broadcast.146
  105.3 0.7 reduce.25
  106.1 0.8 select_reduce_fusion.3
  (39 shorter events, 1.9 us)
Async XLA Ops:
  0.0 1.9 %copy-start = (bf16[384,4096]{1,0:T(8,128)(2,1)S(1)}, bf16[384,4096]{1,0:T(8,128)(2,1)}, u32[]{:S(2)}) copy-start(bf16[384,4096]{1,0:T(8,128)(2,1)} %param.5) | copy-start | bytes 9437188
  7.9 1.1 %copy-start.2 = (pred[768]{0:T(1024)(128)(4,1)S(1)}, pred[768]{0:T(1024)(128)(4,1)}, u32[]{:S(2)}) copy-start(pred[768]{0:T(1024)(128)(4,1)} %constant.58.clone.1) | copy-start | bytes 2308
  8.0 0.9 copy-start.1
  10.8 35.9 %all-to-all-start = ((bf16[8,96,768]{2,1,0:T(8,128)(2,1)}), bf16[8,96,768]{2,1,0:T(8,128)(2,1)}, u32[]{:S(2)}, u32[]{:S(2)}) async-start(bf16[8,96,768]{2,1,0:T(8,128)(2,1)} %bitcast.21), calls=%async_computation | async-start | bytes 2359296 | tf_op jit(solution)/shard_map/all_to_all | solution.py:67
  19.1 8.6 %collective-permute-start.1 = (bf16[384,384]{1,0:T(8,128)(2,1)S(1)}, bf16[384,384]{1,0:T(8,128)(2,1)S(1)}, u32[]{:S(2)}, u32[]{:S(2)}) collective-permute-start(bf16[384,384]{1,0:T(8,128)(2,1)S(1)} %slice.77), channel_id=1, source_target_pairs={{0,2},{2,0},{1,3},{3,1},{4,6},{6,4},{5,7},{7,5},{8,10},{10,8},{9,1... | collective-permute-start | bytes 884744 | tf_op jit(solution)/shard_map/ppermute | solution.py:75
  20.6 7.0 %collective-permute-start = (s32[384]{0:T(512)S(1)}, s32[384]{0:T(512)S(1)}, u32[]{:S(2)}, u32[]{:S(2)}) collective-permute-start(s32[384]{0:T(512)S(1)} %convert_add_fusion), channel_id=1, source_target_pairs={{0,2},{2,0},{1,3},{3,1},{4,6},{6,4},{5,7},{7,5},{8,10},{10,8},{9,1... | collective-permute-start | bytes 4616 | tf_op jit(solution)/shard_map/ppermute | solution.py:76
  46.7 32.7 %all-to-all-start.1 = ((bf16[8,192,384]{2,1,0:T(8,128)(2,1)}), bf16[8,192,384]{2,1,0:T(8,128)(2,1)}, u32[]{:S(2)}, u32[]{:S(2)}) async-start(bf16[8,192,384]{2,1,0:T(8,128)(2,1)} %pad_maximum_fusion), calls=%async_computation.1 | async-start | bytes 2359296 | tf_op jit(solution)/shard_map/all_to_all | solution.py:94
  53.0 8.6 %collective-permute-start.2 = (f32[2,768]{1,0:T(2,128)S(1)}, f32[2,768]{1,0:T(2,128)S(1)}, u32[]{:S(2)}, u32[]{:S(2)}) collective-permute-start(f32[2,768]{1,0:T(2,128)S(1)} %pad_maximum_fusion.2), channel_id=1, source_target_pairs={{0,1},{1,0},{2,3},{3,2},{4,5},{5,4},{6,7},{7,6},{8,9},{9,8},{10,11... | collective-permute-start | bytes 18440 | tf_op jit(solution)/shard_map/ppermute | solution.py:87
  59.4 21.7 %collective-permute-start.5 = (f32[2,768]{1,0:T(2,128)S(1)}, f32[2,768]{1,0:T(2,128)S(1)}, u32[]{:S(2)}, u32[]{:S(2)}) collective-permute-start(f32[2,768]{1,0:T(2,128)S(1)} %pad_maximum_fusion.2), channel_id=1, source_target_pairs={{0,2},{2,0},{1,3},{3,1},{4,6},{6,4},{5,7},{7,5},{8,10},{10,8},{9,1... | collective-permute-start | bytes 18440 | tf_op jit(solution)/shard_map/ppermute | solution.py:87
  60.9 24.3 %collective-permute-start.3 = (bf16[768,640]{1,0:T(8,128)(2,1)}, bf16[768,640]{1,0:T(8,128)(2,1)}, u32[]{:S(2)}, u32[]{:S(2)}) collective-permute-start(bf16[768,640]{1,0:T(8,128)(2,1)} %slice.76), channel_id=1, source_target_pairs={{0,1},{1,0},{2,3},{3,2},{4,5},{5,4},{6,7},{7,6},{8,9},{9,8},{10,11... | collective-permute-start | bytes 2949128 | tf_op jit(solution)/shard_map/ppermute | solution.py:86
  61.1 24.3 %collective-permute-start.6 = (bf16[768,640]{1,0:T(8,128)(2,1)}, bf16[768,640]{1,0:T(8,128)(2,1)}, u32[]{:S(2)}, u32[]{:S(2)}) collective-permute-start(bf16[768,640]{1,0:T(8,128)(2,1)} %slice.76), channel_id=1, source_target_pairs={{0,2},{2,0},{1,3},{3,1},{4,6},{6,4},{5,7},{7,5},{8,10},{10,8},{9,1... | collective-permute-start | bytes 2949128 | tf_op jit(solution)/shard_map/ppermute | solution.py:86
  79.4 2.0 %copy-start.3 = (f32[768,768]{0,1:T(8,128)S(1)}, f32[768,768]{0,1:T(8,128)}, u32[]{:S(2)}) copy-start(f32[768,768]{0,1:T(8,128)} %fusion.30) | copy-start | bytes 7077892
  81.0 2.1 %collective-permute-start.4 = (bf16[768,384]{1,0:T(8,128)(2,1)S(1)}, bf16[768,384]{1,0:T(8,128)(2,1)S(1)}, u32[]{:S(2)}, u32[]{:S(2)}) collective-permute-start(bf16[768,384]{1,0:T(8,128)(2,1)S(1)} %bitcast.16), channel_id=1, source_target_pairs={{0,1},{1,0},{2,3},{3,2},{4,5},{5,4},{6,7},{7,6},{8,9},{9,8},{10,11... | collective-permute-start | bytes 1769480 | tf_op jit(solution)/shard_map/ppermute | solution.py:97
  89.8 2.9 %collective-permute-start.7 = (f32[768]{0:T(1024)S(1)}, f32[768]{0:T(1024)S(1)}, u32[]{:S(2)}, u32[]{:S(2)}) collective-permute-start(f32[768]{0:T(1024)S(1)} %slice.87), channel_id=1, source_target_pairs={{0,1},{1,0},{2,3},{3,2},{4,5},{5,4},{6,7},{7,6},{8,9},{9,8},{10,11... | collective-permute-start | bytes 9224 | tf_op jit(solution)/shard_map/ppermute | solution.py:124

commit v21 on v16

--- a/solution.py
+++ b/solution.py
@@ -68,7 +68,7 @@
         return got.reshape(n_slot, -1)
 
     if n_split == 4:
-        half = emb_w - 3 * emb_w // 8
+        half = emb_w - emb_w // 4
         cross = [(0, 2), (2, 0), (1, 3), (3, 1)]
         pair = [(0, 1), (1, 0), (2, 3), (3, 2)]
         raw_b = embeds[:, half:]

time: 106 us -> 130 us (1.23)
  waiting for transfers between devices: 40.3 us -> 65.3 us
  local copies, waits for them, and re-layouts: 6.75 us -> 3.42 us
  blocking collectives: 9.64 us -> 11.9 us
    ppermute x1, waiting for transfers between devices: 0.01 us -> 19.3 us  [local(): lax.ppermute(own_m, 'split', cross)]
    all_to_all x1, waiting for transfers between devices: 17.5 us -> 25.1 us  [route(): got = lax.all_to_all(send, 'grp', split_axis=0, concat_axis=0, tiled=True)]
    ppermute x1, waiting for transfers between devices: 0.01 us -> 5.2 us  [local(): par_b = lax.ppermute(raw_b, 'split', cross)]
    ppermute x1, waiting for transfers between devices: 5.02 us -> 0.01 us  [local(): par_place = lax.ppermute(place, 'split', cross)]
    dot_general x4, matrix products: 3.49 us -> 6.79 us  [block_best(): jnp.einsum('qe,ke->qk', qb, kb, preferred_element_type=jnp.float32)]
    dot_general x4, matrix products: 12.7 us -> 9.67 us  [block_best(): scores = jnp.einsum('qe,ke->qk', qa, ka, preferred_element_type=jnp.float32)]
    all_to_all x1, starting transfers between devices: 7.25 us -> 4.27 us  [route(): got = lax.all_to_all(send, 'grp', split_axis=0, concat_axis=0, tiled=True)]
    ppermute x1, starting transfers between devices: 0.5 us -> 3.03 us  [local(): par_place = lax.ppermute(place, 'split', cross)]
  transfers between devices with their start and end apart: 10 -> 10, of which waited for: 3 -> 4; matrix products, arithmetic and copies ran while one was open for 22% -> 20% of each run, Pallas kernels for 0% -> 0%
where the time goes in v21:
time: 130 us
  waiting for transfers between devices  65.3 us (50%)
  matrix products  26.5 us (20%)
  starting transfers between devices  16.8 us (13%)
  blocking collectives  11.9 us (9%)
  other arithmetic  5.59 us (4%)
  local copies, waits for them, and re-layouts  3.42 us (3%)
    all_to_all x1, waiting for transfers between devices, route(): got = lax.all_to_all(send, 'grp', split_axis=0, concat_axis=0, tiled=True)  25.1 us
    ppermute x1, waiting for transfers between devices, local(): lax.ppermute(own_m, 'split', cross)  19.3 us
    all_to_all x1, waiting for transfers between devices, local(): got = lax.all_to_all(send, 'grp', split_axis=0, concat_axis=0, tiled=True)  15.6 us
    all_to_all x1, blocking collectives, local(): lax.all_to_all(best.reshape(n_grp, cap), 'grp', split_axis=0, concat_axis...  11.9 us
    dot_general x4, matrix products, block_best(): scores = jnp.einsum('qe,ke->qk', qa, ka, preferred_element_type=jnp.float32)  9.67 us
    dot_general x4, matrix products, block_best(): jnp.einsum('qe,ke->qk', qb, kb, preferred_element_type=jnp.float32)  6.79 us
    dot_general x1, matrix products, embed_rows(): jnp.einsum('...h,he->...e', rows, weight, preferred_element_type=jnp.floa...  5.94 us
    all_to_all x1, starting transfers between devices, local(): got = lax.all_to_all(send, 'grp', split_axis=0, concat_axis=0, tiled=True)  5.81 us
  transfers between devices with their start and end apart: 10, of which 4 were waited for; matrix products, arithmetic and copies ran while one was open for 20% of the time, Pallas kernels for 0%

profile of v21, /device:TPU:0, one launch (start us, length us, event | category | flops | bytes accessed | tf_op | source)
XLA Modules:
  0.0 129.7 jit_solution(12702487151541492089)
XLA Ops:
  0.0 0.9 fusion.13
  1.1 3.0 %collective-permute-start = (s32[384]{0:T(512)S(1)}, s32[384]{0:T(512)S(1)}, u32[]{:S(2)}, u32[]{:S(2)}) collective-permute-start(s32[384]{0:T(512)S(1)} %convert_add_fusion), channel_id=1, source_target_pairs={{0,2},{2,0},{1,3},{3,1},{4,6},{6,4},{5,7},{7,5},{8,10},{10,8},{9,1... | collective-permute-start | bytes 4616 | tf_op jit(solution)/shard_map/ppermute | solution.py:76
  4.1 5.9 %multiply_reduce_fusion = (f32[384]{0:T(512)S(1)}, f32[384,1024]{1,0:T(8,128)S(1)}) fusion(bf16[384,4096]{1,0:T(8,128)(2,1)S(1)} %copy-done, bf16[4096,1024]{1,0:T(8,128)(2,1)} %param.6), kind=kOutput, calls=%fused_computation.6 | convolution fusion | flops 3222011392 | bytes 13108736 | tf_op jit(solution)/shard_map/...h,he->...e/dot_general | solution.py:14
  10.3 0.8 collective-permute-start.1
  11.1 0.4 convolution_convert_fusion.2
  11.5 5.2 %collective-permute-done.1 = bf16[384,256]{1,0:T(8,128)(2,1)S(1)} collective-permute-done((bf16[384,256]{1,0:T(8,128)(2,1)S(1)}, bf16[384,256]{1,0:T(8,128)(2,1)S(1)}, u32[]{:S(2)}, u32[]{:S(2)}) %collective-permute-start.1) | collective-permute-done | bytes 196640 | tf_op jit(solution)/shard_map/ppermute | solution.py:75
  16.7 0.4 convolution_convert_fusion.1
  17.1 1.0 pad_maximum_fusion
  18.0 5.8 %all-to-all-start.1 = ((bf16[8,192,256]{2,1,0:T(8,128)(2,1)}), bf16[8,192,256]{2,1,0:T(8,128)(2,1)}, u32[]{:S(2)}, u32[]{:S(2)}) async-start(bf16[8,192,256]{2,1,0:T(8,128)(2,1)} %pad_maximum_fusion), calls=%async_computation.1 | async-start | bytes 1572864 | tf_op jit(solution)/shard_map/all_to_all | solution.py:94
  24.2 3.2 %convolution_convert_fusion = bf16[768,896]{1,0:T(8,128)(2,1)} fusion(bf16[384,1024]{1,0:T(8,128)(2,1)} %copy-done.4, bf16[384,128]{1,0:T(8,128)(2,1)S(1)} %select_convert_fusion, pred[896]{0:T(1024)(128)(4,1)S(1)} %copy-done.6, pred[896]{0:T(1024)(128)(4,1)S(1)} %iota_compare_fusion.9, s32[384]{0:T(512)S(1)} %convert_add_fusion), kind=kOutput, calls=%fused_computation.4 | convolution fusion | flops 530153472 | bytes 2166016 | tf_op jit(solution)/shard_map/dot_general | solution.py:65
  27.4 15.6 %all-to-all-done.1 = bf16[8,192,256]{2,1,0:T(8,128)(2,1)} async-done(((bf16[8,192,256]{2,1,0:T(8,128)(2,1)}), bf16[8,192,256]{2,1,0:T(8,128)(2,1)}, u32[]{:S(2)}, u32[]{:S(2)}) %all-to-all-start.1) | async-done | bytes 786464 | tf_op jit(solution)/shard_map/all_to_all | solution.py:94
  43.0 4.3 %all-to-all-start = ((bf16[8,96,896]{2,1,0:T(8,128)(2,1)}), bf16[8,96,896]{2,1,0:T(8,128)(2,1)}, u32[]{:S(2)}, u32[]{:S(2)}) async-start(bf16[8,96,896]{2,1,0:T(8,128)(2,1)} %bitcast.27), calls=%async_computation | async-start | bytes 2752512 | tf_op jit(solution)/shard_map/all_to_all | solution.py:67
  47.3 1.2 fusion.23
  48.5 1.9 %fusion.24 = f32[768,768]{0,1:T(8,128)} fusion(bf16[768,256]{1,0:T(8,128)(2,1)S(1)} %bitcast.22, bf16[768,256]{1,0:T(8,128)(2,1)S(1)} %bitcast.25), kind=kOutput, calls=%fused_computation.72 | convolution fusion | flops 301989888 | bytes 3145728 | tf_op jit(solution)/shard_map/qe,ke->qk/dot_general | solution.py:109
  50.5 2.0 %fusion.26 = f32[768,768]{0,1:T(8,128)} fusion(bf16[768,256]{1,0:T(8,128)(2,1)S(1)} %collective-permute-done.6, bf16[768,256]{1,0:T(8,128)(2,1)S(1)} %bitcast.26), kind=kOutput, calls=%fused_computation.74 | convolution fusion | flops 301989888 | bytes 3145728 | tf_op jit(solution)/shard_map/qe,ke->qk/dot_general | solution.py:109
  52.4 1.9 %fusion.25 = f32[768,768]{0,1:T(8,128)} fusion(bf16[768,256]{1,0:T(8,128)(2,1)S(1)} %bitcast.23, bf16[768,256]{1,0:T(8,128)(2,1)S(1)} %collective-permute-done.6), kind=kOutput, calls=%fused_computation.73 | convolution fusion | flops 301989888 | bytes 3145728 | tf_op jit(solution)/shard_map/qe,ke->qk/dot_general | solution.py:109
  54.3 25.1 %all-to-all-done = bf16[8,96,896]{2,1,0:T(8,128)(2,1)} async-done(((bf16[8,96,896]{2,1,0:T(8,128)(2,1)}), bf16[8,96,896]{2,1,0:T(8,128)(2,1)}, u32[]{:S(2)}, u32[]{:S(2)}) %all-to-all-start) | async-done | bytes 1376288 | tf_op jit(solution)/shard_map/all_to_all | solution.py:67
  79.4 1.8 %convert_reduce_fusion = (f32[768]{0:T(1024)S(1)}, f32[768]{0:T(1024)S(1)}) fusion(bf16[768,896]{1,0:T(8,128)(2,1)} %bitcast.1), kind=kLoop, calls=%fused_computation.24 | loop fusion | flops 6144 | bytes 12288 | tf_op jit(solution)/shard_map/eq | solution.py:110
  81.2 1.3 %slice.65 = bf16[768,768]{1,0:T(8,128)(2,1)S(1)} slice(bf16[768,896]{1,0:T(8,128)(2,1)} %bitcast.1), slice={[0:768], [0:768]} | slice | bytes 2359296 | tf_op jit(solution)/shard_map/slice | solution.py:31
  82.6 1.6 %collective-permute-start.3 = (bf16[768,768]{1,0:T(8,128)(2,1)S(1)}, bf16[768,768]{1,0:T(8,128)(2,1)S(1)}, u32[]{:S(2)}, u32[]{:S(2)}) collective-permute-start(bf16[768,768]{1,0:T(8,128)(2,1)S(1)} %slice.65), channel_id=1, source_target_pairs={{0,2},{2,0},{1,3},{3,1},{4,6},{6,4},{5,7},{7,5},{8,10},{10,8},{9,1... | collective-permute-start | bytes 3538952 | tf_op jit(solution)/shard_map/ppermute | solution.py:86
  84.2 0.6 collective-permute-start.4
  84.8 0.5 collective-permute-start.2
  85.3 2.7 %fusion.21 = f32[768,768]{0,1:T(8,128)S(1)} fusion(bf16[768,896]{1,0:T(8,128)(2,1)} %bitcast.1), kind=kOutput, calls=%fused_computation.69 | convolution fusion | flops 905969664 | bytes 3538944 | tf_op jit(solution)/shard_map/qe,ke->qk/dot_general | solution.py:108
  88.0 1.0 select_reduce_fusion.3
  89.1 19.3 %collective-permute-done.2 = f32[2,768]{1,0:T(2,128)S(1)} collective-permute-done((f32[2,768]{1,0:T(2,128)S(1)}, f32[2,768]{1,0:T(2,128)S(1)}, u32[]{:S(2)}, u32[]{:S(2)}) %collective-permute-start.2) | collective-permute-done | bytes 6176 | tf_op jit(solution)/shard_map/ppermute | solution.py:87
  108.5 1.4 %select_reduce_fusion = f32[768]{0:T(1024)S(1)} fusion(f32[768,768]{0,1:T(8,128)S(1)} %copy-done.3, bf16[768,768]{1,0:T(8,128)(2,1)S(1)} %collective-permute-done.5, bf16[768,768]{1,0:T(8,128)(2,1)S(1)} %collective-permute-done.3, f32[768]{0:T(1024)S(1)} %get-tuple-element.10, f32[768]{0:T(1024)S(1)} %get-tuple-element.9, f32[768]{0:T(1024)S(1)} %get-tuple-element.8, ...), kind=kOutput, calls=%fused_computation | convolution fusion | flops 910097664 | bytes 4734720 | tf_op jit(solution)/shard_map/qe,ke->qk/dot_general | solution.py:108
  110.2 2.8 %select_reduce_fusion.2 = f32[768]{0:T(1024)S(1)} fusion(f32[768,768]{0,1:T(8,128)S(1)} %copy-done.2, bf16[768,768]{1,0:T(8,128)(2,1)S(1)} %collective-permute-done.3, f32[768]{0:T(1024)S(1)} %get-tuple-element.6, f32[768]{0:T(1024)S(1)} %get-tuple-element.5, f32[768]{0:T(1024)S(1)} %get-tuple-element.8, f32[768]{0:T(1024)S(1)} %get-tuple-element.7, ...), kind=kOutput, calls=%fused_computation.2 | convolution fusion | flops 910097664 | bytes 4734720 | tf_op jit(solution)/shard_map/qe,ke->qk/dot_general | solution.py:108
  113.0 2.7 %select_reduce_fusion.1 = f32[768]{0:T(1024)S(1)} fusion(f32[768,768]{0,1:T(8,128)S(1)} %copy-done.1, bf16[768,768]{1,0:T(8,128)(2,1)S(1)} %collective-permute-done.5, f32[768]{0:T(1024)S(1)} %get-tuple-element.6, f32[768]{0:T(1024)S(1)} %get-tuple-element.5, f32[768]{0:T(1024)S(1)} %get-tuple-element.10, f32[768]{0:T(1024)S(1)} %get-tuple-element.9, ...), kind=kOutput, calls=%fused_computation.1 | convolution fusion | flops 910097664 | bytes 4734720 | tf_op jit(solution)/shard_map/qe,ke->qk/dot_general | solution.py:108
  115.8 11.9 %all_to_all.19 = f32[8,1,96]{2,1,0:T(1,128)S(1)} all-to-all(f32[8,1,96]{2,1,0:T(1,128)S(1)} %all_to_all.14), channel_id=1, replica_groups=mesh['grp'=8,'split'=4] {'grp'}, dimensions={0} | all-to-all | bytes 6144 | tf_op jit(solution)/shard_map/all_to_all | solution.py:122
  127.7 0.5 broadcast.144
  128.2 0.7 reduce.21
  129.0 0.8 select_reduce_fusion.4
  (44 shorter events, 1.3 us)
Async XLA Ops:
  0.0 4.1 %copy-start = (bf16[384,4096]{1,0:T(8,128)(2,1)S(1)}, bf16[384,4096]{1,0:T(8,128)(2,1)}, u32[]{:S(2)}) copy-start(bf16[384,4096]{1,0:T(8,128)(2,1)} %param.5) | copy-start | bytes 9437188
  1.1 10.4 %collective-permute-start = (s32[384]{0:T(512)S(1)}, s32[384]{0:T(512)S(1)}, u32[]{:S(2)}, u32[]{:S(2)}) collective-permute-start(s32[384]{0:T(512)S(1)} %convert_add_fusion), channel_id=1, source_target_pairs={{0,2},{2,0},{1,3},{3,1},{4,6},{6,4},{5,7},{7,5},{8,10},{10,8},{9,1... | collective-permute-start | bytes 4616 | tf_op jit(solution)/shard_map/ppermute | solution.py:76
  10.2 0.9 copy-start.4
  10.3 13.6 %copy-start.5 = (s32[384]{0:T(512)S(1)}, s32[384]{0:T(512)}, u32[]{:S(2)}) copy-start(s32[384]{0:T(512)} %param.8) | copy-start | bytes 4612
  10.3 13.9 %copy-start.6 = (pred[896]{0:T(1024)(128)(4,1)S(1)}, pred[896]{0:T(1024)(128)(4,1)}, u32[]{:S(2)}) copy-start(pred[896]{0:T(1024)(128)(4,1)} %constant.58.clone.1) | copy-start | bytes 2692
  10.3 6.4 %collective-permute-start.1 = (bf16[384,256]{1,0:T(8,128)(2,1)S(1)}, bf16[384,256]{1,0:T(8,128)(2,1)S(1)}, u32[]{:S(2)}, u32[]{:S(2)}) collective-permute-start(bf16[384,256]{1,0:T(8,128)(2,1)S(1)} %slice.66), channel_id=1, source_target_pairs={{0,2},{2,0},{1,3},{3,1},{4,6},{6,4},{5,7},{7,5},{8,10},{10,8},{9,1... | collective-permute-start | bytes 589832 | tf_op jit(solution)/shard_map/ppermute | solution.py:75
  18.0 25.0 %all-to-all-start.1 = ((bf16[8,192,256]{2,1,0:T(8,128)(2,1)}), bf16[8,192,256]{2,1,0:T(8,128)(2,1)}, u32[]{:S(2)}, u32[]{:S(2)}) async-start(bf16[8,192,256]{2,1,0:T(8,128)(2,1)} %pad_maximum_fusion), calls=%async_computation.1 | async-start | bytes 1572864 | tf_op jit(solution)/shard_map/all_to_all | solution.py:94
  43.0 36.4 %all-to-all-start = ((bf16[8,96,896]{2,1,0:T(8,128)(2,1)}), bf16[8,96,896]{2,1,0:T(8,128)(2,1)}, u32[]{:S(2)}, u32[]{:S(2)}) async-start(bf16[8,96,896]{2,1,0:T(8,128)(2,1)} %bitcast.27), calls=%async_computation | async-start | bytes 2752512 | tf_op jit(solution)/shard_map/all_to_all | solution.py:67
  48.5 2.0 %collective-permute-start.6 = (bf16[768,256]{1,0:T(8,128)(2,1)S(1)}, bf16[768,256]{1,0:T(8,128)(2,1)S(1)}, u32[]{:S(2)}, u32[]{:S(2)}) collective-permute-start(bf16[768,256]{1,0:T(8,128)(2,1)S(1)} %bitcast.21), channel_id=1, source_target_pairs={{0,1},{1,0},{2,3},{3,2},{4,5},{5,4},{6,7},{7,6},{8,9},{9,8},{10,11... | collective-permute-start | bytes 1179656 | tf_op jit(solution)/shard_map/ppermute | solution.py:97
  82.6 25.9 %collective-permute-start.3 = (bf16[768,768]{1,0:T(8,128)(2,1)S(1)}, bf16[768,768]{1,0:T(8,128)(2,1)S(1)}, u32[]{:S(2)}, u32[]{:S(2)}) collective-permute-start(bf16[768,768]{1,0:T(8,128)(2,1)S(1)} %slice.65), channel_id=1, source_target_pairs={{0,2},{2,0},{1,3},{3,1},{4,6},{6,4},{5,7},{7,5},{8,10},{10,8},{9,1... | collective-permute-start | bytes 3538952 | tf_op jit(solution)/shard_map/ppermute | solution.py:86
  84.2 24.3 %collective-permute-start.5 = (bf16[768,768]{1,0:T(8,128)(2,1)S(1)}, bf16[768,768]{1,0:T(8,128)(2,1)S(1)}, u32[]{:S(2)}, u32[]{:S(2)}) collective-permute-start(bf16[768,768]{1,0:T(8,128)(2,1)S(1)} %slice.65), channel_id=1, source_target_pairs={{0,1},{1,0},{2,3},{3,2},{4,5},{5,4},{6,7},{7,6},{8,9},{9,8},{10,11... | collective-permute-start | bytes 3538952 | tf_op jit(solution)/shard_map/ppermute | solution.py:86
  84.2 4.8 %collective-permute-start.4 = (f32[2,768]{1,0:T(2,128)S(1)}, f32[2,768]{1,0:T(2,128)S(1)}, u32[]{:S(2)}, u32[]{:S(2)}) collective-permute-start(f32[2,768]{1,0:T(2,128)S(1)} %pad_maximum_fusion.1), channel_id=1, source_target_pairs={{0,1},{1,0},{2,3},{3,2},{4,5},{5,4},{6,7},{7,6},{8,9},{9,8},{10,11... | collective-permute-start | bytes 18440 | tf_op jit(solution)/shard_map/ppermute | solution.py:87
  84.8 23.6 %collective-permute-start.2 = (f32[2,768]{1,0:T(2,128)S(1)}, f32[2,768]{1,0:T(2,128)S(1)}, u32[]{:S(2)}, u32[]{:S(2)}) collective-permute-start(f32[2,768]{1,0:T(2,128)S(1)} %pad_maximum_fusion.1), channel_id=1, source_target_pairs={{0,2},{2,0},{1,3},{3,1},{4,6},{6,4},{5,7},{7,5},{8,10},{10,8},{9,1... | collective-permute-start | bytes 18440 | tf_op jit(solution)/shard_map/ppermute | solution.py:87
  88.0 20.5 %copy-start.3 = (f32[768,768]{0,1:T(8,128)S(1)}, f32[768,768]{0,1:T(8,128)}, u32[]{:S(2)}) copy-start(f32[768,768]{0,1:T(8,128)} %fusion.26) | copy-start | bytes 7077892
  108.5 1.7 %copy-start.2 = (f32[768,768]{0,1:T(8,128)S(1)}, f32[768,768]{0,1:T(8,128)}, u32[]{:S(2)}) copy-start(f32[768,768]{0,1:T(8,128)} %fusion.24) | copy-start | bytes 7077892
  110.0 3.0 %copy-start.1 = (f32[768,768]{0,1:T(8,128)S(1)}, f32[768,768]{0,1:T(8,128)}, u32[]{:S(2)}) copy-start(f32[768,768]{0,1:T(8,128)} %fusion.25) | copy-start | bytes 7077892
  110.0 5.7 %collective-permute-start.7 = (f32[768]{0:T(1024)S(1)}, f32[768]{0:T(1024)S(1)}, u32[]{:S(2)}, u32[]{:S(2)}) collective-permute-start(f32[768]{0:T(1024)S(1)} %select_reduce_fusion), channel_id=1, source_target_pairs={{0,1},{1,0},{2,3},{3,2},{4,5},{5,4},{6,7},{7,6},{8,9},{9,8},{10,11... | collective-permute-start | bytes 9224 | tf_op jit(solution)/shard_map/ppermute | solution.py:120
